TPU v7x, 32 devices: a whole 2x2x4 slice. The times are simulated.
32 devices in a mesh: row: 8 (over z, x), col: 4 (over y, core).
Axes of the slice: x: 2, y: 2, z: 4, core: 2. Of those that a mesh axis runs over, the one named last changes fastest.
Arguments:
- eigvecs: bfloat16 [64, 2048, 128], P('row'), may hold values from -0.125 to 0.125
- coupling: bfloat16 [64, 2048, 2, 512], P('row', None, None, 'col'), may hold values from -0.25 to 0.25
- mode_counts: int32 [64], P('row'), may hold values from 32 to 128, as said below
- tree_segments: int32 [64, 2], P('row'), may hold values from 0 to 15, all different within a row; in each aligned block of 8 rows (0 to 7, 8 to 15, ...) at most 2 rows name the same one
- eigvals: float32 [64, 128], P('row'), may hold values from 0.5 to 8
- interface_stiffness: float32 [8192, 8192], P('row', 'col'), as said below
Outputs:
- reduced_ii: float32 [8192, 8192], P('row', 'col')
- reduced_mi: float32 [8192, 8192], P('row', 'col')
- reduced_mm: float32 [8192, 8192], P('row', 'col')
Inputs may be any that keep to these rules, and one draw needn't show every extreme that they name: `mode_counts`: some substructure has exactly 128 live modes. `tree_segments`: each substructure names two different segments; among the 8 substructures of one index of row no segment is named more than 2 times, a bound that some block reaches. `interface_stiffness`: symmetric; its leading 512 x 512 block is positive definite.
All inputs are finite; a program needn't handle non-finite values.
Results may differ from a plain program's by a relative error of at most 0.0003.
Values sent between devices are 32-bit elements; how exact they have to be, the bound alone decides.
No kernel may reach another device: no remote copies, remote signals or barrier semaphores. Data moves between devices by JAX's collectives and lax.ppermute only.
A program may use at most 128 MiB of HBM per device.

v0:
```python
import jax
import jax.numpy as jnp
from jax import lax
from jax.sharding import PartitionSpec as P

MSLOT = 128
PANEL = 512
NSEG = 16


def spread_2(block, axis, source):
    block = jnp.where(lax.axis_index(axis) == source, block, jnp.zeros_like(block))
    return lax.psum(block, axis)


def outer_update(base, left, right):
    contract = (((1,), (1,)), ((), ()))
    return base - lax.dot_general(left, right, contract, precision=lax.Precision.HIGHEST)


def per_device(eigvecs, coupling, mode_counts, tree_segments, eigvals, interface_stiffness):
    highest = lax.Precision.HIGHEST
    row_count = lax.axis_size("row")
    col_count = lax.axis_size("col")
    row_index = lax.axis_index("row")
    col_index = lax.axis_index("col")
    sub_local = eigvecs.shape[0]
    block_width = interface_stiffness.shape[1]
    live_all = jnp.arange(MSLOT, dtype=jnp.int32)[None, :] < mode_counts[:, None]
    pieces = jnp.einsum("sim,sitp->stmp", eigvecs, coupling, preferred_element_type=jnp.float32)
    pieces = pieces * live_all.astype(jnp.float32)[:, None, :, None]
    seg_ids = jnp.arange(NSEG, dtype=jnp.int32)
    seg_match = (tree_segments[:, :, None] == seg_ids[None, None, :]).astype(jnp.float32)
    spread = jnp.einsum("stg,stmp->smgp", seg_match, pieces, precision=highest)
    landed = lax.all_to_all(spread, "col", split_axis=2, concat_axis=3, tiled=True)
    block_mi = landed.reshape(sub_local * MSLOT, block_width)
    head_ii = interface_stiffness[:, :PANEL]
    head_mi = block_mi[:, :PANEL]
    rows_ii, rows_mi = (spread_2(head_ii, "col", 0), spread_2(head_mi, "col", 0))
    corner = spread_2(rows_ii[:PANEL], "row", 0)
    ratio = row_count // col_count
    column_ii = []
    column_mi = []
    for offset in range(ratio):
        part_ii, part_mi = (
            spread_2(rows_ii, "row", ratio * col_index + offset),
            spread_2(rows_mi, "row", ratio * col_index + offset),
        )
        column_ii.append(part_ii)
        column_mi.append(part_mi)
    cols_ii = jnp.concatenate(column_ii, axis=0)
    cols_mi = jnp.concatenate(column_mi, axis=0)
    factor = jnp.linalg.cholesky(corner)
    stacked = jnp.concatenate([rows_ii, rows_mi, cols_ii, cols_mi], axis=0)
    solved = lax.linalg.triangular_solve(
        factor, stacked, left_side=False, lower=True, transpose_a=True
    )
    first = rows_ii.shape[0]
    second = first + rows_mi.shape[0]
    third = second + cols_ii.shape[0]
    low_row_ii = solved[:first]
    low_row_mi = solved[first:second]
    low_col_ii = solved[second:third]
    low_col_mi = solved[third:]
    col_ids = col_index * block_width + jnp.arange(block_width, dtype=jnp.int32)
    in_panel = col_ids[None, :] < PANEL
    padded_ii = jnp.pad(low_row_ii, ((0, 0), (0, block_width - PANEL)))
    padded_mi = jnp.pad(low_row_mi, ((0, 0), (0, block_width - PANEL)))
    reduced_ii = jnp.where(
        in_panel, padded_ii, outer_update(interface_stiffness, low_row_ii, low_col_ii)
    )
    reduced_mi = jnp.where(in_panel, padded_mi, outer_update(block_mi, low_row_mi, low_col_ii))
    diag_values = jnp.where(live_all, eigvals, 1.0).reshape(-1)
    mode_rows = diag_values.shape[0]
    mode_width = low_col_mi.shape[0]
    row_ids = row_index * mode_rows + jnp.arange(mode_rows, dtype=jnp.int32)
    mode_cols = col_index * mode_width + jnp.arange(mode_width, dtype=jnp.int32)
    base_mm = jnp.where(row_ids[:, None] == mode_cols[None, :], diag_values[:, None], 0.0)
    reduced_mm = outer_update(base_mm, low_row_mi, low_col_mi)
    return (reduced_ii, reduced_mi, reduced_mm)


def solution(mesh):
    in_specs = (
        P("row", None, None),
        P("row", None, None, "col"),
        P("row"),
        P("row", None),
        P("row", None),
        P("row", "col"),
    )
    out_specs = (P("row", "col"), P("row", "col"), P("row", "col"))
    return jax.shard_map(
        per_device, mesh=mesh, in_specs=in_specs, out_specs=out_specs, check_vma=False
    )
```

profile of v0, /device:TPU:6, one launch (start us, length us, event | category | flops | bytes accessed | tf_op | source)
XLA Modules:
  0.0 813.0 jit_solution(17704234175735468526)
XLA Ops:
  8.6 7.2 fusion.6
  27.0 6.1 all-to-all-start
  33.1 9.2 %copy.26 = f32[1024,2048]{0,1:T(8,128)} copy(f32[1024,2048]{1,0:T(8,128)} %param.11) | data formatting | bytes 16777216 | tf_op args[5]
  42.4 82.3 %all-to-all-done = f32[8,128,16,128]{3,1,0,2:T(8,128)} async-done(((f32[8,128,16,128]{3,1,0,2:T(8,128)}), f32[8,128,16,128]{3,1,0,2:T(8,128)}, u32[]{:S(2)}, u32[]{:S(2)}) %all-to-all-start) | async-done | bytes 8388640 | tf_op jit(solution)/shard_map/all_to_all | solution.py:35
  124.7 9.9 %copy.29 = f32[8,128,4,4,128]{1,0,4,2,3:T(8,128)} copy(f32[8,128,4,4,128]{4,1,0,3,2:T(8,128)} %bitcast.6) | data formatting | bytes 16777216 | tf_op jit(solution)/shard_map/all_to_all | solution.py:35
  144.5 86.2 %all-reduce.10.cloned.1.call-done = (f32[1024,512]{0,1:T(8,128)}, f32[1024,512]{0,1:T(8,128)}) async-done(((f32[1024,512]{0,1:T(8,128)}, f32[1024,512]{0,1:T(8,128)}), (f32[1024,512]{0,1:T(8,128)}, f32[1024,512]{0,1:T(8,128)})) %all-reduce.10.cloned.1.call-update) | async-done | bytes 4194320 | tf_op jit(solution)/shard_map/psum | solution.py:13
  240.2 301.3 %all-reduce.8.cloned.1.call-done = (f32[1024,512]{0,1:T(8,128)}, f32[1024,512]{0,1:T(8,128)}, f32[1024,512]{0,1:T(8,128)}, f32[1024,512]{0,1:T(8,128)}, f32[512,512]{0,1:T(8,128)}) async-done(((f32[1024,512]{0,1:T(8,128)}, f32[1024,512]{0,1:T(8,128)}, f32[1024,512]{0,1:T(8,128)}, f32[1024,512]{0,1:T(8,128)}, f32[512,512]{0,1:T(8,128)}), (f32[1024,512]{0,1:T(8,128)}, f32[1024,512]{0,1:T(8,128)}, ...) | async-done | bytes 9437200 | tf_op jit(solution)/shard_map/psum | solution.py:13
  544.6 11.7 %cholesky.103 = f32[128,128]{1,0:T(8,128)S(1)} custom-call(f32[128,128]{1,0:T(8,128)S(1)} %cholesky.263), custom_call_target="Cholesky" | custom-call | tf_op jit(solution)/shard_map/jit(cholesky)/cholesky | solution.py:53
  556.4 9.8 %custom-call.30 = f32[1,128,128]{1,2,0:T(8,128)S(1)} custom-call(f32[1,128,128]{2,1,0:T(8,128)S(1)} %get-tuple-element.55), custom_call_target="InvertDiagBlocksLowerTriangular" | custom-call | tf_op jit(solution)/shard_map/jit(cholesky)/cholesky | solution.py:53
  567.1 12.1 %cholesky.215 = f32[128,128]{1,0:T(8,128)S(1)} custom-call(f32[128,128]{1,0:T(8,128)S(1)} %cholesky.267), custom_call_target="Cholesky" | custom-call | tf_op jit(solution)/shard_map/jit(cholesky)/cholesky | solution.py:53
  579.3 9.8 %custom-call.31 = f32[1,128,128]{1,2,0:T(8,128)S(1)} custom-call(f32[1,128,128]{2,1,0:T(8,128)S(1)} %get-tuple-element.53), custom_call_target="InvertDiagBlocksLowerTriangular" | custom-call | tf_op jit(solution)/shard_map/jit(cholesky)/cholesky | solution.py:53
  590.2 11.7 %cholesky.236 = f32[128,128]{1,0:T(8,128)S(1)} custom-call(f32[128,128]{1,0:T(8,128)S(1)} %cholesky.272), custom_call_target="Cholesky" | custom-call | tf_op jit(solution)/shard_map/jit(cholesky)/cholesky | solution.py:53
  602.1 9.8 %custom-call.32 = f32[1,128,128]{1,2,0:T(8,128)S(1)} custom-call(f32[1,128,128]{2,1,0:T(8,128)S(1)} %get-tuple-element.51), custom_call_target="InvertDiagBlocksLowerTriangular" | custom-call | tf_op jit(solution)/shard_map/jit(cholesky)/cholesky | solution.py:53
  612.7 11.9 %cholesky.253 = f32[128,128]{1,0:T(8,128)S(1)} custom-call(f32[128,128]{1,0:T(8,128)S(1)} %convolution_subtract_fusion.4), custom_call_target="Cholesky" | custom-call | tf_op jit(solution)/shard_map/jit(cholesky)/cholesky | solution.py:53
  629.9 8.4 %while.1 = (s32[]{:T(128)}, f32[512,512]{0,1:T(8,128)S(1)}, s32[4,2]{0,1:T(2,128)S(1)}, f32[4,128,128]{2,1,0:T(8,128)S(1)}, s32[]{:T(128)}) while((s32[]{:T(128)}, f32[512,512]{0,1:T(8,128)S(1)}, s32[4,2]{0,1:T(2,128)S(1)}, f32[4,128,128]{2,1,0:T(8,128)S(1)}, s32[]{:T(128)}) %tuple.36), condition=%wide.while_cond, body=%wide.while_body.sunk | while | flops 2 | bytes 393329 | solution.py:55
  638.3 39.3 %custom-call.33 = f32[4,128,128]{1,2,0:T(8,128)S(1)} custom-call(f32[4,128,128]{2,1,0:T(8,128)S(1)} %get-tuple-element.10), custom_call_target="InvertDiagBlocksLowerTriangular" | custom-call | tf_op jit(solution)/shard_map/triangular_solve | solution.py:55
  700.9 7.6 convolution_subtract_fusion.1
  711.4 9.1 %fusion.8 = f32[6144,128]{0,1:T(8,128)S(1)} fusion(f32[6144,128]{0,1:T(8,128)S(1)} %fusion.48, f32[6144,128]{0,1:T(8,128)S(1)} %fusion.49, f32[6144,128]{0,1:T(8,128)S(1)} %fusion.33, f32[6144,512]{0,1:T(8,128)} %constant_dynamic-update-slice_fusion, f32[512,512]{0,1:T(8,128)} %copy-done.4), kind=kOutput, calls=%fused_computation.17 | convolution fusion | flops 3629383680 | bytes 15925248 | tf_op jit(solution)/shard_map/triangular_solve | solution.py:55
  725.2 6.1 pad_maximum_fusion
  732.0 19.0 %subtract_select_fusion = f32[1024,2048]{0,1:T(8,128)} fusion(f32[1024,512]{0,1:T(8,128)S(1)} %get-tuple-element.42, pred[2048]{0:T(1024)(128)(4,1)S(1)} %broadcast_compare_fusion, f32[6144,512]{0,1:T(8,128)} %pad_maximum_fusion, f32[256,8,8,128]{3,2,1,0:T(8,128)S(1)} %bitcast.79), kind=kOutput, calls=%fused_computation.13 | convolution fusion | flops 12889096192 | bytes 25167872 | tf_op jit(solution)/shard_map/dot_general | solution.py:18
  751.0 18.7 %subtract_select_fusion.1 = f32[1024,2048]{0,1:T(8,128)} fusion(f32[1024,2048]{0,1:T(8,128)} %copy.26, f32[1024,512]{0,1:T(8,128)S(1)} %get-tuple-element.43, pred[2048]{0:T(1024)(128)(4,1)S(1)} %broadcast_compare_fusion, f32[6144,512]{0,1:T(8,128)} %pad_maximum_fusion), kind=kOutput, calls=%fused_computation.14 | convolution fusion | flops 12889096192 | bytes 25167872 | tf_op jit(solution)/shard_map/dot_general | solution.py:18
  769.7 9.3 %copy.42 = f32[1024,2048]{1,0:T(8,128)} copy(f32[1024,2048]{0,1:T(8,128)} %subtract_select_fusion.1) | data formatting | bytes 16777216
  779.0 9.1 %copy.43 = f32[1024,2048]{1,0:T(8,128)} copy(f32[1024,2048]{0,1:T(8,128)} %subtract_select_fusion) | data formatting | bytes 16777216
  788.1 17.9 %select_subtract_fusion = f32[1024,2048]{1,0:T(8,128)} fusion(f32[1024]{0:T(1024)S(1)} %select_bitcast_fusion.3, s32[2048]{0:T(1024)S(1)} %iota_add_fusion, s32[1024]{0:T(1024)S(1)} %iota_add_fusion.1, f32[6144,128]{0,1:T(8,128)} %copy-done.2, f32[6144,128]{0,1:T(8,128)} %copy-done.1, f32[6144,128]{0,1:T(8,128)} %copy-done, f32[6144,128]{0,1:T(8,128)S(1)} %fusion.33), kind=kOutput, calls=%fused_computation.12 | convolution fusion | flops 12895911936 | bytes 20987904 | tf_op jit(solution)/shard_map/dot_general | solution.py:18
  (106 shorter events, 80.6 us)
Async XLA Ops:
  27.0 97.7 %all-to-all-start = ((f32[8,128,16,128]{3,1,0,2:T(8,128)}), f32[8,128,16,128]{3,1,0,2:T(8,128)}, u32[]{:S(2)}, u32[]{:S(2)}) async-start(f32[8,128,16,128]{3,1,0,2:T(8,128)} %copy.28), calls=%async_computation | async-start | bytes 16777216 | tf_op jit(solution)/shard_map/all_to_all | solution.py:35
  33.1 197.6 %all-reduce.10.cloned.1.call-start = ((), (), s32[]{:S(2)}) async-start(), calls=%async_computation.2 | async-start | bytes 8388608 | tf_op jit(solution)/shard_map/psum | solution.py:13
  144.3 397.3 %all-reduce.8.cloned.1.call-start = ((), (), s32[]{:S(2)}) async-start(), calls=%async_computation.1 | async-start | bytes 18874368 | tf_op jit(solution)/shard_map/psum | solution.py:13
  230.7 2.4 copy-start.3
  233.2 3.2 copy-start.5
  239.5 0.7 copy-start.8
  239.5 0.7 copy-start.9
  638.3 45.8 %copy-start.4 = (f32[512,512]{0,1:T(8,128)}, f32[512,512]{0,1:T(8,128)S(1)}, u32[]{:S(2)}) copy-start(f32[512,512]{0,1:T(8,128)S(1)} %get-tuple-element.131) | copy-start | bytes 3145732
  680.8 3.3 copy-start.7
  684.1 2.3 copy-start.6
  700.8 23.2 %copy-start = (f32[6144,128]{0,1:T(8,128)}, f32[6144,128]{0,1:T(8,128)S(1)}, u32[]{:S(2)}) copy-start(f32[6144,128]{0,1:T(8,128)S(1)} %fusion.49) | copy-start | bytes 9437188
  711.4 12.7 %copy-start.1 = (f32[6144,128]{0,1:T(8,128)}, f32[6144,128]{0,1:T(8,128)S(1)}, u32[]{:S(2)}) copy-start(f32[6144,128]{0,1:T(8,128)S(1)} %fusion.48) | copy-start | bytes 9437188
  723.5 1.7 copy-start.2
  723.5 7.9 slice-start
  725.2 6.8 slice-start.1
Sparse Core Ops, SparseCore 0:
  144.4 86.2 all-reduce.9
  239.6 301.8 all-reduce.7
where the time goes:
time: 823 us; the launch traced here: 813 us
  waiting for transfers between devices  470 us (57%)
  other arithmetic  141 us (17%)
  matrix products  105 us (13%)
  local copies, waits for them, and re-layouts  73.6 us (9%)
  between operations  17.2 us (2%)
    psum x2, waiting for transfers between devices, spread_2(): return lax.psum(block, axis)  388 us
    all_to_all x1, waiting for transfers between devices, per_device(): lax.all_to_all(spread, 'col', split_axis=2, concat_axis=3, tiled=True)  82.3 us
    another operation x15, other arithmetic, per_device(): factor = jnp.linalg.cholesky(corner)  79.5 us
    dot_general x3, matrix products, outer_update(): lax.dot_general(left, right, contract, precision=lax.Precision.HIGHEST)  55.5 us
    another operation x4, other arithmetic, per_device(): lax.linalg.triangular_solve(factor, stacked, left_side=False, lower=True,...  45.6 us
    unnamed x32, local copies, waits for them, and re-layouts  45.1 us
    another operation x7, matrix products, per_device(): lax.linalg.triangular_solve(factor, stacked, left_side=False, lower=True,...  35.5 us
  transfers between devices with their start and end apart: 3, of which 3 were waited for; matrix products, arithmetic and copies ran while one was open for 1% of the time, Pallas kernels for 0%

commit v1 on v0

v1 whole, which is shorter than its diff:
```python
import jax
import jax.numpy as jnp
from jax import lax
from jax.sharding import PartitionSpec as P

MSLOT = 128
PANEL = 512
MOST = 2
SUB_ROW = 8

AXES = ("row", "col")


def dot_t(left, right, precision):
    contract = (((1,), (1,)), ((), ()))
    return lax.dot_general(left, right, contract, precision=precision)


def pick(index, options):
    out = options[0]
    for i in range(1, len(options)):
        out = jnp.where(index == i, options[i], out)
    return out


def seg0_slots(tseg, cap0):
    has0 = jnp.any(tseg == 0, axis=1)
    rank0 = jnp.cumsum(has0.astype(jnp.int32)) - 1
    slot = jnp.where(has0, rank0, cap0)
    return has0, rank0, slot


def per_device(eigvecs, coupling, mode_counts, tree_segments, eigvals, stiff):
    high = lax.Precision.HIGH
    R = lax.axis_size("row")
    C = lax.axis_size("col")
    r = lax.axis_index("row")
    c = lax.axis_index("col")
    nsub = eigvecs.shape[0]
    H, W = stiff.shape
    Ec = coupling.shape[3]
    G = W // PANEL
    ratio = R // C
    npair = 2 * nsub
    cap = min(MOST * G * ((nsub + SUB_ROW - 1) // SUB_ROW), npair)
    cap0 = min(MOST * ((nsub + SUB_ROW - 1) // SUB_ROW), nsub)

    live = jnp.arange(MSLOT, dtype=jnp.int32)[None, :] < mode_counts[:, None]
    pieces = jnp.einsum("sim,sitp->stmp", eigvecs, coupling, preferred_element_type=jnp.float32)
    pieces = pieces * live.astype(jnp.float32)[:, None, :, None]
    flat = pieces.reshape(npair, MSLOT, Ec)
    flat_pad = jnp.concatenate([flat, jnp.zeros((1, MSLOT, Ec), jnp.float32)], axis=0)

    tseg = tree_segments
    dest = (tseg // G).reshape(npair)
    onehot = dest[:, None] == jnp.arange(C, dtype=jnp.int32)[None, :]
    rank_pd = jnp.cumsum(onehot.astype(jnp.int32), axis=0) - 1
    rank = jnp.sum(jnp.where(onehot, rank_pd, 0), axis=1)
    match = onehot[:, :, None] & (rank_pd[:, :, None] == jnp.arange(cap, dtype=jnp.int32)[None, None, :])
    send_idx = jnp.where(jnp.any(match, axis=0), jnp.argmax(match, axis=0), npair)
    send = flat_pad[send_idx]
    recv = lax.all_to_all(send, "col", 0, 0, tiled=True)
    recv_pad = jnp.concatenate([recv, jnp.zeros((C, 1, MSLOT, Ec), jnp.float32)], axis=1)
    my_seg = c * G + jnp.arange(G, dtype=jnp.int32)
    seg_hit = tseg[:, :, None] == my_seg[None, None, :]
    rank2 = rank.reshape(nsub, 2)
    slot_tab = jnp.where(
        jnp.any(seg_hit, axis=1), jnp.sum(jnp.where(seg_hit, rank2[:, :, None], 0), axis=1), cap
    )
    gathered = recv_pad[:, slot_tab]
    block_mi = gathered.transpose(1, 3, 2, 0, 4).reshape(nsub * MSLOT, W)

    has0, rank0, slot_r = seg0_slots(tseg, cap0)
    t0 = jnp.where(tseg[:, 0] == 0, 0, 1)
    sel = has0[:, None] & (rank0[:, None] == jnp.arange(cap0, dtype=jnp.int32)[None, :])
    sel_sub = jnp.argmax(sel, axis=0)
    zidx = jnp.where(jnp.any(sel, axis=0), sel_sub * 2 + t0[sel_sub], npair)
    z_local = flat_pad[zidx]
    z_all = lax.all_gather(z_local, "col", axis=0, tiled=False)
    z_rows = z_all.transpose(1, 2, 0, 3).reshape(cap0 * MSLOT, C * Ec)

    kpp_src = stiff[:PANEL, :PANEL]
    rs = PANEL // R
    got = [kpp_src[:rs]]
    for i in range(1, R):
        got.append(lax.ppermute(kpp_src[i * rs:(i + 1) * rs], AXES, [(0, i * C)]))
    kpp_part = pick(r, got)
    kpp_col0 = lax.all_gather(kpp_part, "row", axis=0, tiled=True)
    cs = PANEL // C
    got = [kpp_col0[:cs]]
    for k in range(1, C):
        got.append(lax.ppermute(kpp_col0[k * cs:(k + 1) * cs], AXES, [(i * C, i * C + k) for i in range(R)]))
    kpp = lax.all_gather(pick(c, got), "col", axis=0, tiled=True)

    m_src = stiff[:, :PANEL]
    rps = W // R
    zps = cap0 * MSLOT // C
    got = [m_src[:rps]]
    for k in range(1, C):
        got.append(lax.ppermute(m_src[k * rps:(k + 1) * rps], AXES, [(i * C, i * C + k) for i in range(R)]))
    m_row = lax.all_gather(pick(c, got), "col", axis=0, tiled=True)
    got = []
    for k in range(C):
        payload = jnp.concatenate([m_src[k * rps:(k + 1) * rps], z_rows[k * zps:(k + 1) * zps]], axis=0)
        perm = [(i * C, ((i % ratio) * C + k) * C + i // ratio) for i in range(R)]
        got.append(lax.ppermute(payload, AXES, perm))
    col_parts = lax.all_gather(pick(r % C, got), "row", axis=0, tiled=False)
    m_col = col_parts[:, :rps].reshape(W, PANEL)
    z_col = col_parts[:, rps:].reshape(ratio * cap0 * MSLOT, PANEL)

    tseg_all = lax.all_gather(tseg, "row", axis=0, tiled=False)
    tseg_c = lax.dynamic_slice_in_dim(tseg_all, c * ratio, ratio, axis=0)
    slot_c = []
    for j in range(ratio):
        has_j, rank_j, _ = seg0_slots(tseg_c[j], cap0)
        slot_c.append(jnp.where(has_j, j * cap0 + rank_j, ratio * cap0))
    slot_c = jnp.concatenate(slot_c)

    factor = jnp.linalg.cholesky(kpp)
    stacked = jnp.concatenate([m_row, m_col, z_rows, z_col], axis=0)
    solved = lax.linalg.triangular_solve(factor, stacked, left_side=False, lower=True, transpose_a=True)
    low_r = solved[:H]
    low_c = solved[H:H + W]
    lowmi_r = solved[H + W:H + W + cap0 * MSLOT]
    lowmi_c = solved[H + W + cap0 * MSLOT:]

    col_ids = c * W + jnp.arange(W, dtype=jnp.int32)
    in_panel = col_ids[None, :] < PANEL
    reduced_ii = jnp.where(
        in_panel, jnp.pad(low_r, ((0, 0), (0, W - PANEL))), stiff - dot_t(low_r, low_c, high)
    )

    upd = dot_t(lowmi_r, low_c, high).reshape(cap0, MSLOT, W)
    upd = jnp.concatenate([upd, jnp.zeros((1, MSLOT, W), jnp.float32)], axis=0)
    upd_full = upd[slot_r].reshape(nsub * MSLOT, W)
    lmi = jnp.concatenate(
        [lowmi_r.reshape(cap0, MSLOT, PANEL), jnp.zeros((1, MSLOT, PANEL), jnp.float32)], axis=0
    )
    lmi_full = lmi[slot_r].reshape(nsub * MSLOT, PANEL)
    reduced_mi = jnp.where(
        in_panel, jnp.pad(lmi_full, ((0, 0), (0, W - PANEL))), block_mi - upd_full
    )

    nc = ratio * cap0
    vv = dot_t(lowmi_r, lowmi_c, high).reshape(cap0, MSLOT, nc, MSLOT)
    vv = jnp.pad(vv, ((0, 1), (0, 0), (0, 1), (0, 0)))
    vv_full = vv[slot_r][:, :, slot_c].reshape(nsub * MSLOT, ratio * nsub * MSLOT)
    diag_values = jnp.where(live, eigvals, 1.0).reshape(-1)
    mode_rows = diag_values.shape[0]
    mode_width = ratio * nsub * MSLOT
    row_ids = r * mode_rows + jnp.arange(mode_rows, dtype=jnp.int32)
    mode_cols = c * mode_width + jnp.arange(mode_width, dtype=jnp.int32)
    base_mm = jnp.where(row_ids[:, None] == mode_cols[None, :], diag_values[:, None], 0.0)
    reduced_mm = base_mm - vv_full
    return (reduced_ii, reduced_mi, reduced_mm)


def solution(mesh):
    in_specs = (
        P("row", None, None),
        P("row", None, None, "col"),
        P("row"),
        P("row", None),
        P("row", None),
        P("row", "col"),
    )
    out_specs = (P("row", "col"), P("row", "col"), P("row", "col"))
    return jax.shard_map(
        per_device, mesh=mesh, in_specs=in_specs, out_specs=out_specs, check_vma=False
    )
```

time: 823 us -> 508 us (0.62)
  waiting for transfers between devices: 470 us -> 87.3 us
  matrix products: 105 us -> 60.8 us
  local copies, waits for them, and re-layouts: 73.6 us -> 114 us
  blocking collectives: 0 us -> 31.9 us
  other arithmetic: 141 us -> 166 us
  starting transfers between devices: 6.33 us -> 21.7 us
    psum x2 -> x0, waiting for transfers between devices: 388 us -> none  [spread_2(): return lax.psum(block, axis)]
    all_to_all x1, waiting for transfers between devices: 82.3 us -> 0.01 us  [per_device(): recv = lax.all_to_all(send, 'col', 0, 0, tiled=True)]
    ppermute x0 -> x17, waiting for transfers between devices: none -> 50.6 us  [the longest x4 49.1 us: per_device(): got.append(lax.ppermute(payload, AXES, perm))]
    dot_general x4 -> x3, matrix products: 60.1 us -> 20.6 us  [dot_t(): return lax.dot_general(left, right, contract, precision=precision)]
    all_gather x0 -> x4, waiting for transfers between devices: none -> 36.6 us  [the longest x1 36.6 us: per_device(): kpp_col0 = lax.all_gather(kpp_part, 'row', axis=0, tiled=True)]
    all_gather x0 -> x2, blocking collectives: none -> 31.9 us  [the longest x1 22.7 us: per_device(): tseg_all = lax.all_gather(tseg, 'row', axis=0, tiled=False)]
    gather x0 -> x9, local copies, waits for them, and re-layouts: none -> 27.4 us  [the longest x3 14.5 us: per_device(): vv[slot_r][:, :, slot_c].reshape(nsub * MSLOT, ratio * nsub * MSLOT)]
    ppermute x0 -> x17, starting transfers between devices: none -> 17 us  [the longest x7 4.67 us: per_device(): got.append(lax.ppermute(kpp_src[i * rs:(i + 1) * rs], AXES, [(0, i * C)]))]
  transfers between devices with their start and end apart: 3 -> 22, of which waited for: 3 -> 3; matrix products, arithmetic and copies ran while one was open for 1% -> 42% of each run, Pallas kernels for 0% -> 0%
where the time goes in v1:
time: 508 us; the launch traced here: 499 us
  other arithmetic  166 us (33%)
  local copies, waits for them, and re-layouts  114 us (22%)
  waiting for transfers between devices  87.3 us (17%)
  matrix products  60.8 us (12%)
  blocking collectives  31.9 us (6%)
  starting transfers between devices  21.7 us (4%)
  between operations  17.6 us (3%)
    another operation x14, other arithmetic, per_device(): factor = jnp.linalg.cholesky(kpp)  89.1 us
    ppermute x4, waiting for transfers between devices, per_device(): got.append(lax.ppermute(payload, AXES, perm))  49.1 us
    another operation x4, other arithmetic, per_device(): lax.linalg.triangular_solve(factor, stacked, left_side=False, lower=True,...  40 us
    all_gather x1, waiting for transfers between devices, per_device(): kpp_col0 = lax.all_gather(kpp_part, 'row', axis=0, tiled=True)  36.6 us
    unnamed x28, local copies, waits for them, and re-layouts  35.3 us
    another operation x7, matrix products, per_device(): lax.linalg.triangular_solve(factor, stacked, left_side=False, lower=True,...  31.1 us
    all_gather x1, blocking collectives, per_device(): tseg_all = lax.all_gather(tseg, 'row', axis=0, tiled=False)  22.7 us
    dot_general x3, matrix products, dot_t(): return lax.dot_general(left, right, contract, precision=precision)  20.6 us
  transfers between devices with their start and end apart: 22, of which 3 were waited for; matrix products, arithmetic and copies ran while one was open for 42% of the time, Pallas kernels for 0%

profile of v1, /device:TPU:6, one launch (start us, length us, event | category | flops | bytes accessed | tf_op | source)
XLA Modules:
  0.0 499.3 jit_solution(14517924495313933292)
XLA Ops:
  20.3 7.2 %fusion.25 = f32[8,2,128,128]{3,2,1,0:T(8,128)S(1)} fusion(bf16[8,2048,128]{2,1,0:T(8,128)(2,1)} %param.6, bf16[8,2048,2,128]{3,2,1,0:T(2,128)(2,1)} %param.7, f32[8,128]{1,0:T(8,128)S(1)} %fusion.58), kind=kOutput, calls=%fused_computation.41 | convolution fusion | flops 1074003968 | bytes 13635584 | tf_op jit(solution)/shard_map/sim,sitp->stmp/dot_general | solution.py:49
  30.4 36.6 %all-gather.11.cloned.1.call-done = f32[512,512]{1,0:T(8,128)} async-done(((f32[64,512]{1,0:T(8,128)}), f32[512,512]{1,0:T(8,128)}) %all-gather.11.cloned.1.call-update) | async-done | bytes 1048592 | tf_op jit(solution)/shard_map/all_gather | solution.py:88
  71.2 9.2 %all-gather = f32[8,128,128]{2,1,0:T(8,128)S(1)} all-gather(f32[2,128,128]{2,1,0:T(8,128)S(1)} %gather_fusion.1), channel_id=2, replica_groups=mesh['row'=8,'col'=4] {'col'}, dimensions={0}, use_global_device_ids=true | all-gather | bytes 655360 | tf_op jit(solution)/shard_map/all_gather | solution.py:79
  103.1 49.1 %collective-permute-done.5 = f32[320,512]{1,0:T(8,128)} collective-permute-done((f32[320,512]{1,0:T(8,128)}, f32[320,512]{1,0:T(8,128)}, u32[]{:S(2)}, u32[]{:S(2)}) %collective-permute-start.5) | collective-permute-done | bytes 655392 | tf_op jit(solution)/shard_map/ppermute | solution.py:106
  162.8 22.7 %all-gather.3 = s32[8,8,2]{1,2,0:T(2,128)S(1)} all-gather(s32[1,8,2]{1,2,0:T(2,128)S(1)} %bitcast.144), channel_id=4, replica_groups=mesh['row'=8,'col'=4] {'row'}, dimensions={0}, use_global_device_ids=true | all-gather | bytes 576 | tf_op jit(solution)/shard_map/all_gather | solution.py:111
  185.7 9.3 %copy.124 = f32[1024,2048]{0,1:T(8,128)} copy(f32[1024,2048]{1,0:T(8,128)} %param.11) | data formatting | bytes 16777216 | tf_op args[5]
  202.5 10.1 %copy.133 = f32[8,128,4,4,128]{1,0,4,3,2:T(8,128)} copy(f32[8,128,4,4,128]{4,1,3,2,0:T(8,128)} %bitcast.128) | data formatting | bytes 16777216 | tf_op jit(solution)/shard_map/transpose | solution.py:71
  215.7 11.7 %cholesky.104 = f32[128,128]{1,0:T(8,128)S(1)} custom-call(f32[128,128]{1,0:T(8,128)S(1)} %cholesky.266), custom_call_target="Cholesky" | custom-call | tf_op jit(solution)/shard_map/jit(cholesky)/cholesky | solution.py:119
  227.6 9.8 %custom-call.30 = f32[1,128,128]{1,2,0:T(8,128)S(1)} custom-call(f32[1,128,128]{2,1,0:T(8,128)S(1)} %get-tuple-element.74), custom_call_target="InvertDiagBlocksLowerTriangular" | custom-call | tf_op jit(solution)/shard_map/jit(cholesky)/cholesky | solution.py:119
  238.1 11.7 %cholesky.217 = f32[128,128]{1,0:T(8,128)S(1)} custom-call(f32[128,128]{1,0:T(8,128)S(1)} %cholesky.270), custom_call_target="Cholesky" | custom-call | tf_op jit(solution)/shard_map/jit(cholesky)/cholesky | solution.py:119
  249.8 20.5 %custom-call.31 = f32[1,128,128]{1,2,0:T(8,128)S(1)} custom-call(f32[1,128,128]{2,1,0:T(8,128)S(1)} %get-tuple-element.71), custom_call_target="InvertDiagBlocksLowerTriangular" | custom-call | tf_op jit(solution)/shard_map/jit(cholesky)/cholesky | solution.py:119
  271.1 11.7 %cholesky.238 = f32[128,128]{1,0:T(8,128)S(1)} custom-call(f32[128,128]{1,0:T(8,128)S(1)} %cholesky.275), custom_call_target="Cholesky" | custom-call | tf_op jit(solution)/shard_map/jit(cholesky)/cholesky | solution.py:119
  282.8 9.8 %custom-call.32 = f32[1,128,128]{1,2,0:T(8,128)S(1)} custom-call(f32[1,128,128]{2,1,0:T(8,128)S(1)} %get-tuple-element.68), custom_call_target="InvertDiagBlocksLowerTriangular" | custom-call | tf_op jit(solution)/shard_map/jit(cholesky)/cholesky | solution.py:119
  293.2 11.7 %cholesky.255 = f32[128,128]{1,0:T(8,128)S(1)} custom-call(f32[128,128]{1,0:T(8,128)S(1)} %convolution_subtract_fusion.2), custom_call_target="Cholesky" | custom-call | tf_op jit(solution)/shard_map/jit(cholesky)/cholesky | solution.py:119
  309.6 8.0 %while.1 = (s32[]{:T(128)}, f32[512,512]{1,0:T(8,128)S(1)}, s32[4,2]{0,1:T(2,128)S(1)}, f32[4,128,128]{2,1,0:T(8,128)S(1)}, s32[]{:T(128)}) while((s32[]{:T(128)}, f32[512,512]{1,0:T(8,128)S(1)}, s32[4,2]{0,1:T(2,128)S(1)}, f32[4,128,128]{2,1,0:T(8,128)S(1)}, s32[]{:T(128)}) %tuple.62), condition=%wide.while_cond, body=%wide.while_body.sunk | while | flops 2 | bytes 131189 | solution.py:121
  317.7 39.3 %custom-call.33 = f32[4,128,128]{1,2,0:T(8,128)S(1)} custom-call(f32[4,128,128]{2,1,0:T(8,128)S(1)} %get-tuple-element.14), custom_call_target="InvertDiagBlocksLowerTriangular" | custom-call | tf_op jit(solution)/shard_map/triangular_solve | solution.py:121
  374.8 7.9 %fusion.14 = f32[3840,128]{1,0:T(8,128)S(1)} fusion(f32[3840,128]{0,1:T(8,128)S(1)} %fusion.22, f32[3840,128]{0,1:T(8,128)S(1)} %fusion.23, f32[512,512]{1,0:T(8,128)} %copy-done.4), kind=kOutput, calls=%fused_computation.29 | convolution fusion | flops 1510932480 | bytes 6029312 | tf_op jit(solution)/shard_map/triangular_solve | solution.py:121
  384.6 11.3 %fusion.3 = f32[3840,128]{1,0:T(8,128)S(1)} fusion(f32[3840,128]{0,1:T(8,128)S(1)} %fusion.21, f32[3840,128]{0,1:T(8,128)S(1)} %fusion.22, f32[3840,128]{0,1:T(8,128)S(1)} %fusion.23, f32[512,512]{1,0:T(8,128)} %copy-done.4), kind=kOutput, calls=%fused_computation.18 | convolution fusion | flops 2267873280 | bytes 8060928 | tf_op jit(solution)/shard_map/triangular_solve | solution.py:121
  409.7 14.3 %subtract_select_fusion = f32[1024,2048]{0,1:T(8,128)} fusion(f32[1024,2048]{0,1:T(8,128)} %copy.124, f32[1024,512]{0,1:T(8,128)S(1)} %slice-done, pred[2048]{0:T(1024)(128)(4,1)S(1)} %broadcast_compare_fusion, f32[3840,512]{0,1:T(8,128)} %copy-done.2), kind=kOutput, calls=%fused_computation.15 | convolution fusion | flops 6446645248 | bytes 25167872 | tf_op jit(solution)/shard_map/dot_general | solution.py:16
  424.0 9.1 %copy.137 = f32[1024,2048]{1,0:T(8,128)} copy(f32[1024,2048]{0,1:T(8,128)} %subtract_select_fusion) | data formatting | bytes 16777216
  439.6 9.3 %copy.143 = f32[1024,2048]{0,1:T(8,128)} copy(f32[1024,2048]{1,0:T(8,128)} %bitcast.130) | data formatting | bytes 16777216 | tf_op jit(solution)/shard_map/reshape | solution.py:135
  451.8 10.2 %fusion = f32[1024,2048]{0,1:T(8,128)} fusion(f32[1024,2048]{0,1:T(8,128)} %copy.143, f32[256,8,8,128]{3,2,1,0:T(8,128)} %bitcast.131, f32[1024,512]{0,1:T(8,128)} %copy.142, pred[2048]{0:T(1024)(128)(4,1)S(1)} %broadcast_compare_fusion), kind=kLoop, calls=%fused_computation.12 | loop fusion | flops 4194304 | bytes 27265024 | tf_op jit(solution)/shard_map/jit(_where)/select_n | solution.py:140
  462.0 9.2 %copy.138 = f32[1024,2048]{1,0:T(8,128)} copy(f32[1024,2048]{0,1:T(8,128)} %fusion) | data formatting | bytes 16777216
  478.8 8.1 %copy.136 = f32[8,128,16,128]{3,2,1,0:T(8,128)S(1)} copy(f32[8,128,16,128]{3,1,0,2:T(8,128)} %bitcast.129) | data formatting | bytes 16777216 | tf_op jit(solution)/shard_map/gather | solution.py:147
  (198 shorter events, 131.8 us)
Async XLA Ops:
  7.2 59.8 %all-gather.11.cloned.1.call-start = ((), (), s32[]{:S(2)}) async-start(), calls=%async_computation.2 | async-start | bytes 1179648 | tf_op jit(solution)/shard_map/all_gather | solution.py:88
  8.5 5.9 %collective-permute-start.7 = (f32[64,512]{1,0:T(8,128)S(1)}, f32[64,512]{1,0:T(8,128)S(1)}, u32[]{:S(2)}, u32[]{:S(2)}) collective-permute-start(f32[64,512]{1,0:T(8,128)S(1)} %get-tuple-element.51), channel_id=1, source_target_pairs={{0,28}} | collective-permute-start | bytes 393224 | tf_op jit(solution)/shard_map/ppermute | solution.py:86
  9.2 5.9 %collective-permute-start.8 = (f32[64,512]{1,0:T(8,128)S(1)}, f32[64,512]{1,0:T(8,128)S(1)}, u32[]{:S(2)}, u32[]{:S(2)}) collective-permute-start(f32[64,512]{1,0:T(8,128)S(1)} %get-tuple-element.50), channel_id=1, source_target_pairs={{0,24}} | collective-permute-start | bytes 393224 | tf_op jit(solution)/shard_map/ppermute | solution.py:86
  9.9 5.9 %collective-permute-start.9 = (f32[64,512]{1,0:T(8,128)S(1)}, f32[64,512]{1,0:T(8,128)S(1)}, u32[]{:S(2)}, u32[]{:S(2)}) collective-permute-start(f32[64,512]{1,0:T(8,128)S(1)} %get-tuple-element.49), channel_id=1, source_target_pairs={{0,20}} | collective-permute-start | bytes 393224 | tf_op jit(solution)/shard_map/ppermute | solution.py:86
  10.6 6.7 %collective-permute-start.10 = (f32[64,512]{1,0:T(8,128)S(1)}, f32[64,512]{1,0:T(8,128)S(1)}, u32[]{:S(2)}, u32[]{:S(2)}) collective-permute-start(f32[64,512]{1,0:T(8,128)S(1)} %get-tuple-element.48), channel_id=1, source_target_pairs={{0,16}} | collective-permute-start | bytes 393224 | tf_op jit(solution)/shard_map/ppermute | solution.py:86
  11.3 7.3 %collective-permute-start.11 = (f32[64,512]{1,0:T(8,128)S(1)}, f32[64,512]{1,0:T(8,128)S(1)}, u32[]{:S(2)}, u32[]{:S(2)}) collective-permute-start(f32[64,512]{1,0:T(8,128)S(1)} %get-tuple-element.47), channel_id=1, source_target_pairs={{0,12}} | collective-permute-start | bytes 393224 | tf_op jit(solution)/shard_map/ppermute | solution.py:86
  14.4 4.2 collective-permute-start.12
  15.1 3.5 collective-permute-start.13
  15.8 82.1 %collective-permute-start = (f32[256,512]{1,0:T(8,128)}, f32[256,512]{1,0:T(8,128)}, u32[]{:S(2)}, u32[]{:S(2)}) collective-permute-start(f32[256,512]{1,0:T(8,128)} %get-tuple-element.56), channel_id=1, source_target_pairs={{0,3},{4,7},{8,11},{12,15},{16,19},{20,23},{24,27},{28,31}} | collective-permute-start | bytes 1572872 | tf_op jit(solution)/shard_map/ppermute | solution.py:100
  17.3 82.0 %collective-permute-start.1 = (f32[256,512]{1,0:T(8,128)}, f32[256,512]{1,0:T(8,128)}, u32[]{:S(2)}, u32[]{:S(2)}) collective-permute-start(f32[256,512]{1,0:T(8,128)} %get-tuple-element.55), channel_id=1, source_target_pairs={{0,2},{4,6},{8,10},{12,14},{16,18},{20,22},{24,26},{28,30}} | collective-permute-start | bytes 1572872 | tf_op jit(solution)/shard_map/ppermute | solution.py:100
  20.3 192.4 %all-gather.13.cloned.1.call-start = ((), (), s32[]{:S(2)}) async-start(), calls=%async_computation.3 | async-start | bytes 1310720 | tf_op jit(solution)/shard_map/all_gather | solution.py:93
  69.8 16.3 %collective-permute-start.14 = (f32[128,512]{0,1:T(8,128)}, f32[128,512]{0,1:T(8,128)}, u32[]{:S(2)}, u32[]{:S(2)}) collective-permute-start(f32[128,512]{0,1:T(8,128)} %copy.144), channel_id=1, source_target_pairs={{0,3},{4,7},{8,11},{12,15},{16,19},{20,23},{24,27},{28,31}} | collective-permute-start | bytes 786440 | tf_op jit(solution)/shard_map/ppermute | solution.py:92
  82.6 8.6 %collective-permute-start.15 = (f32[128,512]{0,1:T(8,128)}, f32[128,512]{0,1:T(8,128)}, u32[]{:S(2)}, u32[]{:S(2)}) collective-permute-start(f32[128,512]{0,1:T(8,128)} %copy.145), channel_id=1, source_target_pairs={{0,2},{4,6},{8,10},{12,14},{16,18},{20,22},{24,26},{28,30}} | collective-permute-start | bytes 786440 | tf_op jit(solution)/shard_map/ppermute | solution.py:92
  84.7 7.2 %collective-permute-start.16 = (f32[128,512]{0,1:T(8,128)}, f32[128,512]{0,1:T(8,128)}, u32[]{:S(2)}, u32[]{:S(2)}) collective-permute-start(f32[128,512]{0,1:T(8,128)} %copy.146), channel_id=1, source_target_pairs={{0,1},{4,5},{8,9},{12,13},{16,17},{20,21},{24,25},{28,29}} | collective-permute-start | bytes 786440 | tf_op jit(solution)/shard_map/ppermute | solution.py:92
  86.1 13.2 %collective-permute-start.2 = (f32[256,512]{1,0:T(8,128)S(1)}, f32[256,512]{1,0:T(8,128)}, u32[]{:S(2)}, u32[]{:S(2)}) collective-permute-start(f32[256,512]{1,0:T(8,128)S(1)} %get-tuple-element.54), channel_id=1, source_target_pairs={{0,1},{4,5},{8,9},{12,13},{16,17},{20,21},{24,25},{28,29}} | collective-permute-start | bytes 1572872 | tf_op jit(solution)/shard_map/ppermute | solution.py:100
  91.2 12.0 %collective-permute-start.3 = (f32[320,512]{1,0:T(8,128)}, f32[320,512]{1,0:T(8,128)S(1)}, u32[]{:S(2)}, u32[]{:S(2)}) collective-permute-start(f32[320,512]{1,0:T(8,128)} %pad_maximum_fusion.2), channel_id=1, source_target_pairs={{0,12},{4,28},{8,13},{12,29},{16,14},{20,30},{24,15},{28,31}} | collective-permute-start | bytes 1966088 | tf_op jit(solution)/shard_map/ppermute | solution.py:106
  93.6 263.4 %all-gather.15.cloned.1.call-start = ((), (), s32[]{:S(2)}) async-start(), calls=%async_computation.4 | async-start | bytes 5898240 | tf_op jit(solution)/shard_map/all_gather | solution.py:107
  95.6 7.5 %collective-permute-start.4 = (f32[320,512]{1,0:T(8,128)}, f32[320,512]{1,0:T(8,128)}, u32[]{:S(2)}, u32[]{:S(2)}) collective-permute-start(f32[320,512]{1,0:T(8,128)} %pad_maximum_fusion.3), channel_id=1, source_target_pairs={{0,8},{4,24},{8,9},{12,25},{16,10},{20,26},{24,11},{28,27}} | collective-permute-start | bytes 1966088 | tf_op jit(solution)/shard_map/ppermute | solution.py:106
  98.0 54.2 %collective-permute-start.5 = (f32[320,512]{1,0:T(8,128)}, f32[320,512]{1,0:T(8,128)}, u32[]{:S(2)}, u32[]{:S(2)}) collective-permute-start(f32[320,512]{1,0:T(8,128)} %pad_maximum_fusion.4), channel_id=1, source_target_pairs={{0,4},{4,20},{8,5},{12,21},{16,6},{20,22},{24,7},{28,23}} | collective-permute-start | bytes 1966088 | tf_op jit(solution)/shard_map/ppermute | solution.py:106
  102.4 49.8 %collective-permute-start.6 = (f32[320,512]{1,0:T(8,128)}, f32[320,512]{1,0:T(8,128)S(1)}, u32[]{:S(2)}, u32[]{:S(2)}) collective-permute-start(f32[320,512]{1,0:T(8,128)} %pad_maximum_fusion.5), channel_id=1, source_target_pairs={{0,0},{4,16},{8,1},{12,17},{16,2},{20,18},{24,3},{28,19}} | collective-permute-start | bytes 1966088 | tf_op jit(solution)/shard_map/ppermute | solution.py:106
  158.1 37.7 %all-to-all-start = ((f32[4,8,128,128]{3,2,1,0:T(8,128)}), f32[4,8,128,128]{3,2,1,0:T(8,128)}, u32[]{:S(2)}, u32[]{:S(2)}) async-start(f32[4,8,128,128]{3,2,1,0:T(8,128)} %bitcast.26), calls=%async_computation | async-start | bytes 4194304 | tf_op jit(solution)/shard_map/all_to_all | solution.py:62
  162.6 200.4 %all-gather.9.cloned.1.call-start = ((), (), s32[]{:S(2)}) async-start(), calls=%async_computation.1 | async-start | bytes 2621440 | tf_op jit(solution)/shard_map/all_gather | solution.py:101
  317.7 45.4 %copy-start.4 = (f32[512,512]{1,0:T(8,128)}, f32[512,512]{1,0:T(8,128)S(1)}, u32[]{:S(2)}) copy-start(f32[512,512]{1,0:T(8,128)S(1)} %get-tuple-element.138) | copy-start | bytes 3145732
  374.8 23.7 %copy-start = (f32[3840,128]{0,1:T(8,128)}, f32[3840,128]{0,1:T(8,128)S(1)}, u32[]{:S(2)}) copy-start(f32[3840,128]{0,1:T(8,128)S(1)} %fusion.22) | copy-start | bytes 5898244
  (9 other events, 58.8 us)
Sparse Core Ops, SparseCore 0:
  20.4 46.5 all-gather.10
  93.7 17.5 all-gather.12
  154.6 88.2 all-gather.14
  244.3 21.2 all-gather.8

commit v2 on v1

--- a/solution.py
+++ b/solution.py
@@ -1,7 +1,11 @@
+import functools
+
 import jax
 import jax.numpy as jnp
 from jax import lax
 from jax.sharding import PartitionSpec as P
+from jax.experimental import pallas as pl
+from jax.experimental.pallas import tpu as pltpu
 
 MSLOT = 128
 PANEL = 512
@@ -11,9 +15,85 @@
 AXES = ("row", "col")
 
 
-def dot_t(left, right, precision):
+def split_bf16(x):
+    hi = lax.reduce_precision(x, exponent_bits=8, mantissa_bits=7)
+    return hi.astype(jnp.bfloat16), (x - hi).astype(jnp.bfloat16)
+
+
+def update_kernel(kind, tm, tn, flags_ref, info_ref, slots_ref, base_ref, a_ref, bhi_ref, blo_ref, out_ref):
+    j = pl.program_id(0)
+    i = pl.program_id(1)
+    is_panel = (info_ref[0] == 1) & (info_ref[1] + j * tn == 0)
+    active = jnp.logical_and(jnp.logical_not(is_panel), flags_ref[i] != 0)
+
+    def base():
+        if kind == "gather":
+            return base_ref[0]
+        if kind == "diag":
+            rows = info_ref[2] + i * tm + lax.broadcasted_iota(jnp.int32, (tm, tn), 0)
+            cols = info_ref[1] + j * tn + lax.broadcasted_iota(jnp.int32, (tm, tn), 1)
+            return jnp.where(rows == cols, base_ref[...], 0.0)
+        return base_ref[...]
+
+    @pl.when(is_panel)
+    def _():
+        out_ref[...] = a_ref[...]
+
+    @pl.when(active)
+    def _():
+        a = a_ref[...]
+        a_hi = a.astype(jnp.bfloat16)
+        a_lo = (a - a_hi.astype(jnp.float32)).astype(jnp.bfloat16)
+        dn = (((1,), (1,)), ((), ()))
+        b_hi = bhi_ref[...]
+        acc = lax.dot_general(a_hi, b_hi, dn, preferred_element_type=jnp.float32)
+        acc = acc + lax.dot_general(a_hi, blo_ref[...], dn, preferred_element_type=jnp.float32)
+        acc = acc + lax.dot_general(a_lo, b_hi, dn, preferred_element_type=jnp.float32)
+        out_ref[...] = base() - acc
+
+    @pl.when(jnp.logical_and(jnp.logical_not(is_panel), flags_ref[i] == 0))
+    def _():
+        out_ref[...] = base()
+
+
+def panel_update(kind, base, a, b, flags, info, slots, rows, width):
+    tm, tn = MSLOT, PANEL
+    b_hi, b_lo = split_bf16(b)
+    if kind == "gather":
+        nseg = width // tn
+        base_spec = pl.BlockSpec((1, tm, tn), lambda j, i, f, n, s: (s[i * nseg + j], 0, 0))
+    elif kind == "diag":
+        base_spec = pl.BlockSpec((tm, 1), lambda j, i, f, n, s: (i, 0))
+    else:
+        base_spec = pl.BlockSpec((tm, tn), lambda j, i, f, n, s: (i, j))
+    grid_spec = pltpu.PrefetchScalarGridSpec(
+        num_scalar_prefetch=3,
+        grid=(width // tn, rows // tm),
+        in_specs=[
+            base_spec,
+            pl.BlockSpec((tm, PANEL), lambda j, i, f, n, s: (i, 0)),
+            pl.BlockSpec((tn, PANEL), lambda j, i, f, n, s: (j, 0)),
+            pl.BlockSpec((tn, PANEL), lambda j, i, f, n, s: (j, 0)),
+        ],
+        out_specs=pl.BlockSpec((tm, tn), lambda j, i, f, n, s: (i, j)),
+    )
+    flops = 6 * rows * width * PANEL
+    cost = pl.CostEstimate(flops=flops, transcendentals=0, bytes_accessed=rows * width * 8 + width * PANEL * 4)
+    return pl.pallas_call(
+        functools.partial(update_kernel, kind, tm, tn),
+        grid_spec=grid_spec,
+        out_shape=jax.ShapeDtypeStruct((rows, width), jnp.float32),
+        cost_estimate=cost,
+    )(flags, info, slots, base, a, b_hi, b_lo)
+
+
+def dot_t(left, right):
     contract = (((1,), (1,)), ((), ()))
-    return lax.dot_general(left, right, contract, precision=precision)
+    l_hi, l_lo = split_bf16(left)
+    r_hi, r_lo = split_bf16(right)
+    out = lax.dot_general(l_hi, r_hi, contract, preferred_element_type=jnp.float32)
+    out = out + lax.dot_general(l_hi, r_lo, contract, preferred_element_type=jnp.float32)
+    return out + lax.dot_general(l_lo, r_hi, contract, preferred_element_type=jnp.float32)
 
 
 def pick(index, options):
@@ -31,7 +111,6 @@
 
 
 def per_device(eigvecs, coupling, mode_counts, tree_segments, eigvals, stiff):
-    high = lax.Precision.HIGH
     R = lax.axis_size("row")
     C = lax.axis_size("col")
     r = lax.axis_index("row")
@@ -59,16 +138,20 @@
     match = onehot[:, :, None] & (rank_pd[:, :, None] == jnp.arange(cap, dtype=jnp.int32)[None, None, :])
     send_idx = jnp.where(jnp.any(match, axis=0), jnp.argmax(match, axis=0), npair)
     send = flat_pad[send_idx]
-    recv = lax.all_to_all(send, "col", 0, 0, tiled=True)
-    recv_pad = jnp.concatenate([recv, jnp.zeros((C, 1, MSLOT, Ec), jnp.float32)], axis=1)
+    shifted = [send[c]]
+    for k in range(1, C):
+        out_k = lax.dynamic_index_in_dim(send, (c + k) % C, axis=0, keepdims=False)
+        shifted.append(lax.ppermute(out_k, "col", [(i, (i + k) % C) for i in range(C)]))
+    shifted = jnp.stack(shifted)
+    recv = shifted[(c - jnp.arange(C, dtype=jnp.int32)) % C]
+    recv_t = recv.transpose(1, 2, 0, 3).reshape(cap, MSLOT, C * Ec)
+    recv_t = jnp.concatenate([recv_t, jnp.zeros((1, MSLOT, PANEL), jnp.float32)], axis=0)
     my_seg = c * G + jnp.arange(G, dtype=jnp.int32)
     seg_hit = tseg[:, :, None] == my_seg[None, None, :]
     rank2 = rank.reshape(nsub, 2)
     slot_tab = jnp.where(
         jnp.any(seg_hit, axis=1), jnp.sum(jnp.where(seg_hit, rank2[:, :, None], 0), axis=1), cap
     )
-    gathered = recv_pad[:, slot_tab]
-    block_mi = gathered.transpose(1, 3, 2, 0, 4).reshape(nsub * MSLOT, W)
 
     has0, rank0, slot_r = seg0_slots(tseg, cap0)
     t0 = jnp.where(tseg[:, 0] == 0, 0, 1)
@@ -117,41 +200,39 @@
     slot_c = jnp.concatenate(slot_c)
 
     factor = jnp.linalg.cholesky(kpp)
+    eye = jnp.eye(PANEL, dtype=jnp.float32)
+    finv = lax.linalg.triangular_solve(factor, eye, left_side=True, lower=True)
     stacked = jnp.concatenate([m_row, m_col, z_rows, z_col], axis=0)
-    solved = lax.linalg.triangular_solve(factor, stacked, left_side=False, lower=True, transpose_a=True)
+    solved = dot_t(stacked, finv)
     low_r = solved[:H]
     low_c = solved[H:H + W]
     lowmi_r = solved[H + W:H + W + cap0 * MSLOT]
     lowmi_c = solved[H + W + cap0 * MSLOT:]
 
-    col_ids = c * W + jnp.arange(W, dtype=jnp.int32)
-    in_panel = col_ids[None, :] < PANEL
-    reduced_ii = jnp.where(
-        in_panel, jnp.pad(low_r, ((0, 0), (0, W - PANEL))), stiff - dot_t(low_r, low_c, high)
-    )
-
-    upd = dot_t(lowmi_r, low_c, high).reshape(cap0, MSLOT, W)
-    upd = jnp.concatenate([upd, jnp.zeros((1, MSLOT, W), jnp.float32)], axis=0)
-    upd_full = upd[slot_r].reshape(nsub * MSLOT, W)
+    ones = jnp.ones((H // MSLOT,), jnp.int32)
+    none = jnp.zeros((1,), jnp.int32)
+    info = jnp.stack([jnp.int32(1), c * W, r * H, jnp.int32(0)]).astype(jnp.int32)
+    reduced_ii = panel_update("array", stiff, low_r, low_c, ones, info, none, H, W)
+
     lmi = jnp.concatenate(
         [lowmi_r.reshape(cap0, MSLOT, PANEL), jnp.zeros((1, MSLOT, PANEL), jnp.float32)], axis=0
     )
     lmi_full = lmi[slot_r].reshape(nsub * MSLOT, PANEL)
-    reduced_mi = jnp.where(
-        in_panel, jnp.pad(lmi_full, ((0, 0), (0, W - PANEL))), block_mi - upd_full
+    flags = has0.astype(jnp.int32)
+    reduced_mi = panel_update(
+        "gather", recv_t, lmi_full, low_c, flags, info, slot_tab.reshape(-1).astype(jnp.int32), nsub * MSLOT, W
     )
 
     nc = ratio * cap0
-    vv = dot_t(lowmi_r, lowmi_c, high).reshape(cap0, MSLOT, nc, MSLOT)
-    vv = jnp.pad(vv, ((0, 1), (0, 0), (0, 1), (0, 0)))
-    vv_full = vv[slot_r][:, :, slot_c].reshape(nsub * MSLOT, ratio * nsub * MSLOT)
-    diag_values = jnp.where(live, eigvals, 1.0).reshape(-1)
+    lmc = jnp.concatenate(
+        [lowmi_c.reshape(nc, MSLOT, PANEL), jnp.zeros((1, MSLOT, PANEL), jnp.float32)], axis=0
+    )
+    mode_width = ratio * nsub * MSLOT
+    lmc_full = lmc[slot_c].reshape(mode_width, PANEL)
+    diag_values = jnp.where(live, eigvals, 1.0).reshape(-1, 1)
     mode_rows = diag_values.shape[0]
-    mode_width = ratio * nsub * MSLOT
-    row_ids = r * mode_rows + jnp.arange(mode_rows, dtype=jnp.int32)
-    mode_cols = c * mode_width + jnp.arange(mode_width, dtype=jnp.int32)
-    base_mm = jnp.where(row_ids[:, None] == mode_cols[None, :], diag_values[:, None], 0.0)
-    reduced_mm = base_mm - vv_full
+    info_mm = jnp.stack([jnp.int32(0), c * mode_width, r * mode_rows, jnp.int32(0)]).astype(jnp.int32)
+    reduced_mm = panel_update("diag", diag_values, lmi_full, lmc_full, flags, info_mm, none, mode_rows, mode_width)
     return (reduced_ii, reduced_mi, reduced_mm)
 
 

time: 508 us -> 484 us (0.953)
  Pallas kernels: 0 us -> 80.8 us
  local copies, waits for them, and re-layouts: 114 us -> 48.2 us
  matrix products: 60.8 us -> 41 us
  other arithmetic: 166 us -> 150 us
    pallas_call x0 -> x3, Pallas kernels: none -> 80.8 us  [panel_update(): pl.pallas_call(functools.partial(update_kernel, kind, tm, tn), grid_spec=...]
    unnamed x28 -> x23, local copies, waits for them, and re-layouts: 35.3 us -> 3.65 us
    another operation x7, matrix products: 31.1 us -> 3.77 us  [per_device(): finv = lax.linalg.triangular_solve(factor, eye, left_side=True, lower=True)]
    gather x5 -> x2, local copies, waits for them, and re-layouts: 23.5 us -> 4.83 us  [the longest x1 2.83 us: per_device(): lmc_full = lmc[slot_c].reshape(mode_width, PANEL)]
    another operation x14, other arithmetic: 89.1 us -> 78.7 us  [per_device(): factor = jnp.linalg.cholesky(kpp)]
    select_n x3 -> x4, other arithmetic: 10.3 us -> 0.16 us  [the longest x1 0.08 us: per_device(): lmc_full = lmc[slot_c].reshape(mode_width, PANEL)]
    convert_element_type x0 -> x3, other arithmetic: none -> 10.1 us  [the longest x2 9.96 us: split_bf16(): return (hi.astype(jnp.bfloat16), (x - hi).astype(jnp.bfloat16))]
    transpose x1, local copies, waits for them, and re-layouts: 10.1 us -> 0.34 us  [per_device(): z_rows = z_all.transpose(1, 2, 0, 3).reshape(cap0 * MSLOT, C * Ec)]
  transfers between devices with their start and end apart: 22 -> 24, of which waited for: 3 -> 3; matrix products, arithmetic and copies ran while one was open for 42% -> 40% of each run, Pallas kernels for 0% -> 0%
where the time goes in v2:
time: 484 us; the launch traced here: 475 us
  other arithmetic  150 us (31%)
  waiting for transfers between devices  86.1 us (18%)
  Pallas kernels  80.8 us (17%)
  local copies, waits for them, and re-layouts  48.2 us (10%)
  matrix products  41 us (8%)
  blocking collectives  32.4 us (7%)
  starting transfers between devices  19.8 us (4%)
  between operations  17.4 us (4%)
    pallas_call x3, Pallas kernels, panel_update(): pl.pallas_call(functools.partial(update_kernel, kind, tm, tn), grid_spec=...  80.8 us
    another operation x14, other arithmetic, per_device(): factor = jnp.linalg.cholesky(kpp)  78.7 us
    ppermute x4, waiting for transfers between devices, per_device(): got.append(lax.ppermute(payload, AXES, perm))  47.2 us
    another operation x3, other arithmetic, per_device(): finv = lax.linalg.triangular_solve(factor, eye, left_side=True, lower=True)  40.3 us
    all_gather x1, waiting for transfers between devices, per_device(): kpp_col0 = lax.all_gather(kpp_part, 'row', axis=0, tiled=True)  36 us
    all_gather x1, blocking collectives, per_device(): tseg_all = lax.all_gather(tseg, 'row', axis=0, tiled=False)  23.2 us
    dot_general x1, matrix products, dot_t(): lax.dot_general(l_lo, r_hi, contract, preferred_element_type=jnp.float32)  13.2 us
    another operation x13, local copies, waits for them, and re-layouts  10.9 us
  transfers between devices with their start and end apart: 24, of which 3 were waited for; matrix products, arithmetic and copies ran while one was open for 40% of the time, Pallas kernels for 0%

profile of v2, /device:TPU:6, one launch (start us, length us, event | category | flops | bytes accessed | tf_op | source)
XLA Modules:
  0.0 475.2 jit_solution(11642925768890594942)
XLA Ops:
  20.2 7.2 %fusion.7 = f32[8,2,128,128]{3,2,1,0:T(8,128)S(1)} fusion(bf16[8,2048,128]{2,1,0:T(8,128)(2,1)} %param.6, bf16[8,2048,2,128]{3,2,1,0:T(2,128)(2,1)} %param.7, f32[8,128]{1,0:T(8,128)S(1)} %fusion.49), kind=kOutput, calls=%fused_computation.26 | convolution fusion | flops 1074003968 | bytes 13635584 | tf_op jit(solution)/shard_map/sim,sitp->stmp/dot_general | solution.py:128
  30.6 36.0 %all-gather.11.cloned.1.call-done = f32[512,512]{1,0:T(8,128)} async-done(((f32[64,512]{1,0:T(8,128)}), f32[512,512]{1,0:T(8,128)}) %all-gather.11.cloned.1.call-update) | async-done | bytes 1048592 | tf_op jit(solution)/shard_map/all_gather | solution.py:171
  70.1 9.2 %all-gather = f32[8,128,128]{2,1,0:T(8,128)S(1)} all-gather(f32[2,128,128]{2,1,0:T(8,128)S(1)} %gather_fusion.1), channel_id=2, replica_groups=mesh['row'=8,'col'=4] {'col'}, dimensions={0}, use_global_device_ids=true | all-gather | bytes 655360 | tf_op jit(solution)/shard_map/all_gather | solution.py:162
  102.8 47.2 %collective-permute-done.5 = f32[320,512]{1,0:T(8,128)} collective-permute-done((f32[320,512]{1,0:T(8,128)}, f32[320,512]{1,0:T(8,128)}, u32[]{:S(2)}, u32[]{:S(2)}) %collective-permute-start.5) | collective-permute-done | bytes 655392 | tf_op jit(solution)/shard_map/ppermute | solution.py:189
  157.7 23.2 %all-gather.3 = s32[8,8,2]{1,2,0:T(2,128)S(1)} all-gather(s32[1,8,2]{1,2,0:T(2,128)S(1)} %bitcast.150), channel_id=4, replica_groups=mesh['row'=8,'col'=4] {'row'}, dimensions={0}, use_global_device_ids=true | all-gather | bytes 576 | tf_op jit(solution)/shard_map/all_gather | solution.py:194
  196.8 11.7 %cholesky.104 = f32[128,128]{1,0:T(8,128)S(1)} custom-call(f32[128,128]{1,0:T(8,128)S(1)} %cholesky.266), custom_call_target="Cholesky" | custom-call | tf_op jit(solution)/shard_map/jit(cholesky)/cholesky | solution.py:202
  208.7 9.8 %custom-call.30 = f32[1,128,128]{1,2,0:T(8,128)S(1)} custom-call(f32[1,128,128]{2,1,0:T(8,128)S(1)} %get-tuple-element.64), custom_call_target="InvertDiagBlocksLowerTriangular" | custom-call | tf_op jit(solution)/shard_map/jit(cholesky)/cholesky | solution.py:202
  219.2 11.8 %cholesky.217 = f32[128,128]{1,0:T(8,128)S(1)} custom-call(f32[128,128]{1,0:T(8,128)S(1)} %cholesky.270), custom_call_target="Cholesky" | custom-call | tf_op jit(solution)/shard_map/jit(cholesky)/cholesky | solution.py:202
  231.0 9.8 %custom-call.31 = f32[1,128,128]{1,2,0:T(8,128)S(1)} custom-call(f32[1,128,128]{2,1,0:T(8,128)S(1)} %get-tuple-element.61), custom_call_target="InvertDiagBlocksLowerTriangular" | custom-call | tf_op jit(solution)/shard_map/jit(cholesky)/cholesky | solution.py:202
  241.5 11.7 %cholesky.238 = f32[128,128]{1,0:T(8,128)S(1)} custom-call(f32[128,128]{1,0:T(8,128)S(1)} %cholesky.275), custom_call_target="Cholesky" | custom-call | tf_op jit(solution)/shard_map/jit(cholesky)/cholesky | solution.py:202
  253.9 9.8 %custom-call.32 = f32[1,128,128]{1,2,0:T(8,128)S(1)} custom-call(f32[1,128,128]{2,1,0:T(8,128)S(1)} %get-tuple-element.58), custom_call_target="InvertDiagBlocksLowerTriangular" | custom-call | tf_op jit(solution)/shard_map/jit(cholesky)/cholesky | solution.py:202
  264.3 11.9 %cholesky.255 = f32[128,128]{1,0:T(8,128)S(1)} custom-call(f32[128,128]{1,0:T(8,128)S(1)} %convolution_subtract_fusion.5), custom_call_target="Cholesky" | custom-call | tf_op jit(solution)/shard_map/jit(cholesky)/cholesky | solution.py:202
  280.1 10.4 %while.1 = (s32[]{:T(128)}, f32[512,512]{1,0:T(8,128)S(1)}, s32[4,2]{0,1:T(2,128)S(1)}, f32[4,128,128]{2,1,0:T(8,128)}, s32[]{:T(128)}) while((s32[]{:T(128)}, f32[512,512]{1,0:T(8,128)S(1)}, s32[4,2]{0,1:T(2,128)S(1)}, f32[4,128,128]{2,1,0:T(8,128)}, s32[]{:T(128)}) %tuple.63), condition=%wide.while_cond, body=%wide.while_body.sunk | while | flops 2 | bytes 132205 | solution.py:204
  290.5 40.1 %custom-call.33 = f32[4,128,128]{1,2,0:T(8,128)S(1)} custom-call(f32[4,128,128]{2,1,0:T(8,128)} %get-tuple-element.14), custom_call_target="InvertDiagBlocksLowerTriangular" | custom-call | tf_op jit(solution)/shard_map/triangular_solve | solution.py:204
  335.9 4.7 slice.265
  340.6 8.5 %fusion.19 = f32[3840,512]{1,0:T(8,128)} fusion(f32[128,512]{1,0:T(8,128)S(1)} %fusion.35, f32[128,512]{1,0:T(8,128)S(1)} %fusion.36, f32[128,512]{1,0:T(8,128)S(1)} %fusion.38, f32[128,512]{1,0:T(8,128)S(1)} %fusion.26, f32[512,512]{1,0:T(8,128)S(1)} %bitcast.140, f32[256,512]{1,0:T(8,128)S(1)} %bitcast.137, f32[2048,512]{1,0:T(8,128)} %bitcast.130, ...), kind=kOutput, calls=%fused_computation.52 | convolution fusion | flops 2024669184 | bytes 16777216 | tf_op jit(solution)/shard_map/dot_general | solution.py:95
  349.1 6.5 %fusion.62 = f32[3840,512]{1,0:T(8,128)} fusion(f32[128,512]{1,0:T(8,128)S(1)} %fusion.35, f32[128,512]{1,0:T(8,128)S(1)} %fusion.36, f32[128,512]{1,0:T(8,128)S(1)} %fusion.38, f32[128,512]{1,0:T(8,128)S(1)} %fusion.26, f32[512,512]{1,0:T(8,128)S(1)} %bitcast.141, f32[256,512]{1,0:T(8,128)S(1)} %bitcast.138, f32[2048,512]{1,0:T(8,128)S(1)} %bitcast.132, ...), kind=kOutput, calls=%fused_computation.170 | convolution fusion | flops 2024407040 | bytes 16777216 | tf_op jit(solution)/shard_map/dot_general | solution.py:94
  355.6 13.2 %add_add_fusion = f32[3840,512]{1,0:T(8,128)} fusion(f32[3840,512]{1,0:T(8,128)} %fusion.62, f32[3840,512]{1,0:T(8,128)} %fusion.19, f32[512,512]{1,0:T(8,128)S(1)} %bitcast.142, f32[256,512]{1,0:T(8,128)S(1)} %bitcast.139, f32[2048,512]{1,0:T(8,128)} %bitcast.131, f32[1024,512]{1,0:T(8,128)} %all-gather.9.cloned.1.call-done, f32[128,512]{1,0:T(8,128)S(1)} %fusion.35, ...), kind=kOutput, calls=%fused_computation.14 | convolution fusion | flops 2030305280 | bytes 32505856 | tf_op jit(solution)/shard_map/dot_general | solution.py:96
  368.7 3.1 slice.271.a_ref
  371.8 5.0 %fusion.3 = (bf16[2048,512]{1,0:T(8,128)(2,1)}, bf16[2048,512]{1,0:T(8,128)(2,1)}) fusion(f32[3840,512]{1,0:T(8,128)} %add_add_fusion), kind=kLoop, calls=%fused_computation.19 | loop fusion | flops 4194304 | bytes 8388608 | tf_op jit(solution)/shard_map/convert_element_type | solution.py:20
  380.0 4.9 %fusion.4 = (bf16[2048,512]{1,0:T(8,128)(2,1)}, bf16[2048,512]{1,0:T(8,128)(2,1)}) fusion(f32[16,128,512]{2,1,0:T(8,128)} %gather_fusion.5), kind=kLoop, calls=%fused_computation.20 | loop fusion | flops 4194304 | bytes 8388608 | tf_op jit(solution)/shard_map/convert_element_type | solution.py:20
  387.4 32.5 %shard_map.85 = f32[1024,2048]{1,0:T(8,128)} custom-call(s32[8]{0:T(128)} %broadcast_29_flags_ref.2.flags_ref, s32[4]{0:T(128)} %get-tuple-element.76.info_ref, s32[1]{0:T(128)} %constant.250.clone.1.slots_ref, f32[1024,2048]{1,0:T(8,128)} %base_ref.1, f32[1024,512]{1,0:T(8,128)} %slice.271.a_ref, bf16[2048,512]{1,0:T(8,128)(2,1)} %get-tuple-element.40.bhi_ref, ...), custom_call_target="tpu_custom_call" | custom-call | flops 6442450944 | bytes 20971520 | tf_op jit(solution)/shard_map/pallas_call | solution.py:82
  419.9 23.9 %shard_map.86 = f32[1024,2048]{1,0:T(8,128)} custom-call(s32[8]{0:T(128)} %get-tuple-element.71.flags_ref, s32[4]{0:T(128)} %get-tuple-element.76.info_ref, s32[32]{0:T(128)} %select_n.327.slots_ref, f32[9,128,512]{2,1,0:T(8,128)} %concatenate.67.base_ref, f32[1024,512]{1,0:T(8,128)} %bitcast.144, bf16[2048,512]{1,0:T(8,128)(2,1)} %get-tuple-element.40.bhi_ref, ...), custom_call_target="tpu_custom_call" | custom-call | flops 6442450944 | bytes 20971520 | tf_op jit(solution)/shard_map/pallas_call | solution.py:82
  443.8 24.4 %shard_map.87 = f32[1024,2048]{1,0:T(8,128)} custom-call(s32[8]{0:T(128)} %get-tuple-element.71.flags_ref, s32[4]{0:T(128)} %get-tuple-element.75.info_ref, s32[1]{0:T(128)} %constant.250.clone.1.slots_ref, f32[1024,1]{1,0:T(8,128)} %copy.76.base_ref, f32[1024,512]{1,0:T(8,128)} %bitcast.145, bf16[2048,512]{1,0:T(8,128)(2,1)} %get-tuple-element.42.bhi_ref, ...), custom_call_target="tpu_custom_call" | custom-call | flops 6442450944 | bytes 20971520 | tf_op jit(solution)/shard_map/pallas_call | solution.py:82
  (196 shorter events, 91.7 us)
Async XLA Ops:
  7.2 59.4 %all-gather.11.cloned.1.call-start = ((), (), s32[]{:S(2)}) async-start(), calls=%async_computation.1 | async-start | bytes 1179648 | tf_op jit(solution)/shard_map/all_gather | solution.py:171
  8.5 5.7 %collective-permute-start.13 = (f32[64,512]{1,0:T(8,128)S(1)}, f32[64,512]{1,0:T(8,128)S(1)}, u32[]{:S(2)}, u32[]{:S(2)}) collective-permute-start(f32[64,512]{1,0:T(8,128)S(1)} %get-tuple-element.32), channel_id=1, source_target_pairs={{0,4}} | collective-permute-start | bytes 393224 | tf_op jit(solution)/shard_map/ppermute | solution.py:169
  9.2 5.7 %collective-permute-start.12 = (f32[64,512]{1,0:T(8,128)S(1)}, f32[64,512]{1,0:T(8,128)S(1)}, u32[]{:S(2)}, u32[]{:S(2)}) collective-permute-start(f32[64,512]{1,0:T(8,128)S(1)} %get-tuple-element.33), channel_id=1, source_target_pairs={{0,8}} | collective-permute-start | bytes 393224 | tf_op jit(solution)/shard_map/ppermute | solution.py:169
  9.9 5.8 %collective-permute-start.11 = (f32[64,512]{1,0:T(8,128)S(1)}, f32[64,512]{1,0:T(8,128)S(1)}, u32[]{:S(2)}, u32[]{:S(2)}) collective-permute-start(f32[64,512]{1,0:T(8,128)S(1)} %get-tuple-element.34), channel_id=1, source_target_pairs={{0,12}} | collective-permute-start | bytes 393224 | tf_op jit(solution)/shard_map/ppermute | solution.py:169
  10.6 6.6 %collective-permute-start.10 = (f32[64,512]{1,0:T(8,128)S(1)}, f32[64,512]{1,0:T(8,128)S(1)}, u32[]{:S(2)}, u32[]{:S(2)}) collective-permute-start(f32[64,512]{1,0:T(8,128)S(1)} %get-tuple-element.35), channel_id=1, source_target_pairs={{0,16}} | collective-permute-start | bytes 393224 | tf_op jit(solution)/shard_map/ppermute | solution.py:169
  11.3 7.2 %collective-permute-start.9 = (f32[64,512]{1,0:T(8,128)S(1)}, f32[64,512]{1,0:T(8,128)S(1)}, u32[]{:S(2)}, u32[]{:S(2)}) collective-permute-start(f32[64,512]{1,0:T(8,128)S(1)} %get-tuple-element.36), channel_id=1, source_target_pairs={{0,20}} | collective-permute-start | bytes 393224 | tf_op jit(solution)/shard_map/ppermute | solution.py:169
  14.2 4.2 collective-permute-start.8
  14.9 3.5 collective-permute-start.7
  15.7 82.8 %collective-permute-start.2 = (f32[256,512]{1,0:T(8,128)}, f32[256,512]{1,0:T(8,128)}, u32[]{:S(2)}, u32[]{:S(2)}) collective-permute-start(f32[256,512]{1,0:T(8,128)} %get-tuple-element.29), channel_id=1, source_target_pairs={{0,1},{4,5},{8,9},{12,13},{16,17},{20,21},{24,25},{28,29}} | collective-permute-start | bytes 1572872 | tf_op jit(solution)/shard_map/ppermute | solution.py:183
  17.1 82.6 %collective-permute-start.1 = (f32[256,512]{1,0:T(8,128)S(1)}, f32[256,512]{1,0:T(8,128)}, u32[]{:S(2)}, u32[]{:S(2)}) collective-permute-start(f32[256,512]{1,0:T(8,128)S(1)} %get-tuple-element.30), channel_id=1, source_target_pairs={{0,2},{4,6},{8,10},{12,14},{16,18},{20,22},{24,26},{28,30}} | collective-permute-start | bytes 1572872 | tf_op jit(solution)/shard_map/ppermute | solution.py:183
  20.1 173.3 %all-gather.13.cloned.1.call-start = ((), (), s32[]{:S(2)}) async-start(), calls=%async_computation.2 | async-start | bytes 1310720 | tf_op jit(solution)/shard_map/all_gather | solution.py:176
  68.7 16.0 %collective-permute-start.14 = (f32[128,512]{0,1:T(8,128)}, f32[128,512]{0,1:T(8,128)}, u32[]{:S(2)}, u32[]{:S(2)}) collective-permute-start(f32[128,512]{0,1:T(8,128)} %copy.78), channel_id=1, source_target_pairs={{0,3},{4,7},{8,11},{12,15},{16,19},{20,23},{24,27},{28,31}} | collective-permute-start | bytes 786440 | tf_op jit(solution)/shard_map/ppermute | solution.py:175
  81.4 8.6 %collective-permute-start.15 = (f32[128,512]{0,1:T(8,128)}, f32[128,512]{0,1:T(8,128)}, u32[]{:S(2)}, u32[]{:S(2)}) collective-permute-start(f32[128,512]{0,1:T(8,128)} %copy.79), channel_id=1, source_target_pairs={{0,2},{4,6},{8,10},{12,14},{16,18},{20,22},{24,26},{28,30}} | collective-permute-start | bytes 786440 | tf_op jit(solution)/shard_map/ppermute | solution.py:175
  82.7 8.8 %collective-permute-start.16 = (f32[128,512]{0,1:T(8,128)}, f32[128,512]{0,1:T(8,128)}, u32[]{:S(2)}, u32[]{:S(2)}) collective-permute-start(f32[128,512]{0,1:T(8,128)} %copy.80), channel_id=1, source_target_pairs={{0,1},{4,5},{8,9},{12,13},{16,17},{20,21},{24,25},{28,29}} | collective-permute-start | bytes 786440 | tf_op jit(solution)/shard_map/ppermute | solution.py:175
  84.7 15.0 %collective-permute-start = (f32[256,512]{1,0:T(8,128)S(1)}, f32[256,512]{1,0:T(8,128)}, u32[]{:S(2)}, u32[]{:S(2)}) collective-permute-start(f32[256,512]{1,0:T(8,128)S(1)} %get-tuple-element.31), channel_id=1, source_target_pairs={{0,3},{4,7},{8,11},{12,15},{16,19},{20,23},{24,27},{28,31}} | collective-permute-start | bytes 1572872 | tf_op jit(solution)/shard_map/ppermute | solution.py:183
  89.9 12.9 %collective-permute-start.3 = (f32[320,512]{1,0:T(8,128)}, f32[320,512]{1,0:T(8,128)}, u32[]{:S(2)}, u32[]{:S(2)}) collective-permute-start(f32[320,512]{1,0:T(8,128)} %pad_maximum_fusion.3), channel_id=1, source_target_pairs={{0,12},{4,28},{8,13},{12,29},{16,14},{20,30},{24,15},{28,31}} | collective-permute-start | bytes 1966088 | tf_op jit(solution)/shard_map/ppermute | solution.py:189
  93.2 241.3 %all-gather.15.cloned.1.call-start = ((), (), s32[]{:S(2)}) async-start(), calls=%async_computation.3 | async-start | bytes 5898240 | tf_op jit(solution)/shard_map/all_gather | solution.py:190
  95.0 7.8 %collective-permute-start.4 = (f32[320,512]{1,0:T(8,128)}, f32[320,512]{1,0:T(8,128)}, u32[]{:S(2)}, u32[]{:S(2)}) collective-permute-start(f32[320,512]{1,0:T(8,128)} %pad_maximum_fusion.4), channel_id=1, source_target_pairs={{0,8},{4,24},{8,9},{12,25},{16,10},{20,26},{24,11},{28,27}} | collective-permute-start | bytes 1966088 | tf_op jit(solution)/shard_map/ppermute | solution.py:189
  98.5 51.6 %collective-permute-start.5 = (f32[320,512]{1,0:T(8,128)}, f32[320,512]{1,0:T(8,128)}, u32[]{:S(2)}, u32[]{:S(2)}) collective-permute-start(f32[320,512]{1,0:T(8,128)} %pad_maximum_fusion.5), channel_id=1, source_target_pairs={{0,4},{4,20},{8,5},{12,21},{16,6},{20,22},{24,7},{28,23}} | collective-permute-start | bytes 1966088 | tf_op jit(solution)/shard_map/ppermute | solution.py:189
  102.1 47.9 %collective-permute-start.6 = (f32[320,512]{1,0:T(8,128)S(1)}, f32[320,512]{1,0:T(8,128)S(1)}, u32[]{:S(2)}, u32[]{:S(2)}) collective-permute-start(f32[320,512]{1,0:T(8,128)S(1)} %pad_maximum_fusion.6), channel_id=1, source_target_pairs={{0,0},{4,16},{8,1},{12,17},{16,2},{20,18},{24,3},{28,19}} | collective-permute-start | bytes 1966088 | tf_op jit(solution)/shard_map/ppermute | solution.py:189
  152.3 188.3 %all-gather.9.cloned.1.call-start = ((), (), s32[]{:S(2)}) async-start(), calls=%async_computation | async-start | bytes 2621440 | tf_op jit(solution)/shard_map/all_gather | solution.py:184
  155.9 29.3 %collective-permute-start.18 = (f32[8,128,128]{2,1,0:T(8,128)}, f32[8,128,128]{2,1,0:T(8,128)S(1)}, u32[]{:S(2)}, u32[]{:S(2)}) collective-permute-start(f32[8,128,128]{2,1,0:T(8,128)} %get-tuple-element.44), channel_id=1, source_target_pairs={{0,2},{1,3},{2,0},{3,1},{4,6},{5,7},{6,4},{7,5},{8,10},{9,11},{10,... | collective-permute-start | bytes 1572872 | tf_op jit(solution)/shard_map/ppermute | solution.py:144
  155.9 29.3 %collective-permute-start.17 = (f32[8,128,128]{2,1,0:T(8,128)S(1)}, f32[8,128,128]{2,1,0:T(8,128)S(1)}, u32[]{:S(2)}, u32[]{:S(2)}) collective-permute-start(f32[8,128,128]{2,1,0:T(8,128)S(1)} %get-tuple-element.45), channel_id=1, source_target_pairs={{0,1},{1,2},{2,3},{3,0},{4,5},{5,6},{6,7},{7,4},{8,9},{9,10},{10,1... | collective-permute-start | bytes 1572872 | tf_op jit(solution)/shard_map/ppermute | solution.py:144
  155.9 29.3 %collective-permute-start.19 = (f32[8,128,128]{2,1,0:T(8,128)S(1)}, f32[8,128,128]{2,1,0:T(8,128)}, u32[]{:S(2)}, u32[]{:S(2)}) collective-permute-start(f32[8,128,128]{2,1,0:T(8,128)S(1)} %get-tuple-element.46), channel_id=1, source_target_pairs={{0,3},{1,0},{2,1},{3,2},{4,7},{5,4},{6,5},{7,6},{8,11},{9,8},{10,9... | collective-permute-start | bytes 1572872 | tf_op jit(solution)/shard_map/ppermute | solution.py:144
  (11 other events, 100.3 us)
Sparse Core Ops, SparseCore 0:
  20.3 46.3 all-gather.10
  93.3 16.2 all-gather.12
  152.4 88.5 all-gather.14
  242.4 20.9 all-gather.8

commit v3 on v2

--- a/solution.py
+++ b/solution.py
@@ -20,24 +20,21 @@
     return hi.astype(jnp.bfloat16), (x - hi).astype(jnp.bfloat16)
 
 
-def update_kernel(kind, tm, tn, flags_ref, info_ref, slots_ref, base_ref, a_ref, bhi_ref, blo_ref, out_ref):
-    j = pl.program_id(0)
-    i = pl.program_id(1)
-    is_panel = (info_ref[0] == 1) & (info_ref[1] + j * tn == 0)
-    active = jnp.logical_and(jnp.logical_not(is_panel), flags_ref[i] != 0)
-
-    def base():
+def update_kernel(kind, tm, width, nbase, flags_ref, info_ref, slots_ref, *refs):
+    base_refs = refs[:nbase]
+    a_ref, bhi_ref, blo_ref, out_ref = refs[nbase:]
+    i = pl.program_id(0)
+    active = flags_ref[i] != 0
+
+    def base_cols(g):
+        cols = pl.ds(g * PANEL, PANEL)
         if kind == "gather":
-            return base_ref[0]
+            return base_refs[g][0]
         if kind == "diag":
-            rows = info_ref[2] + i * tm + lax.broadcasted_iota(jnp.int32, (tm, tn), 0)
-            cols = info_ref[1] + j * tn + lax.broadcasted_iota(jnp.int32, (tm, tn), 1)
-            return jnp.where(rows == cols, base_ref[...], 0.0)
-        return base_ref[...]
-
-    @pl.when(is_panel)
-    def _():
-        out_ref[...] = a_ref[...]
+            rows = info_ref[2] + i * tm + lax.broadcasted_iota(jnp.int32, (tm, PANEL), 0)
+            ids = info_ref[1] + g * PANEL + lax.broadcasted_iota(jnp.int32, (tm, PANEL), 1)
+            return jnp.where(rows == ids, base_refs[0][...], 0.0)
+        return base_refs[0][:, cols]
 
     @pl.when(active)
     def _():
@@ -45,46 +42,58 @@
         a_hi = a.astype(jnp.bfloat16)
         a_lo = (a - a_hi.astype(jnp.float32)).astype(jnp.bfloat16)
         dn = (((1,), (1,)), ((), ()))
-        b_hi = bhi_ref[...]
-        acc = lax.dot_general(a_hi, b_hi, dn, preferred_element_type=jnp.float32)
-        acc = acc + lax.dot_general(a_hi, blo_ref[...], dn, preferred_element_type=jnp.float32)
-        acc = acc + lax.dot_general(a_lo, b_hi, dn, preferred_element_type=jnp.float32)
-        out_ref[...] = base() - acc
-
-    @pl.when(jnp.logical_and(jnp.logical_not(is_panel), flags_ref[i] == 0))
+        for g in range(width // PANEL):
+            rows = pl.ds(g * PANEL, PANEL)
+            b_hi = bhi_ref[rows, :]
+            acc = lax.dot_general(a_hi, b_hi, dn, preferred_element_type=jnp.float32)
+            acc = acc + lax.dot_general(a_hi, blo_ref[rows, :], dn, preferred_element_type=jnp.float32)
+            acc = acc + lax.dot_general(a_lo, b_hi, dn, preferred_element_type=jnp.float32)
+            out_ref[:, pl.ds(g * PANEL, PANEL)] = base_cols(g) - acc
+
+    @pl.when(jnp.logical_not(active))
     def _():
-        out_ref[...] = base()
+        for g in range(width // PANEL):
+            out_ref[:, pl.ds(g * PANEL, PANEL)] = base_cols(g)
+
+    @pl.when((info_ref[0] == 1) & (info_ref[1] == 0))
+    def _():
+        out_ref[:, pl.ds(0, PANEL)] = a_ref[...]
 
 
 def panel_update(kind, base, a, b, flags, info, slots, rows, width):
-    tm, tn = MSLOT, PANEL
+    tm = MSLOT
     b_hi, b_lo = split_bf16(b)
+    nseg = width // PANEL
     if kind == "gather":
-        nseg = width // tn
-        base_spec = pl.BlockSpec((1, tm, tn), lambda j, i, f, n, s: (s[i * nseg + j], 0, 0))
+        bases = [base] * nseg
+        base_specs = [
+            pl.BlockSpec((1, tm, PANEL), lambda i, f, n, s, g=g: (s[i * nseg + g], 0, 0)) for g in range(nseg)
+        ]
     elif kind == "diag":
-        base_spec = pl.BlockSpec((tm, 1), lambda j, i, f, n, s: (i, 0))
+        bases = [base]
+        base_specs = [pl.BlockSpec((tm, 1), lambda i, f, n, s: (i, 0))]
     else:
-        base_spec = pl.BlockSpec((tm, tn), lambda j, i, f, n, s: (i, j))
+        bases = [base]
+        base_specs = [pl.BlockSpec((tm, width), lambda i, f, n, s: (i, 0))]
     grid_spec = pltpu.PrefetchScalarGridSpec(
         num_scalar_prefetch=3,
-        grid=(width // tn, rows // tm),
-        in_specs=[
-            base_spec,
-            pl.BlockSpec((tm, PANEL), lambda j, i, f, n, s: (i, 0)),
-            pl.BlockSpec((tn, PANEL), lambda j, i, f, n, s: (j, 0)),
-            pl.BlockSpec((tn, PANEL), lambda j, i, f, n, s: (j, 0)),
+        grid=(rows // tm,),
+        in_specs=base_specs + [
+            pl.BlockSpec((tm, PANEL), lambda i, f, n, s: (i, 0)),
+            pl.BlockSpec((width, PANEL), lambda i, f, n, s: (0, 0)),
+            pl.BlockSpec((width, PANEL), lambda i, f, n, s: (0, 0)),
         ],
-        out_specs=pl.BlockSpec((tm, tn), lambda j, i, f, n, s: (i, j)),
+        out_specs=pl.BlockSpec((tm, width), lambda i, f, n, s: (i, 0)),
     )
     flops = 6 * rows * width * PANEL
     cost = pl.CostEstimate(flops=flops, transcendentals=0, bytes_accessed=rows * width * 8 + width * PANEL * 4)
     return pl.pallas_call(
-        functools.partial(update_kernel, kind, tm, tn),
+        functools.partial(update_kernel, kind, tm, width, len(bases)),
         grid_spec=grid_spec,
         out_shape=jax.ShapeDtypeStruct((rows, width), jnp.float32),
         cost_estimate=cost,
-    )(flags, info, slots, base, a, b_hi, b_lo)
+        compiler_params=pltpu.CompilerParams(vmem_limit_bytes=48 * 1024 * 1024),
+    )(flags, info, slots, *bases, a, b_hi, b_lo)
 
 
 def dot_t(left, right):

time: 484 us -> 455 us (0.940)
  the two profiles are of different devices: /device:TPU:6 before, /device:TPU:2 now
where the time goes in v3:
time: 455 us; the launch traced here: 447 us
  other arithmetic  149 us (33%)
  starting transfers between devices  61.7 us (14%)
  local copies, waits for them, and re-layouts  52.8 us (12%)
  waiting for transfers between devices  50 us (11%)
  matrix products  46.5 us (10%)
  Pallas kernels  40.6 us (9%)
  blocking collectives  29.7 us (7%)
  between operations  17.5 us (4%)
    another operation x14, other arithmetic, per_device(): factor = jnp.linalg.cholesky(kpp)  78.8 us
    another operation x3, other arithmetic, per_device(): finv = lax.linalg.triangular_solve(factor, eye, left_side=True, lower=True)  41.2 us
    pallas_call x3, Pallas kernels, panel_update(): pl.pallas_call(functools.partial(update_kernel, kind, tm, width, len(base...  40.6 us
    all_gather x1, waiting for transfers between devices, per_device(): kpp_col0 = lax.all_gather(kpp_part, 'row', axis=0, tiled=True)  33.7 us
    ppermute x3, starting transfers between devices, per_device(): lax.ppermute(out_k, 'col', [(i, (i + k) % C) for i in range(C)])  27.4 us
    all_gather x1, blocking collectives, per_device(): tseg_all = lax.all_gather(tseg, 'row', axis=0, tiled=False)  23.2 us
    ppermute x4, waiting for transfers between devices, per_device(): got.append(lax.ppermute(payload, AXES, perm))  15.7 us
    another operation x13, local copies, waits for them, and re-layouts  14.1 us
  transfers between devices with their start and end apart: 24, of which 4 were waited for; matrix products, arithmetic and copies ran while one was open for 44% of the time, Pallas kernels for 0%

profile of v3, /device:TPU:2, one launch (start us, length us, event | category | flops | bytes accessed | tf_op | source)
XLA Modules:
  0.0 447.5 jit_solution(16447680102420317486)
XLA Ops:
  23.1 7.2 %fusion.7 = f32[8,2,128,128]{3,2,1,0:T(8,128)S(1)} fusion(bf16[8,2048,128]{2,1,0:T(8,128)(2,1)} %param.6, bf16[8,2048,2,128]{3,2,1,0:T(2,128)(2,1)} %param.7, f32[8,128]{1,0:T(8,128)S(1)} %fusion.49), kind=kOutput, calls=%fused_computation.26 | convolution fusion | flops 1074003968 | bytes 13635584 | tf_op jit(solution)/shard_map/sim,sitp->stmp/dot_general | solution.py:137
  33.0 33.7 %all-gather.11.cloned.1.call-done = f32[512,512]{1,0:T(8,128)} async-done(((f32[64,512]{1,0:T(8,128)}), f32[512,512]{1,0:T(8,128)}) %all-gather.11.cloned.1.call-update) | async-done | bytes 1048592 | tf_op jit(solution)/shard_map/all_gather | solution.py:180
  71.3 6.5 %all-gather = f32[8,128,128]{2,1,0:T(8,128)S(1)} all-gather(f32[2,128,128]{2,1,0:T(8,128)S(1)} %gather_fusion.1), channel_id=2, replica_groups=mesh['row'=8,'col'=4] {'col'}, dimensions={0}, use_global_device_ids=true | all-gather | bytes 655360 | tf_op jit(solution)/shard_map/all_gather | solution.py:171
  79.9 5.6 %collective-permute-start.15 = (f32[128,512]{0,1:T(8,128)}, f32[128,512]{0,1:T(8,128)}, u32[]{:S(2)}, u32[]{:S(2)}) collective-permute-start(f32[128,512]{0,1:T(8,128)} %copy.79), channel_id=1, source_target_pairs={{0,2},{4,6},{8,10},{12,14},{16,18},{20,22},{24,26},{28,30}} | collective-permute-start | bytes 786440 | tf_op jit(solution)/shard_map/ppermute | solution.py:184
  110.3 15.6 %collective-permute-done.5 = f32[320,512]{1,0:T(8,128)} collective-permute-done((f32[320,512]{1,0:T(8,128)}, f32[320,512]{1,0:T(8,128)}, u32[]{:S(2)}, u32[]{:S(2)}) %collective-permute-start.5) | collective-permute-done | bytes 655392 | tf_op jit(solution)/shard_map/ppermute | solution.py:198
  131.8 25.7 %collective-permute-start.18 = (f32[8,128,128]{2,1,0:T(8,128)}, f32[8,128,128]{2,1,0:T(8,128)S(1)}, u32[]{:S(2)}, u32[]{:S(2)}) collective-permute-start(f32[8,128,128]{2,1,0:T(8,128)} %get-tuple-element.44), channel_id=1, source_target_pairs={{0,2},{1,3},{2,0},{3,1},{4,6},{5,7},{6,4},{7,5},{8,10},{9,11},{10,... | collective-permute-start | bytes 1572872 | tf_op jit(solution)/shard_map/ppermute | solution.py:153
  159.2 23.2 %all-gather.3 = s32[8,8,2]{1,2,0:T(2,128)S(1)} all-gather(s32[1,8,2]{1,2,0:T(2,128)S(1)} %bitcast.151), channel_id=4, replica_groups=mesh['row'=8,'col'=4] {'row'}, dimensions={0}, use_global_device_ids=true | all-gather | bytes 576 | tf_op jit(solution)/shard_map/all_gather | solution.py:203
  197.5 11.7 %cholesky.104 = f32[128,128]{1,0:T(8,128)S(1)} custom-call(f32[128,128]{1,0:T(8,128)S(1)} %cholesky.266), custom_call_target="Cholesky" | custom-call | tf_op jit(solution)/shard_map/jit(cholesky)/cholesky | solution.py:211
  209.4 9.8 %custom-call.30 = f32[1,128,128]{1,2,0:T(8,128)S(1)} custom-call(f32[1,128,128]{2,1,0:T(8,128)S(1)} %get-tuple-element.64), custom_call_target="InvertDiagBlocksLowerTriangular" | custom-call | tf_op jit(solution)/shard_map/jit(cholesky)/cholesky | solution.py:211
  221.8 11.9 %cholesky.217 = f32[128,128]{1,0:T(8,128)S(1)} custom-call(f32[128,128]{1,0:T(8,128)S(1)} %cholesky.270), custom_call_target="Cholesky" | custom-call | tf_op jit(solution)/shard_map/jit(cholesky)/cholesky | solution.py:211
  233.7 9.8 %custom-call.31 = f32[1,128,128]{1,2,0:T(8,128)S(1)} custom-call(f32[1,128,128]{2,1,0:T(8,128)S(1)} %get-tuple-element.61), custom_call_target="InvertDiagBlocksLowerTriangular" | custom-call | tf_op jit(solution)/shard_map/jit(cholesky)/cholesky | solution.py:211
  245.1 11.7 %cholesky.238 = f32[128,128]{1,0:T(8,128)S(1)} custom-call(f32[128,128]{1,0:T(8,128)S(1)} %cholesky.275), custom_call_target="Cholesky" | custom-call | tf_op jit(solution)/shard_map/jit(cholesky)/cholesky | solution.py:211
  257.5 9.8 %custom-call.32 = f32[1,128,128]{1,2,0:T(8,128)S(1)} custom-call(f32[1,128,128]{2,1,0:T(8,128)S(1)} %get-tuple-element.58), custom_call_target="InvertDiagBlocksLowerTriangular" | custom-call | tf_op jit(solution)/shard_map/jit(cholesky)/cholesky | solution.py:211
  268.8 11.9 %cholesky.255 = f32[128,128]{1,0:T(8,128)S(1)} custom-call(f32[128,128]{1,0:T(8,128)S(1)} %convolution_subtract_fusion.5), custom_call_target="Cholesky" | custom-call | tf_op jit(solution)/shard_map/jit(cholesky)/cholesky | solution.py:211
  285.7 14.1 %while.1 = (s32[]{:T(128)}, f32[512,512]{1,0:T(8,128)}, s32[4,2]{0,1:T(2,128)S(1)}, f32[4,128,128]{2,1,0:T(8,128)}, s32[]{:T(128)}) while((s32[]{:T(128)}, f32[512,512]{1,0:T(8,128)}, s32[4,2]{0,1:T(2,128)S(1)}, f32[4,128,128]{2,1,0:T(8,128)}, s32[]{:T(128)}) %tuple.63), condition=%wide.while_cond, body=%wide.while_body.sunk | while | flops 2 | bytes 132205 | solution.py:213
  299.7 40.1 %custom-call.33 = f32[4,128,128]{1,2,0:T(8,128)S(1)} custom-call(f32[4,128,128]{2,1,0:T(8,128)} %get-tuple-element.14), custom_call_target="InvertDiagBlocksLowerTriangular" | custom-call | tf_op jit(solution)/shard_map/triangular_solve | solution.py:213
  351.7 8.5 %fusion.19 = f32[3840,512]{1,0:T(8,128)} fusion(f32[128,512]{1,0:T(8,128)S(1)} %fusion.35, f32[128,512]{1,0:T(8,128)S(1)} %fusion.36, f32[128,512]{1,0:T(8,128)S(1)} %fusion.38, f32[128,512]{1,0:T(8,128)S(1)} %fusion.26, f32[512,512]{1,0:T(8,128)S(1)} %bitcast.142, f32[256,512]{1,0:T(8,128)S(1)} %bitcast.139, f32[2048,512]{1,0:T(8,128)} %bitcast.132, ...), kind=kOutput, calls=%fused_computation.52 | convolution fusion | flops 2024669184 | bytes 16777216 | tf_op jit(solution)/shard_map/dot_general | solution.py:104
  360.2 6.5 %fusion.62 = f32[3840,512]{1,0:T(8,128)} fusion(f32[128,512]{1,0:T(8,128)S(1)} %fusion.35, f32[128,512]{1,0:T(8,128)S(1)} %fusion.36, f32[128,512]{1,0:T(8,128)S(1)} %fusion.38, f32[128,512]{1,0:T(8,128)S(1)} %fusion.26, f32[512,512]{1,0:T(8,128)S(1)} %bitcast.143, f32[256,512]{1,0:T(8,128)S(1)} %bitcast.140, f32[2048,512]{1,0:T(8,128)S(1)} %bitcast.134, ...), kind=kOutput, calls=%fused_computation.170 | convolution fusion | flops 2024407040 | bytes 16777216 | tf_op jit(solution)/shard_map/dot_general | solution.py:103
  366.7 13.2 %add_add_fusion = f32[3840,512]{1,0:T(8,128)} fusion(f32[3840,512]{1,0:T(8,128)} %fusion.62, f32[3840,512]{1,0:T(8,128)} %fusion.19, f32[512,512]{1,0:T(8,128)S(1)} %bitcast.144, f32[256,512]{1,0:T(8,128)S(1)} %bitcast.141, f32[2048,512]{1,0:T(8,128)} %bitcast.133, f32[1024,512]{1,0:T(8,128)} %all-gather.9.cloned.1.call-done, f32[128,512]{1,0:T(8,128)S(1)} %fusion.35, ...), kind=kOutput, calls=%fused_computation.14 | convolution fusion | flops 2030305280 | bytes 32505856 | tf_op jit(solution)/shard_map/dot_general | solution.py:105
  382.9 5.0 %fusion.3 = (bf16[2048,512]{1,0:T(8,128)(2,1)}, bf16[2048,512]{1,0:T(8,128)(2,1)}) fusion(f32[3840,512]{1,0:T(8,128)} %add_add_fusion), kind=kLoop, calls=%fused_computation.19 | loop fusion | flops 4194304 | bytes 8388608 | tf_op jit(solution)/shard_map/convert_element_type | solution.py:20
  391.1 4.9 %fusion.4 = (bf16[2048,512]{1,0:T(8,128)(2,1)}, bf16[2048,512]{1,0:T(8,128)(2,1)}) fusion(f32[16,128,512]{2,1,0:T(8,128)} %gather_fusion.5), kind=kLoop, calls=%fused_computation.20 | loop fusion | flops 4194304 | bytes 8388608 | tf_op jit(solution)/shard_map/convert_element_type | solution.py:20
  399.9 21.1 %shard_map.85 = f32[1024,2048]{1,0:T(8,128)} custom-call(s32[8]{0:T(128)S(1)} %broadcast_29_flags_ref.2.flags_ref, s32[4]{0:T(128)S(1)} %get-tuple-element.76.info_ref, s32[1]{0:T(128)} %constant.250.clone.1.slots_ref, f32[1024,2048]{1,0:T(8,128)} %refs_0_.1, f32[1024,512]{1,0:T(8,128)S(1)} %copy-done.1, bf16[2048,512]{1,0:T(8,128)(2,1)S(1)} %copy-done, ...), custom_call_target="tpu_custom_call" | custom-call | flops 6442450944 | bytes 20971520 | tf_op jit(solution)/shard_map/pallas_call | solution.py:90
  421.0 10.5 %shard_map.86 = f32[1024,2048]{1,0:T(8,128)} custom-call(s32[8]{0:T(128)S(1)} %get-tuple-element.71.flags_ref, s32[4]{0:T(128)S(1)} %get-tuple-element.76.info_ref, s32[32]{0:T(128)S(1)} %select_n.327.slots_ref, f32[9,128,512]{2,1,0:T(8,128)} %concatenate.67.refs_0_.refs_1_.refs_2_.refs_3_, f32[9,128,512]{2,1,0:T(8,128)} %concatenate.67.refs_0_.refs_1_.refs_2_.refs_3_, ...), custom_call_target="tpu_custom_call" | custom-call | flops 6442450944 | bytes 20971520 | tf_op jit(solution)/shard_map/pallas_call | solution.py:90
  431.5 9.0 %shard_map.87 = f32[1024,2048]{1,0:T(8,128)} custom-call(s32[8]{0:T(128)S(1)} %get-tuple-element.71.flags_ref, s32[4]{0:T(128)S(1)} %get-tuple-element.75.info_ref, s32[1]{0:T(128)} %constant.250.clone.1.slots_ref, f32[1024,1]{1,0:T(8,128)S(1)} %copy.76.refs_0_, f32[1024,512]{1,0:T(8,128)S(1)} %bitcast.129, bf16[2048,512]{1,0:T(8,128)(2,1)S(1)} %copy-done.2, ...), custom_call_target="tpu_custom_call" | custom-call | flops 6442450944 | bytes 20971520 | tf_op jit(solution)/shard_map/pallas_call | solution.py:90
  (206 shorter events, 117.0 us)
Async XLA Ops:
  7.2 59.5 %all-gather.11.cloned.1.call-start = ((), (), s32[]{:S(2)}) async-start(), calls=%async_computation.1 | async-start | bytes 1179648 | tf_op jit(solution)/shard_map/all_gather | solution.py:180
  8.5 6.9 %collective-permute-start.13 = (f32[64,512]{1,0:T(8,128)S(1)}, f32[64,512]{1,0:T(8,128)S(1)}, u32[]{:S(2)}, u32[]{:S(2)}) collective-permute-start(f32[64,512]{1,0:T(8,128)S(1)} %get-tuple-element.32), channel_id=1, source_target_pairs={{0,4}} | collective-permute-start | bytes 393224 | tf_op jit(solution)/shard_map/ppermute | solution.py:178
  9.8 6.2 %collective-permute-start.12 = (f32[64,512]{1,0:T(8,128)S(1)}, f32[64,512]{1,0:T(8,128)S(1)}, u32[]{:S(2)}, u32[]{:S(2)}) collective-permute-start(f32[64,512]{1,0:T(8,128)S(1)} %get-tuple-element.33), channel_id=1, source_target_pairs={{0,8}} | collective-permute-start | bytes 393224 | tf_op jit(solution)/shard_map/ppermute | solution.py:178
  10.5 6.3 %collective-permute-start.11 = (f32[64,512]{1,0:T(8,128)S(1)}, f32[64,512]{1,0:T(8,128)S(1)}, u32[]{:S(2)}, u32[]{:S(2)}) collective-permute-start(f32[64,512]{1,0:T(8,128)S(1)} %get-tuple-element.34), channel_id=1, source_target_pairs={{0,12}} | collective-permute-start | bytes 393224 | tf_op jit(solution)/shard_map/ppermute | solution.py:178
  11.2 7.7 %collective-permute-start.10 = (f32[64,512]{1,0:T(8,128)S(1)}, f32[64,512]{1,0:T(8,128)S(1)}, u32[]{:S(2)}, u32[]{:S(2)}) collective-permute-start(f32[64,512]{1,0:T(8,128)S(1)} %get-tuple-element.35), channel_id=1, source_target_pairs={{0,16}} | collective-permute-start | bytes 393224 | tf_op jit(solution)/shard_map/ppermute | solution.py:178
  11.9 9.5 %collective-permute-start.9 = (f32[64,512]{1,0:T(8,128)S(1)}, f32[64,512]{1,0:T(8,128)S(1)}, u32[]{:S(2)}, u32[]{:S(2)}) collective-permute-start(f32[64,512]{1,0:T(8,128)S(1)} %get-tuple-element.36), channel_id=1, source_target_pairs={{0,20}} | collective-permute-start | bytes 393224 | tf_op jit(solution)/shard_map/ppermute | solution.py:178
  15.4 6.0 %collective-permute-start.8 = (f32[64,512]{1,0:T(8,128)S(1)}, f32[64,512]{1,0:T(8,128)S(1)}, u32[]{:S(2)}, u32[]{:S(2)}) collective-permute-start(f32[64,512]{1,0:T(8,128)S(1)} %get-tuple-element.37), channel_id=1, source_target_pairs={{0,24}} | collective-permute-start | bytes 393224 | tf_op jit(solution)/shard_map/ppermute | solution.py:178
  16.1 5.3 %collective-permute-start.7 = (f32[64,512]{1,0:T(8,128)S(1)}, f32[64,512]{1,0:T(8,128)S(1)}, u32[]{:S(2)}, u32[]{:S(2)}) collective-permute-start(f32[64,512]{1,0:T(8,128)S(1)} %get-tuple-element.38), channel_id=1, source_target_pairs={{0,28}} | collective-permute-start | bytes 393224 | tf_op jit(solution)/shard_map/ppermute | solution.py:178
  16.8 86.4 %collective-permute-start.2 = (f32[256,512]{1,0:T(8,128)}, f32[256,512]{1,0:T(8,128)}, u32[]{:S(2)}, u32[]{:S(2)}) collective-permute-start(f32[256,512]{1,0:T(8,128)} %get-tuple-element.29), channel_id=1, source_target_pairs={{0,1},{4,5},{8,9},{12,13},{16,17},{20,21},{24,25},{28,29}} | collective-permute-start | bytes 1572872 | tf_op jit(solution)/shard_map/ppermute | solution.py:192
  18.9 86.7 %collective-permute-start.1 = (f32[256,512]{1,0:T(8,128)S(1)}, f32[256,512]{1,0:T(8,128)}, u32[]{:S(2)}, u32[]{:S(2)}) collective-permute-start(f32[256,512]{1,0:T(8,128)S(1)} %get-tuple-element.30), channel_id=1, source_target_pairs={{0,2},{4,6},{8,10},{12,14},{16,18},{20,22},{24,26},{28,30}} | collective-permute-start | bytes 1572872 | tf_op jit(solution)/shard_map/ppermute | solution.py:192
  23.1 170.2 %all-gather.13.cloned.1.call-start = ((), (), s32[]{:S(2)}) async-start(), calls=%async_computation.2 | async-start | bytes 1310720 | tf_op jit(solution)/shard_map/all_gather | solution.py:185
  68.8 19.4 %collective-permute-start.14 = (f32[128,512]{0,1:T(8,128)}, f32[128,512]{0,1:T(8,128)}, u32[]{:S(2)}, u32[]{:S(2)}) collective-permute-start(f32[128,512]{0,1:T(8,128)} %copy.78), channel_id=1, source_target_pairs={{0,3},{4,7},{8,11},{12,15},{16,19},{20,23},{24,27},{28,31}} | collective-permute-start | bytes 786440 | tf_op jit(solution)/shard_map/ppermute | solution.py:184
  79.9 11.4 %collective-permute-start.15 = (f32[128,512]{0,1:T(8,128)}, f32[128,512]{0,1:T(8,128)}, u32[]{:S(2)}, u32[]{:S(2)}) collective-permute-start(f32[128,512]{0,1:T(8,128)} %copy.79), channel_id=1, source_target_pairs={{0,2},{4,6},{8,10},{12,14},{16,18},{20,22},{24,26},{28,30}} | collective-permute-start | bytes 786440 | tf_op jit(solution)/shard_map/ppermute | solution.py:184
  85.5 10.1 %collective-permute-start.16 = (f32[128,512]{0,1:T(8,128)}, f32[128,512]{0,1:T(8,128)}, u32[]{:S(2)}, u32[]{:S(2)}) collective-permute-start(f32[128,512]{0,1:T(8,128)} %copy.80), channel_id=1, source_target_pairs={{0,1},{4,5},{8,9},{12,13},{16,17},{20,21},{24,25},{28,29}} | collective-permute-start | bytes 786440 | tf_op jit(solution)/shard_map/ppermute | solution.py:184
  88.2 17.5 %collective-permute-start = (f32[256,512]{1,0:T(8,128)S(1)}, f32[256,512]{1,0:T(8,128)}, u32[]{:S(2)}, u32[]{:S(2)}) collective-permute-start(f32[256,512]{1,0:T(8,128)S(1)} %get-tuple-element.31), channel_id=1, source_target_pairs={{0,3},{4,7},{8,11},{12,15},{16,19},{20,23},{24,27},{28,31}} | collective-permute-start | bytes 1572872 | tf_op jit(solution)/shard_map/ppermute | solution.py:192
  91.3 18.9 %collective-permute-start.3 = (f32[320,512]{1,0:T(8,128)}, f32[320,512]{1,0:T(8,128)}, u32[]{:S(2)}, u32[]{:S(2)}) collective-permute-start(f32[320,512]{1,0:T(8,128)} %pad_maximum_fusion.3), channel_id=1, source_target_pairs={{0,12},{4,28},{8,13},{12,29},{16,14},{20,30},{24,15},{28,31}} | collective-permute-start | bytes 1966088 | tf_op jit(solution)/shard_map/ppermute | solution.py:198
  96.4 249.3 %all-gather.15.cloned.1.call-start = ((), (), s32[]{:S(2)}) async-start(), calls=%async_computation.3 | async-start | bytes 5898240 | tf_op jit(solution)/shard_map/all_gather | solution.py:199
  98.2 12.0 %collective-permute-start.4 = (f32[320,512]{1,0:T(8,128)}, f32[320,512]{1,0:T(8,128)}, u32[]{:S(2)}, u32[]{:S(2)}) collective-permute-start(f32[320,512]{1,0:T(8,128)} %pad_maximum_fusion.4), channel_id=1, source_target_pairs={{0,8},{4,24},{8,9},{12,25},{16,10},{20,26},{24,11},{28,27}} | collective-permute-start | bytes 1966088 | tf_op jit(solution)/shard_map/ppermute | solution.py:198
  103.2 22.6 %collective-permute-start.5 = (f32[320,512]{1,0:T(8,128)}, f32[320,512]{1,0:T(8,128)}, u32[]{:S(2)}, u32[]{:S(2)}) collective-permute-start(f32[320,512]{1,0:T(8,128)} %pad_maximum_fusion.5), channel_id=1, source_target_pairs={{0,4},{4,20},{8,5},{12,21},{16,6},{20,22},{24,7},{28,23}} | collective-permute-start | bytes 1966088 | tf_op jit(solution)/shard_map/ppermute | solution.py:198
  107.8 18.1 %collective-permute-start.6 = (f32[320,512]{1,0:T(8,128)S(1)}, f32[320,512]{1,0:T(8,128)S(1)}, u32[]{:S(2)}, u32[]{:S(2)}) collective-permute-start(f32[320,512]{1,0:T(8,128)S(1)} %pad_maximum_fusion.6), channel_id=1, source_target_pairs={{0,0},{4,16},{8,1},{12,17},{16,2},{20,18},{24,3},{28,19}} | collective-permute-start | bytes 1966088 | tf_op jit(solution)/shard_map/ppermute | solution.py:198
  128.1 223.6 %all-gather.9.cloned.1.call-start = ((), (), s32[]{:S(2)}) async-start(), calls=%async_computation | async-start | bytes 2621440 | tf_op jit(solution)/shard_map/all_gather | solution.py:193
  131.8 53.3 %collective-permute-start.18 = (f32[8,128,128]{2,1,0:T(8,128)}, f32[8,128,128]{2,1,0:T(8,128)S(1)}, u32[]{:S(2)}, u32[]{:S(2)}) collective-permute-start(f32[8,128,128]{2,1,0:T(8,128)} %get-tuple-element.44), channel_id=1, source_target_pairs={{0,2},{1,3},{2,0},{3,1},{4,6},{5,7},{6,4},{7,5},{8,10},{9,11},{10,... | collective-permute-start | bytes 1572872 | tf_op jit(solution)/shard_map/ppermute | solution.py:153
  157.5 27.6 %collective-permute-start.17 = (f32[8,128,128]{2,1,0:T(8,128)}, f32[8,128,128]{2,1,0:T(8,128)S(1)}, u32[]{:S(2)}, u32[]{:S(2)}) collective-permute-start(f32[8,128,128]{2,1,0:T(8,128)} %get-tuple-element.45), channel_id=1, source_target_pairs={{0,1},{1,2},{2,3},{3,0},{4,5},{5,6},{6,7},{7,4},{8,9},{9,10},{10,1... | collective-permute-start | bytes 1572872 | tf_op jit(solution)/shard_map/ppermute | solution.py:153
  157.5 27.6 %collective-permute-start.19 = (f32[8,128,128]{2,1,0:T(8,128)S(1)}, f32[8,128,128]{2,1,0:T(8,128)S(1)}, u32[]{:S(2)}, u32[]{:S(2)}) collective-permute-start(f32[8,128,128]{2,1,0:T(8,128)S(1)} %get-tuple-element.46), channel_id=1, source_target_pairs={{0,3},{1,0},{2,1},{3,2},{4,7},{5,4},{6,5},{7,6},{8,11},{9,8},{10,9... | collective-permute-start | bytes 1572872 | tf_op jit(solution)/shard_map/ppermute | solution.py:153
  (16 other events, 291.2 us)
Sparse Core Ops, SparseCore 0:
  23.2 43.4 all-gather.10
  96.5 14.0 all-gather.12
  128.2 112.7 all-gather.14
  242.4 21.8 all-gather.8

commit v4 on v3

--- a/solution.py
+++ b/solution.py
@@ -13,6 +13,89 @@
 SUB_ROW = 8
 
 AXES = ("row", "col")
+LEAF = 128
+
+
+def mm3(a, b, dn):
+    a_hi = a.astype(jnp.bfloat16)
+    a_lo = (a - a_hi.astype(jnp.float32)).astype(jnp.bfloat16)
+    b_hi = b.astype(jnp.bfloat16)
+    b_lo = (b - b_hi.astype(jnp.float32)).astype(jnp.bfloat16)
+    out = lax.dot_general(a_hi, b_hi, dn, preferred_element_type=jnp.float32)
+    out = out + lax.dot_general(a_hi, b_lo, dn, preferred_element_type=jnp.float32)
+    return out + lax.dot_general(a_lo, b_hi, dn, preferred_element_type=jnp.float32)
+
+
+NN = (((1,), (0,)), ((), ()))
+NT = (((1,), (1,)), ((), ()))
+
+
+def leaf_inverse(d):
+    n = d.shape[0]
+    sub = lax.broadcasted_iota(jnp.int32, (n, n), 0)
+    lane = lax.broadcasted_iota(jnp.int32, (n, n), 1)
+    sub_c = lax.broadcasted_iota(jnp.int32, (n, 1), 0)
+    lane_r = lax.broadcasted_iota(jnp.int32, (1, n), 1)
+    eye = jnp.where(sub == lane, 1.0, 0.0).astype(jnp.float32)
+
+    def step(k, carry):
+        dm, em, xm = carry
+        colk = jnp.sum(jnp.where(lane == k, dm, 0.0), axis=1, keepdims=True)
+        rowk = jnp.sum(jnp.where(sub == k, dm, 0.0), axis=0, keepdims=True)
+        dkk = jnp.sum(jnp.where(lane_r == k, rowk, 0.0), axis=1, keepdims=True)
+        s = 1.0 / jnp.sqrt(dkk)
+        lc = jnp.where(sub_c > k, colk * s, 0.0)
+        lr = jnp.where(lane_r > k, rowk * s, 0.0)
+        dm = dm - lc * lr
+        erow = jnp.sum(jnp.where(sub == k, em, 0.0), axis=0, keepdims=True)
+        xk = erow * s
+        xm = jnp.where(sub == k, xk, xm)
+        em = em - lc * xk
+        return dm, em, xm
+
+    _, _, xm = lax.fori_loop(0, n, step, (d, eye, jnp.zeros_like(d)))
+    return xm
+
+
+def chol_inv_kernel(a_ref, x_ref, w_ref, l_ref):
+    n = a_ref.shape[0]
+    nb = n // LEAF
+    w_ref[...] = a_ref[...]
+    for kb in range(nb):
+        o = kb * LEAF
+        blk = pl.ds(o, LEAF)
+        xkk = leaf_inverse(w_ref[blk, blk])
+        x_ref[blk, blk] = xkk
+        if kb + 1 < nb:
+            rest = pl.ds(o + LEAF, n - o - LEAF)
+            panel = mm3(w_ref[rest, blk], xkk, NT)
+            l_ref[rest, blk] = panel
+            w_ref[rest, rest] = w_ref[rest, rest] - mm3(panel, panel, NT)
+    for i in range(1, nb):
+        bi = pl.ds(i * LEAF, LEAF)
+        xii = x_ref[bi, bi]
+        for j in range(i):
+            bj = pl.ds(j * LEAF, LEAF)
+            acc = None
+            for k in range(j, i):
+                bk = pl.ds(k * LEAF, LEAF)
+                term = mm3(l_ref[bi, bk], x_ref[bk, bj], NN)
+                acc = term if acc is None else acc + term
+            x_ref[bi, bj] = -mm3(xii, acc, NN)
+        for j in range(i + 1, nb):
+            x_ref[bi, pl.ds(j * LEAF, LEAF)] = jnp.zeros((LEAF, LEAF), jnp.float32)
+    x_ref[pl.ds(0, LEAF), pl.ds(LEAF, n - LEAF)] = jnp.zeros((LEAF, n - LEAF), jnp.float32)
+
+
+def chol_inverse(a):
+    n = a.shape[0]
+    return pl.pallas_call(
+        chol_inv_kernel,
+        out_shape=jax.ShapeDtypeStruct((n, n), jnp.float32),
+        in_specs=[pl.BlockSpec(memory_space=pltpu.VMEM)],
+        out_specs=pl.BlockSpec(memory_space=pltpu.VMEM),
+        scratch_shapes=[pltpu.VMEM((n, n), jnp.float32), pltpu.VMEM((n, n), jnp.float32)],
+    )(a)
 
 
 def split_bf16(x):
@@ -208,9 +291,7 @@
         slot_c.append(jnp.where(has_j, j * cap0 + rank_j, ratio * cap0))
     slot_c = jnp.concatenate(slot_c)
 
-    factor = jnp.linalg.cholesky(kpp)
-    eye = jnp.eye(PANEL, dtype=jnp.float32)
-    finv = lax.linalg.triangular_solve(factor, eye, left_side=True, lower=True)
+    finv = chol_inverse(kpp)
     stacked = jnp.concatenate([m_row, m_col, z_rows, z_col], axis=0)
     solved = dot_t(stacked, finv)
     low_r = solved[:H]

time: 455 us -> 369 us (0.81)
  the two profiles are of different devices: /device:TPU:2 before, /device:TPU:6 now
where the time goes in v4:
time: 369 us; the launch traced here: 366 us
  Pallas kernels  120 us (33%)
  waiting for transfers between devices  89.4 us (24%)
  matrix products  35.1 us (10%)
  local copies, waits for them, and re-layouts  33 us (9%)
  blocking collectives  29.6 us (8%)
  other arithmetic  26.4 us (7%)
  starting transfers between devices  18.3 us (5%)
  between operations  14.4 us (4%)
    pallas_call x1, Pallas kernels, chol_inverse(): pl.pallas_call(chol_inv_kernel, out_shape=jax.ShapeDtypeStruct((n, n), jn...  78.8 us
    ppermute x4, waiting for transfers between devices, per_device(): got.append(lax.ppermute(payload, AXES, perm))  49.5 us
    pallas_call x3, Pallas kernels, panel_update(): pl.pallas_call(functools.partial(update_kernel, kind, tm, width, len(base...  40.7 us
    all_gather x1, waiting for transfers between devices, per_device(): kpp_col0 = lax.all_gather(kpp_part, 'row', axis=0, tiled=True)  36.5 us
    all_gather x1, blocking collectives, per_device(): tseg_all = lax.all_gather(tseg, 'row', axis=0, tiled=False)  22.8 us
    dot_general x1, matrix products, dot_t(): lax.dot_general(l_lo, r_hi, contract, preferred_element_type=jnp.float32)  13.2 us
    convert_element_type x2, other arithmetic, split_bf16(): return (hi.astype(jnp.bfloat16), (x - hi).astype(jnp.bfloat16))  9.99 us
    dot_general x1, matrix products, dot_t(): lax.dot_general(l_hi, r_lo, contract, preferred_element_type=jnp.float32)  8.47 us
  transfers between devices with their start and end apart: 24, of which 3 were waited for; matrix products, arithmetic and copies ran while one was open for 12% of the time, Pallas kernels for 22%

profile of v4, /device:TPU:6, one launch (start us, length us, event | category | flops | bytes accessed | tf_op | source)
XLA Modules:
  0.0 365.8 jit_solution(6814919426780094717)
XLA Ops:
  11.9 2.3 fusion.33
  20.2 7.2 %fusion.7 = f32[8,2,128,128]{3,2,1,0:T(8,128)S(1)} fusion(bf16[8,2048,128]{2,1,0:T(8,128)(2,1)} %param.6, bf16[8,2048,2,128]{3,2,1,0:T(2,128)(2,1)} %param.7, f32[8,128]{1,0:T(8,128)S(1)} %fusion.23), kind=kOutput, calls=%fused_computation.24 | convolution fusion | flops 1074003968 | bytes 13635584 | tf_op jit(solution)/shard_map/sim,sitp->stmp/dot_general | solution.py:220
  30.1 36.5 %all-gather.11.cloned.1.call-done = f32[512,512]{1,0:T(8,128)} async-done(((f32[64,512]{1,0:T(8,128)}), f32[512,512]{1,0:T(8,128)}) %all-gather.11.cloned.1.call-update) | async-done | bytes 1048592 | tf_op jit(solution)/shard_map/all_gather | solution.py:263
  66.6 1.9 fusion.35
  69.1 6.9 %all-gather = f32[8,128,128]{2,1,0:T(8,128)S(1)} all-gather(f32[2,128,128]{2,1,0:T(8,128)S(1)} %gather_fusion.1), channel_id=2, replica_groups=mesh['row'=8,'col'=4] {'col'}, dimensions={0}, use_global_device_ids=true | all-gather | bytes 655360 | tf_op jit(solution)/shard_map/all_gather | solution.py:254
  81.4 3.3 collective-permute-done.15
  89.7 1.9 pad_maximum_fusion.4
  93.0 2.2 select_select_fusion.1
  96.0 49.4 %collective-permute-done.5 = f32[320,512]{1,0:T(8,128)} collective-permute-done((f32[320,512]{1,0:T(8,128)}, f32[320,512]{1,0:T(8,128)}, u32[]{:S(2)}, u32[]{:S(2)}) %collective-permute-start.5) | collective-permute-done | bytes 655392 | tf_op jit(solution)/shard_map/ppermute | solution.py:281
  145.5 2.2 select_select_fusion
  153.2 22.8 %all-gather.3 = s32[8,8,2]{1,2,0:T(2,128)S(1)} all-gather(s32[1,8,2]{1,2,0:T(2,128)S(1)} %bitcast.103), channel_id=4, replica_groups=mesh['row'=8,'col'=4] {'row'}, dimensions={0}, use_global_device_ids=true | all-gather | bytes 576 | tf_op jit(solution)/shard_map/all_gather | solution.py:286
  180.0 2.0 gather_fusion.3
  185.6 78.8 %shard_map.85 = f32[512,512]{1,0:T(8,128)} custom-call(f32[512,512]{1,0:T(8,128)} %all-gather.13.cloned.1.call-done.a_ref), custom_call_target="tpu_custom_call" | custom-call | tf_op jit(solution)/shard_map/pallas_call | solution.py:92
  265.8 4.8 %slice.151 = f32[8,256,512]{2,1,0:T(8,128)} slice(f32[8,320,512]{2,1,0:T(8,128)} %bitcast.89), slice={[0:8], [0:256], [0:512]} | slice | bytes 8388608 | tf_op jit(solution)/shard_map/slice | solution.py:283
  270.5 8.5 %fusion.13 = f32[3840,512]{1,0:T(8,128)} fusion(f32[512,512]{1,0:T(8,128)S(1)} %copy-done.6, f32[512,512]{1,0:T(8,128)S(1)} %bitcast.94, f32[256,512]{1,0:T(8,128)S(1)} %bitcast.91, f32[2048,512]{1,0:T(8,128)} %bitcast.84, f32[1024,512]{1,0:T(8,128)} %all-gather.9.cloned.1.call-done), kind=kOutput, calls=%fused_computation.31 | convolution fusion | flops 2023882752 | bytes 16777216 | tf_op jit(solution)/shard_map/dot_general | solution.py:187
  279.0 6.3 %fusion.17 = f32[3840,512]{1,0:T(8,128)} fusion(f32[512,512]{1,0:T(8,128)S(1)} %copy-done.6, f32[512,512]{1,0:T(8,128)S(1)} %bitcast.95, f32[256,512]{1,0:T(8,128)S(1)} %bitcast.92, f32[2048,512]{1,0:T(8,128)S(1)} %bitcast.86, f32[1024,512]{1,0:T(8,128)S(1)} %copy-done.7), kind=kOutput, calls=%fused_computation.40 | convolution fusion | flops 2023620608 | bytes 16777216 | tf_op jit(solution)/shard_map/dot_general | solution.py:186
  285.3 13.2 %add_add_fusion = f32[3840,512]{1,0:T(8,128)} fusion(f32[3840,512]{1,0:T(8,128)} %fusion.17, f32[3840,512]{1,0:T(8,128)} %fusion.13, f32[512,512]{1,0:T(8,128)S(1)} %bitcast.96, f32[256,512]{1,0:T(8,128)S(1)} %bitcast.93, f32[2048,512]{1,0:T(8,128)} %bitcast.85, f32[1024,512]{1,0:T(8,128)} %all-gather.9.cloned.1.call-done, f32[512,512]{1,0:T(8,128)S(1)} %copy-done.6), kind=kOutput, calls=%fused_computation.12 | convolution fusion | flops 2029518848 | bytes 32505856 | tf_op jit(solution)/shard_map/dot_general | solution.py:188
  298.5 3.1 slice.157.refs_1_
  301.6 5.0 %fusion.3 = (bf16[2048,512]{1,0:T(8,128)(2,1)}, bf16[2048,512]{1,0:T(8,128)(2,1)}) fusion(f32[3840,512]{1,0:T(8,128)} %add_add_fusion), kind=kLoop, calls=%fused_computation.17 | loop fusion | flops 4194304 | bytes 8388608 | tf_op jit(solution)/shard_map/convert_element_type | solution.py:103
  306.9 2.8 gather_fusion.5
  309.7 5.0 %fusion.4 = (bf16[2048,512]{1,0:T(8,128)(2,1)}, bf16[2048,512]{1,0:T(8,128)(2,1)}) fusion(f32[16,128,512]{2,1,0:T(8,128)} %gather_fusion.5), kind=kLoop, calls=%fused_computation.18 | loop fusion | flops 4194304 | bytes 8388608 | tf_op jit(solution)/shard_map/convert_element_type | solution.py:103
  318.6 21.2 %shard_map.86 = f32[1024,2048]{1,0:T(8,128)} custom-call(s32[8]{0:T(128)S(1)} %broadcast_29_flags_ref.2.flags_ref, s32[4]{0:T(128)S(1)} %get-tuple-element.45.info_ref, s32[1]{0:T(128)} %constant.115.clone.1.slots_ref, f32[1024,2048]{1,0:T(8,128)} %refs_0_.1, f32[1024,512]{1,0:T(8,128)S(1)} %copy-done.1, bf16[2048,512]{1,0:T(8,128)(2,1)S(1)} %copy-done, ...), custom_call_target="tpu_custom_call" | custom-call | flops 6442450944 | bytes 20971520 | tf_op jit(solution)/shard_map/pallas_call | solution.py:173
  339.7 10.6 %shard_map.87 = f32[1024,2048]{1,0:T(8,128)} custom-call(s32[8]{0:T(128)S(1)} %get-tuple-element.42.flags_ref, s32[4]{0:T(128)S(1)} %get-tuple-element.45.info_ref, s32[32]{0:T(128)S(1)} %select_n.322.slots_ref, f32[9,128,512]{2,1,0:T(8,128)} %concatenate.59.refs_0_.refs_1_.refs_2_.refs_3_, f32[9,128,512]{2,1,0:T(8,128)} %concatenate.59.refs_0_.refs_1_.refs_2_.refs_3_, ...), custom_call_target="tpu_custom_call" | custom-call | flops 6442450944 | bytes 20971520 | tf_op jit(solution)/shard_map/pallas_call | solution.py:173
  350.3 9.0 %shard_map.88 = f32[1024,2048]{1,0:T(8,128)} custom-call(s32[8]{0:T(128)S(1)} %get-tuple-element.42.flags_ref, s32[4]{0:T(128)S(1)} %get-tuple-element.44.info_ref, s32[1]{0:T(128)} %constant.115.clone.1.slots_ref, f32[1024,1]{1,0:T(8,128)S(1)} %copy.43.refs_0_, f32[1024,512]{1,0:T(8,128)S(1)} %bitcast.81, bf16[2048,512]{1,0:T(8,128)(2,1)S(1)} %copy-done.2, ...), custom_call_target="tpu_custom_call" | custom-call | flops 6442450944 | bytes 20971520 | tf_op jit(solution)/shard_map/pallas_call | solution.py:173
  (148 shorter events, 44.7 us)
Async XLA Ops:
  7.2 59.4 %all-gather.11.cloned.1.call-start = ((), (), s32[]{:S(2)}) async-start(), calls=%async_computation.1 | async-start | bytes 1179648 | tf_op jit(solution)/shard_map/all_gather | solution.py:263
  8.5 5.7 %collective-permute-start.13 = (f32[64,512]{1,0:T(8,128)S(1)}, f32[64,512]{1,0:T(8,128)S(1)}, u32[]{:S(2)}, u32[]{:S(2)}) collective-permute-start(f32[64,512]{1,0:T(8,128)S(1)} %get-tuple-element.14), channel_id=1, source_target_pairs={{0,4}} | collective-permute-start | bytes 393224 | tf_op jit(solution)/shard_map/ppermute | solution.py:261
  9.2 5.7 %collective-permute-start.12 = (f32[64,512]{1,0:T(8,128)S(1)}, f32[64,512]{1,0:T(8,128)S(1)}, u32[]{:S(2)}, u32[]{:S(2)}) collective-permute-start(f32[64,512]{1,0:T(8,128)S(1)} %get-tuple-element.15), channel_id=1, source_target_pairs={{0,8}} | collective-permute-start | bytes 393224 | tf_op jit(solution)/shard_map/ppermute | solution.py:261
  9.9 5.7 %collective-permute-start.11 = (f32[64,512]{1,0:T(8,128)S(1)}, f32[64,512]{1,0:T(8,128)S(1)}, u32[]{:S(2)}, u32[]{:S(2)}) collective-permute-start(f32[64,512]{1,0:T(8,128)S(1)} %get-tuple-element.16), channel_id=1, source_target_pairs={{0,12}} | collective-permute-start | bytes 393224 | tf_op jit(solution)/shard_map/ppermute | solution.py:261
  10.6 6.5 %collective-permute-start.10 = (f32[64,512]{1,0:T(8,128)S(1)}, f32[64,512]{1,0:T(8,128)S(1)}, u32[]{:S(2)}, u32[]{:S(2)}) collective-permute-start(f32[64,512]{1,0:T(8,128)S(1)} %get-tuple-element.17), channel_id=1, source_target_pairs={{0,16}} | collective-permute-start | bytes 393224 | tf_op jit(solution)/shard_map/ppermute | solution.py:261
  11.3 7.2 %collective-permute-start.9 = (f32[64,512]{1,0:T(8,128)S(1)}, f32[64,512]{1,0:T(8,128)S(1)}, u32[]{:S(2)}, u32[]{:S(2)}) collective-permute-start(f32[64,512]{1,0:T(8,128)S(1)} %get-tuple-element.18), channel_id=1, source_target_pairs={{0,20}} | collective-permute-start | bytes 393224 | tf_op jit(solution)/shard_map/ppermute | solution.py:261
  14.2 4.2 %collective-permute-start.8 = (f32[64,512]{1,0:T(8,128)S(1)}, f32[64,512]{1,0:T(8,128)S(1)}, u32[]{:S(2)}, u32[]{:S(2)}) collective-permute-start(f32[64,512]{1,0:T(8,128)S(1)} %get-tuple-element.19), channel_id=1, source_target_pairs={{0,24}} | collective-permute-start | bytes 393224 | tf_op jit(solution)/shard_map/ppermute | solution.py:261
  14.9 3.6 collective-permute-start.7
  15.6 76.0 %collective-permute-start.2 = (f32[256,512]{1,0:T(8,128)}, f32[256,512]{1,0:T(8,128)}, u32[]{:S(2)}, u32[]{:S(2)}) collective-permute-start(f32[256,512]{1,0:T(8,128)} %get-tuple-element.11), channel_id=1, source_target_pairs={{0,1},{4,5},{8,9},{12,13},{16,17},{20,21},{24,25},{28,29}} | collective-permute-start | bytes 1572872 | tf_op jit(solution)/shard_map/ppermute | solution.py:275
  17.1 75.9 %collective-permute-start.1 = (f32[256,512]{1,0:T(8,128)S(1)}, f32[256,512]{1,0:T(8,128)}, u32[]{:S(2)}, u32[]{:S(2)}) collective-permute-start(f32[256,512]{1,0:T(8,128)S(1)} %get-tuple-element.12), channel_id=1, source_target_pairs={{0,2},{4,6},{8,10},{12,14},{16,18},{20,22},{24,26},{28,30}} | collective-permute-start | bytes 1572872 | tf_op jit(solution)/shard_map/ppermute | solution.py:275
  20.1 165.4 %all-gather.13.cloned.1.call-start = ((), (), s32[]{:S(2)}) async-start(), calls=%async_computation.2 | async-start | bytes 1310720 | tf_op jit(solution)/shard_map/all_gather | solution.py:268
  68.4 10.7 %collective-permute-start.16 = (f32[128,512]{1,0:T(8,128)S(1)}, f32[128,512]{1,0:T(8,128)S(1)}, u32[]{:S(2)}, u32[]{:S(2)}) collective-permute-start(f32[128,512]{1,0:T(8,128)S(1)} %get-tuple-element.29), channel_id=1, source_target_pairs={{0,1},{4,5},{8,9},{12,13},{16,17},{20,21},{24,25},{28,29}} | collective-permute-start | bytes 786440 | tf_op jit(solution)/shard_map/ppermute | solution.py:267
  76.4 8.4 %collective-permute-start.15 = (f32[128,512]{1,0:T(8,128)S(1)}, f32[128,512]{1,0:T(8,128)}, u32[]{:S(2)}, u32[]{:S(2)}) collective-permute-start(f32[128,512]{1,0:T(8,128)S(1)} %get-tuple-element.30), channel_id=1, source_target_pairs={{0,2},{4,6},{8,10},{12,14},{16,18},{20,22},{24,26},{28,30}} | collective-permute-start | bytes 786440 | tf_op jit(solution)/shard_map/ppermute | solution.py:267
  77.7 7.8 %collective-permute-start.14 = (f32[128,512]{1,0:T(8,128)}, f32[128,512]{1,0:T(8,128)}, u32[]{:S(2)}, u32[]{:S(2)}) collective-permute-start(f32[128,512]{1,0:T(8,128)} %get-tuple-element.31), channel_id=1, source_target_pairs={{0,3},{4,7},{8,11},{12,15},{16,19},{20,23},{24,27},{28,31}} | collective-permute-start | bytes 786440 | tf_op jit(solution)/shard_map/ppermute | solution.py:267
  79.1 13.9 %collective-permute-start = (f32[256,512]{1,0:T(8,128)S(1)}, f32[256,512]{1,0:T(8,128)}, u32[]{:S(2)}, u32[]{:S(2)}) collective-permute-start(f32[256,512]{1,0:T(8,128)S(1)} %get-tuple-element.13), channel_id=1, source_target_pairs={{0,3},{4,7},{8,11},{12,15},{16,19},{20,23},{24,27},{28,31}} | collective-permute-start | bytes 1572872 | tf_op jit(solution)/shard_map/ppermute | solution.py:275
  84.7 11.3 %collective-permute-start.3 = (f32[320,512]{1,0:T(8,128)}, f32[320,512]{1,0:T(8,128)S(1)}, u32[]{:S(2)}, u32[]{:S(2)}) collective-permute-start(f32[320,512]{1,0:T(8,128)} %pad_maximum_fusion.2), channel_id=1, source_target_pairs={{0,12},{4,28},{8,13},{12,29},{16,14},{20,30},{24,15},{28,31}} | collective-permute-start | bytes 1966088 | tf_op jit(solution)/shard_map/ppermute | solution.py:281
  87.3 177.1 %all-gather.15.cloned.1.call-start = ((), (), s32[]{:S(2)}) async-start(), calls=%async_computation.3 | async-start | bytes 5898240 | tf_op jit(solution)/shard_map/all_gather | solution.py:282
  88.2 7.8 %collective-permute-start.4 = (f32[320,512]{1,0:T(8,128)}, f32[320,512]{1,0:T(8,128)}, u32[]{:S(2)}, u32[]{:S(2)}) collective-permute-start(f32[320,512]{1,0:T(8,128)} %pad_maximum_fusion.3), channel_id=1, source_target_pairs={{0,8},{4,24},{8,9},{12,25},{16,10},{20,26},{24,11},{28,27}} | collective-permute-start | bytes 1966088 | tf_op jit(solution)/shard_map/ppermute | solution.py:281
  91.7 53.8 %collective-permute-start.5 = (f32[320,512]{1,0:T(8,128)}, f32[320,512]{1,0:T(8,128)}, u32[]{:S(2)}, u32[]{:S(2)}) collective-permute-start(f32[320,512]{1,0:T(8,128)} %pad_maximum_fusion.4), channel_id=1, source_target_pairs={{0,4},{4,20},{8,5},{12,21},{16,6},{20,22},{24,7},{28,23}} | collective-permute-start | bytes 1966088 | tf_op jit(solution)/shard_map/ppermute | solution.py:281
  95.3 50.2 %collective-permute-start.6 = (f32[320,512]{1,0:T(8,128)S(1)}, f32[320,512]{1,0:T(8,128)S(1)}, u32[]{:S(2)}, u32[]{:S(2)}) collective-permute-start(f32[320,512]{1,0:T(8,128)S(1)} %pad_maximum_fusion.5), channel_id=1, source_target_pairs={{0,0},{4,16},{8,1},{12,17},{16,2},{20,18},{24,3},{28,19}} | collective-permute-start | bytes 1966088 | tf_op jit(solution)/shard_map/ppermute | solution.py:281
  147.7 122.8 %all-gather.9.cloned.1.call-start = ((), (), s32[]{:S(2)}) async-start(), calls=%async_computation | async-start | bytes 2621440 | tf_op jit(solution)/shard_map/all_gather | solution.py:276
  151.4 26.0 %collective-permute-start.18 = (f32[8,128,128]{2,1,0:T(8,128)}, f32[8,128,128]{2,1,0:T(8,128)S(1)}, u32[]{:S(2)}, u32[]{:S(2)}) collective-permute-start(f32[8,128,128]{2,1,0:T(8,128)} %get-tuple-element.26), channel_id=1, source_target_pairs={{0,2},{1,3},{2,0},{3,1},{4,6},{5,7},{6,4},{7,5},{8,10},{9,11},{10,... | collective-permute-start | bytes 1572872 | tf_op jit(solution)/shard_map/ppermute | solution.py:236
  151.4 26.0 %collective-permute-start.17 = (f32[8,128,128]{2,1,0:T(8,128)}, f32[8,128,128]{2,1,0:T(8,128)S(1)}, u32[]{:S(2)}, u32[]{:S(2)}) collective-permute-start(f32[8,128,128]{2,1,0:T(8,128)} %get-tuple-element.27), channel_id=1, source_target_pairs={{0,1},{1,2},{2,3},{3,0},{4,5},{5,6},{6,7},{7,4},{8,9},{9,10},{10,1... | collective-permute-start | bytes 1572872 | tf_op jit(solution)/shard_map/ppermute | solution.py:236
  151.4 26.0 %collective-permute-start.19 = (f32[8,128,128]{2,1,0:T(8,128)S(1)}, f32[8,128,128]{2,1,0:T(8,128)S(1)}, u32[]{:S(2)}, u32[]{:S(2)}) collective-permute-start(f32[8,128,128]{2,1,0:T(8,128)S(1)} %get-tuple-element.28), channel_id=1, source_target_pairs={{0,3},{1,0},{2,1},{3,2},{4,7},{5,4},{6,5},{7,6},{8,11},{9,8},{10,9... | collective-permute-start | bytes 1572872 | tf_op jit(solution)/shard_map/ppermute | solution.py:236
  (15 other events, 98.2 us)
Sparse Core Ops, SparseCore 0:
  20.2 46.2 all-gather.10
  87.4 17.1 all-gather.12
  147.9 88.6 all-gather.14
  238.0 20.7 all-gather.8

commit v5 on v4

--- a/solution.py
+++ b/solution.py
@@ -92,6 +92,7 @@
     return pl.pallas_call(
         chol_inv_kernel,
         out_shape=jax.ShapeDtypeStruct((n, n), jnp.float32),
+        cost_estimate=pl.CostEstimate(flops=60 * n ** 3, transcendentals=n, bytes_accessed=8 * n * n),
         in_specs=[pl.BlockSpec(memory_space=pltpu.VMEM)],
         out_specs=pl.BlockSpec(memory_space=pltpu.VMEM),
         scratch_shapes=[pltpu.VMEM((n, n), jnp.float32), pltpu.VMEM((n, n), jnp.float32)],
@@ -179,6 +180,34 @@
     )(flags, info, slots, *bases, a, b_hi, b_lo)
 
 
+def solve_kernel(x_ref, fhi_ref, flo_ref, out_ref):
+    x = x_ref[...]
+    x_hi = x.astype(jnp.bfloat16)
+    x_lo = (x - x_hi.astype(jnp.float32)).astype(jnp.bfloat16)
+    f_hi = fhi_ref[...]
+    acc = lax.dot_general(x_hi, f_hi, NT, preferred_element_type=jnp.float32)
+    acc = acc + lax.dot_general(x_hi, flo_ref[...], NT, preferred_element_type=jnp.float32)
+    out_ref[...] = acc + lax.dot_general(x_lo, f_hi, NT, preferred_element_type=jnp.float32)
+
+
+def apply_inverse(x, finv):
+    rows = x.shape[0]
+    tm = 256 if rows % 256 == 0 else MSLOT
+    f_hi, f_lo = split_bf16(finv)
+    return pl.pallas_call(
+        solve_kernel,
+        grid=(rows // tm,),
+        in_specs=[
+            pl.BlockSpec((tm, PANEL), lambda i: (i, 0)),
+            pl.BlockSpec((PANEL, PANEL), lambda i: (0, 0)),
+            pl.BlockSpec((PANEL, PANEL), lambda i: (0, 0)),
+        ],
+        out_specs=pl.BlockSpec((tm, PANEL), lambda i: (i, 0)),
+        out_shape=jax.ShapeDtypeStruct((rows, PANEL), jnp.float32),
+        cost_estimate=pl.CostEstimate(flops=6 * rows * PANEL * PANEL, transcendentals=0, bytes_accessed=8 * rows * PANEL),
+    )(x, f_hi, f_lo)
+
+
 def dot_t(left, right):
     contract = (((1,), (1,)), ((), ()))
     l_hi, l_lo = split_bf16(left)
@@ -293,7 +322,7 @@
 
     finv = chol_inverse(kpp)
     stacked = jnp.concatenate([m_row, m_col, z_rows, z_col], axis=0)
-    solved = dot_t(stacked, finv)
+    solved = apply_inverse(stacked, finv)
     low_r = solved[:H]
     low_c = solved[H:H + W]
     lowmi_r = solved[H + W:H + W + cap0 * MSLOT]

time: 369 us -> 365 us (0.989)
  matrix products: 35.1 us -> 7.19 us
  Pallas kernels: 120 us -> 135 us
  other arithmetic: 26.4 us -> 34.1 us
    dot_general x3 -> x0, matrix products: 28 us -> none  [the longest x1 13.2 us: dot_t(): lax.dot_general(l_lo, r_hi, contract, preferred_element_type=jnp.float32)]
    pallas_call x0 -> x1, Pallas kernels: none -> 15.9 us  [apply_inverse(): pl.pallas_call(solve_kernel, grid=(rows // tm,), in_specs=[pl.BlockSpec((...]
    concatenate x0 -> x1, other arithmetic: none -> 5.41 us  [per_device(): stacked = jnp.concatenate([m_row, m_col, z_rows, z_col], axis=0)]
    convert_element_type x2 -> x3, other arithmetic: 9.99 us -> 12.3 us  [split_bf16(): return (hi.astype(jnp.bfloat16), (x - hi).astype(jnp.bfloat16))]
  transfers between devices with their start and end apart: 24 -> 24, of which waited for: 3 -> 3; matrix products, arithmetic and copies ran while one was open for 12% -> 13% of each run, Pallas kernels for 22% -> 22%
where the time goes in v5:
time: 365 us; the launch traced here: 361 us
  Pallas kernels  135 us (37%)
  waiting for transfers between devices  89 us (24%)
  other arithmetic  34.1 us (9%)
  local copies, waits for them, and re-layouts  33.3 us (9%)
  blocking collectives  29.7 us (8%)
  starting transfers between devices  18.3 us (5%)
  between operations  14.4 us (4%)
  matrix products  7.19 us (2%)
    pallas_call x1, Pallas kernels, chol_inverse(): pl.pallas_call(chol_inv_kernel, out_shape=jax.ShapeDtypeStruct((n, n), jn...  78.6 us
    ppermute x4, waiting for transfers between devices, per_device(): got.append(lax.ppermute(payload, AXES, perm))  49.4 us
    pallas_call x3, Pallas kernels, panel_update(): pl.pallas_call(functools.partial(update_kernel, kind, tm, width, len(base...  40.2 us
    all_gather x1, waiting for transfers between devices, per_device(): kpp_col0 = lax.all_gather(kpp_part, 'row', axis=0, tiled=True)  36.2 us
    all_gather x1, blocking collectives, per_device(): tseg_all = lax.all_gather(tseg, 'row', axis=0, tiled=False)  22.9 us
    pallas_call x1, Pallas kernels, apply_inverse(): pl.pallas_call(solve_kernel, grid=(rows // tm,), in_specs=[pl.BlockSpec((...  15.9 us
    convert_element_type x3, other arithmetic, split_bf16(): return (hi.astype(jnp.bfloat16), (x - hi).astype(jnp.bfloat16))  12.3 us
    select_n x4, other arithmetic, pick(): out = jnp.where(index == i, options[i], out)  7.97 us
  transfers between devices with their start and end apart: 24, of which 3 were waited for; matrix products, arithmetic and copies ran while one was open for 13% of the time, Pallas kernels for 22%

profile of v5, /device:TPU:6, one launch (start us, length us, event | category | flops | bytes accessed | tf_op | source)
XLA Modules:
  0.0 360.8 jit_solution(834851081098660777)
XLA Ops:
  11.9 2.3 fusion.28
  20.2 7.2 %fusion.5 = f32[8,2,128,128]{3,2,1,0:T(8,128)S(1)} fusion(bf16[8,2048,128]{2,1,0:T(8,128)(2,1)} %param.6, bf16[8,2048,2,128]{3,2,1,0:T(2,128)(2,1)} %param.7, f32[8,128]{1,0:T(8,128)S(1)} %fusion.18), kind=kOutput, calls=%fused_computation.20 | convolution fusion | flops 1074003968 | bytes 13635584 | tf_op jit(solution)/shard_map/sim,sitp->stmp/dot_general | solution.py:249
  30.4 36.2 %all-gather.11.cloned.1.call-done = f32[512,512]{1,0:T(8,128)} async-done(((f32[64,512]{1,0:T(8,128)}), f32[512,512]{1,0:T(8,128)}) %all-gather.11.cloned.1.call-update) | async-done | bytes 1048592 | tf_op jit(solution)/shard_map/all_gather | solution.py:292
  66.6 1.9 fusion.29
  69.1 6.9 %all-gather = f32[8,128,128]{2,1,0:T(8,128)S(1)} all-gather(f32[2,128,128]{2,1,0:T(8,128)S(1)} %gather_fusion.1), channel_id=2, replica_groups=mesh['row'=8,'col'=4] {'col'}, dimensions={0}, use_global_device_ids=true | all-gather | bytes 655360 | tf_op jit(solution)/shard_map/all_gather | solution.py:283
  81.4 3.3 collective-permute-done.15
  89.8 1.9 pad_maximum_fusion.4
  93.0 2.2 select_select_fusion.1
  96.0 49.4 %collective-permute-done.5 = f32[320,512]{1,0:T(8,128)} collective-permute-done((f32[320,512]{1,0:T(8,128)}, f32[320,512]{1,0:T(8,128)}, u32[]{:S(2)}, u32[]{:S(2)}) %collective-permute-start.5) | collective-permute-done | bytes 655392 | tf_op jit(solution)/shard_map/ppermute | solution.py:310
  145.5 2.2 select_select_fusion
  153.2 22.9 %all-gather.3 = s32[8,8,2]{1,2,0:T(2,128)S(1)} all-gather(s32[1,8,2]{1,2,0:T(2,128)S(1)} %bitcast.97), channel_id=4, replica_groups=mesh['row'=8,'col'=4] {'row'}, dimensions={0}, use_global_device_ids=true | all-gather | bytes 576 | tf_op jit(solution)/shard_map/all_gather | solution.py:315
  180.1 2.0 gather_fusion.3
  185.7 78.6 %shard_map.85 = f32[512,512]{1,0:T(8,128)} custom-call(f32[512,512]{1,0:T(8,128)} %all-gather.13.cloned.1.call-done.a_ref), custom_call_target="tpu_custom_call" | custom-call | flops 8053063680 | bytes 2097152 | tf_op jit(solution)/shard_map/pallas_call | solution.py:92
  264.4 2.3 fusion.10
  268.1 4.7 %slice.151 = f32[8,256,512]{2,1,0:T(8,128)} slice(f32[8,320,512]{2,1,0:T(8,128)} %bitcast.87), slice={[0:8], [0:256], [0:512]} | slice | bytes 8388608 | tf_op jit(solution)/shard_map/slice | solution.py:312
  272.8 5.4 %pad_maximum_fusion.x_ref = f32[3840,512]{1,0:T(8,128)} fusion(f32[512,512]{1,0:T(8,128)S(1)} %bitcast.90, f32[256,512]{1,0:T(8,128)S(1)} %bitcast.89, f32[2048,512]{1,0:T(8,128)} %bitcast.82, f32[1024,512]{1,0:T(8,128)} %all-gather.9.cloned.1.call-done), kind=kLoop, calls=%fused_computation.8 | loop fusion | flops 5898240 | bytes 15728640 | tf_op jit(solution)/shard_map/concatenate | solution.py:324
  278.2 15.9 %shard_map.86 = f32[3840,512]{1,0:T(8,128)} custom-call(f32[3840,512]{1,0:T(8,128)} %pad_maximum_fusion.x_ref, bf16[512,512]{1,0:T(8,128)(2,1)} %get-tuple-element.30.fhi_ref, bf16[512,512]{1,0:T(8,128)(2,1)} %get-tuple-element.29.flo_ref), custom_call_target="tpu_custom_call" | custom-call | flops 6039797760 | bytes 15728640 | tf_op jit(solution)/shard_map/pallas_call | solution.py:197
  294.0 3.1 slice.157.refs_1_
  297.1 5.0 %fusion.2 = (bf16[2048,512]{1,0:T(8,128)(2,1)}, bf16[2048,512]{1,0:T(8,128)(2,1)}) fusion(f32[3840,512]{1,0:T(8,128)} %shard_map.86), kind=kLoop, calls=%fused_computation.13 | loop fusion | flops 4194304 | bytes 8388608 | tf_op jit(solution)/shard_map/convert_element_type | solution.py:104
  302.4 2.8 gather_fusion.5
  305.2 5.0 %fusion.3 = (bf16[2048,512]{1,0:T(8,128)(2,1)}, bf16[2048,512]{1,0:T(8,128)(2,1)}) fusion(f32[16,128,512]{2,1,0:T(8,128)} %gather_fusion.5), kind=kLoop, calls=%fused_computation.14 | loop fusion | flops 4194304 | bytes 8388608 | tf_op jit(solution)/shard_map/convert_element_type | solution.py:104
  314.1 20.9 %shard_map.87 = f32[1024,2048]{1,0:T(8,128)} custom-call(s32[8]{0:T(128)S(1)} %broadcast_29_flags_ref.2.flags_ref, s32[4]{0:T(128)S(1)} %get-tuple-element.47.info_ref, s32[1]{0:T(128)} %constant.115.clone.1.slots_ref, f32[1024,2048]{1,0:T(8,128)} %refs_0_.1, f32[1024,512]{1,0:T(8,128)S(1)} %copy-done.1, bf16[2048,512]{1,0:T(8,128)(2,1)S(1)} %copy-done, ...), custom_call_target="tpu_custom_call" | custom-call | flops 6442450944 | bytes 20971520 | tf_op jit(solution)/shard_map/pallas_call | solution.py:174
  335.0 10.3 %shard_map.88 = f32[1024,2048]{1,0:T(8,128)} custom-call(s32[8]{0:T(128)S(1)} %get-tuple-element.44.flags_ref, s32[4]{0:T(128)S(1)} %get-tuple-element.47.info_ref, s32[32]{0:T(128)S(1)} %select_n.322.slots_ref, f32[9,128,512]{2,1,0:T(8,128)} %concatenate.59.refs_0_.refs_1_.refs_2_.refs_3_, f32[9,128,512]{2,1,0:T(8,128)} %concatenate.59.refs_0_.refs_1_.refs_2_.refs_3_, ...), custom_call_target="tpu_custom_call" | custom-call | flops 6442450944 | bytes 20971520 | tf_op jit(solution)/shard_map/pallas_call | solution.py:174
  345.3 9.0 %shard_map.89 = f32[1024,2048]{1,0:T(8,128)} custom-call(s32[8]{0:T(128)S(1)} %get-tuple-element.44.flags_ref, s32[4]{0:T(128)S(1)} %get-tuple-element.46.info_ref, s32[1]{0:T(128)} %constant.115.clone.1.slots_ref, f32[1024,1]{1,0:T(8,128)S(1)} %copy.42.refs_0_, f32[1024,512]{1,0:T(8,128)S(1)} %bitcast.81, bf16[2048,512]{1,0:T(8,128)(2,1)S(1)} %copy-done.2, ...), custom_call_target="tpu_custom_call" | custom-call | flops 6442450944 | bytes 20971520 | tf_op jit(solution)/shard_map/pallas_call | solution.py:174
  (142 shorter events, 45.0 us)
Async XLA Ops:
  7.2 59.4 %all-gather.11.cloned.1.call-start = ((), (), s32[]{:S(2)}) async-start(), calls=%async_computation.1 | async-start | bytes 1179648 | tf_op jit(solution)/shard_map/all_gather | solution.py:292
  8.5 5.7 %collective-permute-start.13 = (f32[64,512]{1,0:T(8,128)S(1)}, f32[64,512]{1,0:T(8,128)S(1)}, u32[]{:S(2)}, u32[]{:S(2)}) collective-permute-start(f32[64,512]{1,0:T(8,128)S(1)} %get-tuple-element.9), channel_id=1, source_target_pairs={{0,4}} | collective-permute-start | bytes 393224 | tf_op jit(solution)/shard_map/ppermute | solution.py:290
  9.2 5.7 %collective-permute-start.12 = (f32[64,512]{1,0:T(8,128)S(1)}, f32[64,512]{1,0:T(8,128)S(1)}, u32[]{:S(2)}, u32[]{:S(2)}) collective-permute-start(f32[64,512]{1,0:T(8,128)S(1)} %get-tuple-element.10), channel_id=1, source_target_pairs={{0,8}} | collective-permute-start | bytes 393224 | tf_op jit(solution)/shard_map/ppermute | solution.py:290
  9.9 5.8 %collective-permute-start.11 = (f32[64,512]{1,0:T(8,128)S(1)}, f32[64,512]{1,0:T(8,128)S(1)}, u32[]{:S(2)}, u32[]{:S(2)}) collective-permute-start(f32[64,512]{1,0:T(8,128)S(1)} %get-tuple-element.11), channel_id=1, source_target_pairs={{0,12}} | collective-permute-start | bytes 393224 | tf_op jit(solution)/shard_map/ppermute | solution.py:290
  10.6 6.6 %collective-permute-start.10 = (f32[64,512]{1,0:T(8,128)S(1)}, f32[64,512]{1,0:T(8,128)S(1)}, u32[]{:S(2)}, u32[]{:S(2)}) collective-permute-start(f32[64,512]{1,0:T(8,128)S(1)} %get-tuple-element.12), channel_id=1, source_target_pairs={{0,16}} | collective-permute-start | bytes 393224 | tf_op jit(solution)/shard_map/ppermute | solution.py:290
  11.3 7.2 %collective-permute-start.9 = (f32[64,512]{1,0:T(8,128)S(1)}, f32[64,512]{1,0:T(8,128)S(1)}, u32[]{:S(2)}, u32[]{:S(2)}) collective-permute-start(f32[64,512]{1,0:T(8,128)S(1)} %get-tuple-element.13), channel_id=1, source_target_pairs={{0,20}} | collective-permute-start | bytes 393224 | tf_op jit(solution)/shard_map/ppermute | solution.py:290
  14.2 4.2 %collective-permute-start.8 = (f32[64,512]{1,0:T(8,128)S(1)}, f32[64,512]{1,0:T(8,128)S(1)}, u32[]{:S(2)}, u32[]{:S(2)}) collective-permute-start(f32[64,512]{1,0:T(8,128)S(1)} %get-tuple-element.14), channel_id=1, source_target_pairs={{0,24}} | collective-permute-start | bytes 393224 | tf_op jit(solution)/shard_map/ppermute | solution.py:290
  14.9 3.6 collective-permute-start.7
  15.7 76.1 %collective-permute-start.2 = (f32[256,512]{1,0:T(8,128)}, f32[256,512]{1,0:T(8,128)}, u32[]{:S(2)}, u32[]{:S(2)}) collective-permute-start(f32[256,512]{1,0:T(8,128)} %get-tuple-element.18), channel_id=1, source_target_pairs={{0,1},{4,5},{8,9},{12,13},{16,17},{20,21},{24,25},{28,29}} | collective-permute-start | bytes 1572872 | tf_op jit(solution)/shard_map/ppermute | solution.py:304
  17.1 75.9 %collective-permute-start.1 = (f32[256,512]{1,0:T(8,128)S(1)}, f32[256,512]{1,0:T(8,128)}, u32[]{:S(2)}, u32[]{:S(2)}) collective-permute-start(f32[256,512]{1,0:T(8,128)S(1)} %get-tuple-element.19), channel_id=1, source_target_pairs={{0,2},{4,6},{8,10},{12,14},{16,18},{20,22},{24,26},{28,30}} | collective-permute-start | bytes 1572872 | tf_op jit(solution)/shard_map/ppermute | solution.py:304
  20.1 165.6 %all-gather.13.cloned.1.call-start = ((), (), s32[]{:S(2)}) async-start(), calls=%async_computation.2 | async-start | bytes 1310720 | tf_op jit(solution)/shard_map/all_gather | solution.py:297
  68.4 10.6 %collective-permute-start.16 = (f32[128,512]{1,0:T(8,128)S(1)}, f32[128,512]{1,0:T(8,128)S(1)}, u32[]{:S(2)}, u32[]{:S(2)}) collective-permute-start(f32[128,512]{1,0:T(8,128)S(1)} %get-tuple-element.31), channel_id=1, source_target_pairs={{0,1},{4,5},{8,9},{12,13},{16,17},{20,21},{24,25},{28,29}} | collective-permute-start | bytes 786440 | tf_op jit(solution)/shard_map/ppermute | solution.py:296
  76.4 8.4 %collective-permute-start.15 = (f32[128,512]{1,0:T(8,128)S(1)}, f32[128,512]{1,0:T(8,128)}, u32[]{:S(2)}, u32[]{:S(2)}) collective-permute-start(f32[128,512]{1,0:T(8,128)S(1)} %get-tuple-element.32), channel_id=1, source_target_pairs={{0,2},{4,6},{8,10},{12,14},{16,18},{20,22},{24,26},{28,30}} | collective-permute-start | bytes 786440 | tf_op jit(solution)/shard_map/ppermute | solution.py:296
  77.7 7.8 %collective-permute-start.14 = (f32[128,512]{1,0:T(8,128)}, f32[128,512]{1,0:T(8,128)}, u32[]{:S(2)}, u32[]{:S(2)}) collective-permute-start(f32[128,512]{1,0:T(8,128)} %get-tuple-element.33), channel_id=1, source_target_pairs={{0,3},{4,7},{8,11},{12,15},{16,19},{20,23},{24,27},{28,31}} | collective-permute-start | bytes 786440 | tf_op jit(solution)/shard_map/ppermute | solution.py:296
  79.1 13.9 %collective-permute-start = (f32[256,512]{1,0:T(8,128)S(1)}, f32[256,512]{1,0:T(8,128)}, u32[]{:S(2)}, u32[]{:S(2)}) collective-permute-start(f32[256,512]{1,0:T(8,128)S(1)} %get-tuple-element.20), channel_id=1, source_target_pairs={{0,3},{4,7},{8,11},{12,15},{16,19},{20,23},{24,27},{28,31}} | collective-permute-start | bytes 1572872 | tf_op jit(solution)/shard_map/ppermute | solution.py:304
  84.7 11.3 %collective-permute-start.3 = (f32[320,512]{1,0:T(8,128)}, f32[320,512]{1,0:T(8,128)S(1)}, u32[]{:S(2)}, u32[]{:S(2)}) collective-permute-start(f32[320,512]{1,0:T(8,128)} %pad_maximum_fusion.2), channel_id=1, source_target_pairs={{0,12},{4,28},{8,13},{12,29},{16,14},{20,30},{24,15},{28,31}} | collective-permute-start | bytes 1966088 | tf_op jit(solution)/shard_map/ppermute | solution.py:310
  87.3 179.4 %all-gather.15.cloned.1.call-start = ((), (), s32[]{:S(2)}) async-start(), calls=%async_computation.3 | async-start | bytes 5898240 | tf_op jit(solution)/shard_map/all_gather | solution.py:311
  88.3 7.8 %collective-permute-start.4 = (f32[320,512]{1,0:T(8,128)}, f32[320,512]{1,0:T(8,128)}, u32[]{:S(2)}, u32[]{:S(2)}) collective-permute-start(f32[320,512]{1,0:T(8,128)} %pad_maximum_fusion.3), channel_id=1, source_target_pairs={{0,8},{4,24},{8,9},{12,25},{16,10},{20,26},{24,11},{28,27}} | collective-permute-start | bytes 1966088 | tf_op jit(solution)/shard_map/ppermute | solution.py:310
  91.7 53.8 %collective-permute-start.5 = (f32[320,512]{1,0:T(8,128)}, f32[320,512]{1,0:T(8,128)}, u32[]{:S(2)}, u32[]{:S(2)}) collective-permute-start(f32[320,512]{1,0:T(8,128)} %pad_maximum_fusion.4), channel_id=1, source_target_pairs={{0,4},{4,20},{8,5},{12,21},{16,6},{20,22},{24,7},{28,23}} | collective-permute-start | bytes 1966088 | tf_op jit(solution)/shard_map/ppermute | solution.py:310
  95.3 50.2 %collective-permute-start.6 = (f32[320,512]{1,0:T(8,128)S(1)}, f32[320,512]{1,0:T(8,128)S(1)}, u32[]{:S(2)}, u32[]{:S(2)}) collective-permute-start(f32[320,512]{1,0:T(8,128)S(1)} %pad_maximum_fusion.5), channel_id=1, source_target_pairs={{0,0},{4,16},{8,1},{12,17},{16,2},{20,18},{24,3},{28,19}} | collective-permute-start | bytes 1966088 | tf_op jit(solution)/shard_map/ppermute | solution.py:310
  147.7 125.0 %all-gather.9.cloned.1.call-start = ((), (), s32[]{:S(2)}) async-start(), calls=%async_computation | async-start | bytes 2621440 | tf_op jit(solution)/shard_map/all_gather | solution.py:305
  151.4 26.1 %collective-permute-start.18 = (f32[8,128,128]{2,1,0:T(8,128)}, f32[8,128,128]{2,1,0:T(8,128)S(1)}, u32[]{:S(2)}, u32[]{:S(2)}) collective-permute-start(f32[8,128,128]{2,1,0:T(8,128)} %get-tuple-element.26), channel_id=1, source_target_pairs={{0,2},{1,3},{2,0},{3,1},{4,6},{5,7},{6,4},{7,5},{8,10},{9,11},{10,... | collective-permute-start | bytes 1572872 | tf_op jit(solution)/shard_map/ppermute | solution.py:265
  151.4 26.1 %collective-permute-start.17 = (f32[8,128,128]{2,1,0:T(8,128)}, f32[8,128,128]{2,1,0:T(8,128)S(1)}, u32[]{:S(2)}, u32[]{:S(2)}) collective-permute-start(f32[8,128,128]{2,1,0:T(8,128)} %get-tuple-element.27), channel_id=1, source_target_pairs={{0,1},{1,2},{2,3},{3,0},{4,5},{5,6},{6,7},{7,4},{8,9},{9,10},{10,1... | collective-permute-start | bytes 1572872 | tf_op jit(solution)/shard_map/ppermute | solution.py:265
  151.4 26.2 %collective-permute-start.19 = (f32[8,128,128]{2,1,0:T(8,128)S(1)}, f32[8,128,128]{2,1,0:T(8,128)S(1)}, u32[]{:S(2)}, u32[]{:S(2)}) collective-permute-start(f32[8,128,128]{2,1,0:T(8,128)S(1)} %get-tuple-element.28), channel_id=1, source_target_pairs={{0,3},{1,0},{2,1},{3,2},{4,7},{5,4},{6,5},{7,6},{8,11},{9,8},{10,9... | collective-permute-start | bytes 1572872 | tf_op jit(solution)/shard_map/ppermute | solution.py:265
  (12 other events, 68.7 us)
Sparse Core Ops, SparseCore 0:
  20.3 46.2 all-gather.10
  87.4 17.1 all-gather.12
  147.9 88.5 all-gather.14
  237.9 20.8 all-gather.8

commit v6 on v5

--- a/solution.py
+++ b/solution.py
@@ -251,6 +251,21 @@
     flat = pieces.reshape(npair, MSLOT, Ec)
     flat_pad = jnp.concatenate([flat, jnp.zeros((1, MSLOT, Ec), jnp.float32)], axis=0)
 
+    kpp_src = stiff[:PANEL, :PANEL]
+    rs = PANEL // R
+    got = [kpp_src[:rs]]
+    for i in range(1, R):
+        got.append(lax.ppermute(kpp_src[i * rs:(i + 1) * rs], AXES, [(0, i * C)]))
+    kpp_part = pick(r, got)
+    kpp_col0 = lax.all_gather(kpp_part, "row", axis=0, tiled=True)
+    cs = PANEL // C
+    got = [kpp_col0[:cs]]
+    for k in range(1, C):
+        got.append(lax.ppermute(kpp_col0[k * cs:(k + 1) * cs], AXES, [(i * C, i * C + k) for i in range(R)]))
+    kpp = lax.all_gather(pick(c, got), "col", axis=0, tiled=True)
+
+    finv = chol_inverse(kpp)
+
     tseg = tree_segments
     dest = (tseg // G).reshape(npair)
     onehot = dest[:, None] == jnp.arange(C, dtype=jnp.int32)[None, :]
@@ -259,6 +274,7 @@
     match = onehot[:, :, None] & (rank_pd[:, :, None] == jnp.arange(cap, dtype=jnp.int32)[None, None, :])
     send_idx = jnp.where(jnp.any(match, axis=0), jnp.argmax(match, axis=0), npair)
     send = flat_pad[send_idx]
+    send, _ = lax.optimization_barrier((send, finv))
     shifted = [send[c]]
     for k in range(1, C):
         out_k = lax.dynamic_index_in_dim(send, (c + k) % C, axis=0, keepdims=False)
@@ -282,19 +298,6 @@
     z_local = flat_pad[zidx]
     z_all = lax.all_gather(z_local, "col", axis=0, tiled=False)
     z_rows = z_all.transpose(1, 2, 0, 3).reshape(cap0 * MSLOT, C * Ec)
-
-    kpp_src = stiff[:PANEL, :PANEL]
-    rs = PANEL // R
-    got = [kpp_src[:rs]]
-    for i in range(1, R):
-        got.append(lax.ppermute(kpp_src[i * rs:(i + 1) * rs], AXES, [(0, i * C)]))
-    kpp_part = pick(r, got)
-    kpp_col0 = lax.all_gather(kpp_part, "row", axis=0, tiled=True)
-    cs = PANEL // C
-    got = [kpp_col0[:cs]]
-    for k in range(1, C):
-        got.append(lax.ppermute(kpp_col0[k * cs:(k + 1) * cs], AXES, [(i * C, i * C + k) for i in range(R)]))
-    kpp = lax.all_gather(pick(c, got), "col", axis=0, tiled=True)
 
     m_src = stiff[:, :PANEL]
     rps = W // R
@@ -312,7 +315,8 @@
     m_col = col_parts[:, :rps].reshape(W, PANEL)
     z_col = col_parts[:, rps:].reshape(ratio * cap0 * MSLOT, PANEL)
 
-    tseg_all = lax.all_gather(tseg, "row", axis=0, tiled=False)
+    tseg_late, _ = lax.optimization_barrier((tseg, finv))
+    tseg_all = lax.all_gather(tseg_late, "row", axis=0, tiled=False)
     tseg_c = lax.dynamic_slice_in_dim(tseg_all, c * ratio, ratio, axis=0)
     slot_c = []
     for j in range(ratio):
@@ -320,7 +324,6 @@
         slot_c.append(jnp.where(has_j, j * cap0 + rank_j, ratio * cap0))
     slot_c = jnp.concatenate(slot_c)
 
-    finv = chol_inverse(kpp)
     stacked = jnp.concatenate([m_row, m_col, z_rows, z_col], axis=0)
     solved = apply_inverse(stacked, finv)
     low_r = solved[:H]

time: 365 us -> 383 us (1.049)
  waiting for transfers between devices: 89 us -> 109 us
    ppermute x3, waiting for transfers between devices: 0.01 us -> 22.9 us  [per_device(): lax.ppermute(out_k, 'col', [(i, (i + k) % C) for i in range(C)])]
  transfers between devices with their start and end apart: 24 -> 24, of which waited for: 3 -> 6; matrix products, arithmetic and copies ran while one was open for 13% -> 12% of each run, Pallas kernels for 22% -> 21%
where the time goes in v6:
time: 383 us; the launch traced here: 379 us
  Pallas kernels  135 us (35%)
  waiting for transfers between devices  109 us (28%)
  local copies, waits for them, and re-layouts  33.2 us (9%)
  other arithmetic  33.1 us (9%)
  blocking collectives  29.6 us (8%)
  starting transfers between devices  18.1 us (5%)
  between operations  14.3 us (4%)
  matrix products  7.19 us (2%)
    pallas_call x1, Pallas kernels, chol_inverse(): pl.pallas_call(chol_inv_kernel, out_shape=jax.ShapeDtypeStruct((n, n), jn...  78.8 us
    ppermute x4, waiting for transfers between devices, per_device(): got.append(lax.ppermute(payload, AXES, perm))  46 us
    pallas_call x3, Pallas kernels, panel_update(): pl.pallas_call(functools.partial(update_kernel, kind, tm, width, len(base...  40.1 us
    all_gather x1, waiting for transfers between devices, per_device(): kpp_col0 = lax.all_gather(kpp_part, 'row', axis=0, tiled=True)  36.2 us
    ppermute x3, waiting for transfers between devices, per_device(): lax.ppermute(out_k, 'col', [(i, (i + k) % C) for i in range(C)])  22.9 us
    all_gather x1, blocking collectives, per_device(): tseg_all = lax.all_gather(tseg_late, 'row', axis=0, tiled=False)  22.8 us
    pallas_call x1, Pallas kernels, apply_inverse(): pl.pallas_call(solve_kernel, grid=(rows // tm,), in_specs=[pl.BlockSpec((...  15.9 us
    convert_element_type x3, other arithmetic, split_bf16(): return (hi.astype(jnp.bfloat16), (x - hi).astype(jnp.bfloat16))  11 us
  transfers between devices with their start and end apart: 24, of which 6 were waited for; matrix products, arithmetic and copies ran while one was open for 12% of the time, Pallas kernels for 21%

profile of v6, /device:TPU:6, one launch (start us, length us, event | category | flops | bytes accessed | tf_op | source)
XLA Modules:
  0.0 378.7 jit_solution(4650326316228100930)
XLA Ops:
  11.9 2.5 fusion.28
  20.3 7.2 %fusion.5 = f32[8,2,128,128]{3,2,1,0:T(8,128)S(1)} fusion(bf16[8,2048,128]{2,1,0:T(8,128)(2,1)} %param.6, bf16[8,2048,2,128]{3,2,1,0:T(2,128)(2,1)} %param.7, f32[8,128]{1,0:T(8,128)S(1)} %fusion.18), kind=kOutput, calls=%fused_computation.20 | convolution fusion | flops 1074003968 | bytes 13635584 | tf_op jit(solution)/shard_map/sim,sitp->stmp/dot_general | solution.py:249
  30.6 36.2 %all-gather.11.cloned.1.call-done = f32[512,512]{1,0:T(8,128)} async-done(((f32[64,512]{1,0:T(8,128)}), f32[512,512]{1,0:T(8,128)}) %all-gather.11.cloned.1.call-update) | async-done | bytes 1048592 | tf_op jit(solution)/shard_map/all_gather | solution.py:260
  69.4 6.9 %all-gather = f32[8,128,128]{2,1,0:T(8,128)S(1)} all-gather(f32[2,128,128]{2,1,0:T(8,128)S(1)} %gather_fusion.1), channel_id=2, replica_groups=mesh['row'=8,'col'=4] {'col'}, dimensions={0}, use_global_device_ids=true | all-gather | bytes 655360 | tf_op jit(solution)/shard_map/all_gather | solution.py:299
  81.7 3.4 collective-permute-done.15
  95.1 2.3 select_select_fusion.1
  99.2 46.0 %collective-permute-done.5 = f32[320,512]{1,0:T(8,128)} collective-permute-done((f32[320,512]{1,0:T(8,128)}, f32[320,512]{1,0:T(8,128)}, u32[]{:S(2)}, u32[]{:S(2)}) %collective-permute-start.5) | collective-permute-done | bytes 655392 | tf_op jit(solution)/shard_map/ppermute | solution.py:313
  145.1 2.1 select_select_fusion
  149.9 2.0 gather_fusion.2
  152.0 78.8 %shard_map.85 = f32[512,512]{1,0:T(8,128)} custom-call(f32[512,512]{1,0:T(8,128)} %all-gather.13.cloned.1.call-done.a_ref), custom_call_target="tpu_custom_call" | custom-call | flops 8053063680 | bytes 2097152 | tf_op jit(solution)/shard_map/pallas_call | solution.py:92
  230.8 22.8 %all-gather.3 = s32[8,8,2]{1,2,0:T(2,128)S(1)} all-gather(s32[1,8,2]{1,2,0:T(2,128)S(1)} %bitcast.97), channel_id=4, replica_groups=mesh['row'=8,'col'=4] {'row'}, dimensions={0}, use_global_device_ids=true | all-gather | bytes 576 | tf_op jit(solution)/shard_map/all_gather | solution.py:319
  256.4 10.7 %collective-permute-done.19 = f32[8,128,128]{2,1,0:T(8,128)S(1)} collective-permute-done((f32[8,128,128]{2,1,0:T(8,128)S(1)}, f32[8,128,128]{2,1,0:T(8,128)S(1)}, u32[]{:S(2)}, u32[]{:S(2)}) %collective-permute-start.19) | collective-permute-done | bytes 524320 | tf_op jit(solution)/shard_map/ppermute | solution.py:281
  267.0 11.2 %collective-permute-done.18 = f32[8,128,128]{2,1,0:T(8,128)S(1)} collective-permute-done((f32[8,128,128]{2,1,0:T(8,128)S(1)}, f32[8,128,128]{2,1,0:T(8,128)S(1)}, u32[]{:S(2)}, u32[]{:S(2)}) %collective-permute-start.18) | collective-permute-done | bytes 524320 | tf_op jit(solution)/shard_map/ppermute | solution.py:281
  279.4 2.0 gather_fusion.3
  286.3 4.6 %slice.151 = f32[8,256,512]{2,1,0:T(8,128)} slice(f32[8,320,512]{2,1,0:T(8,128)} %bitcast.87), slice={[0:8], [0:256], [0:512]} | slice | bytes 8388608 | tf_op jit(solution)/shard_map/slice | solution.py:315
  290.9 5.4 %pad_maximum_fusion.x_ref = f32[3840,512]{1,0:T(8,128)} fusion(f32[512,512]{1,0:T(8,128)S(1)} %bitcast.90, f32[256,512]{1,0:T(8,128)S(1)} %bitcast.89, f32[2048,512]{1,0:T(8,128)} %bitcast.82, f32[1024,512]{1,0:T(8,128)} %all-gather.9.cloned.1.call-done), kind=kLoop, calls=%fused_computation.8 | loop fusion | flops 5898240 | bytes 15728640 | tf_op jit(solution)/shard_map/concatenate | solution.py:327
  296.3 15.9 %shard_map.86 = f32[3840,512]{1,0:T(8,128)} custom-call(f32[3840,512]{1,0:T(8,128)} %pad_maximum_fusion.x_ref, bf16[512,512]{1,0:T(8,128)(2,1)} %get-tuple-element.34.fhi_ref, bf16[512,512]{1,0:T(8,128)(2,1)} %get-tuple-element.33.flo_ref), custom_call_target="tpu_custom_call" | custom-call | flops 6039797760 | bytes 15728640 | tf_op jit(solution)/shard_map/pallas_call | solution.py:197
  312.2 3.1 slice.157.refs_1_
  315.3 4.9 %fusion.2 = (bf16[2048,512]{1,0:T(8,128)(2,1)}, bf16[2048,512]{1,0:T(8,128)(2,1)}) fusion(f32[3840,512]{1,0:T(8,128)} %shard_map.86), kind=kLoop, calls=%fused_computation.13 | loop fusion | flops 4194304 | bytes 8388608 | tf_op jit(solution)/shard_map/convert_element_type | solution.py:104
  320.5 2.8 gather_fusion.5
  323.3 4.9 %fusion.3 = (bf16[2048,512]{1,0:T(8,128)(2,1)}, bf16[2048,512]{1,0:T(8,128)(2,1)}) fusion(f32[16,128,512]{2,1,0:T(8,128)} %gather_fusion.5), kind=kLoop, calls=%fused_computation.14 | loop fusion | flops 4194304 | bytes 8388608 | tf_op jit(solution)/shard_map/convert_element_type | solution.py:104
  332.1 20.9 %shard_map.87 = f32[1024,2048]{1,0:T(8,128)} custom-call(s32[8]{0:T(128)S(1)} %broadcast_29_flags_ref.2.flags_ref, s32[4]{0:T(128)S(1)} %get-tuple-element.51.info_ref, s32[1]{0:T(128)} %constant.115.clone.1.slots_ref, f32[1024,2048]{1,0:T(8,128)} %refs_0_.1, f32[1024,512]{1,0:T(8,128)S(1)} %copy-done.1, bf16[2048,512]{1,0:T(8,128)(2,1)S(1)} %copy-done, ...), custom_call_target="tpu_custom_call" | custom-call | flops 6442450944 | bytes 20971520 | tf_op jit(solution)/shard_map/pallas_call | solution.py:174
  353.1 10.2 %shard_map.88 = f32[1024,2048]{1,0:T(8,128)} custom-call(s32[8]{0:T(128)S(1)} %get-tuple-element.48.flags_ref, s32[4]{0:T(128)S(1)} %get-tuple-element.51.info_ref, s32[32]{0:T(128)S(1)} %select_n.322.slots_ref, f32[9,128,512]{2,1,0:T(8,128)} %concatenate.59.refs_0_.refs_1_.refs_2_.refs_3_, f32[9,128,512]{2,1,0:T(8,128)} %concatenate.59.refs_0_.refs_1_.refs_2_.refs_3_, ...), custom_call_target="tpu_custom_call" | custom-call | flops 6442450944 | bytes 20971520 | tf_op jit(solution)/shard_map/pallas_call | solution.py:174
  363.2 9.0 %shard_map.89 = f32[1024,2048]{1,0:T(8,128)} custom-call(s32[8]{0:T(128)S(1)} %get-tuple-element.48.flags_ref, s32[4]{0:T(128)S(1)} %get-tuple-element.50.info_ref, s32[1]{0:T(128)} %constant.115.clone.1.slots_ref, f32[1024,1]{1,0:T(8,128)S(1)} %copy.42.refs_0_, f32[1024,512]{1,0:T(8,128)S(1)} %bitcast.81, bf16[2048,512]{1,0:T(8,128)(2,1)S(1)} %copy-done.2, ...), custom_call_target="tpu_custom_call" | custom-call | flops 6442450944 | bytes 20971520 | tf_op jit(solution)/shard_map/pallas_call | solution.py:174
  (138 shorter events, 48.8 us)
Async XLA Ops:
  7.2 59.6 %all-gather.11.cloned.1.call-start = ((), (), s32[]{:S(2)}) async-start(), calls=%async_computation.1 | async-start | bytes 1179648 | tf_op jit(solution)/shard_map/all_gather | solution.py:260
  8.5 5.9 %collective-permute-start.13 = (f32[64,512]{1,0:T(8,128)S(1)}, f32[64,512]{1,0:T(8,128)S(1)}, u32[]{:S(2)}, u32[]{:S(2)}) collective-permute-start(f32[64,512]{1,0:T(8,128)S(1)} %get-tuple-element.13), channel_id=1, source_target_pairs={{0,4}} | collective-permute-start | bytes 393224 | tf_op jit(solution)/shard_map/ppermute | solution.py:258
  9.2 5.8 %collective-permute-start.12 = (f32[64,512]{1,0:T(8,128)S(1)}, f32[64,512]{1,0:T(8,128)S(1)}, u32[]{:S(2)}, u32[]{:S(2)}) collective-permute-start(f32[64,512]{1,0:T(8,128)S(1)} %get-tuple-element.14), channel_id=1, source_target_pairs={{0,8}} | collective-permute-start | bytes 393224 | tf_op jit(solution)/shard_map/ppermute | solution.py:258
  9.9 5.9 %collective-permute-start.11 = (f32[64,512]{1,0:T(8,128)S(1)}, f32[64,512]{1,0:T(8,128)S(1)}, u32[]{:S(2)}, u32[]{:S(2)}) collective-permute-start(f32[64,512]{1,0:T(8,128)S(1)} %get-tuple-element.15), channel_id=1, source_target_pairs={{0,12}} | collective-permute-start | bytes 393224 | tf_op jit(solution)/shard_map/ppermute | solution.py:258
  10.6 6.7 %collective-permute-start.10 = (f32[64,512]{1,0:T(8,128)S(1)}, f32[64,512]{1,0:T(8,128)S(1)}, u32[]{:S(2)}, u32[]{:S(2)}) collective-permute-start(f32[64,512]{1,0:T(8,128)S(1)} %get-tuple-element.16), channel_id=1, source_target_pairs={{0,16}} | collective-permute-start | bytes 393224 | tf_op jit(solution)/shard_map/ppermute | solution.py:258
  11.3 7.3 %collective-permute-start.9 = (f32[64,512]{1,0:T(8,128)S(1)}, f32[64,512]{1,0:T(8,128)S(1)}, u32[]{:S(2)}, u32[]{:S(2)}) collective-permute-start(f32[64,512]{1,0:T(8,128)S(1)} %get-tuple-element.17), channel_id=1, source_target_pairs={{0,20}} | collective-permute-start | bytes 393224 | tf_op jit(solution)/shard_map/ppermute | solution.py:258
  14.4 4.2 %collective-permute-start.8 = (f32[64,512]{1,0:T(8,128)S(1)}, f32[64,512]{1,0:T(8,128)S(1)}, u32[]{:S(2)}, u32[]{:S(2)}) collective-permute-start(f32[64,512]{1,0:T(8,128)S(1)} %get-tuple-element.18), channel_id=1, source_target_pairs={{0,24}} | collective-permute-start | bytes 393224 | tf_op jit(solution)/shard_map/ppermute | solution.py:258
  15.1 3.5 collective-permute-start.7
  15.8 78.0 %collective-permute-start.2 = (f32[256,512]{1,0:T(8,128)}, f32[256,512]{1,0:T(8,128)}, u32[]{:S(2)}, u32[]{:S(2)}) collective-permute-start(f32[256,512]{1,0:T(8,128)} %get-tuple-element.22), channel_id=1, source_target_pairs={{0,1},{4,5},{8,9},{12,13},{16,17},{20,21},{24,25},{28,29}} | collective-permute-start | bytes 1572872 | tf_op jit(solution)/shard_map/ppermute | solution.py:307
  17.3 77.8 %collective-permute-start.1 = (f32[256,512]{1,0:T(8,128)}, f32[256,512]{1,0:T(8,128)}, u32[]{:S(2)}, u32[]{:S(2)}) collective-permute-start(f32[256,512]{1,0:T(8,128)} %get-tuple-element.23), channel_id=1, source_target_pairs={{0,2},{4,6},{8,10},{12,14},{16,18},{20,22},{24,26},{28,30}} | collective-permute-start | bytes 1572872 | tf_op jit(solution)/shard_map/ppermute | solution.py:307
  20.3 131.7 %all-gather.13.cloned.1.call-start = ((), (), s32[]{:S(2)}) async-start(), calls=%async_computation.2 | async-start | bytes 1310720 | tf_op jit(solution)/shard_map/all_gather | solution.py:265
  68.7 10.6 %collective-permute-start.16 = (f32[128,512]{1,0:T(8,128)S(1)}, f32[128,512]{1,0:T(8,128)S(1)}, u32[]{:S(2)}, u32[]{:S(2)}) collective-permute-start(f32[128,512]{1,0:T(8,128)S(1)} %get-tuple-element.35), channel_id=1, source_target_pairs={{0,1},{4,5},{8,9},{12,13},{16,17},{20,21},{24,25},{28,29}} | collective-permute-start | bytes 786440 | tf_op jit(solution)/shard_map/ppermute | solution.py:264
  76.6 8.5 %collective-permute-start.15 = (f32[128,512]{1,0:T(8,128)}, f32[128,512]{1,0:T(8,128)S(1)}, u32[]{:S(2)}, u32[]{:S(2)}) collective-permute-start(f32[128,512]{1,0:T(8,128)} %get-tuple-element.36), channel_id=1, source_target_pairs={{0,2},{4,6},{8,10},{12,14},{16,18},{20,22},{24,26},{28,30}} | collective-permute-start | bytes 786440 | tf_op jit(solution)/shard_map/ppermute | solution.py:264
  77.9 8.7 %collective-permute-start.14 = (f32[128,512]{1,0:T(8,128)}, f32[128,512]{1,0:T(8,128)}, u32[]{:S(2)}, u32[]{:S(2)}) collective-permute-start(f32[128,512]{1,0:T(8,128)} %get-tuple-element.37), channel_id=1, source_target_pairs={{0,3},{4,7},{8,11},{12,15},{16,19},{20,23},{24,27},{28,31}} | collective-permute-start | bytes 786440 | tf_op jit(solution)/shard_map/ppermute | solution.py:264
  79.3 15.8 %collective-permute-start = (f32[256,512]{1,0:T(8,128)S(1)}, f32[256,512]{1,0:T(8,128)}, u32[]{:S(2)}, u32[]{:S(2)}) collective-permute-start(f32[256,512]{1,0:T(8,128)S(1)} %get-tuple-element.24), channel_id=1, source_target_pairs={{0,3},{4,7},{8,11},{12,15},{16,19},{20,23},{24,27},{28,31}} | collective-permute-start | bytes 1572872 | tf_op jit(solution)/shard_map/ppermute | solution.py:307
  85.1 14.1 %collective-permute-start.3 = (f32[320,512]{1,0:T(8,128)}, f32[320,512]{1,0:T(8,128)}, u32[]{:S(2)}, u32[]{:S(2)}) collective-permute-start(f32[320,512]{1,0:T(8,128)} %pad_maximum_fusion.2), channel_id=1, source_target_pairs={{0,12},{4,28},{8,13},{12,29},{16,14},{20,30},{24,15},{28,31}} | collective-permute-start | bytes 1966088 | tf_op jit(solution)/shard_map/ppermute | solution.py:313
  88.4 196.6 %all-gather.15.cloned.1.call-start = ((), (), s32[]{:S(2)}) async-start(), calls=%async_computation.3 | async-start | bytes 5898240 | tf_op jit(solution)/shard_map/all_gather | solution.py:314
  90.4 8.8 %collective-permute-start.4 = (f32[320,512]{1,0:T(8,128)}, f32[320,512]{1,0:T(8,128)}, u32[]{:S(2)}, u32[]{:S(2)}) collective-permute-start(f32[320,512]{1,0:T(8,128)} %pad_maximum_fusion.3), channel_id=1, source_target_pairs={{0,8},{4,24},{8,9},{12,25},{16,10},{20,26},{24,11},{28,27}} | collective-permute-start | bytes 1966088 | tf_op jit(solution)/shard_map/ppermute | solution.py:313
  93.8 51.3 %collective-permute-start.5 = (f32[320,512]{1,0:T(8,128)}, f32[320,512]{1,0:T(8,128)}, u32[]{:S(2)}, u32[]{:S(2)}) collective-permute-start(f32[320,512]{1,0:T(8,128)} %pad_maximum_fusion.4), channel_id=1, source_target_pairs={{0,4},{4,20},{8,5},{12,21},{16,6},{20,22},{24,7},{28,23}} | collective-permute-start | bytes 1966088 | tf_op jit(solution)/shard_map/ppermute | solution.py:313
  98.3 46.8 %collective-permute-start.6 = (f32[320,512]{1,0:T(8,128)}, f32[320,512]{1,0:T(8,128)S(1)}, u32[]{:S(2)}, u32[]{:S(2)}) collective-permute-start(f32[320,512]{1,0:T(8,128)} %pad_maximum_fusion.5), channel_id=1, source_target_pairs={{0,0},{4,16},{8,1},{12,17},{16,2},{20,18},{24,3},{28,19}} | collective-permute-start | bytes 1966088 | tf_op jit(solution)/shard_map/ppermute | solution.py:313
  147.3 143.6 %all-gather.9.cloned.1.call-start = ((), (), s32[]{:S(2)}) async-start(), calls=%async_computation | async-start | bytes 2621440 | tf_op jit(solution)/shard_map/all_gather | solution.py:308
  254.1 12.9 %collective-permute-start.19 = (f32[8,128,128]{2,1,0:T(8,128)S(1)}, f32[8,128,128]{2,1,0:T(8,128)S(1)}, u32[]{:S(2)}, u32[]{:S(2)}) collective-permute-start(f32[8,128,128]{2,1,0:T(8,128)S(1)} %get-tuple-element.30), channel_id=1, source_target_pairs={{0,3},{1,0},{2,1},{3,2},{4,7},{5,4},{6,5},{7,6},{8,11},{9,8},{10,9... | collective-permute-start | bytes 1572872 | tf_op jit(solution)/shard_map/ppermute | solution.py:281
  254.2 24.0 %collective-permute-start.18 = (f32[8,128,128]{2,1,0:T(8,128)S(1)}, f32[8,128,128]{2,1,0:T(8,128)S(1)}, u32[]{:S(2)}, u32[]{:S(2)}) collective-permute-start(f32[8,128,128]{2,1,0:T(8,128)S(1)} %get-tuple-element.31), channel_id=1, source_target_pairs={{0,2},{1,3},{2,0},{3,1},{4,6},{5,7},{6,4},{7,5},{8,10},{9,11},{10,... | collective-permute-start | bytes 1572872 | tf_op jit(solution)/shard_map/ppermute | solution.py:281
  254.3 25.0 %collective-permute-start.17 = (f32[8,128,128]{2,1,0:T(8,128)S(1)}, f32[8,128,128]{2,1,0:T(8,128)S(1)}, u32[]{:S(2)}, u32[]{:S(2)}) collective-permute-start(f32[8,128,128]{2,1,0:T(8,128)S(1)} %get-tuple-element.32), channel_id=1, source_target_pairs={{0,1},{1,2},{2,3},{3,0},{4,5},{5,6},{6,7},{7,4},{8,9},{9,10},{10,1... | collective-permute-start | bytes 1572872 | tf_op jit(solution)/shard_map/ppermute | solution.py:281
  (10 other events, 186.8 us)
Sparse Core Ops, SparseCore 0:
  20.4 46.2 all-gather.10
  88.5 17.2 all-gather.12
  147.4 88.6 all-gather.14
  237.5 24.7 all-gather.8

commit v7 on v6

--- a/solution.py
+++ b/solution.py
@@ -306,22 +306,22 @@
     for k in range(1, C):
         got.append(lax.ppermute(m_src[k * rps:(k + 1) * rps], AXES, [(i * C, i * C + k) for i in range(R)]))
     m_row = lax.all_gather(pick(c, got), "col", axis=0, tiled=True)
+    slot_row = jnp.zeros((8, PANEL), jnp.float32).at[0, :nsub].set(slot_r.astype(jnp.float32))
     got = []
     for k in range(C):
-        payload = jnp.concatenate([m_src[k * rps:(k + 1) * rps], z_rows[k * zps:(k + 1) * zps]], axis=0)
+        payload = jnp.concatenate(
+            [m_src[k * rps:(k + 1) * rps], z_rows[k * zps:(k + 1) * zps], slot_row], axis=0
+        )
         perm = [(i * C, ((i % ratio) * C + k) * C + i // ratio) for i in range(R)]
         got.append(lax.ppermute(payload, AXES, perm))
     col_parts = lax.all_gather(pick(r % C, got), "row", axis=0, tiled=False)
     m_col = col_parts[:, :rps].reshape(W, PANEL)
-    z_col = col_parts[:, rps:].reshape(ratio * cap0 * MSLOT, PANEL)
-
-    tseg_late, _ = lax.optimization_barrier((tseg, finv))
-    tseg_all = lax.all_gather(tseg_late, "row", axis=0, tiled=False)
-    tseg_c = lax.dynamic_slice_in_dim(tseg_all, c * ratio, ratio, axis=0)
+    z_col = col_parts[:, rps:rps + zps].reshape(ratio * cap0 * MSLOT, PANEL)
+
     slot_c = []
     for j in range(ratio):
-        has_j, rank_j, _ = seg0_slots(tseg_c[j], cap0)
-        slot_c.append(jnp.where(has_j, j * cap0 + rank_j, ratio * cap0))
+        got_slot = col_parts[j * C, rps + zps, :nsub].astype(jnp.int32)
+        slot_c.append(jnp.where(got_slot < cap0, j * cap0 + got_slot, ratio * cap0))
     slot_c = jnp.concatenate(slot_c)
 
     stacked = jnp.concatenate([m_row, m_col, z_rows, z_col], axis=0)

time: 383 us -> 391 us (1.021)
  waiting for transfers between devices: 109 us -> 133 us
  blocking collectives: 29.6 us -> 12.3 us
    all_gather x1 -> x0, blocking collectives: 22.8 us -> none  [per_device(): tseg_all = lax.all_gather(tseg_late, 'row', axis=0, tiled=False)]
    ppermute x4, waiting for transfers between devices: 46 us -> 65.9 us  [per_device(): got.append(lax.ppermute(payload, AXES, perm))]
    ppermute x3, waiting for transfers between devices: 22.9 us -> 30.3 us  [per_device(): lax.ppermute(out_k, 'col', [(i, (i + k) % C) for i in range(C)])]
    all_gather x1, blocking collectives: 6.86 us -> 12.3 us  [per_device(): z_all = lax.all_gather(z_local, 'col', axis=0, tiled=False)]
    concatenate x4 -> x1, other arithmetic: 5.66 us -> 1.62 us  [per_device(): jnp.concatenate([m_src[k * rps:(k + 1) * rps], z_rows[k * zps:(k + 1) * z...]
  transfers between devices with their start and end apart: 24 -> 24, of which waited for: 6 -> 4; matrix products, arithmetic and copies ran while one was open for 12% -> 12% of each run, Pallas kernels for 21% -> 20%
where the time goes in v7:
time: 391 us; the launch traced here: 385 us
  Pallas kernels  135 us (35%)
  waiting for transfers between devices  133 us (34%)
  local copies, waits for them, and re-layouts  34.5 us (9%)
  other arithmetic  32.8 us (8%)
  starting transfers between devices  15.5 us (4%)
  between operations  14.4 us (4%)
  blocking collectives  12.3 us (3%)
  matrix products  7.19 us (2%)
    pallas_call x1, Pallas kernels, chol_inverse(): pl.pallas_call(chol_inv_kernel, out_shape=jax.ShapeDtypeStruct((n, n), jn...  78.6 us
    ppermute x4, waiting for transfers between devices, per_device(): got.append(lax.ppermute(payload, AXES, perm))  65.9 us
    pallas_call x3, Pallas kernels, panel_update(): pl.pallas_call(functools.partial(update_kernel, kind, tm, width, len(base...  40.1 us
    all_gather x1, waiting for transfers between devices, per_device(): kpp_col0 = lax.all_gather(kpp_part, 'row', axis=0, tiled=True)  37.1 us
    ppermute x3, waiting for transfers between devices, per_device(): lax.ppermute(out_k, 'col', [(i, (i + k) % C) for i in range(C)])  30.3 us
    pallas_call x1, Pallas kernels, apply_inverse(): pl.pallas_call(solve_kernel, grid=(rows // tm,), in_specs=[pl.BlockSpec((...  15.9 us
    all_gather x1, blocking collectives, per_device(): z_all = lax.all_gather(z_local, 'col', axis=0, tiled=False)  12.3 us
    convert_element_type x3, other arithmetic, split_bf16(): return (hi.astype(jnp.bfloat16), (x - hi).astype(jnp.bfloat16))  12.2 us
  transfers between devices with their start and end apart: 24, of which 4 were waited for; matrix products, arithmetic and copies ran while one was open for 12% of the time, Pallas kernels for 20%

profile of v7, /device:TPU:6, one launch (start us, length us, event | category | flops | bytes accessed | tf_op | source)
XLA Modules:
  0.0 384.6 jit_solution(7196173409981129156)
XLA Ops:
  11.9 2.3 fusion.35
  20.2 7.2 %fusion.5 = f32[8,2,128,128]{3,2,1,0:T(8,128)S(1)} fusion(bf16[8,2048,128]{2,1,0:T(8,128)(2,1)} %param.8, bf16[8,2048,2,128]{3,2,1,0:T(2,128)(2,1)} %param.9, f32[8,128]{1,0:T(8,128)S(1)} %fusion.22), kind=kOutput, calls=%fused_computation.20 | convolution fusion | flops 1074003968 | bytes 13635584 | tf_op jit(solution)/shard_map/sim,sitp->stmp/dot_general | solution.py:249
  29.5 37.1 %all-gather.9.cloned.1.call-done = f32[512,512]{1,0:T(8,128)} async-done(((f32[64,512]{1,0:T(8,128)}), f32[512,512]{1,0:T(8,128)}) %all-gather.9.cloned.1.call-update) | async-done | bytes 1048592 | tf_op jit(solution)/shard_map/all_gather | solution.py:260
  66.6 1.9 fusion.36
  72.4 12.3 %all-gather = f32[8,128,128]{2,1,0:T(8,128)S(1)} all-gather(f32[2,128,128]{2,1,0:T(8,128)S(1)} %gather_fusion.1), channel_id=2, replica_groups=mesh['row'=8,'col'=4] {'col'}, dimensions={0}, use_global_device_ids=true | all-gather | bytes 655360 | tf_op jit(solution)/shard_map/all_gather | solution.py:299
  89.3 2.2 select_select_fusion.1
  96.6 65.8 %collective-permute-done.5 = f32[328,512]{1,0:T(8,128)} collective-permute-done((f32[328,512]{1,0:T(8,128)}, f32[328,512]{1,0:T(8,128)}, u32[]{:S(2)}, u32[]{:S(2)}) %collective-permute-start.5) | collective-permute-done | bytes 671776 | tf_op jit(solution)/shard_map/ppermute | solution.py:316
  162.4 2.2 select_select_fusion
  167.7 78.6 %shard_map.85 = f32[512,512]{1,0:T(8,128)} custom-call(f32[512,512]{1,0:T(8,128)} %all-gather.11.cloned.1.call-done.a_ref), custom_call_target="tpu_custom_call" | custom-call | flops 8053063680 | bytes 2097152 | tf_op jit(solution)/shard_map/pallas_call | solution.py:92
  248.5 2.3 fusion.10
  250.8 9.3 %collective-permute-done.19 = f32[8,128,128]{2,1,0:T(8,128)S(1)} collective-permute-done((f32[8,128,128]{2,1,0:T(8,128)}, f32[8,128,128]{2,1,0:T(8,128)S(1)}, u32[]{:S(2)}, u32[]{:S(2)}) %collective-permute-start.19) | collective-permute-done | bytes 524320 | tf_op jit(solution)/shard_map/ppermute | solution.py:281
  260.1 21.0 %collective-permute-done.18 = f32[8,128,128]{2,1,0:T(8,128)S(1)} collective-permute-done((f32[8,128,128]{2,1,0:T(8,128)}, f32[8,128,128]{2,1,0:T(8,128)S(1)}, u32[]{:S(2)}, u32[]{:S(2)}) %collective-permute-start.18) | collective-permute-done | bytes 524320 | tf_op jit(solution)/shard_map/ppermute | solution.py:281
  283.7 2.0 gather_fusion.3
  285.7 1.9 copy_bitcast_fusion
  290.6 4.7 %slice.166 = f32[8,256,512]{2,1,0:T(8,128)} slice(f32[8,328,512]{2,1,0:T(8,128)} %bitcast.84), slice={[0:8], [0:256], [0:512]} | slice | bytes 8388608 | tf_op jit(solution)/shard_map/slice | solution.py:318
  296.6 5.4 %pad_maximum_fusion.x_ref = f32[3840,512]{1,0:T(8,128)} fusion(f32[512,512]{1,0:T(8,128)S(1)} %bitcast.89, f32[256,512]{1,0:T(8,128)S(1)} %bitcast.88, f32[2048,512]{1,0:T(8,128)} %bitcast.79, f32[1024,512]{1,0:T(8,128)} %all-gather.7.cloned.1.call-done), kind=kLoop, calls=%fused_computation.8 | loop fusion | flops 5898240 | bytes 15728640 | tf_op jit(solution)/shard_map/concatenate | solution.py:327
  302.0 15.9 %shard_map.86 = f32[3840,512]{1,0:T(8,128)} custom-call(f32[3840,512]{1,0:T(8,128)} %pad_maximum_fusion.x_ref, bf16[512,512]{1,0:T(8,128)(2,1)} %get-tuple-element.42.fhi_ref, bf16[512,512]{1,0:T(8,128)(2,1)} %get-tuple-element.41.flo_ref), custom_call_target="tpu_custom_call" | custom-call | flops 6039797760 | bytes 15728640 | tf_op jit(solution)/shard_map/pallas_call | solution.py:197
  317.9 3.1 slice.172.refs_1_
  321.0 5.0 %fusion.2 = (bf16[2048,512]{1,0:T(8,128)(2,1)}, bf16[2048,512]{1,0:T(8,128)(2,1)}) fusion(f32[3840,512]{1,0:T(8,128)} %shard_map.86), kind=kLoop, calls=%fused_computation.13 | loop fusion | flops 4194304 | bytes 8388608 | tf_op jit(solution)/shard_map/convert_element_type | solution.py:104
  326.3 2.8 gather_fusion.5
  329.1 4.9 %fusion.3 = (bf16[2048,512]{1,0:T(8,128)(2,1)}, bf16[2048,512]{1,0:T(8,128)(2,1)}) fusion(f32[16,128,512]{2,1,0:T(8,128)} %gather_fusion.5), kind=kLoop, calls=%fused_computation.14 | loop fusion | flops 4194304 | bytes 8388608 | tf_op jit(solution)/shard_map/convert_element_type | solution.py:104
  337.9 20.9 %shard_map.87 = f32[1024,2048]{1,0:T(8,128)} custom-call(s32[8]{0:T(128)S(1)} %broadcast_29_flags_ref.2.flags_ref, s32[4]{0:T(128)S(1)} %get-tuple-element.63.info_ref, s32[1]{0:T(128)} %constant.135.clone.1.slots_ref, f32[1024,2048]{1,0:T(8,128)} %refs_0_.1, f32[1024,512]{1,0:T(8,128)S(1)} %copy-done.1, bf16[2048,512]{1,0:T(8,128)(2,1)S(1)} %copy-done, ...), custom_call_target="tpu_custom_call" | custom-call | flops 6442450944 | bytes 20971520 | tf_op jit(solution)/shard_map/pallas_call | solution.py:174
  358.8 10.2 %shard_map.88 = f32[1024,2048]{1,0:T(8,128)} custom-call(s32[8]{0:T(128)S(1)} %get-tuple-element.56.flags_ref, s32[4]{0:T(128)S(1)} %get-tuple-element.63.info_ref, s32[32]{0:T(128)S(1)} %select_n.328.slots_ref, f32[9,128,512]{2,1,0:T(8,128)} %concatenate.61.refs_0_.refs_1_.refs_2_.refs_3_, f32[9,128,512]{2,1,0:T(8,128)} %concatenate.61.refs_0_.refs_1_.refs_2_.refs_3_, ...), custom_call_target="tpu_custom_call" | custom-call | flops 6442450944 | bytes 20971520 | tf_op jit(solution)/shard_map/pallas_call | solution.py:174
  369.1 9.0 %shard_map.89 = f32[1024,2048]{1,0:T(8,128)} custom-call(s32[8]{0:T(128)S(1)} %get-tuple-element.56.flags_ref, s32[4]{0:T(128)S(1)} %get-tuple-element.62.info_ref, s32[1]{0:T(128)} %constant.135.clone.1.slots_ref, f32[1024,1]{1,0:T(8,128)S(1)} %copy.42.refs_0_, f32[1024,512]{1,0:T(8,128)S(1)} %bitcast.78, bf16[2048,512]{1,0:T(8,128)(2,1)S(1)} %copy-done.2, ...), custom_call_target="tpu_custom_call" | custom-call | flops 6442450944 | bytes 20971520 | tf_op jit(solution)/shard_map/pallas_call | solution.py:174
  (147 shorter events, 42.2 us)
Async XLA Ops:
  7.2 59.4 %all-gather.9.cloned.1.call-start = ((), (), s32[]{:S(2)}) async-start(), calls=%async_computation.1 | async-start | bytes 1179648 | tf_op jit(solution)/shard_map/all_gather | solution.py:260
  8.5 5.7 %collective-permute-start.13 = (f32[64,512]{1,0:T(8,128)S(1)}, f32[64,512]{1,0:T(8,128)S(1)}, u32[]{:S(2)}, u32[]{:S(2)}) collective-permute-start(f32[64,512]{1,0:T(8,128)S(1)} %get-tuple-element.21), channel_id=1, source_target_pairs={{0,4}} | collective-permute-start | bytes 393224 | tf_op jit(solution)/shard_map/ppermute | solution.py:258
  9.2 5.7 %collective-permute-start.12 = (f32[64,512]{1,0:T(8,128)S(1)}, f32[64,512]{1,0:T(8,128)S(1)}, u32[]{:S(2)}, u32[]{:S(2)}) collective-permute-start(f32[64,512]{1,0:T(8,128)S(1)} %get-tuple-element.22), channel_id=1, source_target_pairs={{0,8}} | collective-permute-start | bytes 393224 | tf_op jit(solution)/shard_map/ppermute | solution.py:258
  9.9 5.7 %collective-permute-start.11 = (f32[64,512]{1,0:T(8,128)S(1)}, f32[64,512]{1,0:T(8,128)S(1)}, u32[]{:S(2)}, u32[]{:S(2)}) collective-permute-start(f32[64,512]{1,0:T(8,128)S(1)} %get-tuple-element.23), channel_id=1, source_target_pairs={{0,12}} | collective-permute-start | bytes 393224 | tf_op jit(solution)/shard_map/ppermute | solution.py:258
  10.6 6.6 %collective-permute-start.10 = (f32[64,512]{1,0:T(8,128)S(1)}, f32[64,512]{1,0:T(8,128)S(1)}, u32[]{:S(2)}, u32[]{:S(2)}) collective-permute-start(f32[64,512]{1,0:T(8,128)S(1)} %get-tuple-element.24), channel_id=1, source_target_pairs={{0,16}} | collective-permute-start | bytes 393224 | tf_op jit(solution)/shard_map/ppermute | solution.py:258
  11.3 7.2 %collective-permute-start.9 = (f32[64,512]{1,0:T(8,128)S(1)}, f32[64,512]{1,0:T(8,128)S(1)}, u32[]{:S(2)}, u32[]{:S(2)}) collective-permute-start(f32[64,512]{1,0:T(8,128)S(1)} %get-tuple-element.25), channel_id=1, source_target_pairs={{0,20}} | collective-permute-start | bytes 393224 | tf_op jit(solution)/shard_map/ppermute | solution.py:258
  14.2 4.2 %collective-permute-start.8 = (f32[64,512]{1,0:T(8,128)S(1)}, f32[64,512]{1,0:T(8,128)S(1)}, u32[]{:S(2)}, u32[]{:S(2)}) collective-permute-start(f32[64,512]{1,0:T(8,128)S(1)} %get-tuple-element.26), channel_id=1, source_target_pairs={{0,24}} | collective-permute-start | bytes 393224 | tf_op jit(solution)/shard_map/ppermute | solution.py:258
  14.9 3.6 collective-permute-start.7
  15.7 73.6 %collective-permute-start.2 = (f32[256,512]{1,0:T(8,128)S(1)}, f32[256,512]{1,0:T(8,128)}, u32[]{:S(2)}, u32[]{:S(2)}) collective-permute-start(f32[256,512]{1,0:T(8,128)S(1)} %get-tuple-element.30), channel_id=1, source_target_pairs={{0,1},{4,5},{8,9},{12,13},{16,17},{20,21},{24,25},{28,29}} | collective-permute-start | bytes 1572872 | tf_op jit(solution)/shard_map/ppermute | solution.py:307
  17.1 72.1 %collective-permute-start.1 = (f32[256,512]{1,0:T(8,128)S(1)}, f32[256,512]{1,0:T(8,128)}, u32[]{:S(2)}, u32[]{:S(2)}) collective-permute-start(f32[256,512]{1,0:T(8,128)S(1)} %get-tuple-element.31), channel_id=1, source_target_pairs={{0,2},{4,6},{8,10},{12,14},{16,18},{20,22},{24,26},{28,30}} | collective-permute-start | bytes 1572872 | tf_op jit(solution)/shard_map/ppermute | solution.py:307
  20.1 147.5 %all-gather.11.cloned.1.call-start = ((), (), s32[]{:S(2)}) async-start(), calls=%async_computation.2 | async-start | bytes 1310720 | tf_op jit(solution)/shard_map/all_gather | solution.py:265
  68.5 16.6 %collective-permute-start.16 = (f32[128,512]{1,0:T(8,128)S(1)}, f32[128,512]{1,0:T(8,128)S(1)}, u32[]{:S(2)}, u32[]{:S(2)}) collective-permute-start(f32[128,512]{1,0:T(8,128)S(1)} %get-tuple-element.43), channel_id=1, source_target_pairs={{0,1},{4,5},{8,9},{12,13},{16,17},{20,21},{24,25},{28,29}} | collective-permute-start | bytes 786440 | tf_op jit(solution)/shard_map/ppermute | solution.py:264
  69.8 17.5 %collective-permute-start.15 = (f32[128,512]{1,0:T(8,128)}, f32[128,512]{1,0:T(8,128)}, u32[]{:S(2)}, u32[]{:S(2)}) collective-permute-start(f32[128,512]{1,0:T(8,128)} %get-tuple-element.44), channel_id=1, source_target_pairs={{0,2},{4,6},{8,10},{12,14},{16,18},{20,22},{24,26},{28,30}} | collective-permute-start | bytes 786440 | tf_op jit(solution)/shard_map/ppermute | solution.py:264
  71.1 16.2 %collective-permute-start.14 = (f32[128,512]{1,0:T(8,128)}, f32[128,512]{1,0:T(8,128)}, u32[]{:S(2)}, u32[]{:S(2)}) collective-permute-start(f32[128,512]{1,0:T(8,128)} %get-tuple-element.45), channel_id=1, source_target_pairs={{0,3},{4,7},{8,11},{12,15},{16,19},{20,23},{24,27},{28,31}} | collective-permute-start | bytes 786440 | tf_op jit(solution)/shard_map/ppermute | solution.py:264
  85.9 3.4 collective-permute-start
  89.2 200.1 %all-gather.13.cloned.1.call-start = ((), (), s32[]{:S(2)}) async-start(), calls=%async_computation.3 | async-start | bytes 6045696 | tf_op jit(solution)/shard_map/all_gather | solution.py:317
  93.1 3.4 collective-permute-start.6
  93.8 2.8 collective-permute-start.3
  94.5 2.1 collective-permute-start.4
  95.2 67.2 %collective-permute-start.5 = (f32[328,512]{1,0:T(8,128)}, f32[328,512]{1,0:T(8,128)}, u32[]{:S(2)}, u32[]{:S(2)}) collective-permute-start(f32[328,512]{1,0:T(8,128)} %get-tuple-element.61), channel_id=1, source_target_pairs={{0,4},{4,20},{8,5},{12,21},{16,6},{20,22},{24,7},{28,23}} | collective-permute-start | bytes 2015240 | tf_op jit(solution)/shard_map/ppermute | solution.py:316
  164.6 132.0 %all-gather.7.cloned.1.call-start = ((), (), s32[]{:S(2)}) async-start(), calls=%async_computation | async-start | bytes 2621440 | tf_op jit(solution)/shard_map/all_gather | solution.py:308
  247.5 12.6 %collective-permute-start.19 = (f32[8,128,128]{2,1,0:T(8,128)}, f32[8,128,128]{2,1,0:T(8,128)S(1)}, u32[]{:S(2)}, u32[]{:S(2)}) collective-permute-start(f32[8,128,128]{2,1,0:T(8,128)} %get-tuple-element.38), channel_id=1, source_target_pairs={{0,3},{1,0},{2,1},{3,2},{4,7},{5,4},{6,5},{7,6},{8,11},{9,8},{10,9... | collective-permute-start | bytes 1572872 | tf_op jit(solution)/shard_map/ppermute | solution.py:281
  247.5 33.6 %collective-permute-start.18 = (f32[8,128,128]{2,1,0:T(8,128)}, f32[8,128,128]{2,1,0:T(8,128)S(1)}, u32[]{:S(2)}, u32[]{:S(2)}) collective-permute-start(f32[8,128,128]{2,1,0:T(8,128)} %get-tuple-element.39), channel_id=1, source_target_pairs={{0,2},{1,3},{2,0},{3,1},{4,6},{5,7},{6,4},{7,5},{8,10},{9,11},{10,... | collective-permute-start | bytes 1572872 | tf_op jit(solution)/shard_map/ppermute | solution.py:281
  247.5 33.6 %collective-permute-start.17 = (f32[8,128,128]{2,1,0:T(8,128)S(1)}, f32[8,128,128]{2,1,0:T(8,128)S(1)}, u32[]{:S(2)}, u32[]{:S(2)}) collective-permute-start(f32[8,128,128]{2,1,0:T(8,128)S(1)} %get-tuple-element.40), channel_id=1, source_target_pairs={{0,1},{1,2},{2,3},{3,0},{4,5},{5,6},{6,7},{7,4},{8,9},{9,10},{10,1... | collective-permute-start | bytes 1572872 | tf_op jit(solution)/shard_map/ppermute | solution.py:281
  (18 other events, 167.5 us)
Sparse Core Ops, SparseCore 0:
  20.3 46.2 all-gather.8
  89.3 17.1 all-gather.10
  164.7 87.7 all-gather.12
  254.0 28.4 all-gather.6

commit v8 on v7

--- a/solution.py
+++ b/solution.py
@@ -305,16 +305,13 @@
     got = [m_src[:rps]]
     for k in range(1, C):
         got.append(lax.ppermute(m_src[k * rps:(k + 1) * rps], AXES, [(i * C, i * C + k) for i in range(R)]))
-    m_row = lax.all_gather(pick(c, got), "col", axis=0, tiled=True)
+    a_slice = pick(c, got)
+    m_row = lax.all_gather(a_slice, "col", axis=0, tiled=True)
     slot_row = jnp.zeros((8, PANEL), jnp.float32).at[0, :nsub].set(slot_r.astype(jnp.float32))
-    got = []
-    for k in range(C):
-        payload = jnp.concatenate(
-            [m_src[k * rps:(k + 1) * rps], z_rows[k * zps:(k + 1) * zps], slot_row], axis=0
-        )
-        perm = [(i * C, ((i % ratio) * C + k) * C + i // ratio) for i in range(R)]
-        got.append(lax.ppermute(payload, AXES, perm))
-    col_parts = lax.all_gather(pick(r % C, got), "row", axis=0, tiled=False)
+    payload = jnp.concatenate([a_slice, lax.dynamic_slice_in_dim(z_rows, c * zps, zps), slot_row], axis=0)
+    perm = [(i * C + k, ((i % ratio) * C + k) * C + i // ratio) for i in range(R) for k in range(C)]
+    b_slice = lax.ppermute(payload, AXES, perm)
+    col_parts = lax.all_gather(b_slice, "row", axis=0, tiled=False)
     m_col = col_parts[:, :rps].reshape(W, PANEL)
     z_col = col_parts[:, rps:rps + zps].reshape(ratio * cap0 * MSLOT, PANEL)
 

time: 391 us -> 366 us (0.936)
  waiting for transfers between devices: 133 us -> 104 us
  starting transfers between devices: 15.5 us -> 28.2 us
  other arithmetic: 32.8 us -> 28.2 us
    ppermute x4 -> x1, waiting for transfers between devices: 65.9 us -> 32 us  [per_device(): b_slice = lax.ppermute(payload, AXES, perm)]
    ppermute x3, starting transfers between devices: 0.51 us -> 11.8 us  [per_device(): lax.ppermute(out_k, 'col', [(i, (i + k) % C) for i in range(C)])]
    select_n x4 -> x3, other arithmetic: 7.87 us -> 4.85 us  [pick(): out = jnp.where(index == i, options[i], out)]
  transfers between devices with their start and end apart: 24 -> 21, of which waited for: 4 -> 5; matrix products, arithmetic and copies ran while one was open for 12% -> 11% of each run, Pallas kernels for 20% -> 22%
where the time goes in v8:
time: 366 us; the launch traced here: 361 us
  Pallas kernels  135 us (37%)
  waiting for transfers between devices  104 us (28%)
  local copies, waits for them, and re-layouts  34.5 us (9%)
  starting transfers between devices  28.2 us (8%)
  other arithmetic  28.2 us (8%)
  between operations  14.3 us (4%)
  blocking collectives  10.3 us (3%)
  matrix products  7.19 us (2%)
    pallas_call x1, Pallas kernels, chol_inverse(): pl.pallas_call(chol_inv_kernel, out_shape=jax.ShapeDtypeStruct((n, n), jn...  78.6 us
    pallas_call x3, Pallas kernels, panel_update(): pl.pallas_call(functools.partial(update_kernel, kind, tm, width, len(base...  40.3 us
    all_gather x1, waiting for transfers between devices, per_device(): kpp_col0 = lax.all_gather(kpp_part, 'row', axis=0, tiled=True)  37.1 us
    ppermute x1, waiting for transfers between devices, per_device(): b_slice = lax.ppermute(payload, AXES, perm)  32 us
    ppermute x3, waiting for transfers between devices, per_device(): lax.ppermute(out_k, 'col', [(i, (i + k) % C) for i in range(C)])  30.9 us
    pallas_call x1, Pallas kernels, apply_inverse(): pl.pallas_call(solve_kernel, grid=(rows // tm,), in_specs=[pl.BlockSpec((...  15.8 us
    convert_element_type x3, other arithmetic, split_bf16(): return (hi.astype(jnp.bfloat16), (x - hi).astype(jnp.bfloat16))  12.2 us
    ppermute x3, starting transfers between devices, per_device(): lax.ppermute(out_k, 'col', [(i, (i + k) % C) for i in range(C)])  11.8 us
  transfers between devices with their start and end apart: 21, of which 5 were waited for; matrix products, arithmetic and copies ran while one was open for 11% of the time, Pallas kernels for 22%

profile of v8, /device:TPU:6, one launch (start us, length us, event | category | flops | bytes accessed | tf_op | source)
XLA Modules:
  0.0 361.0 jit_solution(15524281679771137366)
XLA Ops:
  11.9 2.3 fusion.31
  20.4 7.2 %fusion.5 = f32[8,2,128,128]{3,2,1,0:T(8,128)S(1)} fusion(bf16[8,2048,128]{2,1,0:T(8,128)(2,1)} %param.8, bf16[8,2048,2,128]{3,2,1,0:T(2,128)(2,1)} %param.9, f32[8,128]{1,0:T(8,128)S(1)} %fusion.18), kind=kOutput, calls=%fused_computation.20 | convolution fusion | flops 1074003968 | bytes 13635584 | tf_op jit(solution)/shard_map/sim,sitp->stmp/dot_general | solution.py:249
  29.5 37.1 %all-gather.9.cloned.1.call-done = f32[512,512]{1,0:T(8,128)} async-done(((f32[64,512]{1,0:T(8,128)}), f32[512,512]{1,0:T(8,128)}) %all-gather.9.cloned.1.call-update) | async-done | bytes 1048592 | tf_op jit(solution)/shard_map/all_gather | solution.py:260
  66.6 1.9 fusion.32
  73.9 3.5 collective-permute-done.12
  79.2 10.3 %all-gather = f32[8,128,128]{2,1,0:T(8,128)S(1)} all-gather(f32[2,128,128]{2,1,0:T(8,128)S(1)} %gather_fusion.1), channel_id=2, replica_groups=mesh['row'=8,'col'=4] {'col'}, dimensions={0}, use_global_device_ids=true | all-gather | bytes 655360 | tf_op jit(solution)/shard_map/all_gather | solution.py:299
  92.1 4.0 %collective-permute-start.3 = (f32[328,512]{1,0:T(8,128)S(1)}, f32[328,512]{1,0:T(8,128)S(1)}, u32[]{:S(2)}, u32[]{:S(2)}) collective-permute-start(f32[328,512]{1,0:T(8,128)S(1)} %select_maximum_fusion), channel_id=1, source_target_pairs={{0,0},{1,4},{2,8},{3,12},{4,16},{5,20},{6,24},{7,28},{8,1},{9,5},{... | collective-permute-start | bytes 2015240 | tf_op jit(solution)/shard_map/ppermute | solution.py:313
  96.1 32.0 %collective-permute-done.3 = f32[328,512]{1,0:T(8,128)S(1)} collective-permute-done((f32[328,512]{1,0:T(8,128)S(1)}, f32[328,512]{1,0:T(8,128)S(1)}, u32[]{:S(2)}, u32[]{:S(2)}) %collective-permute-start.3) | collective-permute-done | bytes 671776 | tf_op jit(solution)/shard_map/ppermute | solution.py:313
  132.0 78.6 %shard_map.85 = f32[512,512]{1,0:T(8,128)} custom-call(f32[512,512]{1,0:T(8,128)} %all-gather.11.cloned.1.call-done.a_ref), custom_call_target="tpu_custom_call" | custom-call | flops 8053063680 | bytes 2097152 | tf_op jit(solution)/shard_map/pallas_call | solution.py:92
  211.8 11.7 %collective-permute-start.16 = (f32[8,128,128]{2,1,0:T(8,128)}, f32[8,128,128]{2,1,0:T(8,128)S(1)}, u32[]{:S(2)}, u32[]{:S(2)}) collective-permute-start(f32[8,128,128]{2,1,0:T(8,128)} %get-tuple-element.36), channel_id=1, source_target_pairs={{0,3},{1,0},{2,1},{3,2},{4,7},{5,4},{6,5},{7,6},{8,11},{9,8},{10,9... | collective-permute-start | bytes 1572872 | tf_op jit(solution)/shard_map/ppermute | solution.py:281
  224.1 2.4 fusion.10
  226.5 9.6 %collective-permute-done.16 = f32[8,128,128]{2,1,0:T(8,128)S(1)} collective-permute-done((f32[8,128,128]{2,1,0:T(8,128)}, f32[8,128,128]{2,1,0:T(8,128)S(1)}, u32[]{:S(2)}, u32[]{:S(2)}) %collective-permute-start.16) | collective-permute-done | bytes 524320 | tf_op jit(solution)/shard_map/ppermute | solution.py:281
  236.1 21.4 %collective-permute-done.15 = f32[8,128,128]{2,1,0:T(8,128)S(1)} collective-permute-done((f32[8,128,128]{2,1,0:T(8,128)}, f32[8,128,128]{2,1,0:T(8,128)S(1)}, u32[]{:S(2)}, u32[]{:S(2)}) %collective-permute-start.15) | collective-permute-done | bytes 524320 | tf_op jit(solution)/shard_map/ppermute | solution.py:281
  260.0 2.0 gather_fusion.3
  266.9 4.7 %slice.142 = f32[8,256,512]{2,1,0:T(8,128)} slice(f32[8,328,512]{2,1,0:T(8,128)} %bitcast.84), slice={[0:8], [0:256], [0:512]} | slice | bytes 8388608 | tf_op jit(solution)/shard_map/slice | solution.py:315
  273.0 5.4 %pad_maximum_fusion.x_ref = f32[3840,512]{1,0:T(8,128)} fusion(f32[512,512]{1,0:T(8,128)S(1)} %bitcast.87, f32[256,512]{1,0:T(8,128)S(1)} %bitcast.89, f32[2048,512]{1,0:T(8,128)} %bitcast.79, f32[1024,512]{1,0:T(8,128)} %all-gather.7.cloned.1.call-done), kind=kLoop, calls=%fused_computation.8 | loop fusion | flops 5898240 | bytes 15728640 | tf_op jit(solution)/shard_map/concatenate | solution.py:324
  278.3 15.8 %shard_map.86 = f32[3840,512]{1,0:T(8,128)} custom-call(f32[3840,512]{1,0:T(8,128)} %pad_maximum_fusion.x_ref, bf16[512,512]{1,0:T(8,128)(2,1)} %get-tuple-element.40.fhi_ref, bf16[512,512]{1,0:T(8,128)(2,1)} %get-tuple-element.39.flo_ref), custom_call_target="tpu_custom_call" | custom-call | flops 6039797760 | bytes 15728640 | tf_op jit(solution)/shard_map/pallas_call | solution.py:197
  294.2 3.1 slice.148.refs_1_
  297.3 5.0 %fusion.2 = (bf16[2048,512]{1,0:T(8,128)(2,1)}, bf16[2048,512]{1,0:T(8,128)(2,1)}) fusion(f32[3840,512]{1,0:T(8,128)} %shard_map.86), kind=kLoop, calls=%fused_computation.13 | loop fusion | flops 4194304 | bytes 8388608 | tf_op jit(solution)/shard_map/convert_element_type | solution.py:104
  302.6 2.8 gather_fusion.5
  305.4 4.8 %fusion.3 = (bf16[2048,512]{1,0:T(8,128)(2,1)}, bf16[2048,512]{1,0:T(8,128)(2,1)}) fusion(f32[16,128,512]{2,1,0:T(8,128)} %gather_fusion.5), kind=kLoop, calls=%fused_computation.14 | loop fusion | flops 4194304 | bytes 8388608 | tf_op jit(solution)/shard_map/convert_element_type | solution.py:104
  314.1 20.9 %shard_map.87 = f32[1024,2048]{1,0:T(8,128)} custom-call(s32[8]{0:T(128)S(1)} %broadcast_29_flags_ref.2.flags_ref, s32[4]{0:T(128)S(1)} %get-tuple-element.53.info_ref, s32[1]{0:T(128)} %constant.133.clone.1.slots_ref, f32[1024,2048]{1,0:T(8,128)} %refs_0_.1, f32[1024,512]{1,0:T(8,128)S(1)} %copy-done.1, bf16[2048,512]{1,0:T(8,128)(2,1)S(1)} %copy-done, ...), custom_call_target="tpu_custom_call" | custom-call | flops 6442450944 | bytes 20971520 | tf_op jit(solution)/shard_map/pallas_call | solution.py:174
  335.1 10.4 %shard_map.88 = f32[1024,2048]{1,0:T(8,128)} custom-call(s32[8]{0:T(128)S(1)} %get-tuple-element.50.flags_ref, s32[4]{0:T(128)S(1)} %get-tuple-element.53.info_ref, s32[32]{0:T(128)S(1)} %select_n.301.slots_ref, f32[9,128,512]{2,1,0:T(8,128)} %concatenate.49.refs_0_.refs_1_.refs_2_.refs_3_, f32[9,128,512]{2,1,0:T(8,128)} %concatenate.49.refs_0_.refs_1_.refs_2_.refs_3_, ...), custom_call_target="tpu_custom_call" | custom-call | flops 6442450944 | bytes 20971520 | tf_op jit(solution)/shard_map/pallas_call | solution.py:174
  345.5 9.0 %shard_map.89 = f32[1024,2048]{1,0:T(8,128)} custom-call(s32[8]{0:T(128)S(1)} %get-tuple-element.50.flags_ref, s32[4]{0:T(128)S(1)} %get-tuple-element.52.info_ref, s32[1]{0:T(128)} %constant.133.clone.1.slots_ref, f32[1024,1]{1,0:T(8,128)S(1)} %copy.42.refs_0_, f32[1024,512]{1,0:T(8,128)S(1)} %bitcast.78, bf16[2048,512]{1,0:T(8,128)(2,1)S(1)} %copy-done.2, ...), custom_call_target="tpu_custom_call" | custom-call | flops 6442450944 | bytes 20971520 | tf_op jit(solution)/shard_map/pallas_call | solution.py:174
  (136 shorter events, 41.0 us)
Async XLA Ops:
  7.2 59.4 %all-gather.9.cloned.1.call-start = ((), (), s32[]{:S(2)}) async-start(), calls=%async_computation.1 | async-start | bytes 1179648 | tf_op jit(solution)/shard_map/all_gather | solution.py:260
  8.6 5.7 %collective-permute-start.10 = (f32[64,512]{1,0:T(8,128)S(1)}, f32[64,512]{1,0:T(8,128)S(1)}, u32[]{:S(2)}, u32[]{:S(2)}) collective-permute-start(f32[64,512]{1,0:T(8,128)S(1)} %get-tuple-element.21), channel_id=1, source_target_pairs={{0,4}} | collective-permute-start | bytes 393224 | tf_op jit(solution)/shard_map/ppermute | solution.py:258
  9.2 5.7 %collective-permute-start.9 = (f32[64,512]{1,0:T(8,128)S(1)}, f32[64,512]{1,0:T(8,128)S(1)}, u32[]{:S(2)}, u32[]{:S(2)}) collective-permute-start(f32[64,512]{1,0:T(8,128)S(1)} %get-tuple-element.22), channel_id=1, source_target_pairs={{0,8}} | collective-permute-start | bytes 393224 | tf_op jit(solution)/shard_map/ppermute | solution.py:258
  9.9 5.8 %collective-permute-start.8 = (f32[64,512]{1,0:T(8,128)S(1)}, f32[64,512]{1,0:T(8,128)S(1)}, u32[]{:S(2)}, u32[]{:S(2)}) collective-permute-start(f32[64,512]{1,0:T(8,128)S(1)} %get-tuple-element.23), channel_id=1, source_target_pairs={{0,12}} | collective-permute-start | bytes 393224 | tf_op jit(solution)/shard_map/ppermute | solution.py:258
  10.6 6.6 %collective-permute-start.7 = (f32[64,512]{1,0:T(8,128)S(1)}, f32[64,512]{1,0:T(8,128)S(1)}, u32[]{:S(2)}, u32[]{:S(2)}) collective-permute-start(f32[64,512]{1,0:T(8,128)S(1)} %get-tuple-element.24), channel_id=1, source_target_pairs={{0,16}} | collective-permute-start | bytes 393224 | tf_op jit(solution)/shard_map/ppermute | solution.py:258
  11.3 7.2 %collective-permute-start.6 = (f32[64,512]{1,0:T(8,128)S(1)}, f32[64,512]{1,0:T(8,128)S(1)}, u32[]{:S(2)}, u32[]{:S(2)}) collective-permute-start(f32[64,512]{1,0:T(8,128)S(1)} %get-tuple-element.25), channel_id=1, source_target_pairs={{0,20}} | collective-permute-start | bytes 393224 | tf_op jit(solution)/shard_map/ppermute | solution.py:258
  14.2 4.2 %collective-permute-start.5 = (f32[64,512]{1,0:T(8,128)S(1)}, f32[64,512]{1,0:T(8,128)S(1)}, u32[]{:S(2)}, u32[]{:S(2)}) collective-permute-start(f32[64,512]{1,0:T(8,128)S(1)} %get-tuple-element.26), channel_id=1, source_target_pairs={{0,24}} | collective-permute-start | bytes 393224 | tf_op jit(solution)/shard_map/ppermute | solution.py:258
  14.9 3.6 collective-permute-start.4
  15.7 74.2 %collective-permute-start.2 = (f32[256,512]{1,0:T(8,128)}, f32[256,512]{1,0:T(8,128)}, u32[]{:S(2)}, u32[]{:S(2)}) collective-permute-start(f32[256,512]{1,0:T(8,128)} %get-tuple-element.28), channel_id=1, source_target_pairs={{0,1},{4,5},{8,9},{12,13},{16,17},{20,21},{24,25},{28,29}} | collective-permute-start | bytes 1572872 | tf_op jit(solution)/shard_map/ppermute | solution.py:307
  17.1 72.8 %collective-permute-start.1 = (f32[256,512]{1,0:T(8,128)S(1)}, f32[256,512]{1,0:T(8,128)}, u32[]{:S(2)}, u32[]{:S(2)}) collective-permute-start(f32[256,512]{1,0:T(8,128)S(1)} %get-tuple-element.29), channel_id=1, source_target_pairs={{0,2},{4,6},{8,10},{12,14},{16,18},{20,22},{24,26},{28,30}} | collective-permute-start | bytes 1572872 | tf_op jit(solution)/shard_map/ppermute | solution.py:307
  20.2 111.8 %all-gather.11.cloned.1.call-start = ((), (), s32[]{:S(2)}) async-start(), calls=%async_computation.2 | async-start | bytes 1310720 | tf_op jit(solution)/shard_map/all_gather | solution.py:265
  68.4 3.9 %collective-permute-start.13 = (f32[128,512]{1,0:T(8,128)}, f32[128,512]{1,0:T(8,128)S(1)}, u32[]{:S(2)}, u32[]{:S(2)}) collective-permute-start(f32[128,512]{1,0:T(8,128)} %get-tuple-element.41), channel_id=1, source_target_pairs={{0,1},{4,5},{8,9},{12,13},{16,17},{20,21},{24,25},{28,29}} | collective-permute-start | bytes 786440 | tf_op jit(solution)/shard_map/ppermute | solution.py:264
  69.1 8.3 %collective-permute-start.12 = (f32[128,512]{1,0:T(8,128)S(1)}, f32[128,512]{1,0:T(8,128)S(1)}, u32[]{:S(2)}, u32[]{:S(2)}) collective-permute-start(f32[128,512]{1,0:T(8,128)S(1)} %get-tuple-element.42), channel_id=1, source_target_pairs={{0,2},{4,6},{8,10},{12,14},{16,18},{20,22},{24,26},{28,30}} | collective-permute-start | bytes 786440 | tf_op jit(solution)/shard_map/ppermute | solution.py:264
  70.4 7.0 %collective-permute-start.11 = (f32[128,512]{1,0:T(8,128)S(1)}, f32[128,512]{1,0:T(8,128)}, u32[]{:S(2)}, u32[]{:S(2)}) collective-permute-start(f32[128,512]{1,0:T(8,128)S(1)} %get-tuple-element.43), channel_id=1, source_target_pairs={{0,3},{4,7},{8,11},{12,15},{16,19},{20,23},{24,27},{28,31}} | collective-permute-start | bytes 786440 | tf_op jit(solution)/shard_map/ppermute | solution.py:264
  72.4 18.3 %collective-permute-start = (f32[256,512]{1,0:T(8,128)S(1)}, f32[256,512]{1,0:T(8,128)}, u32[]{:S(2)}, u32[]{:S(2)}) collective-permute-start(f32[256,512]{1,0:T(8,128)S(1)} %get-tuple-element.30), channel_id=1, source_target_pairs={{0,3},{4,7},{8,11},{12,15},{16,19},{20,23},{24,27},{28,31}} | collective-permute-start | bytes 1572872 | tf_op jit(solution)/shard_map/ppermute | solution.py:307
  79.2 186.4 %all-gather.13.cloned.1.call-start = ((), (), s32[]{:S(2)}) async-start(), calls=%async_computation.3 | async-start | bytes 6045696 | tf_op jit(solution)/shard_map/all_gather | solution.py:314
  92.1 38.7 %copy-start.3 = (f32[256,512]{1,0:T(8,128)}, f32[256,512]{1,0:T(8,128)S(1)}, u32[]{:S(2)}) copy-start(f32[256,512]{1,0:T(8,128)S(1)} %select_select_fusion) | copy-start | bytes 1572868
  92.1 35.9 %collective-permute-start.3 = (f32[328,512]{1,0:T(8,128)S(1)}, f32[328,512]{1,0:T(8,128)S(1)}, u32[]{:S(2)}, u32[]{:S(2)}) collective-permute-start(f32[328,512]{1,0:T(8,128)S(1)} %select_maximum_fusion), channel_id=1, source_target_pairs={{0,0},{1,4},{2,8},{3,12},{4,16},{5,20},{6,24},{7,28},{8,1},{9,5},{... | collective-permute-start | bytes 2015240 | tf_op jit(solution)/shard_map/ppermute | solution.py:313
  128.9 144.0 %all-gather.7.cloned.1.call-start = ((), (), s32[]{:S(2)}) async-start(), calls=%async_computation | async-start | bytes 2621440 | tf_op jit(solution)/shard_map/all_gather | solution.py:309
  211.8 46.6 %copy-start.6 = (f32[1,8,128,128]{3,2,1,0:T(8,128)S(1)}, f32[1,8,128,128]{3,2,1,0:T(8,128)}, u32[]{:S(2)}) copy-start(f32[1,8,128,128]{3,2,1,0:T(8,128)} %get-tuple-element.35) | copy-start | bytes 1572868
  211.8 24.2 %collective-permute-start.16 = (f32[8,128,128]{2,1,0:T(8,128)}, f32[8,128,128]{2,1,0:T(8,128)S(1)}, u32[]{:S(2)}, u32[]{:S(2)}) collective-permute-start(f32[8,128,128]{2,1,0:T(8,128)} %get-tuple-element.36), channel_id=1, source_target_pairs={{0,3},{1,0},{2,1},{3,2},{4,7},{5,4},{6,5},{7,6},{8,11},{9,8},{10,9... | collective-permute-start | bytes 1572872 | tf_op jit(solution)/shard_map/ppermute | solution.py:281
  223.5 33.9 %collective-permute-start.15 = (f32[8,128,128]{2,1,0:T(8,128)}, f32[8,128,128]{2,1,0:T(8,128)S(1)}, u32[]{:S(2)}, u32[]{:S(2)}) collective-permute-start(f32[8,128,128]{2,1,0:T(8,128)} %get-tuple-element.37), channel_id=1, source_target_pairs={{0,2},{1,3},{2,0},{3,1},{4,6},{5,7},{6,4},{7,5},{8,10},{9,11},{10,... | collective-permute-start | bytes 1572872 | tf_op jit(solution)/shard_map/ppermute | solution.py:281
  223.5 33.9 %collective-permute-start.14 = (f32[8,128,128]{2,1,0:T(8,128)S(1)}, f32[8,128,128]{2,1,0:T(8,128)S(1)}, u32[]{:S(2)}, u32[]{:S(2)}) collective-permute-start(f32[8,128,128]{2,1,0:T(8,128)S(1)} %get-tuple-element.38), channel_id=1, source_target_pairs={{0,1},{1,2},{2,3},{3,0},{4,5},{5,6},{6,7},{7,4},{8,9},{9,10},{10,1... | collective-permute-start | bytes 1572872 | tf_op jit(solution)/shard_map/ppermute | solution.py:281
  236.1 21.4 %copy-start.8 = (f32[8,128,128]{2,1,0:T(8,128)}, f32[8,128,128]{2,1,0:T(8,128)S(1)}, u32[]{:S(2)}) copy-start(f32[8,128,128]{2,1,0:T(8,128)S(1)} %collective-permute-done.16) | copy-start | bytes 1572868
  (13 other events, 51.3 us)
Sparse Core Ops, SparseCore 0:
  20.3 46.2 all-gather.8
  79.3 17.9 all-gather.10
  129.1 98.8 all-gather.12
  229.4 28.6 all-gather.6

commit v9 on v8

--- a/solution.py
+++ b/solution.py
@@ -92,7 +92,7 @@
     return pl.pallas_call(
         chol_inv_kernel,
         out_shape=jax.ShapeDtypeStruct((n, n), jnp.float32),
-        cost_estimate=pl.CostEstimate(flops=60 * n ** 3, transcendentals=n, bytes_accessed=8 * n * n),
+        cost_estimate=pl.CostEstimate(flops=800 * n ** 3, transcendentals=n, bytes_accessed=8 * n * n),
         in_specs=[pl.BlockSpec(memory_space=pltpu.VMEM)],
         out_specs=pl.BlockSpec(memory_space=pltpu.VMEM),
         scratch_shapes=[pltpu.VMEM((n, n), jnp.float32), pltpu.VMEM((n, n), jnp.float32)],
@@ -274,7 +274,6 @@
     match = onehot[:, :, None] & (rank_pd[:, :, None] == jnp.arange(cap, dtype=jnp.int32)[None, None, :])
     send_idx = jnp.where(jnp.any(match, axis=0), jnp.argmax(match, axis=0), npair)
     send = flat_pad[send_idx]
-    send, _ = lax.optimization_barrier((send, finv))
     shifted = [send[c]]
     for k in range(1, C):
         out_k = lax.dynamic_index_in_dim(send, (c + k) % C, axis=0, keepdims=False)

time: 366 us -> 354 us (0.967)
  waiting for transfers between devices: 104 us -> 90 us
    ppermute x3, waiting for transfers between devices: 30.9 us -> 17.3 us  [per_device(): lax.ppermute(out_k, 'col', [(i, (i + k) % C) for i in range(C)])]
  transfers between devices with their start and end apart: 21 -> 21, of which waited for: 5 -> 4; matrix products, arithmetic and copies ran while one was open for 11% -> 12% of each run, Pallas kernels for 22% -> 23%
where the time goes in v9:
time: 354 us; the launch traced here: 347 us
  Pallas kernels  134 us (38%)
  waiting for transfers between devices  90 us (25%)
  local copies, waits for them, and re-layouts  34.6 us (10%)
  starting transfers between devices  28.1 us (8%)
  other arithmetic  28.1 us (8%)
  between operations  14.3 us (4%)
  blocking collectives  10.3 us (3%)
  matrix products  7.19 us (2%)
    pallas_call x1, Pallas kernels, chol_inverse(): pl.pallas_call(chol_inv_kernel, out_shape=jax.ShapeDtypeStruct((n, n), jn...  78.7 us
    pallas_call x3, Pallas kernels, panel_update(): pl.pallas_call(functools.partial(update_kernel, kind, tm, width, len(base...  39.7 us
    all_gather x1, waiting for transfers between devices, per_device(): kpp_col0 = lax.all_gather(kpp_part, 'row', axis=0, tiled=True)  37.1 us
    ppermute x1, waiting for transfers between devices, per_device(): b_slice = lax.ppermute(payload, AXES, perm)  32 us
    ppermute x3, waiting for transfers between devices, per_device(): lax.ppermute(out_k, 'col', [(i, (i + k) % C) for i in range(C)])  17.3 us
    pallas_call x1, Pallas kernels, apply_inverse(): pl.pallas_call(solve_kernel, grid=(rows // tm,), in_specs=[pl.BlockSpec((...  15.8 us
    convert_element_type x3, other arithmetic, split_bf16(): return (hi.astype(jnp.bfloat16), (x - hi).astype(jnp.bfloat16))  12.2 us
    ppermute x3, starting transfers between devices, per_device(): lax.ppermute(out_k, 'col', [(i, (i + k) % C) for i in range(C)])  11.8 us
  transfers between devices with their start and end apart: 21, of which 4 were waited for; matrix products, arithmetic and copies ran while one was open for 12% of the time, Pallas kernels for 23%

profile of v9, /device:TPU:6, one launch (start us, length us, event | category | flops | bytes accessed | tf_op | source)
XLA Modules:
  0.0 346.7 jit_solution(2396558117515360701)
XLA Ops:
  11.9 2.3 fusion.31
  20.4 7.2 %fusion.5 = f32[8,2,128,128]{3,2,1,0:T(8,128)S(1)} fusion(bf16[8,2048,128]{2,1,0:T(8,128)(2,1)} %param.8, bf16[8,2048,2,128]{3,2,1,0:T(2,128)(2,1)} %param.9, f32[8,128]{1,0:T(8,128)S(1)} %fusion.18), kind=kOutput, calls=%fused_computation.20 | convolution fusion | flops 1074003968 | bytes 13635584 | tf_op jit(solution)/shard_map/sim,sitp->stmp/dot_general | solution.py:249
  29.5 37.1 %all-gather.9.cloned.1.call-done = f32[512,512]{1,0:T(8,128)} async-done(((f32[64,512]{1,0:T(8,128)}), f32[512,512]{1,0:T(8,128)}) %all-gather.9.cloned.1.call-update) | async-done | bytes 1048592 | tf_op jit(solution)/shard_map/all_gather | solution.py:260
  66.6 1.9 fusion.32
  73.9 3.5 %collective-permute-done.12 = f32[128,512]{1,0:T(8,128)S(1)} collective-permute-done((f32[128,512]{1,0:T(8,128)S(1)}, f32[128,512]{1,0:T(8,128)S(1)}, u32[]{:S(2)}, u32[]{:S(2)}) %collective-permute-start.12) | collective-permute-done | bytes 262176 | tf_op jit(solution)/shard_map/ppermute | solution.py:264
  79.2 10.3 %all-gather = f32[8,128,128]{2,1,0:T(8,128)S(1)} all-gather(f32[2,128,128]{2,1,0:T(8,128)S(1)} %gather_fusion.1), channel_id=2, replica_groups=mesh['row'=8,'col'=4] {'col'}, dimensions={0}, use_global_device_ids=true | all-gather | bytes 655360 | tf_op jit(solution)/shard_map/all_gather | solution.py:298
  92.1 4.0 %collective-permute-start.3 = (f32[328,512]{1,0:T(8,128)S(1)}, f32[328,512]{1,0:T(8,128)S(1)}, u32[]{:S(2)}, u32[]{:S(2)}) collective-permute-start(f32[328,512]{1,0:T(8,128)S(1)} %select_maximum_fusion), channel_id=1, source_target_pairs={{0,0},{1,4},{2,8},{3,12},{4,16},{5,20},{6,24},{7,28},{8,1},{9,5},{... | collective-permute-start | bytes 2015240 | tf_op jit(solution)/shard_map/ppermute | solution.py:312
  96.1 32.0 %collective-permute-done.3 = f32[328,512]{1,0:T(8,128)S(1)} collective-permute-done((f32[328,512]{1,0:T(8,128)S(1)}, f32[328,512]{1,0:T(8,128)S(1)}, u32[]{:S(2)}, u32[]{:S(2)}) %collective-permute-start.3) | collective-permute-done | bytes 671776 | tf_op jit(solution)/shard_map/ppermute | solution.py:312
  132.7 11.8 %collective-permute-start.14 = (f32[8,128,128]{2,1,0:T(8,128)}, f32[8,128,128]{2,1,0:T(8,128)S(1)}, u32[]{:S(2)}, u32[]{:S(2)}) collective-permute-start(f32[8,128,128]{2,1,0:T(8,128)} %get-tuple-element.35), channel_id=1, source_target_pairs={{0,1},{1,2},{2,3},{3,0},{4,5},{5,6},{6,7},{7,4},{8,9},{9,10},{10,1... | collective-permute-start | bytes 1572872 | tf_op jit(solution)/shard_map/ppermute | solution.py:280
  145.4 17.3 %collective-permute-done.14 = f32[8,128,128]{2,1,0:T(8,128)S(1)} collective-permute-done((f32[8,128,128]{2,1,0:T(8,128)}, f32[8,128,128]{2,1,0:T(8,128)S(1)}, u32[]{:S(2)}, u32[]{:S(2)}) %collective-permute-start.14) | collective-permute-done | bytes 524320 | tf_op jit(solution)/shard_map/ppermute | solution.py:280
  165.2 2.0 gather_fusion.3
  167.2 1.9 copy_bitcast_fusion
  170.9 78.7 %shard_map.85 = f32[512,512]{1,0:T(8,128)} custom-call(f32[512,512]{1,0:T(8,128)} %all-gather.11.cloned.1.call-done.a_ref), custom_call_target="tpu_custom_call" | custom-call | flops 107374182400 | bytes 2097152 | tf_op jit(solution)/shard_map/pallas_call | solution.py:92
  249.6 2.3 fusion.10
  253.2 4.7 %slice.142 = f32[8,256,512]{2,1,0:T(8,128)} slice(f32[8,328,512]{2,1,0:T(8,128)} %bitcast.84), slice={[0:8], [0:256], [0:512]} | slice | bytes 8388608 | tf_op jit(solution)/shard_map/slice | solution.py:314
  259.3 5.4 %pad_maximum_fusion.x_ref = f32[3840,512]{1,0:T(8,128)} fusion(f32[512,512]{1,0:T(8,128)S(1)} %bitcast.87, f32[256,512]{1,0:T(8,128)S(1)} %bitcast.89, f32[2048,512]{1,0:T(8,128)} %bitcast.79, f32[1024,512]{1,0:T(8,128)} %all-gather.7.cloned.1.call-done), kind=kLoop, calls=%fused_computation.8 | loop fusion | flops 5898240 | bytes 15728640 | tf_op jit(solution)/shard_map/concatenate | solution.py:323
  264.7 15.8 %shard_map.86 = f32[3840,512]{1,0:T(8,128)} custom-call(f32[3840,512]{1,0:T(8,128)} %pad_maximum_fusion.x_ref, bf16[512,512]{1,0:T(8,128)(2,1)} %get-tuple-element.38.fhi_ref, bf16[512,512]{1,0:T(8,128)(2,1)} %get-tuple-element.37.flo_ref), custom_call_target="tpu_custom_call" | custom-call | flops 6039797760 | bytes 15728640 | tf_op jit(solution)/shard_map/pallas_call | solution.py:197
  280.5 3.1 slice.148.refs_1_
  283.6 4.9 %fusion.2 = (bf16[2048,512]{1,0:T(8,128)(2,1)}, bf16[2048,512]{1,0:T(8,128)(2,1)}) fusion(f32[3840,512]{1,0:T(8,128)} %shard_map.86), kind=kLoop, calls=%fused_computation.13 | loop fusion | flops 4194304 | bytes 8388608 | tf_op jit(solution)/shard_map/convert_element_type | solution.py:104
  288.9 2.8 gather_fusion.5
  291.8 4.9 %fusion.3 = (bf16[2048,512]{1,0:T(8,128)(2,1)}, bf16[2048,512]{1,0:T(8,128)(2,1)}) fusion(f32[16,128,512]{2,1,0:T(8,128)} %gather_fusion.5), kind=kLoop, calls=%fused_computation.14 | loop fusion | flops 4194304 | bytes 8388608 | tf_op jit(solution)/shard_map/convert_element_type | solution.py:104
  300.5 20.9 %shard_map.87 = f32[1024,2048]{1,0:T(8,128)} custom-call(s32[8]{0:T(128)S(1)} %broadcast_29_flags_ref.2.flags_ref, s32[4]{0:T(128)S(1)} %get-tuple-element.51.info_ref, s32[1]{0:T(128)} %constant.133.clone.1.slots_ref, f32[1024,2048]{1,0:T(8,128)} %refs_0_.1, f32[1024,512]{1,0:T(8,128)S(1)} %copy-done.1, bf16[2048,512]{1,0:T(8,128)(2,1)S(1)} %copy-done, ...), custom_call_target="tpu_custom_call" | custom-call | flops 6442450944 | bytes 20971520 | tf_op jit(solution)/shard_map/pallas_call | solution.py:174
  321.4 9.9 %shard_map.88 = f32[1024,2048]{1,0:T(8,128)} custom-call(s32[8]{0:T(128)S(1)} %get-tuple-element.48.flags_ref, s32[4]{0:T(128)S(1)} %get-tuple-element.51.info_ref, s32[32]{0:T(128)S(1)} %select_n.301.slots_ref, f32[9,128,512]{2,1,0:T(8,128)} %concatenate.49.refs_0_.refs_1_.refs_2_.refs_3_, f32[9,128,512]{2,1,0:T(8,128)} %concatenate.49.refs_0_.refs_1_.refs_2_.refs_3_, ...), custom_call_target="tpu_custom_call" | custom-call | flops 6442450944 | bytes 20971520 | tf_op jit(solution)/shard_map/pallas_call | solution.py:174
  331.4 8.8 %shard_map.89 = f32[1024,2048]{1,0:T(8,128)} custom-call(s32[8]{0:T(128)S(1)} %get-tuple-element.48.flags_ref, s32[4]{0:T(128)S(1)} %get-tuple-element.50.info_ref, s32[1]{0:T(128)} %constant.133.clone.1.slots_ref, f32[1024,1]{1,0:T(8,128)S(1)} %copy.42.refs_0_, f32[1024,512]{1,0:T(8,128)S(1)} %bitcast.78, bf16[2048,512]{1,0:T(8,128)(2,1)S(1)} %copy-done.2, ...), custom_call_target="tpu_custom_call" | custom-call | flops 6442450944 | bytes 20971520 | tf_op jit(solution)/shard_map/pallas_call | solution.py:174
  (132 shorter events, 39.1 us)
Async XLA Ops:
  7.2 59.4 %all-gather.9.cloned.1.call-start = ((), (), s32[]{:S(2)}) async-start(), calls=%async_computation.1 | async-start | bytes 1179648 | tf_op jit(solution)/shard_map/all_gather | solution.py:260
  8.6 5.7 %collective-permute-start.10 = (f32[64,512]{1,0:T(8,128)S(1)}, f32[64,512]{1,0:T(8,128)S(1)}, u32[]{:S(2)}, u32[]{:S(2)}) collective-permute-start(f32[64,512]{1,0:T(8,128)S(1)} %get-tuple-element.19), channel_id=1, source_target_pairs={{0,4}} | collective-permute-start | bytes 393224 | tf_op jit(solution)/shard_map/ppermute | solution.py:258
  9.2 5.7 %collective-permute-start.9 = (f32[64,512]{1,0:T(8,128)S(1)}, f32[64,512]{1,0:T(8,128)S(1)}, u32[]{:S(2)}, u32[]{:S(2)}) collective-permute-start(f32[64,512]{1,0:T(8,128)S(1)} %get-tuple-element.20), channel_id=1, source_target_pairs={{0,8}} | collective-permute-start | bytes 393224 | tf_op jit(solution)/shard_map/ppermute | solution.py:258
  9.9 5.8 %collective-permute-start.8 = (f32[64,512]{1,0:T(8,128)S(1)}, f32[64,512]{1,0:T(8,128)S(1)}, u32[]{:S(2)}, u32[]{:S(2)}) collective-permute-start(f32[64,512]{1,0:T(8,128)S(1)} %get-tuple-element.21), channel_id=1, source_target_pairs={{0,12}} | collective-permute-start | bytes 393224 | tf_op jit(solution)/shard_map/ppermute | solution.py:258
  10.6 6.6 %collective-permute-start.7 = (f32[64,512]{1,0:T(8,128)S(1)}, f32[64,512]{1,0:T(8,128)S(1)}, u32[]{:S(2)}, u32[]{:S(2)}) collective-permute-start(f32[64,512]{1,0:T(8,128)S(1)} %get-tuple-element.22), channel_id=1, source_target_pairs={{0,16}} | collective-permute-start | bytes 393224 | tf_op jit(solution)/shard_map/ppermute | solution.py:258
  11.3 7.2 %collective-permute-start.6 = (f32[64,512]{1,0:T(8,128)S(1)}, f32[64,512]{1,0:T(8,128)S(1)}, u32[]{:S(2)}, u32[]{:S(2)}) collective-permute-start(f32[64,512]{1,0:T(8,128)S(1)} %get-tuple-element.23), channel_id=1, source_target_pairs={{0,20}} | collective-permute-start | bytes 393224 | tf_op jit(solution)/shard_map/ppermute | solution.py:258
  14.2 4.2 %collective-permute-start.5 = (f32[64,512]{1,0:T(8,128)S(1)}, f32[64,512]{1,0:T(8,128)S(1)}, u32[]{:S(2)}, u32[]{:S(2)}) collective-permute-start(f32[64,512]{1,0:T(8,128)S(1)} %get-tuple-element.24), channel_id=1, source_target_pairs={{0,24}} | collective-permute-start | bytes 393224 | tf_op jit(solution)/shard_map/ppermute | solution.py:258
  14.9 3.6 %collective-permute-start.4 = (f32[64,512]{1,0:T(8,128)S(1)}, f32[64,512]{1,0:T(8,128)S(1)}, u32[]{:S(2)}, u32[]{:S(2)}) collective-permute-start(f32[64,512]{1,0:T(8,128)S(1)} %get-tuple-element.25), channel_id=1, source_target_pairs={{0,28}} | collective-permute-start | bytes 393224 | tf_op jit(solution)/shard_map/ppermute | solution.py:258
  15.7 74.2 %collective-permute-start.2 = (f32[256,512]{1,0:T(8,128)}, f32[256,512]{1,0:T(8,128)}, u32[]{:S(2)}, u32[]{:S(2)}) collective-permute-start(f32[256,512]{1,0:T(8,128)} %get-tuple-element.26), channel_id=1, source_target_pairs={{0,1},{4,5},{8,9},{12,13},{16,17},{20,21},{24,25},{28,29}} | collective-permute-start | bytes 1572872 | tf_op jit(solution)/shard_map/ppermute | solution.py:306
  17.1 72.8 %collective-permute-start.1 = (f32[256,512]{1,0:T(8,128)S(1)}, f32[256,512]{1,0:T(8,128)}, u32[]{:S(2)}, u32[]{:S(2)}) collective-permute-start(f32[256,512]{1,0:T(8,128)S(1)} %get-tuple-element.27), channel_id=1, source_target_pairs={{0,2},{4,6},{8,10},{12,14},{16,18},{20,22},{24,26},{28,30}} | collective-permute-start | bytes 1572872 | tf_op jit(solution)/shard_map/ppermute | solution.py:306
  20.2 150.8 %all-gather.11.cloned.1.call-start = ((), (), s32[]{:S(2)}) async-start(), calls=%async_computation.2 | async-start | bytes 1310720 | tf_op jit(solution)/shard_map/all_gather | solution.py:265
  68.4 3.9 %collective-permute-start.13 = (f32[128,512]{1,0:T(8,128)}, f32[128,512]{1,0:T(8,128)S(1)}, u32[]{:S(2)}, u32[]{:S(2)}) collective-permute-start(f32[128,512]{1,0:T(8,128)} %get-tuple-element.39), channel_id=1, source_target_pairs={{0,1},{4,5},{8,9},{12,13},{16,17},{20,21},{24,25},{28,29}} | collective-permute-start | bytes 786440 | tf_op jit(solution)/shard_map/ppermute | solution.py:264
  69.1 8.3 %collective-permute-start.12 = (f32[128,512]{1,0:T(8,128)S(1)}, f32[128,512]{1,0:T(8,128)S(1)}, u32[]{:S(2)}, u32[]{:S(2)}) collective-permute-start(f32[128,512]{1,0:T(8,128)S(1)} %get-tuple-element.40), channel_id=1, source_target_pairs={{0,2},{4,6},{8,10},{12,14},{16,18},{20,22},{24,26},{28,30}} | collective-permute-start | bytes 786440 | tf_op jit(solution)/shard_map/ppermute | solution.py:264
  70.4 7.0 %collective-permute-start.11 = (f32[128,512]{1,0:T(8,128)S(1)}, f32[128,512]{1,0:T(8,128)}, u32[]{:S(2)}, u32[]{:S(2)}) collective-permute-start(f32[128,512]{1,0:T(8,128)S(1)} %get-tuple-element.41), channel_id=1, source_target_pairs={{0,3},{4,7},{8,11},{12,15},{16,19},{20,23},{24,27},{28,31}} | collective-permute-start | bytes 786440 | tf_op jit(solution)/shard_map/ppermute | solution.py:264
  72.4 18.3 %collective-permute-start = (f32[256,512]{1,0:T(8,128)S(1)}, f32[256,512]{1,0:T(8,128)}, u32[]{:S(2)}, u32[]{:S(2)}) collective-permute-start(f32[256,512]{1,0:T(8,128)S(1)} %get-tuple-element.28), channel_id=1, source_target_pairs={{0,3},{4,7},{8,11},{12,15},{16,19},{20,23},{24,27},{28,31}} | collective-permute-start | bytes 1572872 | tf_op jit(solution)/shard_map/ppermute | solution.py:306
  79.2 172.7 %all-gather.13.cloned.1.call-start = ((), (), s32[]{:S(2)}) async-start(), calls=%async_computation.3 | async-start | bytes 6045696 | tf_op jit(solution)/shard_map/all_gather | solution.py:313
  92.1 38.6 %copy-start.3 = (f32[256,512]{1,0:T(8,128)}, f32[256,512]{1,0:T(8,128)S(1)}, u32[]{:S(2)}) copy-start(f32[256,512]{1,0:T(8,128)S(1)} %select_select_fusion) | copy-start | bytes 1572868
  92.1 35.9 %collective-permute-start.3 = (f32[328,512]{1,0:T(8,128)S(1)}, f32[328,512]{1,0:T(8,128)S(1)}, u32[]{:S(2)}, u32[]{:S(2)}) collective-permute-start(f32[328,512]{1,0:T(8,128)S(1)} %select_maximum_fusion), channel_id=1, source_target_pairs={{0,0},{1,4},{2,8},{3,12},{4,16},{5,20},{6,24},{7,28},{8,1},{9,5},{... | collective-permute-start | bytes 2015240 | tf_op jit(solution)/shard_map/ppermute | solution.py:312
  129.0 130.3 %all-gather.7.cloned.1.call-start = ((), (), s32[]{:S(2)}) async-start(), calls=%async_computation | async-start | bytes 2621440 | tf_op jit(solution)/shard_map/all_gather | solution.py:308
  131.4 13.4 %copy-start.10 = (f32[8,128]{1,0:T(8,128)S(1)}, f32[8,128]{1,0:T(8,128)}, u32[]{:S(2)}) copy-start(f32[8,128]{1,0:T(8,128)} %param.12) | copy-start | bytes 12292
  132.7 12.7 %collective-permute-start.15 = (f32[8,128,128]{2,1,0:T(8,128)}, f32[8,128,128]{2,1,0:T(8,128)S(1)}, u32[]{:S(2)}, u32[]{:S(2)}) collective-permute-start(f32[8,128,128]{2,1,0:T(8,128)} %get-tuple-element.34), channel_id=1, source_target_pairs={{0,2},{1,3},{2,0},{3,1},{4,6},{5,7},{6,4},{7,5},{8,10},{9,11},{10,... | collective-permute-start | bytes 1572872 | tf_op jit(solution)/shard_map/ppermute | solution.py:280
  132.7 30.0 %collective-permute-start.14 = (f32[8,128,128]{2,1,0:T(8,128)}, f32[8,128,128]{2,1,0:T(8,128)S(1)}, u32[]{:S(2)}, u32[]{:S(2)}) collective-permute-start(f32[8,128,128]{2,1,0:T(8,128)} %get-tuple-element.35), channel_id=1, source_target_pairs={{0,1},{1,2},{2,3},{3,0},{4,5},{5,6},{6,7},{7,4},{8,9},{9,10},{10,1... | collective-permute-start | bytes 1572872 | tf_op jit(solution)/shard_map/ppermute | solution.py:280
  144.4 18.2 %collective-permute-start.16 = (f32[8,128,128]{2,1,0:T(8,128)S(1)}, f32[8,128,128]{2,1,0:T(8,128)S(1)}, u32[]{:S(2)}, u32[]{:S(2)}) collective-permute-start(f32[8,128,128]{2,1,0:T(8,128)S(1)} %get-tuple-element.36), channel_id=1, source_target_pairs={{0,3},{1,0},{2,1},{3,2},{4,7},{5,4},{6,5},{7,6},{8,11},{9,8},{10,9... | collective-permute-start | bytes 1572872 | tf_op jit(solution)/shard_map/ppermute | solution.py:280
  321.4 9.9 %copy-start.2 = (bf16[2048,512]{1,0:T(8,128)(2,1)S(1)}, bf16[2048,512]{1,0:T(8,128)(2,1)}, u32[]{:S(2)}) copy-start(bf16[2048,512]{1,0:T(8,128)(2,1)} %get-tuple-element.32.refs_2_) | copy-start | bytes 6291460
  (11 other events, 39.8 us)
Sparse Core Ops, SparseCore 0:
  20.3 46.2 all-gather.8
  79.3 17.9 all-gather.10
  129.1 98.7 all-gather.12
  229.3 20.7 all-gather.6

commit v10 on v9

--- a/solution.py
+++ b/solution.py
@@ -144,9 +144,8 @@
         out_ref[:, pl.ds(0, PANEL)] = a_ref[...]
 
 
-def panel_update(kind, base, a, b, flags, info, slots, rows, width):
+def panel_update(kind, base, a, b_hi, b_lo, flags, info, slots, rows, width):
     tm = MSLOT
-    b_hi, b_lo = split_bf16(b)
     nseg = width // PANEL
     if kind == "gather":
         bases = [base] * nseg
@@ -180,30 +179,38 @@
     )(flags, info, slots, *bases, a, b_hi, b_lo)
 
 
-def solve_kernel(x_ref, fhi_ref, flo_ref, out_ref):
+def solve_kernel(x_ref, fhi_ref, flo_ref, out_ref, hi_ref, lo_ref):
     x = x_ref[...]
     x_hi = x.astype(jnp.bfloat16)
     x_lo = (x - x_hi.astype(jnp.float32)).astype(jnp.bfloat16)
     f_hi = fhi_ref[...]
     acc = lax.dot_general(x_hi, f_hi, NT, preferred_element_type=jnp.float32)
     acc = acc + lax.dot_general(x_hi, flo_ref[...], NT, preferred_element_type=jnp.float32)
-    out_ref[...] = acc + lax.dot_general(x_lo, f_hi, NT, preferred_element_type=jnp.float32)
-
-
-def apply_inverse(x, finv):
+    acc = acc + lax.dot_general(x_lo, f_hi, NT, preferred_element_type=jnp.float32)
+    out_ref[...] = acc
+    hi = acc.astype(jnp.bfloat16)
+    hi_ref[...] = hi
+    lo_ref[...] = (acc - hi.astype(jnp.float32)).astype(jnp.bfloat16)
+
+
+def apply_inverse(x, f_hi, f_lo):
     rows = x.shape[0]
     tm = 256 if rows % 256 == 0 else MSLOT
-    f_hi, f_lo = split_bf16(finv)
+    spec = pl.BlockSpec((tm, PANEL), lambda i: (i, 0))
     return pl.pallas_call(
         solve_kernel,
         grid=(rows // tm,),
         in_specs=[
-            pl.BlockSpec((tm, PANEL), lambda i: (i, 0)),
+            spec,
             pl.BlockSpec((PANEL, PANEL), lambda i: (0, 0)),
             pl.BlockSpec((PANEL, PANEL), lambda i: (0, 0)),
         ],
-        out_specs=pl.BlockSpec((tm, PANEL), lambda i: (i, 0)),
-        out_shape=jax.ShapeDtypeStruct((rows, PANEL), jnp.float32),
+        out_specs=[spec, spec, spec],
+        out_shape=[
+            jax.ShapeDtypeStruct((rows, PANEL), jnp.float32),
+            jax.ShapeDtypeStruct((rows, PANEL), jnp.bfloat16),
+            jax.ShapeDtypeStruct((rows, PANEL), jnp.bfloat16),
+        ],
         cost_estimate=pl.CostEstimate(flops=6 * rows * PANEL * PANEL, transcendentals=0, bytes_accessed=8 * rows * PANEL),
     )(x, f_hi, f_lo)
 
@@ -320,17 +327,16 @@
         slot_c.append(jnp.where(got_slot < cap0, j * cap0 + got_slot, ratio * cap0))
     slot_c = jnp.concatenate(slot_c)
 
-    stacked = jnp.concatenate([m_row, m_col, z_rows, z_col], axis=0)
-    solved = apply_inverse(stacked, finv)
-    low_r = solved[:H]
-    low_c = solved[H:H + W]
-    lowmi_r = solved[H + W:H + W + cap0 * MSLOT]
-    lowmi_c = solved[H + W + cap0 * MSLOT:]
+    f_hi, f_lo = split_bf16(finv)
+    low_r, _, _ = apply_inverse(m_row, f_hi, f_lo)
+    _, lowc_hi, lowc_lo = apply_inverse(m_col, f_hi, f_lo)
+    lowmi_r, _, _ = apply_inverse(z_rows, f_hi, f_lo)
+    _, lmc_hi, lmc_lo = apply_inverse(z_col, f_hi, f_lo)
 
     ones = jnp.ones((H // MSLOT,), jnp.int32)
     none = jnp.zeros((1,), jnp.int32)
     info = jnp.stack([jnp.int32(1), c * W, r * H, jnp.int32(0)]).astype(jnp.int32)
-    reduced_ii = panel_update("array", stiff, low_r, low_c, ones, info, none, H, W)
+    reduced_ii = panel_update("array", stiff, low_r, lowc_hi, lowc_lo, ones, info, none, H, W)
 
     lmi = jnp.concatenate(
         [lowmi_r.reshape(cap0, MSLOT, PANEL), jnp.zeros((1, MSLOT, PANEL), jnp.float32)], axis=0
@@ -338,19 +344,20 @@
     lmi_full = lmi[slot_r].reshape(nsub * MSLOT, PANEL)
     flags = has0.astype(jnp.int32)
     reduced_mi = panel_update(
-        "gather", recv_t, lmi_full, low_c, flags, info, slot_tab.reshape(-1).astype(jnp.int32), nsub * MSLOT, W
+        "gather", recv_t, lmi_full, lowc_hi, lowc_lo, flags, info, slot_tab.reshape(-1).astype(jnp.int32), nsub * MSLOT, W
     )
 
     nc = ratio * cap0
-    lmc = jnp.concatenate(
-        [lowmi_c.reshape(nc, MSLOT, PANEL), jnp.zeros((1, MSLOT, PANEL), jnp.float32)], axis=0
-    )
     mode_width = ratio * nsub * MSLOT
-    lmc_full = lmc[slot_c].reshape(mode_width, PANEL)
+
+    def spread_cols(part):
+        part = jnp.concatenate([part.reshape(nc, MSLOT, PANEL), jnp.zeros((1, MSLOT, PANEL), part.dtype)], axis=0)
+        return part[slot_c].reshape(mode_width, PANEL)
+
     diag_values = jnp.where(live, eigvals, 1.0).reshape(-1, 1)
     mode_rows = diag_values.shape[0]
     info_mm = jnp.stack([jnp.int32(0), c * mode_width, r * mode_rows, jnp.int32(0)]).astype(jnp.int32)
-    reduced_mm = panel_update("diag", diag_values, lmi_full, lmc_full, flags, info_mm, none, mode_rows, mode_width)
+    reduced_mm = panel_update("diag", diag_values, lmi_full, spread_cols(lmc_hi), spread_cols(lmc_lo), flags, info_mm, none, mode_rows, mode_width)
     return (reduced_ii, reduced_mi, reduced_mm)
 
 

time: 354 us -> 356 us (level)
  the two profiles are of different devices: /device:TPU:6 before, /device:TPU:3 now
where the time goes in v10:
time: 356 us; the launch traced here: 353 us
  Pallas kernels  141 us (40%)
  waiting for transfers between devices  79.7 us (22%)
  local copies, waits for them, and re-layouts  38.4 us (11%)
  blocking collectives  32.1 us (9%)
  starting transfers between devices  25.9 us (7%)
  other arithmetic  14.5 us (4%)
  between operations  14.3 us (4%)
  matrix products  7.2 us (2%)
    pallas_call x1, Pallas kernels, chol_inverse(): pl.pallas_call(chol_inv_kernel, out_shape=jax.ShapeDtypeStruct((n, n), jn...  78.6 us
    pallas_call x3, Pallas kernels, panel_update(): pl.pallas_call(functools.partial(update_kernel, kind, tm, width, len(base...  40.3 us
    all_gather x1, waiting for transfers between devices, per_device(): kpp_col0 = lax.all_gather(kpp_part, 'row', axis=0, tiled=True)  40.3 us
    ppermute x1, waiting for transfers between devices, per_device(): b_slice = lax.ppermute(payload, AXES, perm)  38.3 us
    all_gather x1, blocking collectives, per_device(): z_all = lax.all_gather(z_local, 'col', axis=0, tiled=False)  32.1 us
    pallas_call x4, Pallas kernels, apply_inverse(): pl.pallas_call(solve_kernel, grid=(rows // tm,), in_specs=[spec, pl.Block...  21.9 us
    ppermute x3, starting transfers between devices, per_device(): lax.ppermute(out_k, 'col', [(i, (i + k) % C) for i in range(C)])  12.3 us
    dot_general x1, matrix products, per_device(): jnp.einsum('sim,sitp->stmp', eigvecs, coupling, preferred_element_type=jn...  7.2 us
  transfers between devices with their start and end apart: 21, of which 4 were waited for; matrix products, arithmetic and copies ran while one was open for 10% of the time, Pallas kernels for 25%

profile of v10, /device:TPU:3, one launch (start us, length us, event | category | flops | bytes accessed | tf_op | source)
XLA Modules:
  0.0 353.1 jit_solution(5460700837708450970)
XLA Ops:
  15.8 7.2 %fusion.3 = f32[8,2,128,128]{3,2,1,0:T(8,128)S(1)} fusion(bf16[8,2048,128]{2,1,0:T(8,128)(2,1)} %param.8, bf16[8,2048,2,128]{3,2,1,0:T(2,128)(2,1)} %param.9, f32[8,128]{1,0:T(8,128)S(1)} %fusion.16), kind=kOutput, calls=%fused_computation.14 | convolution fusion | flops 1074003968 | bytes 13635584 | tf_op jit(solution)/shard_map/sim,sitp->stmp/dot_general | solution.py:256
  23.0 40.3 %all-gather.9.cloned.1.call-done = f32[512,512]{1,0:T(8,128)} async-done(((f32[64,512]{1,0:T(8,128)}), f32[512,512]{1,0:T(8,128)}) %all-gather.9.cloned.1.call-update) | async-done | bytes 1048592 | tf_op jit(solution)/shard_map/all_gather | solution.py:267
  71.3 2.0 gather_fusion.2
  73.3 2.9 constant_dynamic-slice_fusion
  76.2 10.0 %collective-permute-start.15 = (f32[8,128,128]{2,1,0:T(8,128)}, f32[8,128,128]{2,1,0:T(8,128)}, u32[]{:S(2)}, u32[]{:S(2)}) collective-permute-start(f32[8,128,128]{2,1,0:T(8,128)} %get-tuple-element.42), channel_id=1, source_target_pairs={{0,2},{1,3},{2,0},{3,1},{4,6},{5,7},{6,4},{7,5},{8,10},{9,11},{10,... | collective-permute-start | bytes 1572872 | tf_op jit(solution)/shard_map/ppermute | solution.py:287
  86.3 2.4 fusion.29
  92.8 2.3 collective-permute-start.16
  95.1 2.1 select_select_fusion
  99.9 32.1 %all-gather = f32[8,128,128]{2,1,0:T(8,128)S(1)} all-gather(f32[2,128,128]{2,1,0:T(8,128)S(1)} %gather_fusion.1), channel_id=2, replica_groups=mesh['row'=8,'col'=4] {'col'}, dimensions={0}, use_global_device_ids=true | all-gather | bytes 655360 | tf_op jit(solution)/shard_map/all_gather | solution.py:305
  133.5 2.5 collective-permute-start.13
  137.8 2.0 gather_fusion.3
  143.4 38.3 %collective-permute-done.13 = f32[328,512]{1,0:T(8,128)} collective-permute-done((f32[328,512]{1,0:T(8,128)}, f32[328,512]{1,0:T(8,128)}, u32[]{:S(2)}, u32[]{:S(2)}) %collective-permute-start.13) | collective-permute-done | bytes 671776 | tf_op jit(solution)/shard_map/ppermute | solution.py:319
  181.8 78.6 %shard_map.85 = f32[512,512]{1,0:T(8,128)} custom-call(f32[512,512]{1,0:T(8,128)} %all-gather.11.cloned.1.call-done.a_ref), custom_call_target="tpu_custom_call" | custom-call | flops 107374182400 | bytes 2097152 | tf_op jit(solution)/shard_map/pallas_call | solution.py:92
  260.4 2.4 fusion.8
  262.8 2.9 shard_map.89
  267.6 5.6 %shard_map.86 = (f32[1024,512]{1,0:T(8,128)}, bf16[1024,512]{1,0:T(8,128)(2,1)}, bf16[1024,512]{1,0:T(8,128)(2,1)}) custom-call(f32[1024,512]{1,0:T(8,128)} %all-gather.7.cloned.1.call-done.x_ref, bf16[512,512]{1,0:T(8,128)(2,1)} %get-tuple-element.46.fhi_ref, bf16[512,512]{1,0:T(8,128)(2,1)} %get-tuple-element.45.flo_ref), custom_call_target="tpu_custom_call" | custom-call | flops 1610612736 | bytes 4194304 | tf_op jit(solution)/shard_map/pallas_call | solution.py:200
  274.6 2.3 slice.133
  276.9 4.6 %slice.132 = f32[8,256,512]{2,1,0:T(8,128)} slice(f32[8,328,512]{2,1,0:T(8,128)} %bitcast.84), slice={[0:8], [0:256], [0:512]} | slice | bytes 8388608 | tf_op jit(solution)/shard_map/slice | solution.py:321
  281.6 3.6 %shard_map.91 = (f32[512,512]{1,0:T(8,128)}, bf16[512,512]{1,0:T(8,128)(2,1)}, bf16[512,512]{1,0:T(8,128)(2,1)}) custom-call(f32[512,512]{1,0:T(8,128)} %bitcast.92, bf16[512,512]{1,0:T(8,128)(2,1)} %get-tuple-element.46.fhi_ref, bf16[512,512]{1,0:T(8,128)(2,1)} %get-tuple-element.45.flo_ref), custom_call_target="tpu_custom_call" | custom-call | flops 805306368 | bytes 2097152 | tf_op jit(solution)/shard_map/pallas_call | solution.py:200
  288.2 3.1 gather_fusion.5
  293.3 9.7 %shard_map.87 = (f32[2048,512]{1,0:T(8,128)}, bf16[2048,512]{1,0:T(8,128)(2,1)}, bf16[2048,512]{1,0:T(8,128)(2,1)}) custom-call(f32[2048,512]{1,0:T(8,128)} %bitcast.85, bf16[512,512]{1,0:T(8,128)(2,1)} %get-tuple-element.46.fhi_ref, bf16[512,512]{1,0:T(8,128)(2,1)} %get-tuple-element.45.flo_ref), custom_call_target="tpu_custom_call" | custom-call | flops 3221225472 | bytes 8388608 | tf_op jit(solution)/shard_map/pallas_call | solution.py:200
  306.3 20.9 %shard_map.88 = f32[1024,2048]{1,0:T(8,128)} custom-call(s32[8]{0:T(128)S(1)} %broadcast_31_flags_ref.2.flags_ref, s32[4]{0:T(128)S(1)} %get-tuple-element.59.info_ref, s32[1]{0:T(128)} %constant.134.clone.1.slots_ref, f32[1024,2048]{1,0:T(8,128)} %refs_0_.1, f32[1024,512]{1,0:T(8,128)S(1)} %copy-done.3, bf16[2048,512]{1,0:T(8,128)(2,1)S(1)} %copy-done.1, ...), custom_call_target="tpu_custom_call" | custom-call | flops 6442450944 | bytes 20971520 | tf_op jit(solution)/shard_map/pallas_call | solution.py:173
  327.2 10.4 %shard_map.90 = f32[1024,2048]{1,0:T(8,128)} custom-call(s32[8]{0:T(128)S(1)} %get-tuple-element.56.flags_ref, s32[4]{0:T(128)S(1)} %get-tuple-element.59.info_ref, s32[32]{0:T(128)S(1)} %select_n.302.slots_ref, f32[9,128,512]{2,1,0:T(8,128)} %concatenate.48.refs_0_.refs_1_.refs_2_.refs_3_, f32[9,128,512]{2,1,0:T(8,128)} %concatenate.48.refs_0_.refs_1_.refs_2_.refs_3_, ...), custom_call_target="tpu_custom_call" | custom-call | flops 6442450944 | bytes 20971520 | tf_op jit(solution)/shard_map/pallas_call | solution.py:173
  337.6 9.0 %shard_map.92 = f32[1024,2048]{1,0:T(8,128)} custom-call(s32[8]{0:T(128)S(1)} %get-tuple-element.56.flags_ref, s32[4]{0:T(128)S(1)} %get-tuple-element.58.info_ref, s32[1]{0:T(128)} %constant.134.clone.1.slots_ref, f32[1024,1]{1,0:T(8,128)S(1)} %copy.42.refs_0_, f32[1024,512]{1,0:T(8,128)S(1)} %bitcast.78, bf16[2048,512]{1,0:T(8,128)(2,1)S(1)} %bitcast.79, ...), custom_call_target="tpu_custom_call" | custom-call | flops 6442450944 | bytes 20971520 | tf_op jit(solution)/shard_map/pallas_call | solution.py:173
  (123 shorter events, 41.5 us)
Async XLA Ops:
  7.2 56.1 %all-gather.9.cloned.1.call-start = ((), (), s32[]{:S(2)}) async-start(), calls=%async_computation.1 | async-start | bytes 1179648 | tf_op jit(solution)/shard_map/all_gather | solution.py:267
  8.5 3.4 collective-permute-start.9
  9.2 3.4 collective-permute-start.8
  9.9 3.4 collective-permute-start.7
  10.6 2.8 collective-permute-start.6
  11.3 2.1 collective-permute-start.5
  11.9 1.4 collective-permute-start.4
  12.6 0.7 collective-permute-start.3
  15.0 166.7 %all-gather.11.cloned.1.call-start = ((), (), s32[]{:S(2)}) async-start(), calls=%async_computation.2 | async-start | bytes 1310720 | tf_op jit(solution)/shard_map/all_gather | solution.py:272
  64.5 4.4 %collective-permute-start.12 = (f32[128,512]{1,0:T(8,128)S(1)}, f32[128,512]{1,0:T(8,128)S(1)}, u32[]{:S(2)}, u32[]{:S(2)}) collective-permute-start(f32[128,512]{1,0:T(8,128)S(1)} %get-tuple-element.47), channel_id=1, source_target_pairs={{0,1},{4,5},{8,9},{12,13},{16,17},{20,21},{24,25},{28,29}} | collective-permute-start | bytes 786440 | tf_op jit(solution)/shard_map/ppermute | solution.py:271
  65.8 3.1 collective-permute-start.11
  66.5 2.4 collective-permute-start.10
  70.6 196.9 %all-gather.7.cloned.1.call-start = ((), (), s32[]{:S(2)}) async-start(), calls=%async_computation | async-start | bytes 2621440 | tf_op jit(solution)/shard_map/all_gather | solution.py:315
  76.2 59.9 %collective-permute-start.15 = (f32[8,128,128]{2,1,0:T(8,128)}, f32[8,128,128]{2,1,0:T(8,128)}, u32[]{:S(2)}, u32[]{:S(2)}) collective-permute-start(f32[8,128,128]{2,1,0:T(8,128)} %get-tuple-element.42), channel_id=1, source_target_pairs={{0,2},{1,3},{2,0},{3,1},{4,6},{5,7},{6,4},{7,5},{8,10},{9,11},{10,... | collective-permute-start | bytes 1572872 | tf_op jit(solution)/shard_map/ppermute | solution.py:287
  86.1 49.9 %collective-permute-start.14 = (f32[8,128,128]{2,1,0:T(8,128)}, f32[8,128,128]{2,1,0:T(8,128)}, u32[]{:S(2)}, u32[]{:S(2)}) collective-permute-start(f32[8,128,128]{2,1,0:T(8,128)} %get-tuple-element.43), channel_id=1, source_target_pairs={{0,1},{1,2},{2,3},{3,0},{4,5},{5,6},{6,7},{7,4},{8,9},{9,10},{10,1... | collective-permute-start | bytes 1572872 | tf_op jit(solution)/shard_map/ppermute | solution.py:287
  88.7 4.1 %collective-permute-start.2 = (f32[256,512]{1,0:T(8,128)}, f32[256,512]{1,0:T(8,128)S(1)}, u32[]{:S(2)}, u32[]{:S(2)}) collective-permute-start(f32[256,512]{1,0:T(8,128)} %get-tuple-element.38), channel_id=1, source_target_pairs={{0,1},{4,5},{8,9},{12,13},{16,17},{20,21},{24,25},{28,29}} | collective-permute-start | bytes 1572872 | tf_op jit(solution)/shard_map/ppermute | solution.py:313
  90.1 5.0 %collective-permute-start.1 = (f32[256,512]{1,0:T(8,128)S(1)}, f32[256,512]{1,0:T(8,128)S(1)}, u32[]{:S(2)}, u32[]{:S(2)}) collective-permute-start(f32[256,512]{1,0:T(8,128)S(1)} %get-tuple-element.39), channel_id=1, source_target_pairs={{0,2},{4,6},{8,10},{12,14},{16,18},{20,22},{24,26},{28,30}} | collective-permute-start | bytes 1572872 | tf_op jit(solution)/shard_map/ppermute | solution.py:313
  90.8 4.3 %collective-permute-start = (f32[256,512]{1,0:T(8,128)S(1)}, f32[256,512]{1,0:T(8,128)}, u32[]{:S(2)}, u32[]{:S(2)}) collective-permute-start(f32[256,512]{1,0:T(8,128)S(1)} %get-tuple-element.40), channel_id=1, source_target_pairs={{0,3},{4,7},{8,11},{12,15},{16,19},{20,23},{24,27},{28,31}} | collective-permute-start | bytes 1572872 | tf_op jit(solution)/shard_map/ppermute | solution.py:313
  92.8 43.2 %collective-permute-start.16 = (f32[8,128,128]{2,1,0:T(8,128)}, f32[8,128,128]{2,1,0:T(8,128)}, u32[]{:S(2)}, u32[]{:S(2)}) collective-permute-start(f32[8,128,128]{2,1,0:T(8,128)} %get-tuple-element.44), channel_id=1, source_target_pairs={{0,3},{1,0},{2,1},{3,2},{4,7},{5,4},{6,5},{7,6},{8,11},{9,8},{10,9... | collective-permute-start | bytes 1572872 | tf_op jit(solution)/shard_map/ppermute | solution.py:287
  97.2 176.0 %all-gather.13.cloned.1.call-start = ((), (), s32[]{:S(2)}) async-start(), calls=%async_computation.3 | async-start | bytes 6045696 | tf_op jit(solution)/shard_map/all_gather | solution.py:320
  97.7 34.9 %copy-start.4 = (f32[256,512]{1,0:T(8,128)S(1)}, f32[256,512]{1,0:T(8,128)}, u32[]{:S(2)}) copy-start(f32[256,512]{1,0:T(8,128)} %select_select_fusion) | copy-start | bytes 1572868
  133.5 48.2 %collective-permute-start.13 = (f32[328,512]{1,0:T(8,128)}, f32[328,512]{1,0:T(8,128)}, u32[]{:S(2)}, u32[]{:S(2)}) collective-permute-start(f32[328,512]{1,0:T(8,128)} %select_maximum_fusion), channel_id=1, source_target_pairs={{0,0},{1,4},{2,8},{3,12},{4,16},{5,20},{6,24},{7,28},{8,1},{9,5},{... | collective-permute-start | bytes 2015240 | tf_op jit(solution)/shard_map/ppermute | solution.py:319
  306.2 20.9 %copy-start.2 = (bf16[2048,512]{1,0:T(8,128)(2,1)S(1)}, bf16[2048,512]{1,0:T(8,128)(2,1)}, u32[]{:S(2)}) copy-start(bf16[2048,512]{1,0:T(8,128)(2,1)} %get-tuple-element.25.refs_2_.refs_5_) | copy-start | bytes 6291460
  327.2 10.4 %copy-start = (bf16[16,128,512]{2,1,0:T(8,128)(2,1)S(1)}, bf16[16,128,512]{2,1,0:T(8,128)(2,1)}, u32[]{:S(2)}) copy-start(bf16[16,128,512]{2,1,0:T(8,128)(2,1)} %gather_fusion.5) | copy-start | bytes 6291460
  (6 other events, 34.0 us)
Sparse Core Ops, SparseCore 0:
  15.2 48.0 all-gather.8
  70.8 30.6 all-gather.10
  103.6 40.9 all-gather.6
  181.9 83.1 all-gather.12

commit v11 on v10

--- a/solution.py
+++ b/solution.py
@@ -281,6 +281,7 @@
     match = onehot[:, :, None] & (rank_pd[:, :, None] == jnp.arange(cap, dtype=jnp.int32)[None, None, :])
     send_idx = jnp.where(jnp.any(match, axis=0), jnp.argmax(match, axis=0), npair)
     send = flat_pad[send_idx]
+    send, _ = lax.optimization_barrier((send, kpp))
     shifted = [send[c]]
     for k in range(1, C):
         out_k = lax.dynamic_index_in_dim(send, (c + k) % C, axis=0, keepdims=False)

time: 356 us -> 340 us (0.955)
  the two profiles are of different devices: /device:TPU:3 before, /device:TPU:0 now
where the time goes in v11:
time: 340 us; the launch traced here: 338 us
  Pallas kernels  141 us (41%)
  starting transfers between devices  69.4 us (20%)
  waiting for transfers between devices  42 us (12%)
  local copies, waits for them, and re-layouts  41.7 us (12%)
  other arithmetic  14.8 us (4%)
  between operations  14.3 us (4%)
  blocking collectives  7.67 us (2%)
  matrix products  7.19 us (2%)
    pallas_call x1, Pallas kernels, chol_inverse(): pl.pallas_call(chol_inv_kernel, out_shape=jax.ShapeDtypeStruct((n, n), jn...  78.7 us
    ppermute x3, starting transfers between devices, per_device(): lax.ppermute(out_k, 'col', [(i, (i + k) % C) for i in range(C)])  45.8 us
    pallas_call x3, Pallas kernels, panel_update(): pl.pallas_call(functools.partial(update_kernel, kind, tm, width, len(base...  40.5 us
    all_gather x1, waiting for transfers between devices, per_device(): kpp_col0 = lax.all_gather(kpp_part, 'row', axis=0, tiled=True)  36.2 us
    pallas_call x4, Pallas kernels, apply_inverse(): pl.pallas_call(solve_kernel, grid=(rows // tm,), in_specs=[spec, pl.Block...  22 us
    ppermute x7, starting transfers between devices, per_device(): got.append(lax.ppermute(kpp_src[i * rs:(i + 1) * rs], AXES, [(0, i * C)]))  12.6 us
    all_gather x1, blocking collectives, per_device(): z_all = lax.all_gather(z_local, 'col', axis=0, tiled=False)  7.67 us
    dot_general x1, matrix products, per_device(): jnp.einsum('sim,sitp->stmp', eigvecs, coupling, preferred_element_type=jn...  7.19 us
  transfers between devices with their start and end apart: 21, of which 5 were waited for; matrix products, arithmetic and copies ran while one was open for 12% of the time, Pallas kernels for 26%

profile of v11, /device:TPU:0, one launch (start us, length us, event | category | flops | bytes accessed | tf_op | source)
XLA Modules:
  0.0 338.4 jit_solution(219511411833124098)
XLA Ops:
  8.5 4.8 %collective-permute-start.9 = (f32[64,512]{1,0:T(8,128)S(1)}, f32[64,512]{1,0:T(8,128)S(1)}, u32[]{:S(2)}, u32[]{:S(2)}) collective-permute-start(f32[64,512]{1,0:T(8,128)S(1)} %get-tuple-element.33), channel_id=1, source_target_pairs={{0,4}} | collective-permute-start | bytes 393224 | tf_op jit(solution)/shard_map/ppermute | solution.py:265
  25.9 2.3 fusion.29
  30.9 36.2 %all-gather.9.cloned.1.call-done = f32[512,512]{1,0:T(8,128)} async-done(((f32[64,512]{1,0:T(8,128)}), f32[512,512]{1,0:T(8,128)}) %all-gather.9.cloned.1.call-update) | async-done | bytes 1048592 | tf_op jit(solution)/shard_map/all_gather | solution.py:267
  70.3 2.8 collective-permute-start.11
  76.9 2.8 collective-permute-done.10
  81.6 7.2 %fusion.3 = f32[8,2,128,128]{3,2,1,0:T(8,128)S(1)} fusion(bf16[8,2048,128]{2,1,0:T(8,128)(2,1)} %param.8, bf16[8,2048,2,128]{3,2,1,0:T(2,128)(2,1)} %param.9, f32[8,128]{1,0:T(8,128)S(1)} %fusion.16), kind=kOutput, calls=%fused_computation.14 | convolution fusion | flops 1074003968 | bytes 13635584 | tf_op jit(solution)/shard_map/sim,sitp->stmp/dot_general | solution.py:256
  94.0 7.7 %all-gather = f32[8,128,128]{2,1,0:T(8,128)S(1)} all-gather(f32[2,128,128]{2,1,0:T(8,128)S(1)} %gather_fusion.1), channel_id=2, replica_groups=mesh['row'=8,'col'=4] {'col'}, dimensions={0}, use_global_device_ids=true | all-gather | bytes 655360 | tf_op jit(solution)/shard_map/all_gather | solution.py:306
  107.6 3.2 constant_dynamic-slice_fusion
  110.7 17.8 %collective-permute-start.16 = (f32[8,128,128]{2,1,0:T(8,128)}, f32[8,128,128]{2,1,0:T(8,128)}, u32[]{:S(2)}, u32[]{:S(2)}) collective-permute-start(f32[8,128,128]{2,1,0:T(8,128)} %get-tuple-element.44), channel_id=1, source_target_pairs={{0,3},{1,0},{2,1},{3,2},{4,7},{5,4},{6,5},{7,6},{8,11},{9,8},{10,9... | collective-permute-start | bytes 1572872 | tf_op jit(solution)/shard_map/ppermute | solution.py:288
  128.6 28.0 %collective-permute-start.15 = (f32[8,128,128]{2,1,0:T(8,128)}, f32[8,128,128]{2,1,0:T(8,128)}, u32[]{:S(2)}, u32[]{:S(2)}) collective-permute-start(f32[8,128,128]{2,1,0:T(8,128)} %get-tuple-element.45), channel_id=1, source_target_pairs={{0,2},{1,3},{2,0},{3,1},{4,6},{5,7},{6,4},{7,5},{8,10},{9,11},{10,... | collective-permute-start | bytes 1572872 | tf_op jit(solution)/shard_map/ppermute | solution.py:288
  156.6 78.7 %shard_map.85 = f32[512,512]{1,0:T(8,128)} custom-call(f32[512,512]{1,0:T(8,128)} %all-gather.11.cloned.1.call-done.a_ref), custom_call_target="tpu_custom_call" | custom-call | flops 107374182400 | bytes 2097152 | tf_op jit(solution)/shard_map/pallas_call | solution.py:92
  235.3 2.3 fusion.8
  237.6 2.9 shard_map.89
  242.5 5.7 %shard_map.86 = (f32[1024,512]{1,0:T(8,128)}, bf16[1024,512]{1,0:T(8,128)(2,1)}, bf16[1024,512]{1,0:T(8,128)(2,1)}) custom-call(f32[1024,512]{1,0:T(8,128)} %all-gather.7.cloned.1.call-done.x_ref, bf16[512,512]{1,0:T(8,128)(2,1)} %get-tuple-element.48.fhi_ref, bf16[512,512]{1,0:T(8,128)(2,1)} %get-tuple-element.47.flo_ref), custom_call_target="tpu_custom_call" | custom-call | flops 1610612736 | bytes 4194304 | tf_op jit(solution)/shard_map/pallas_call | solution.py:200
  248.2 2.9 pad_maximum_fusion
  251.1 3.6 %gather_fusion.3 = f32[4,8,128,128]{3,2,1,0:T(8,128)} fusion(f32[4,8,128,128]{3,2,1,0:T(8,128)} %pad_maximum_fusion, s32[1024]{0:T(1024)S(1)} %pad_clamp_fusion.2), kind=kCustom, calls=%fused_computation.3 | custom fusion | bytes 4194320 | tf_op jit(solution)/shard_map/gather | solution.py:290
  259.7 2.3 slice.133
  261.9 4.6 %slice.132 = f32[8,256,512]{2,1,0:T(8,128)} slice(f32[8,328,512]{2,1,0:T(8,128)} %bitcast.84), slice={[0:8], [0:256], [0:512]} | slice | bytes 8388608 | tf_op jit(solution)/shard_map/slice | solution.py:322
  266.6 3.6 %shard_map.91 = (f32[512,512]{1,0:T(8,128)}, bf16[512,512]{1,0:T(8,128)(2,1)}, bf16[512,512]{1,0:T(8,128)(2,1)}) custom-call(f32[512,512]{1,0:T(8,128)} %bitcast.92, bf16[512,512]{1,0:T(8,128)(2,1)} %get-tuple-element.48.fhi_ref, bf16[512,512]{1,0:T(8,128)(2,1)} %get-tuple-element.47.flo_ref), custom_call_target="tpu_custom_call" | custom-call | flops 805306368 | bytes 2097152 | tf_op jit(solution)/shard_map/pallas_call | solution.py:200
  273.3 3.1 gather_fusion.5
  278.4 9.7 %shard_map.87 = (f32[2048,512]{1,0:T(8,128)}, bf16[2048,512]{1,0:T(8,128)(2,1)}, bf16[2048,512]{1,0:T(8,128)(2,1)}) custom-call(f32[2048,512]{1,0:T(8,128)} %bitcast.85, bf16[512,512]{1,0:T(8,128)(2,1)} %get-tuple-element.48.fhi_ref, bf16[512,512]{1,0:T(8,128)(2,1)} %get-tuple-element.47.flo_ref), custom_call_target="tpu_custom_call" | custom-call | flops 3221225472 | bytes 8388608 | tf_op jit(solution)/shard_map/pallas_call | solution.py:200
  291.3 21.0 %shard_map.88 = f32[1024,2048]{1,0:T(8,128)} custom-call(s32[8]{0:T(128)S(1)} %broadcast_31_flags_ref.2.flags_ref, s32[4]{0:T(128)S(1)} %get-tuple-element.61.info_ref, s32[1]{0:T(128)} %constant.134.clone.1.slots_ref, f32[1024,2048]{1,0:T(8,128)} %refs_0_.1, f32[1024,512]{1,0:T(8,128)S(1)} %copy-done.3, bf16[2048,512]{1,0:T(8,128)(2,1)S(1)} %copy-done.1, ...), custom_call_target="tpu_custom_call" | custom-call | flops 6442450944 | bytes 20971520 | tf_op jit(solution)/shard_map/pallas_call | solution.py:173
  312.3 10.5 %shard_map.90 = f32[1024,2048]{1,0:T(8,128)} custom-call(s32[8]{0:T(128)S(1)} %get-tuple-element.58.flags_ref, s32[4]{0:T(128)S(1)} %get-tuple-element.61.info_ref, s32[32]{0:T(128)S(1)} %select_n.302.slots_ref, f32[9,128,512]{2,1,0:T(8,128)} %concatenate.48.refs_0_.refs_1_.refs_2_.refs_3_, f32[9,128,512]{2,1,0:T(8,128)} %concatenate.48.refs_0_.refs_1_.refs_2_.refs_3_, ...), custom_call_target="tpu_custom_call" | custom-call | flops 6442450944 | bytes 20971520 | tf_op jit(solution)/shard_map/pallas_call | solution.py:173
  322.9 9.0 %shard_map.92 = f32[1024,2048]{1,0:T(8,128)} custom-call(s32[8]{0:T(128)S(1)} %get-tuple-element.58.flags_ref, s32[4]{0:T(128)S(1)} %get-tuple-element.60.info_ref, s32[1]{0:T(128)} %constant.134.clone.1.slots_ref, f32[1024,1]{1,0:T(8,128)S(1)} %copy.42.refs_0_, f32[1024,512]{1,0:T(8,128)S(1)} %bitcast.78, bf16[2048,512]{1,0:T(8,128)(2,1)S(1)} %bitcast.79, ...), custom_call_target="tpu_custom_call" | custom-call | flops 6442450944 | bytes 20971520 | tf_op jit(solution)/shard_map/pallas_call | solution.py:173
  (127 shorter events, 51.3 us)
Async XLA Ops:
  7.2 60.0 %all-gather.9.cloned.1.call-start = ((), (), s32[]{:S(2)}) async-start(), calls=%async_computation.1 | async-start | bytes 1179648 | tf_op jit(solution)/shard_map/all_gather | solution.py:267
  8.5 10.1 %collective-permute-start.9 = (f32[64,512]{1,0:T(8,128)S(1)}, f32[64,512]{1,0:T(8,128)S(1)}, u32[]{:S(2)}, u32[]{:S(2)}) collective-permute-start(f32[64,512]{1,0:T(8,128)S(1)} %get-tuple-element.33), channel_id=1, source_target_pairs={{0,4}} | collective-permute-start | bytes 393224 | tf_op jit(solution)/shard_map/ppermute | solution.py:265
  13.4 6.5 %collective-permute-start.8 = (f32[64,512]{1,0:T(8,128)S(1)}, f32[64,512]{1,0:T(8,128)S(1)}, u32[]{:S(2)}, u32[]{:S(2)}) collective-permute-start(f32[64,512]{1,0:T(8,128)S(1)} %get-tuple-element.34), channel_id=1, source_target_pairs={{0,8}} | collective-permute-start | bytes 393224 | tf_op jit(solution)/shard_map/ppermute | solution.py:265
  14.7 6.6 %collective-permute-start.7 = (f32[64,512]{1,0:T(8,128)S(1)}, f32[64,512]{1,0:T(8,128)S(1)}, u32[]{:S(2)}, u32[]{:S(2)}) collective-permute-start(f32[64,512]{1,0:T(8,128)S(1)} %get-tuple-element.35), channel_id=1, source_target_pairs={{0,12}} | collective-permute-start | bytes 393224 | tf_op jit(solution)/shard_map/ppermute | solution.py:265
  16.0 5.3 %collective-permute-start.6 = (f32[64,512]{1,0:T(8,128)S(1)}, f32[64,512]{1,0:T(8,128)S(1)}, u32[]{:S(2)}, u32[]{:S(2)}) collective-permute-start(f32[64,512]{1,0:T(8,128)S(1)} %get-tuple-element.36), channel_id=1, source_target_pairs={{0,16}} | collective-permute-start | bytes 393224 | tf_op jit(solution)/shard_map/ppermute | solution.py:265
  17.3 4.1 %collective-permute-start.5 = (f32[64,512]{1,0:T(8,128)S(1)}, f32[64,512]{1,0:T(8,128)S(1)}, u32[]{:S(2)}, u32[]{:S(2)}) collective-permute-start(f32[64,512]{1,0:T(8,128)S(1)} %get-tuple-element.37), channel_id=1, source_target_pairs={{0,20}} | collective-permute-start | bytes 393224 | tf_op jit(solution)/shard_map/ppermute | solution.py:265
  18.6 4.2 %collective-permute-start.4 = (f32[64,512]{1,0:T(8,128)S(1)}, f32[64,512]{1,0:T(8,128)S(1)}, u32[]{:S(2)}, u32[]{:S(2)}) collective-permute-start(f32[64,512]{1,0:T(8,128)S(1)} %get-tuple-element.38), channel_id=1, source_target_pairs={{0,24}} | collective-permute-start | bytes 393224 | tf_op jit(solution)/shard_map/ppermute | solution.py:265
  19.9 4.2 %collective-permute-start.3 = (f32[64,512]{1,0:T(8,128)S(1)}, f32[64,512]{1,0:T(8,128)S(1)}, u32[]{:S(2)}, u32[]{:S(2)}) collective-permute-start(f32[64,512]{1,0:T(8,128)S(1)} %get-tuple-element.39), channel_id=1, source_target_pairs={{0,28}} | collective-permute-start | bytes 393224 | tf_op jit(solution)/shard_map/ppermute | solution.py:265
  25.8 81.7 %all-gather.11.cloned.1.call-start = ((), (), s32[]{:S(2)}) async-start(), calls=%async_computation.2 | async-start | bytes 1310720 | tf_op jit(solution)/shard_map/all_gather | solution.py:272
  28.2 61.5 %collective-permute-start.2 = (f32[256,512]{1,0:T(8,128)}, f32[256,512]{1,0:T(8,128)S(1)}, u32[]{:S(2)}, u32[]{:S(2)}) collective-permute-start(f32[256,512]{1,0:T(8,128)} %get-tuple-element.40), channel_id=1, source_target_pairs={{0,1},{4,5},{8,9},{12,13},{16,17},{20,21},{24,25},{28,29}} | collective-permute-start | bytes 1572872 | tf_op jit(solution)/shard_map/ppermute | solution.py:314
  29.5 60.1 %collective-permute-start.1 = (f32[256,512]{1,0:T(8,128)S(1)}, f32[256,512]{1,0:T(8,128)S(1)}, u32[]{:S(2)}, u32[]{:S(2)}) collective-permute-start(f32[256,512]{1,0:T(8,128)S(1)} %get-tuple-element.41), channel_id=1, source_target_pairs={{0,2},{4,6},{8,10},{12,14},{16,18},{20,22},{24,26},{28,30}} | collective-permute-start | bytes 1572872 | tf_op jit(solution)/shard_map/ppermute | solution.py:314
  69.0 5.8 %collective-permute-start.12 = (f32[128,512]{1,0:T(8,128)}, f32[128,512]{1,0:T(8,128)S(1)}, u32[]{:S(2)}, u32[]{:S(2)}) collective-permute-start(f32[128,512]{1,0:T(8,128)} %get-tuple-element.49), channel_id=1, source_target_pairs={{0,1},{4,5},{8,9},{12,13},{16,17},{20,21},{24,25},{28,29}} | collective-permute-start | bytes 786440 | tf_op jit(solution)/shard_map/ppermute | solution.py:271
  70.3 6.6 %collective-permute-start.11 = (f32[128,512]{1,0:T(8,128)S(1)}, f32[128,512]{1,0:T(8,128)S(1)}, u32[]{:S(2)}, u32[]{:S(2)}) collective-permute-start(f32[128,512]{1,0:T(8,128)S(1)} %get-tuple-element.50), channel_id=1, source_target_pairs={{0,2},{4,6},{8,10},{12,14},{16,18},{20,22},{24,26},{28,30}} | collective-permute-start | bytes 786440 | tf_op jit(solution)/shard_map/ppermute | solution.py:271
  73.1 6.7 %collective-permute-start.10 = (f32[128,512]{1,0:T(8,128)S(1)}, f32[128,512]{1,0:T(8,128)S(1)}, u32[]{:S(2)}, u32[]{:S(2)}) collective-permute-start(f32[128,512]{1,0:T(8,128)S(1)} %get-tuple-element.51), channel_id=1, source_target_pairs={{0,3},{4,7},{8,11},{12,15},{16,19},{20,23},{24,27},{28,31}} | collective-permute-start | bytes 786440 | tf_op jit(solution)/shard_map/ppermute | solution.py:271
  74.8 14.8 %collective-permute-start = (f32[256,512]{1,0:T(8,128)S(1)}, f32[256,512]{1,0:T(8,128)}, u32[]{:S(2)}, u32[]{:S(2)}) collective-permute-start(f32[256,512]{1,0:T(8,128)S(1)} %get-tuple-element.42), channel_id=1, source_target_pairs={{0,3},{4,7},{8,11},{12,15},{16,19},{20,23},{24,27},{28,31}} | collective-permute-start | bytes 1572872 | tf_op jit(solution)/shard_map/ppermute | solution.py:314
  81.5 160.9 %all-gather.7.cloned.1.call-start = ((), (), s32[]{:S(2)}) async-start(), calls=%async_computation | async-start | bytes 2621440 | tf_op jit(solution)/shard_map/all_gather | solution.py:316
  91.7 166.6 %all-gather.13.cloned.1.call-start = ((), (), s32[]{:S(2)}) async-start(), calls=%async_computation.3 | async-start | bytes 6045696 | tf_op jit(solution)/shard_map/all_gather | solution.py:321
  93.3 10.0 %copy-start.4 = (f32[256,512]{1,0:T(8,128)S(1)}, f32[256,512]{1,0:T(8,128)}, u32[]{:S(2)}) copy-start(f32[256,512]{1,0:T(8,128)} %select_select_fusion) | copy-start | bytes 1572868
  103.3 3.4 collective-permute-start.13
  110.7 137.4 %collective-permute-start.16 = (f32[8,128,128]{2,1,0:T(8,128)}, f32[8,128,128]{2,1,0:T(8,128)}, u32[]{:S(2)}, u32[]{:S(2)}) collective-permute-start(f32[8,128,128]{2,1,0:T(8,128)} %get-tuple-element.44), channel_id=1, source_target_pairs={{0,3},{1,0},{2,1},{3,2},{4,7},{5,4},{6,5},{7,6},{8,11},{9,8},{10,9... | collective-permute-start | bytes 1572872 | tf_op jit(solution)/shard_map/ppermute | solution.py:288
  128.6 119.6 %collective-permute-start.15 = (f32[8,128,128]{2,1,0:T(8,128)}, f32[8,128,128]{2,1,0:T(8,128)}, u32[]{:S(2)}, u32[]{:S(2)}) collective-permute-start(f32[8,128,128]{2,1,0:T(8,128)} %get-tuple-element.45), channel_id=1, source_target_pairs={{0,2},{1,3},{2,0},{3,1},{4,6},{5,7},{6,4},{7,5},{8,10},{9,11},{10,... | collective-permute-start | bytes 1572872 | tf_op jit(solution)/shard_map/ppermute | solution.py:288
  156.6 91.6 %collective-permute-start.14 = (f32[8,128,128]{2,1,0:T(8,128)}, f32[8,128,128]{2,1,0:T(8,128)}, u32[]{:S(2)}, u32[]{:S(2)}) collective-permute-start(f32[8,128,128]{2,1,0:T(8,128)} %get-tuple-element.46), channel_id=1, source_target_pairs={{0,1},{1,2},{2,3},{3,0},{4,5},{5,6},{6,7},{7,4},{8,9},{9,10},{10,1... | collective-permute-start | bytes 1572872 | tf_op jit(solution)/shard_map/ppermute | solution.py:288
  291.3 21.0 %copy-start.2 = (bf16[2048,512]{1,0:T(8,128)(2,1)S(1)}, bf16[2048,512]{1,0:T(8,128)(2,1)}, u32[]{:S(2)}) copy-start(bf16[2048,512]{1,0:T(8,128)(2,1)} %get-tuple-element.26.refs_2_.refs_5_) | copy-start | bytes 6291460
  312.3 10.5 %copy-start = (bf16[16,128,512]{2,1,0:T(8,128)(2,1)S(1)}, bf16[16,128,512]{2,1,0:T(8,128)(2,1)}, u32[]{:S(2)}) copy-start(bf16[16,128,512]{2,1,0:T(8,128)(2,1)} %gather_fusion.5) | copy-start | bytes 6291460
  (8 other events, 43.4 us)
Sparse Core Ops, SparseCore 0:
  26.0 41.1 all-gather.8
  81.6 15.9 all-gather.10
  99.8 30.3 all-gather.6
  132.2 105.9 all-gather.12

commit v12 on v11

--- a/solution.py
+++ b/solution.py
@@ -43,7 +43,7 @@
         colk = jnp.sum(jnp.where(lane == k, dm, 0.0), axis=1, keepdims=True)
         rowk = jnp.sum(jnp.where(sub == k, dm, 0.0), axis=0, keepdims=True)
         dkk = jnp.sum(jnp.where(lane_r == k, rowk, 0.0), axis=1, keepdims=True)
-        s = 1.0 / jnp.sqrt(dkk)
+        s = lax.rsqrt(dkk)
         lc = jnp.where(sub_c > k, colk * s, 0.0)
         lr = jnp.where(lane_r > k, rowk * s, 0.0)
         dm = dm - lc * lr
@@ -53,7 +53,7 @@
         em = em - lc * xk
         return dm, em, xm
 
-    _, _, xm = lax.fori_loop(0, n, step, (d, eye, jnp.zeros_like(d)))
+    _, _, xm = lax.fori_loop(0, n, step, (d, eye, jnp.zeros_like(d)), unroll=4)
     return xm
 
 

time: 340 us -> 331 us (0.974)
  the two profiles are of different devices: /device:TPU:0 before, /device:TPU:6 now
where the time goes in v12:
time: 331 us; the launch traced here: 325 us
  Pallas kernels  131 us (40%)
  waiting for transfers between devices  76.7 us (23%)
  local copies, waits for them, and re-layouts  41.5 us (13%)
  starting transfers between devices  31.4 us (9%)
  other arithmetic  14.8 us (4%)
  between operations  14.3 us (4%)
  blocking collectives  7.96 us (2%)
  matrix products  7.19 us (2%)
    pallas_call x1, Pallas kernels, chol_inverse(): pl.pallas_call(chol_inv_kernel, out_shape=jax.ShapeDtypeStruct((n, n), jn...  70.2 us
    all_gather x1, waiting for transfers between devices, per_device(): kpp_col0 = lax.all_gather(kpp_part, 'row', axis=0, tiled=True)  45.2 us
    pallas_call x3, Pallas kernels, panel_update(): pl.pallas_call(functools.partial(update_kernel, kind, tm, width, len(base...  39.2 us
    ppermute x1, waiting for transfers between devices, per_device(): b_slice = lax.ppermute(payload, AXES, perm)  27 us
    pallas_call x4, Pallas kernels, apply_inverse(): pl.pallas_call(solve_kernel, grid=(rows // tm,), in_specs=[spec, pl.Block...  22 us
    ppermute x3, starting transfers between devices, per_device(): lax.ppermute(out_k, 'col', [(i, (i + k) % C) for i in range(C)])  14.1 us
    all_gather x1, blocking collectives, per_device(): z_all = lax.all_gather(z_local, 'col', axis=0, tiled=False)  7.96 us
    dot_general x1, matrix products, per_device(): jnp.einsum('sim,sitp->stmp', eigvecs, coupling, preferred_element_type=jn...  7.19 us
  transfers between devices with their start and end apart: 21, of which 3 were waited for; matrix products, arithmetic and copies ran while one was open for 12% of the time, Pallas kernels for 24%

profile of v12, /device:TPU:6, one launch (start us, length us, event | category | flops | bytes accessed | tf_op | source)
XLA Modules:
  0.0 325.3 jit_solution(16258635812013709475)
XLA Ops:
  15.1 2.3 fusion.29
  19.5 45.2 %all-gather.9.cloned.1.call-done = f32[512,512]{1,0:T(8,128)} async-done(((f32[64,512]{1,0:T(8,128)}), f32[512,512]{1,0:T(8,128)}) %all-gather.9.cloned.1.call-update) | async-done | bytes 1048592 | tf_op jit(solution)/shard_map/all_gather | solution.py:267
  71.1 4.4 %collective-permute-done.11 = f32[128,512]{1,0:T(8,128)S(1)} collective-permute-done((f32[128,512]{1,0:T(8,128)S(1)}, f32[128,512]{1,0:T(8,128)S(1)}, u32[]{:S(2)}, u32[]{:S(2)}) %collective-permute-start.11) | collective-permute-done | bytes 262176 | tf_op jit(solution)/shard_map/ppermute | solution.py:271
  77.3 7.2 %fusion.3 = f32[8,2,128,128]{3,2,1,0:T(8,128)S(1)} fusion(bf16[8,2048,128]{2,1,0:T(8,128)(2,1)} %param.8, bf16[8,2048,2,128]{3,2,1,0:T(2,128)(2,1)} %param.9, f32[8,128]{1,0:T(8,128)S(1)} %fusion.16), kind=kOutput, calls=%fused_computation.14 | convolution fusion | flops 1074003968 | bytes 13635584 | tf_op jit(solution)/shard_map/sim,sitp->stmp/dot_general | solution.py:256
  85.4 2.1 select_select_fusion
  89.8 8.0 %all-gather = f32[8,128,128]{2,1,0:T(8,128)S(1)} all-gather(f32[2,128,128]{2,1,0:T(8,128)S(1)} %gather_fusion.1), channel_id=2, replica_groups=mesh['row'=8,'col'=4] {'col'}, dimensions={0}, use_global_device_ids=true | all-gather | bytes 655360 | tf_op jit(solution)/shard_map/all_gather | solution.py:306
  99.4 6.4 %collective-permute-start.13 = (f32[328,512]{1,0:T(8,128)S(1)}, f32[328,512]{1,0:T(8,128)S(1)}, u32[]{:S(2)}, u32[]{:S(2)}) collective-permute-start(f32[328,512]{1,0:T(8,128)S(1)} %select_maximum_fusion), channel_id=1, source_target_pairs={{0,0},{1,4},{2,8},{3,12},{4,16},{5,20},{6,24},{7,28},{8,1},{9,5},{... | collective-permute-start | bytes 2015240 | tf_op jit(solution)/shard_map/ppermute | solution.py:320
  108.4 27.0 %collective-permute-done.13 = f32[328,512]{1,0:T(8,128)S(1)} collective-permute-done((f32[328,512]{1,0:T(8,128)S(1)}, f32[328,512]{1,0:T(8,128)S(1)}, u32[]{:S(2)}, u32[]{:S(2)}) %collective-permute-start.13) | collective-permute-done | bytes 671776 | tf_op jit(solution)/shard_map/ppermute | solution.py:320
  136.3 2.9 constant_dynamic-slice_fusion
  139.2 14.0 %collective-permute-start.16 = (f32[8,128,128]{2,1,0:T(8,128)}, f32[8,128,128]{2,1,0:T(8,128)}, u32[]{:S(2)}, u32[]{:S(2)}) collective-permute-start(f32[8,128,128]{2,1,0:T(8,128)} %get-tuple-element.44), channel_id=1, source_target_pairs={{0,3},{1,0},{2,1},{3,2},{4,7},{5,4},{6,5},{7,6},{8,11},{9,8},{10,9... | collective-permute-start | bytes 1572872 | tf_op jit(solution)/shard_map/ppermute | solution.py:288
  153.3 70.2 %shard_map.85 = f32[512,512]{1,0:T(8,128)} custom-call(f32[512,512]{1,0:T(8,128)} %all-gather.11.cloned.1.call-done.a_ref), custom_call_target="tpu_custom_call" | custom-call | flops 107374182400 | bytes 2097152 | tf_op jit(solution)/shard_map/pallas_call | solution.py:92
  223.5 2.3 fusion.8
  225.9 2.9 shard_map.89
  230.7 5.7 %shard_map.86 = (f32[1024,512]{1,0:T(8,128)}, bf16[1024,512]{1,0:T(8,128)(2,1)}, bf16[1024,512]{1,0:T(8,128)(2,1)}) custom-call(f32[1024,512]{1,0:T(8,128)} %all-gather.7.cloned.1.call-done.x_ref, bf16[512,512]{1,0:T(8,128)(2,1)} %get-tuple-element.48.fhi_ref, bf16[512,512]{1,0:T(8,128)(2,1)} %get-tuple-element.47.flo_ref), custom_call_target="tpu_custom_call" | custom-call | flops 1610612736 | bytes 4194304 | tf_op jit(solution)/shard_map/pallas_call | solution.py:200
  236.4 2.9 pad_maximum_fusion
  239.3 3.6 %gather_fusion.3 = f32[4,8,128,128]{3,2,1,0:T(8,128)} fusion(f32[4,8,128,128]{3,2,1,0:T(8,128)} %pad_maximum_fusion, s32[1024]{0:T(1024)S(1)} %pad_clamp_fusion.2), kind=kCustom, calls=%fused_computation.3 | custom fusion | bytes 4194320 | tf_op jit(solution)/shard_map/gather | solution.py:290
  247.9 2.3 slice.133
  250.2 4.6 %slice.132 = f32[8,256,512]{2,1,0:T(8,128)} slice(f32[8,328,512]{2,1,0:T(8,128)} %bitcast.84), slice={[0:8], [0:256], [0:512]} | slice | bytes 8388608 | tf_op jit(solution)/shard_map/slice | solution.py:322
  254.9 3.6 %shard_map.91 = (f32[512,512]{1,0:T(8,128)}, bf16[512,512]{1,0:T(8,128)(2,1)}, bf16[512,512]{1,0:T(8,128)(2,1)}) custom-call(f32[512,512]{1,0:T(8,128)} %bitcast.92, bf16[512,512]{1,0:T(8,128)(2,1)} %get-tuple-element.48.fhi_ref, bf16[512,512]{1,0:T(8,128)(2,1)} %get-tuple-element.47.flo_ref), custom_call_target="tpu_custom_call" | custom-call | flops 805306368 | bytes 2097152 | tf_op jit(solution)/shard_map/pallas_call | solution.py:200
  261.5 3.1 gather_fusion.5
  266.6 9.7 %shard_map.87 = (f32[2048,512]{1,0:T(8,128)}, bf16[2048,512]{1,0:T(8,128)(2,1)}, bf16[2048,512]{1,0:T(8,128)(2,1)}) custom-call(f32[2048,512]{1,0:T(8,128)} %bitcast.85, bf16[512,512]{1,0:T(8,128)(2,1)} %get-tuple-element.48.fhi_ref, bf16[512,512]{1,0:T(8,128)(2,1)} %get-tuple-element.47.flo_ref), custom_call_target="tpu_custom_call" | custom-call | flops 3221225472 | bytes 8388608 | tf_op jit(solution)/shard_map/pallas_call | solution.py:200
  279.5 20.9 %shard_map.88 = f32[1024,2048]{1,0:T(8,128)} custom-call(s32[8]{0:T(128)S(1)} %broadcast_31_flags_ref.2.flags_ref, s32[4]{0:T(128)S(1)} %get-tuple-element.61.info_ref, s32[1]{0:T(128)} %constant.134.clone.1.slots_ref, f32[1024,2048]{1,0:T(8,128)} %refs_0_.1, f32[1024,512]{1,0:T(8,128)S(1)} %copy-done.3, bf16[2048,512]{1,0:T(8,128)(2,1)S(1)} %copy-done.1, ...), custom_call_target="tpu_custom_call" | custom-call | flops 6442450944 | bytes 20971520 | tf_op jit(solution)/shard_map/pallas_call | solution.py:173
  300.5 9.5 %shard_map.90 = f32[1024,2048]{1,0:T(8,128)} custom-call(s32[8]{0:T(128)S(1)} %get-tuple-element.58.flags_ref, s32[4]{0:T(128)S(1)} %get-tuple-element.61.info_ref, s32[32]{0:T(128)S(1)} %select_n.302.slots_ref, f32[9,128,512]{2,1,0:T(8,128)} %concatenate.48.refs_0_.refs_1_.refs_2_.refs_3_, f32[9,128,512]{2,1,0:T(8,128)} %concatenate.48.refs_0_.refs_1_.refs_2_.refs_3_, ...), custom_call_target="tpu_custom_call" | custom-call | flops 6442450944 | bytes 20971520 | tf_op jit(solution)/shard_map/pallas_call | solution.py:173
  310.0 8.8 %shard_map.92 = f32[1024,2048]{1,0:T(8,128)} custom-call(s32[8]{0:T(128)S(1)} %get-tuple-element.58.flags_ref, s32[4]{0:T(128)S(1)} %get-tuple-element.60.info_ref, s32[1]{0:T(128)} %constant.134.clone.1.slots_ref, f32[1024,1]{1,0:T(8,128)S(1)} %copy.42.refs_0_, f32[1024,512]{1,0:T(8,128)S(1)} %bitcast.78, bf16[2048,512]{1,0:T(8,128)(2,1)S(1)} %bitcast.79, ...), custom_call_target="tpu_custom_call" | custom-call | flops 6442450944 | bytes 20971520 | tf_op jit(solution)/shard_map/pallas_call | solution.py:173
  (127 shorter events, 41.4 us)
Async XLA Ops:
  7.2 57.5 %all-gather.9.cloned.1.call-start = ((), (), s32[]{:S(2)}) async-start(), calls=%async_computation.1 | async-start | bytes 1179648 | tf_op jit(solution)/shard_map/all_gather | solution.py:267
  8.5 3.4 %collective-permute-start.9 = (f32[64,512]{1,0:T(8,128)S(1)}, f32[64,512]{1,0:T(8,128)S(1)}, u32[]{:S(2)}, u32[]{:S(2)}) collective-permute-start(f32[64,512]{1,0:T(8,128)S(1)} %get-tuple-element.33), channel_id=1, source_target_pairs={{0,4}} | collective-permute-start | bytes 393224 | tf_op jit(solution)/shard_map/ppermute | solution.py:265
  9.2 3.4 %collective-permute-start.8 = (f32[64,512]{1,0:T(8,128)S(1)}, f32[64,512]{1,0:T(8,128)S(1)}, u32[]{:S(2)}, u32[]{:S(2)}) collective-permute-start(f32[64,512]{1,0:T(8,128)S(1)} %get-tuple-element.34), channel_id=1, source_target_pairs={{0,8}} | collective-permute-start | bytes 393224 | tf_op jit(solution)/shard_map/ppermute | solution.py:265
  9.9 3.4 %collective-permute-start.7 = (f32[64,512]{1,0:T(8,128)S(1)}, f32[64,512]{1,0:T(8,128)S(1)}, u32[]{:S(2)}, u32[]{:S(2)}) collective-permute-start(f32[64,512]{1,0:T(8,128)S(1)} %get-tuple-element.35), channel_id=1, source_target_pairs={{0,12}} | collective-permute-start | bytes 393224 | tf_op jit(solution)/shard_map/ppermute | solution.py:265
  10.6 2.8 collective-permute-start.6
  11.2 2.1 collective-permute-start.5
  11.9 1.4 collective-permute-start.4
  12.6 0.8 collective-permute-start.3
  15.1 121.2 %all-gather.11.cloned.1.call-start = ((), (), s32[]{:S(2)}) async-start(), calls=%async_computation.2 | async-start | bytes 1310720 | tf_op jit(solution)/shard_map/all_gather | solution.py:272
  17.4 68.0 %collective-permute-start.2 = (f32[256,512]{1,0:T(8,128)}, f32[256,512]{1,0:T(8,128)S(1)}, u32[]{:S(2)}, u32[]{:S(2)}) collective-permute-start(f32[256,512]{1,0:T(8,128)} %get-tuple-element.40), channel_id=1, source_target_pairs={{0,1},{4,5},{8,9},{12,13},{16,17},{20,21},{24,25},{28,29}} | collective-permute-start | bytes 1572872 | tf_op jit(solution)/shard_map/ppermute | solution.py:314
  18.1 67.3 %collective-permute-start.1 = (f32[256,512]{1,0:T(8,128)S(1)}, f32[256,512]{1,0:T(8,128)S(1)}, u32[]{:S(2)}, u32[]{:S(2)}) collective-permute-start(f32[256,512]{1,0:T(8,128)S(1)} %get-tuple-element.41), channel_id=1, source_target_pairs={{0,2},{4,6},{8,10},{12,14},{16,18},{20,22},{24,26},{28,30}} | collective-permute-start | bytes 1572872 | tf_op jit(solution)/shard_map/ppermute | solution.py:314
  66.6 3.1 collective-permute-start.12
  67.2 8.3 %collective-permute-start.11 = (f32[128,512]{1,0:T(8,128)S(1)}, f32[128,512]{1,0:T(8,128)S(1)}, u32[]{:S(2)}, u32[]{:S(2)}) collective-permute-start(f32[128,512]{1,0:T(8,128)S(1)} %get-tuple-element.50), channel_id=1, source_target_pairs={{0,2},{4,6},{8,10},{12,14},{16,18},{20,22},{24,26},{28,30}} | collective-permute-start | bytes 786440 | tf_op jit(solution)/shard_map/ppermute | solution.py:271
  68.5 7.0 %collective-permute-start.10 = (f32[128,512]{1,0:T(8,128)S(1)}, f32[128,512]{1,0:T(8,128)S(1)}, u32[]{:S(2)}, u32[]{:S(2)}) collective-permute-start(f32[128,512]{1,0:T(8,128)S(1)} %get-tuple-element.51), channel_id=1, source_target_pairs={{0,3},{4,7},{8,11},{12,15},{16,19},{20,23},{24,27},{28,31}} | collective-permute-start | bytes 786440 | tf_op jit(solution)/shard_map/ppermute | solution.py:271
  69.7 15.7 %collective-permute-start = (f32[256,512]{1,0:T(8,128)S(1)}, f32[256,512]{1,0:T(8,128)}, u32[]{:S(2)}, u32[]{:S(2)}) collective-permute-start(f32[256,512]{1,0:T(8,128)S(1)} %get-tuple-element.42), channel_id=1, source_target_pairs={{0,3},{4,7},{8,11},{12,15},{16,19},{20,23},{24,27},{28,31}} | collective-permute-start | bytes 1572872 | tf_op jit(solution)/shard_map/ppermute | solution.py:314
  77.3 153.4 %all-gather.7.cloned.1.call-start = ((), (), s32[]{:S(2)}) async-start(), calls=%async_computation | async-start | bytes 2621440 | tf_op jit(solution)/shard_map/all_gather | solution.py:316
  87.5 159.0 %all-gather.13.cloned.1.call-start = ((), (), s32[]{:S(2)}) async-start(), calls=%async_computation.3 | async-start | bytes 6045696 | tf_op jit(solution)/shard_map/all_gather | solution.py:321
  89.0 10.2 %copy-start.9 = (f32[8,128]{1,0:T(8,128)S(1)}, f32[8,128]{1,0:T(8,128)}, u32[]{:S(2)}) copy-start(f32[8,128]{1,0:T(8,128)} %param.12) | copy-start | bytes 12292
  89.0 10.3 %copy-start.4 = (f32[256,512]{1,0:T(8,128)S(1)}, f32[256,512]{1,0:T(8,128)}, u32[]{:S(2)}) copy-start(f32[256,512]{1,0:T(8,128)} %select_select_fusion) | copy-start | bytes 1572868
  99.4 36.0 %collective-permute-start.13 = (f32[328,512]{1,0:T(8,128)S(1)}, f32[328,512]{1,0:T(8,128)S(1)}, u32[]{:S(2)}, u32[]{:S(2)}) collective-permute-start(f32[328,512]{1,0:T(8,128)S(1)} %select_maximum_fusion), channel_id=1, source_target_pairs={{0,0},{1,4},{2,8},{3,12},{4,16},{5,20},{6,24},{7,28},{8,1},{9,5},{... | collective-permute-start | bytes 2015240 | tf_op jit(solution)/shard_map/ppermute | solution.py:320
  139.2 97.2 %collective-permute-start.16 = (f32[8,128,128]{2,1,0:T(8,128)}, f32[8,128,128]{2,1,0:T(8,128)}, u32[]{:S(2)}, u32[]{:S(2)}) collective-permute-start(f32[8,128,128]{2,1,0:T(8,128)} %get-tuple-element.44), channel_id=1, source_target_pairs={{0,3},{1,0},{2,1},{3,2},{4,7},{5,4},{6,5},{7,6},{8,11},{9,8},{10,9... | collective-permute-start | bytes 1572872 | tf_op jit(solution)/shard_map/ppermute | solution.py:288
  153.1 83.3 %collective-permute-start.15 = (f32[8,128,128]{2,1,0:T(8,128)}, f32[8,128,128]{2,1,0:T(8,128)}, u32[]{:S(2)}, u32[]{:S(2)}) collective-permute-start(f32[8,128,128]{2,1,0:T(8,128)} %get-tuple-element.45), channel_id=1, source_target_pairs={{0,2},{1,3},{2,0},{3,1},{4,6},{5,7},{6,4},{7,5},{8,10},{9,11},{10,... | collective-permute-start | bytes 1572872 | tf_op jit(solution)/shard_map/ppermute | solution.py:288
  153.2 83.3 %collective-permute-start.14 = (f32[8,128,128]{2,1,0:T(8,128)}, f32[8,128,128]{2,1,0:T(8,128)}, u32[]{:S(2)}, u32[]{:S(2)}) collective-permute-start(f32[8,128,128]{2,1,0:T(8,128)} %get-tuple-element.46), channel_id=1, source_target_pairs={{0,1},{1,2},{2,3},{3,0},{4,5},{5,6},{6,7},{7,4},{8,9},{9,10},{10,1... | collective-permute-start | bytes 1572872 | tf_op jit(solution)/shard_map/ppermute | solution.py:288
  279.5 20.9 %copy-start.2 = (bf16[2048,512]{1,0:T(8,128)(2,1)S(1)}, bf16[2048,512]{1,0:T(8,128)(2,1)}, u32[]{:S(2)}) copy-start(bf16[2048,512]{1,0:T(8,128)(2,1)} %get-tuple-element.26.refs_2_.refs_5_) | copy-start | bytes 6291460
  (8 other events, 41.6 us)
Sparse Core Ops, SparseCore 0:
  15.2 49.4 all-gather.8
  77.4 17.7 all-gather.10
  97.3 35.0 all-gather.6
  136.4 99.2 all-gather.12

commit v13 on v12

--- a/solution.py
+++ b/solution.py
@@ -30,41 +30,42 @@
 NT = (((1,), (1,)), ((), ()))
 
 
-def leaf_inverse(d):
+def leaf_inverse(d, d_ref, e_ref, x_ref):
     n = d.shape[0]
     sub = lax.broadcasted_iota(jnp.int32, (n, n), 0)
     lane = lax.broadcasted_iota(jnp.int32, (n, n), 1)
     sub_c = lax.broadcasted_iota(jnp.int32, (n, 1), 0)
     lane_r = lax.broadcasted_iota(jnp.int32, (1, n), 1)
-    eye = jnp.where(sub == lane, 1.0, 0.0).astype(jnp.float32)
+    d_ref[...] = d
+    e_ref[...] = jnp.where(sub == lane, 1.0, 0.0).astype(jnp.float32)
+    x_ref[...] = jnp.zeros((n, n), jnp.float32)
 
     def step(k, carry):
-        dm, em, xm = carry
+        dm = d_ref[...]
         colk = jnp.sum(jnp.where(lane == k, dm, 0.0), axis=1, keepdims=True)
-        rowk = jnp.sum(jnp.where(sub == k, dm, 0.0), axis=0, keepdims=True)
+        rowk = d_ref[pl.ds(k, 1), :]
         dkk = jnp.sum(jnp.where(lane_r == k, rowk, 0.0), axis=1, keepdims=True)
         s = lax.rsqrt(dkk)
         lc = jnp.where(sub_c > k, colk * s, 0.0)
         lr = jnp.where(lane_r > k, rowk * s, 0.0)
-        dm = dm - lc * lr
-        erow = jnp.sum(jnp.where(sub == k, em, 0.0), axis=0, keepdims=True)
-        xk = erow * s
-        xm = jnp.where(sub == k, xk, xm)
-        em = em - lc * xk
-        return dm, em, xm
-
-    _, _, xm = lax.fori_loop(0, n, step, (d, eye, jnp.zeros_like(d)), unroll=4)
-    return xm
-
-
-def chol_inv_kernel(a_ref, x_ref, w_ref, l_ref):
+        d_ref[...] = dm - lc * lr
+        xk = e_ref[pl.ds(k, 1), :] * s
+        x_ref[pl.ds(k, 1), :] = xk
+        e_ref[...] = e_ref[...] - lc * xk
+        return carry
+
+    lax.fori_loop(0, n, step, 0, unroll=4)
+    return x_ref[...]
+
+
+def chol_inv_kernel(a_ref, x_ref, w_ref, l_ref, d_ref, e_ref, xl_ref):
     n = a_ref.shape[0]
     nb = n // LEAF
     w_ref[...] = a_ref[...]
     for kb in range(nb):
         o = kb * LEAF
         blk = pl.ds(o, LEAF)
-        xkk = leaf_inverse(w_ref[blk, blk])
+        xkk = leaf_inverse(w_ref[blk, blk], d_ref, e_ref, xl_ref)
         x_ref[blk, blk] = xkk
         if kb + 1 < nb:
             rest = pl.ds(o + LEAF, n - o - LEAF)
@@ -95,7 +96,8 @@
         cost_estimate=pl.CostEstimate(flops=800 * n ** 3, transcendentals=n, bytes_accessed=8 * n * n),
         in_specs=[pl.BlockSpec(memory_space=pltpu.VMEM)],
         out_specs=pl.BlockSpec(memory_space=pltpu.VMEM),
-        scratch_shapes=[pltpu.VMEM((n, n), jnp.float32), pltpu.VMEM((n, n), jnp.float32)],
+        scratch_shapes=[pltpu.VMEM((n, n), jnp.float32), pltpu.VMEM((n, n), jnp.float32)]
+        + [pltpu.VMEM((LEAF, LEAF), jnp.float32)] * 3,
     )(a)
 
 

time: 331 us -> 320 us (0.967)
  Pallas kernels: 131 us -> 122 us
    pallas_call x1, Pallas kernels: 70.2 us -> 59.5 us  [chol_inverse(): pl.pallas_call(chol_inv_kernel, out_shape=jax.ShapeDtypeStruct((n, n), jn...]
  transfers between devices with their start and end apart: 21 -> 21, of which waited for: 3 -> 3; matrix products, arithmetic and copies ran while one was open for 12% -> 13% of each run, Pallas kernels for 24% -> 22%
where the time goes in v13:
time: 320 us; the launch traced here: 316 us
  Pallas kernels  122 us (38%)
  waiting for transfers between devices  76.7 us (24%)
  local copies, waits for them, and re-layouts  41.5 us (13%)
  starting transfers between devices  31.4 us (10%)
  other arithmetic  14.8 us (5%)
  between operations  14.3 us (4%)
  blocking collectives  7.96 us (2%)
  matrix products  7.19 us (2%)
    pallas_call x1, Pallas kernels, chol_inverse(): pl.pallas_call(chol_inv_kernel, out_shape=jax.ShapeDtypeStruct((n, n), jn...  59.5 us
    all_gather x1, waiting for transfers between devices, per_device(): kpp_col0 = lax.all_gather(kpp_part, 'row', axis=0, tiled=True)  45.2 us
    pallas_call x3, Pallas kernels, panel_update(): pl.pallas_call(functools.partial(update_kernel, kind, tm, width, len(base...  40.1 us
    ppermute x1, waiting for transfers between devices, per_device(): b_slice = lax.ppermute(payload, AXES, perm)  27 us
    pallas_call x4, Pallas kernels, apply_inverse(): pl.pallas_call(solve_kernel, grid=(rows // tm,), in_specs=[spec, pl.Block...  22 us
    ppermute x3, starting transfers between devices, per_device(): lax.ppermute(out_k, 'col', [(i, (i + k) % C) for i in range(C)])  14.1 us
    all_gather x1, blocking collectives, per_device(): z_all = lax.all_gather(z_local, 'col', axis=0, tiled=False)  7.96 us
    dot_general x1, matrix products, per_device(): jnp.einsum('sim,sitp->stmp', eigvecs, coupling, preferred_element_type=jn...  7.19 us
  transfers between devices with their start and end apart: 21, of which 3 were waited for; matrix products, arithmetic and copies ran while one was open for 13% of the time, Pallas kernels for 22%

profile of v13, /device:TPU:6, one launch (start us, length us, event | category | flops | bytes accessed | tf_op | source)
XLA Modules:
  0.0 315.6 jit_solution(15915815211119789790)
XLA Ops:
  15.1 2.3 fusion.29
  19.5 45.2 %all-gather.9.cloned.1.call-done = f32[512,512]{1,0:T(8,128)} async-done(((f32[64,512]{1,0:T(8,128)}), f32[512,512]{1,0:T(8,128)}) %all-gather.9.cloned.1.call-update) | async-done | bytes 1048592 | tf_op jit(solution)/shard_map/all_gather | solution.py:269
  71.1 4.4 %collective-permute-done.11 = f32[128,512]{1,0:T(8,128)S(1)} collective-permute-done((f32[128,512]{1,0:T(8,128)S(1)}, f32[128,512]{1,0:T(8,128)S(1)}, u32[]{:S(2)}, u32[]{:S(2)}) %collective-permute-start.11) | collective-permute-done | bytes 262176 | tf_op jit(solution)/shard_map/ppermute | solution.py:273
  77.3 7.2 %fusion.3 = f32[8,2,128,128]{3,2,1,0:T(8,128)S(1)} fusion(bf16[8,2048,128]{2,1,0:T(8,128)(2,1)} %param.8, bf16[8,2048,2,128]{3,2,1,0:T(2,128)(2,1)} %param.9, f32[8,128]{1,0:T(8,128)S(1)} %fusion.16), kind=kOutput, calls=%fused_computation.14 | convolution fusion | flops 1074003968 | bytes 13635584 | tf_op jit(solution)/shard_map/sim,sitp->stmp/dot_general | solution.py:258
  85.4 2.1 select_select_fusion
  89.8 8.0 %all-gather = f32[8,128,128]{2,1,0:T(8,128)S(1)} all-gather(f32[2,128,128]{2,1,0:T(8,128)S(1)} %gather_fusion.1), channel_id=2, replica_groups=mesh['row'=8,'col'=4] {'col'}, dimensions={0}, use_global_device_ids=true | all-gather | bytes 655360 | tf_op jit(solution)/shard_map/all_gather | solution.py:308
  99.4 6.4 %collective-permute-start.13 = (f32[328,512]{1,0:T(8,128)S(1)}, f32[328,512]{1,0:T(8,128)S(1)}, u32[]{:S(2)}, u32[]{:S(2)}) collective-permute-start(f32[328,512]{1,0:T(8,128)S(1)} %select_maximum_fusion), channel_id=1, source_target_pairs={{0,0},{1,4},{2,8},{3,12},{4,16},{5,20},{6,24},{7,28},{8,1},{9,5},{... | collective-permute-start | bytes 2015240 | tf_op jit(solution)/shard_map/ppermute | solution.py:322
  108.4 27.0 %collective-permute-done.13 = f32[328,512]{1,0:T(8,128)S(1)} collective-permute-done((f32[328,512]{1,0:T(8,128)S(1)}, f32[328,512]{1,0:T(8,128)S(1)}, u32[]{:S(2)}, u32[]{:S(2)}) %collective-permute-start.13) | collective-permute-done | bytes 671776 | tf_op jit(solution)/shard_map/ppermute | solution.py:322
  136.3 2.9 constant_dynamic-slice_fusion
  139.2 14.0 %collective-permute-start.16 = (f32[8,128,128]{2,1,0:T(8,128)}, f32[8,128,128]{2,1,0:T(8,128)}, u32[]{:S(2)}, u32[]{:S(2)}) collective-permute-start(f32[8,128,128]{2,1,0:T(8,128)} %get-tuple-element.44), channel_id=1, source_target_pairs={{0,3},{1,0},{2,1},{3,2},{4,7},{5,4},{6,5},{7,6},{8,11},{9,8},{10,9... | collective-permute-start | bytes 1572872 | tf_op jit(solution)/shard_map/ppermute | solution.py:290
  153.3 59.5 %shard_map.85 = f32[512,512]{1,0:T(8,128)} custom-call(f32[512,512]{1,0:T(8,128)} %all-gather.11.cloned.1.call-done.a_ref), custom_call_target="tpu_custom_call" | custom-call | flops 107374182400 | bytes 2097152 | tf_op jit(solution)/shard_map/pallas_call | solution.py:93
  212.8 2.3 fusion.8
  215.2 2.9 shard_map.89
  220.0 5.7 %shard_map.86 = (f32[1024,512]{1,0:T(8,128)}, bf16[1024,512]{1,0:T(8,128)(2,1)}, bf16[1024,512]{1,0:T(8,128)(2,1)}) custom-call(f32[1024,512]{1,0:T(8,128)} %all-gather.7.cloned.1.call-done.x_ref, bf16[512,512]{1,0:T(8,128)(2,1)} %get-tuple-element.48.fhi_ref, bf16[512,512]{1,0:T(8,128)(2,1)} %get-tuple-element.47.flo_ref), custom_call_target="tpu_custom_call" | custom-call | flops 1610612736 | bytes 4194304 | tf_op jit(solution)/shard_map/pallas_call | solution.py:202
  225.8 2.9 pad_maximum_fusion
  228.7 3.6 %gather_fusion.3 = f32[4,8,128,128]{3,2,1,0:T(8,128)} fusion(f32[4,8,128,128]{3,2,1,0:T(8,128)} %pad_maximum_fusion, s32[1024]{0:T(1024)S(1)} %pad_clamp_fusion.2), kind=kCustom, calls=%fused_computation.3 | custom fusion | bytes 4194320 | tf_op jit(solution)/shard_map/gather | solution.py:292
  237.2 2.3 slice.133
  239.5 4.6 %slice.132 = f32[8,256,512]{2,1,0:T(8,128)} slice(f32[8,328,512]{2,1,0:T(8,128)} %bitcast.84), slice={[0:8], [0:256], [0:512]} | slice | bytes 8388608 | tf_op jit(solution)/shard_map/slice | solution.py:324
  244.2 3.6 %shard_map.91 = (f32[512,512]{1,0:T(8,128)}, bf16[512,512]{1,0:T(8,128)(2,1)}, bf16[512,512]{1,0:T(8,128)(2,1)}) custom-call(f32[512,512]{1,0:T(8,128)} %bitcast.92, bf16[512,512]{1,0:T(8,128)(2,1)} %get-tuple-element.48.fhi_ref, bf16[512,512]{1,0:T(8,128)(2,1)} %get-tuple-element.47.flo_ref), custom_call_target="tpu_custom_call" | custom-call | flops 805306368 | bytes 2097152 | tf_op jit(solution)/shard_map/pallas_call | solution.py:202
  250.8 3.1 gather_fusion.5
  256.0 9.7 %shard_map.87 = (f32[2048,512]{1,0:T(8,128)}, bf16[2048,512]{1,0:T(8,128)(2,1)}, bf16[2048,512]{1,0:T(8,128)(2,1)}) custom-call(f32[2048,512]{1,0:T(8,128)} %bitcast.85, bf16[512,512]{1,0:T(8,128)(2,1)} %get-tuple-element.48.fhi_ref, bf16[512,512]{1,0:T(8,128)(2,1)} %get-tuple-element.47.flo_ref), custom_call_target="tpu_custom_call" | custom-call | flops 3221225472 | bytes 8388608 | tf_op jit(solution)/shard_map/pallas_call | solution.py:202
  268.9 20.9 %shard_map.88 = f32[1024,2048]{1,0:T(8,128)} custom-call(s32[8]{0:T(128)S(1)} %broadcast_31_flags_ref.2.flags_ref, s32[4]{0:T(128)S(1)} %get-tuple-element.61.info_ref, s32[1]{0:T(128)} %constant.134.clone.1.slots_ref, f32[1024,2048]{1,0:T(8,128)} %refs_0_.1, f32[1024,512]{1,0:T(8,128)S(1)} %copy-done.3, bf16[2048,512]{1,0:T(8,128)(2,1)S(1)} %copy-done.1, ...), custom_call_target="tpu_custom_call" | custom-call | flops 6442450944 | bytes 20971520 | tf_op jit(solution)/shard_map/pallas_call | solution.py:175
  289.8 10.3 %shard_map.90 = f32[1024,2048]{1,0:T(8,128)} custom-call(s32[8]{0:T(128)S(1)} %get-tuple-element.58.flags_ref, s32[4]{0:T(128)S(1)} %get-tuple-element.61.info_ref, s32[32]{0:T(128)S(1)} %select_n.302.slots_ref, f32[9,128,512]{2,1,0:T(8,128)} %concatenate.48.refs_0_.refs_1_.refs_2_.refs_3_, f32[9,128,512]{2,1,0:T(8,128)} %concatenate.48.refs_0_.refs_1_.refs_2_.refs_3_, ...), custom_call_target="tpu_custom_call" | custom-call | flops 6442450944 | bytes 20971520 | tf_op jit(solution)/shard_map/pallas_call | solution.py:175
  300.1 9.0 %shard_map.92 = f32[1024,2048]{1,0:T(8,128)} custom-call(s32[8]{0:T(128)S(1)} %get-tuple-element.58.flags_ref, s32[4]{0:T(128)S(1)} %get-tuple-element.60.info_ref, s32[1]{0:T(128)} %constant.134.clone.1.slots_ref, f32[1024,1]{1,0:T(8,128)S(1)} %copy.42.refs_0_, f32[1024,512]{1,0:T(8,128)S(1)} %bitcast.78, bf16[2048,512]{1,0:T(8,128)(2,1)S(1)} %bitcast.79, ...), custom_call_target="tpu_custom_call" | custom-call | flops 6442450944 | bytes 20971520 | tf_op jit(solution)/shard_map/pallas_call | solution.py:175
  (127 shorter events, 41.5 us)
Async XLA Ops:
  7.2 57.5 %all-gather.9.cloned.1.call-start = ((), (), s32[]{:S(2)}) async-start(), calls=%async_computation.1 | async-start | bytes 1179648 | tf_op jit(solution)/shard_map/all_gather | solution.py:269
  8.5 3.4 %collective-permute-start.9 = (f32[64,512]{1,0:T(8,128)S(1)}, f32[64,512]{1,0:T(8,128)S(1)}, u32[]{:S(2)}, u32[]{:S(2)}) collective-permute-start(f32[64,512]{1,0:T(8,128)S(1)} %get-tuple-element.33), channel_id=1, source_target_pairs={{0,4}} | collective-permute-start | bytes 393224 | tf_op jit(solution)/shard_map/ppermute | solution.py:267
  9.2 3.4 %collective-permute-start.8 = (f32[64,512]{1,0:T(8,128)S(1)}, f32[64,512]{1,0:T(8,128)S(1)}, u32[]{:S(2)}, u32[]{:S(2)}) collective-permute-start(f32[64,512]{1,0:T(8,128)S(1)} %get-tuple-element.34), channel_id=1, source_target_pairs={{0,8}} | collective-permute-start | bytes 393224 | tf_op jit(solution)/shard_map/ppermute | solution.py:267
  9.9 3.4 %collective-permute-start.7 = (f32[64,512]{1,0:T(8,128)S(1)}, f32[64,512]{1,0:T(8,128)S(1)}, u32[]{:S(2)}, u32[]{:S(2)}) collective-permute-start(f32[64,512]{1,0:T(8,128)S(1)} %get-tuple-element.35), channel_id=1, source_target_pairs={{0,12}} | collective-permute-start | bytes 393224 | tf_op jit(solution)/shard_map/ppermute | solution.py:267
  10.6 2.8 collective-permute-start.6
  11.2 2.1 collective-permute-start.5
  11.9 1.4 collective-permute-start.4
  12.6 0.8 collective-permute-start.3
  15.1 121.2 %all-gather.11.cloned.1.call-start = ((), (), s32[]{:S(2)}) async-start(), calls=%async_computation.2 | async-start | bytes 1310720 | tf_op jit(solution)/shard_map/all_gather | solution.py:274
  17.4 68.0 %collective-permute-start.2 = (f32[256,512]{1,0:T(8,128)}, f32[256,512]{1,0:T(8,128)S(1)}, u32[]{:S(2)}, u32[]{:S(2)}) collective-permute-start(f32[256,512]{1,0:T(8,128)} %get-tuple-element.40), channel_id=1, source_target_pairs={{0,1},{4,5},{8,9},{12,13},{16,17},{20,21},{24,25},{28,29}} | collective-permute-start | bytes 1572872 | tf_op jit(solution)/shard_map/ppermute | solution.py:316
  18.1 67.3 %collective-permute-start.1 = (f32[256,512]{1,0:T(8,128)S(1)}, f32[256,512]{1,0:T(8,128)S(1)}, u32[]{:S(2)}, u32[]{:S(2)}) collective-permute-start(f32[256,512]{1,0:T(8,128)S(1)} %get-tuple-element.41), channel_id=1, source_target_pairs={{0,2},{4,6},{8,10},{12,14},{16,18},{20,22},{24,26},{28,30}} | collective-permute-start | bytes 1572872 | tf_op jit(solution)/shard_map/ppermute | solution.py:316
  66.6 3.1 collective-permute-start.12
  67.2 8.3 %collective-permute-start.11 = (f32[128,512]{1,0:T(8,128)S(1)}, f32[128,512]{1,0:T(8,128)S(1)}, u32[]{:S(2)}, u32[]{:S(2)}) collective-permute-start(f32[128,512]{1,0:T(8,128)S(1)} %get-tuple-element.50), channel_id=1, source_target_pairs={{0,2},{4,6},{8,10},{12,14},{16,18},{20,22},{24,26},{28,30}} | collective-permute-start | bytes 786440 | tf_op jit(solution)/shard_map/ppermute | solution.py:273
  68.5 7.0 %collective-permute-start.10 = (f32[128,512]{1,0:T(8,128)S(1)}, f32[128,512]{1,0:T(8,128)S(1)}, u32[]{:S(2)}, u32[]{:S(2)}) collective-permute-start(f32[128,512]{1,0:T(8,128)S(1)} %get-tuple-element.51), channel_id=1, source_target_pairs={{0,3},{4,7},{8,11},{12,15},{16,19},{20,23},{24,27},{28,31}} | collective-permute-start | bytes 786440 | tf_op jit(solution)/shard_map/ppermute | solution.py:273
  69.7 15.7 %collective-permute-start = (f32[256,512]{1,0:T(8,128)S(1)}, f32[256,512]{1,0:T(8,128)}, u32[]{:S(2)}, u32[]{:S(2)}) collective-permute-start(f32[256,512]{1,0:T(8,128)S(1)} %get-tuple-element.42), channel_id=1, source_target_pairs={{0,3},{4,7},{8,11},{12,15},{16,19},{20,23},{24,27},{28,31}} | collective-permute-start | bytes 1572872 | tf_op jit(solution)/shard_map/ppermute | solution.py:316
  77.3 142.7 %all-gather.7.cloned.1.call-start = ((), (), s32[]{:S(2)}) async-start(), calls=%async_computation | async-start | bytes 2621440 | tf_op jit(solution)/shard_map/all_gather | solution.py:318
  87.5 148.3 %all-gather.13.cloned.1.call-start = ((), (), s32[]{:S(2)}) async-start(), calls=%async_computation.3 | async-start | bytes 6045696 | tf_op jit(solution)/shard_map/all_gather | solution.py:323
  89.0 10.3 %copy-start.4 = (f32[256,512]{1,0:T(8,128)S(1)}, f32[256,512]{1,0:T(8,128)}, u32[]{:S(2)}) copy-start(f32[256,512]{1,0:T(8,128)} %select_select_fusion) | copy-start | bytes 1572868
  99.4 36.0 %collective-permute-start.13 = (f32[328,512]{1,0:T(8,128)S(1)}, f32[328,512]{1,0:T(8,128)S(1)}, u32[]{:S(2)}, u32[]{:S(2)}) collective-permute-start(f32[328,512]{1,0:T(8,128)S(1)} %select_maximum_fusion), channel_id=1, source_target_pairs={{0,0},{1,4},{2,8},{3,12},{4,16},{5,20},{6,24},{7,28},{8,1},{9,5},{... | collective-permute-start | bytes 2015240 | tf_op jit(solution)/shard_map/ppermute | solution.py:322
  139.2 86.6 %collective-permute-start.16 = (f32[8,128,128]{2,1,0:T(8,128)}, f32[8,128,128]{2,1,0:T(8,128)}, u32[]{:S(2)}, u32[]{:S(2)}) collective-permute-start(f32[8,128,128]{2,1,0:T(8,128)} %get-tuple-element.44), channel_id=1, source_target_pairs={{0,3},{1,0},{2,1},{3,2},{4,7},{5,4},{6,5},{7,6},{8,11},{9,8},{10,9... | collective-permute-start | bytes 1572872 | tf_op jit(solution)/shard_map/ppermute | solution.py:290
  153.1 72.6 %collective-permute-start.15 = (f32[8,128,128]{2,1,0:T(8,128)}, f32[8,128,128]{2,1,0:T(8,128)}, u32[]{:S(2)}, u32[]{:S(2)}) collective-permute-start(f32[8,128,128]{2,1,0:T(8,128)} %get-tuple-element.45), channel_id=1, source_target_pairs={{0,2},{1,3},{2,0},{3,1},{4,6},{5,7},{6,4},{7,5},{8,10},{9,11},{10,... | collective-permute-start | bytes 1572872 | tf_op jit(solution)/shard_map/ppermute | solution.py:290
  153.2 72.6 %collective-permute-start.14 = (f32[8,128,128]{2,1,0:T(8,128)}, f32[8,128,128]{2,1,0:T(8,128)}, u32[]{:S(2)}, u32[]{:S(2)}) collective-permute-start(f32[8,128,128]{2,1,0:T(8,128)} %get-tuple-element.46), channel_id=1, source_target_pairs={{0,1},{1,2},{2,3},{3,0},{4,5},{5,6},{6,7},{7,4},{8,9},{9,10},{10,1... | collective-permute-start | bytes 1572872 | tf_op jit(solution)/shard_map/ppermute | solution.py:290
  268.9 20.9 %copy-start.2 = (bf16[2048,512]{1,0:T(8,128)(2,1)S(1)}, bf16[2048,512]{1,0:T(8,128)(2,1)}, u32[]{:S(2)}) copy-start(bf16[2048,512]{1,0:T(8,128)(2,1)} %get-tuple-element.26.refs_2_.refs_5_) | copy-start | bytes 6291460
  289.8 10.3 %copy-start = (bf16[16,128,512]{2,1,0:T(8,128)(2,1)S(1)}, bf16[16,128,512]{2,1,0:T(8,128)(2,1)}, u32[]{:S(2)}) copy-start(bf16[16,128,512]{2,1,0:T(8,128)(2,1)} %gather_fusion.5) | copy-start | bytes 6291460
  (8 other events, 42.3 us)
Sparse Core Ops, SparseCore 0:
  15.2 49.4 all-gather.8
  77.4 17.7 all-gather.10
  97.3 35.0 all-gather.6
  136.4 99.3 all-gather.12

commit v14 on v13

--- a/solution.py
+++ b/solution.py
@@ -54,7 +54,7 @@
         e_ref[...] = e_ref[...] - lc * xk
         return carry
 
-    lax.fori_loop(0, n, step, 0, unroll=4)
+    lax.fori_loop(0, n, step, 0, unroll=8)
     return x_ref[...]
 
 

time: 320 us -> 322 us (level)
  no operation moved by 1% of the time
where the time goes in v14:
time: 322 us; the launch traced here: 316 us
  Pallas kernels  122 us (38%)
  waiting for transfers between devices  76.7 us (24%)
  local copies, waits for them, and re-layouts  41.5 us (13%)
  starting transfers between devices  31.4 us (10%)
  other arithmetic  14.8 us (5%)
  between operations  14.3 us (4%)
  blocking collectives  7.96 us (2%)
  matrix products  7.19 us (2%)
    pallas_call x1, Pallas kernels, chol_inverse(): pl.pallas_call(chol_inv_kernel, out_shape=jax.ShapeDtypeStruct((n, n), jn...  59.8 us
    all_gather x1, waiting for transfers between devices, per_device(): kpp_col0 = lax.all_gather(kpp_part, 'row', axis=0, tiled=True)  45.2 us
    pallas_call x3, Pallas kernels, panel_update(): pl.pallas_call(functools.partial(update_kernel, kind, tm, width, len(base...  40.4 us
    ppermute x1, waiting for transfers between devices, per_device(): b_slice = lax.ppermute(payload, AXES, perm)  27 us
    pallas_call x4, Pallas kernels, apply_inverse(): pl.pallas_call(solve_kernel, grid=(rows // tm,), in_specs=[spec, pl.Block...  22 us
    ppermute x3, starting transfers between devices, per_device(): lax.ppermute(out_k, 'col', [(i, (i + k) % C) for i in range(C)])  14.1 us
    all_gather x1, blocking collectives, per_device(): z_all = lax.all_gather(z_local, 'col', axis=0, tiled=False)  7.96 us
    dot_general x1, matrix products, per_device(): jnp.einsum('sim,sitp->stmp', eigvecs, coupling, preferred_element_type=jn...  7.19 us
  transfers between devices with their start and end apart: 21, of which 3 were waited for; matrix products, arithmetic and copies ran while one was open for 13% of the time, Pallas kernels for 22%

profile of v14, /device:TPU:6, one launch (start us, length us, event | category | flops | bytes accessed | tf_op | source)
XLA Modules:
  0.0 316.0 jit_solution(17980004121539165958)
XLA Ops:
  15.1 2.3 fusion.29
  19.5 45.2 %all-gather.9.cloned.1.call-done = f32[512,512]{1,0:T(8,128)} async-done(((f32[64,512]{1,0:T(8,128)}), f32[512,512]{1,0:T(8,128)}) %all-gather.9.cloned.1.call-update) | async-done | bytes 1048592 | tf_op jit(solution)/shard_map/all_gather | solution.py:269
  71.1 4.4 %collective-permute-done.11 = f32[128,512]{1,0:T(8,128)S(1)} collective-permute-done((f32[128,512]{1,0:T(8,128)S(1)}, f32[128,512]{1,0:T(8,128)S(1)}, u32[]{:S(2)}, u32[]{:S(2)}) %collective-permute-start.11) | collective-permute-done | bytes 262176 | tf_op jit(solution)/shard_map/ppermute | solution.py:273
  77.3 7.2 %fusion.3 = f32[8,2,128,128]{3,2,1,0:T(8,128)S(1)} fusion(bf16[8,2048,128]{2,1,0:T(8,128)(2,1)} %param.8, bf16[8,2048,2,128]{3,2,1,0:T(2,128)(2,1)} %param.9, f32[8,128]{1,0:T(8,128)S(1)} %fusion.16), kind=kOutput, calls=%fused_computation.14 | convolution fusion | flops 1074003968 | bytes 13635584 | tf_op jit(solution)/shard_map/sim,sitp->stmp/dot_general | solution.py:258
  85.4 2.1 select_select_fusion
  89.8 8.0 %all-gather = f32[8,128,128]{2,1,0:T(8,128)S(1)} all-gather(f32[2,128,128]{2,1,0:T(8,128)S(1)} %gather_fusion.1), channel_id=2, replica_groups=mesh['row'=8,'col'=4] {'col'}, dimensions={0}, use_global_device_ids=true | all-gather | bytes 655360 | tf_op jit(solution)/shard_map/all_gather | solution.py:308
  99.4 6.4 %collective-permute-start.13 = (f32[328,512]{1,0:T(8,128)S(1)}, f32[328,512]{1,0:T(8,128)S(1)}, u32[]{:S(2)}, u32[]{:S(2)}) collective-permute-start(f32[328,512]{1,0:T(8,128)S(1)} %select_maximum_fusion), channel_id=1, source_target_pairs={{0,0},{1,4},{2,8},{3,12},{4,16},{5,20},{6,24},{7,28},{8,1},{9,5},{... | collective-permute-start | bytes 2015240 | tf_op jit(solution)/shard_map/ppermute | solution.py:322
  108.4 27.0 %collective-permute-done.13 = f32[328,512]{1,0:T(8,128)S(1)} collective-permute-done((f32[328,512]{1,0:T(8,128)S(1)}, f32[328,512]{1,0:T(8,128)S(1)}, u32[]{:S(2)}, u32[]{:S(2)}) %collective-permute-start.13) | collective-permute-done | bytes 671776 | tf_op jit(solution)/shard_map/ppermute | solution.py:322
  136.3 2.9 constant_dynamic-slice_fusion
  139.2 14.0 %collective-permute-start.16 = (f32[8,128,128]{2,1,0:T(8,128)}, f32[8,128,128]{2,1,0:T(8,128)}, u32[]{:S(2)}, u32[]{:S(2)}) collective-permute-start(f32[8,128,128]{2,1,0:T(8,128)} %get-tuple-element.44), channel_id=1, source_target_pairs={{0,3},{1,0},{2,1},{3,2},{4,7},{5,4},{6,5},{7,6},{8,11},{9,8},{10,9... | collective-permute-start | bytes 1572872 | tf_op jit(solution)/shard_map/ppermute | solution.py:290
  153.3 59.8 %shard_map.85 = f32[512,512]{1,0:T(8,128)} custom-call(f32[512,512]{1,0:T(8,128)} %all-gather.11.cloned.1.call-done.a_ref), custom_call_target="tpu_custom_call" | custom-call | flops 107374182400 | bytes 2097152 | tf_op jit(solution)/shard_map/pallas_call | solution.py:93
  213.1 2.3 fusion.8
  215.4 2.9 shard_map.89
  220.3 5.7 %shard_map.86 = (f32[1024,512]{1,0:T(8,128)}, bf16[1024,512]{1,0:T(8,128)(2,1)}, bf16[1024,512]{1,0:T(8,128)(2,1)}) custom-call(f32[1024,512]{1,0:T(8,128)} %all-gather.7.cloned.1.call-done.x_ref, bf16[512,512]{1,0:T(8,128)(2,1)} %get-tuple-element.48.fhi_ref, bf16[512,512]{1,0:T(8,128)(2,1)} %get-tuple-element.47.flo_ref), custom_call_target="tpu_custom_call" | custom-call | flops 1610612736 | bytes 4194304 | tf_op jit(solution)/shard_map/pallas_call | solution.py:202
  226.0 2.9 pad_maximum_fusion
  228.9 3.6 %gather_fusion.3 = f32[4,8,128,128]{3,2,1,0:T(8,128)} fusion(f32[4,8,128,128]{3,2,1,0:T(8,128)} %pad_maximum_fusion, s32[1024]{0:T(1024)S(1)} %pad_clamp_fusion.2), kind=kCustom, calls=%fused_computation.3 | custom fusion | bytes 4194320 | tf_op jit(solution)/shard_map/gather | solution.py:292
  237.5 2.3 slice.133
  239.7 4.6 %slice.132 = f32[8,256,512]{2,1,0:T(8,128)} slice(f32[8,328,512]{2,1,0:T(8,128)} %bitcast.84), slice={[0:8], [0:256], [0:512]} | slice | bytes 8388608 | tf_op jit(solution)/shard_map/slice | solution.py:324
  244.5 3.6 %shard_map.91 = (f32[512,512]{1,0:T(8,128)}, bf16[512,512]{1,0:T(8,128)(2,1)}, bf16[512,512]{1,0:T(8,128)(2,1)}) custom-call(f32[512,512]{1,0:T(8,128)} %bitcast.92, bf16[512,512]{1,0:T(8,128)(2,1)} %get-tuple-element.48.fhi_ref, bf16[512,512]{1,0:T(8,128)(2,1)} %get-tuple-element.47.flo_ref), custom_call_target="tpu_custom_call" | custom-call | flops 805306368 | bytes 2097152 | tf_op jit(solution)/shard_map/pallas_call | solution.py:202
  251.1 3.1 gather_fusion.5
  256.2 9.7 %shard_map.87 = (f32[2048,512]{1,0:T(8,128)}, bf16[2048,512]{1,0:T(8,128)(2,1)}, bf16[2048,512]{1,0:T(8,128)(2,1)}) custom-call(f32[2048,512]{1,0:T(8,128)} %bitcast.85, bf16[512,512]{1,0:T(8,128)(2,1)} %get-tuple-element.48.fhi_ref, bf16[512,512]{1,0:T(8,128)(2,1)} %get-tuple-element.47.flo_ref), custom_call_target="tpu_custom_call" | custom-call | flops 3221225472 | bytes 8388608 | tf_op jit(solution)/shard_map/pallas_call | solution.py:202
  269.1 20.9 %shard_map.88 = f32[1024,2048]{1,0:T(8,128)} custom-call(s32[8]{0:T(128)S(1)} %broadcast_31_flags_ref.2.flags_ref, s32[4]{0:T(128)S(1)} %get-tuple-element.61.info_ref, s32[1]{0:T(128)} %constant.134.clone.1.slots_ref, f32[1024,2048]{1,0:T(8,128)} %refs_0_.1, f32[1024,512]{1,0:T(8,128)S(1)} %copy-done.3, bf16[2048,512]{1,0:T(8,128)(2,1)S(1)} %copy-done.1, ...), custom_call_target="tpu_custom_call" | custom-call | flops 6442450944 | bytes 20971520 | tf_op jit(solution)/shard_map/pallas_call | solution.py:175
  290.1 10.5 %shard_map.90 = f32[1024,2048]{1,0:T(8,128)} custom-call(s32[8]{0:T(128)S(1)} %get-tuple-element.58.flags_ref, s32[4]{0:T(128)S(1)} %get-tuple-element.61.info_ref, s32[32]{0:T(128)S(1)} %select_n.302.slots_ref, f32[9,128,512]{2,1,0:T(8,128)} %concatenate.48.refs_0_.refs_1_.refs_2_.refs_3_, f32[9,128,512]{2,1,0:T(8,128)} %concatenate.48.refs_0_.refs_1_.refs_2_.refs_3_, ...), custom_call_target="tpu_custom_call" | custom-call | flops 6442450944 | bytes 20971520 | tf_op jit(solution)/shard_map/pallas_call | solution.py:175
  300.5 9.0 %shard_map.92 = f32[1024,2048]{1,0:T(8,128)} custom-call(s32[8]{0:T(128)S(1)} %get-tuple-element.58.flags_ref, s32[4]{0:T(128)S(1)} %get-tuple-element.60.info_ref, s32[1]{0:T(128)} %constant.134.clone.1.slots_ref, f32[1024,1]{1,0:T(8,128)S(1)} %copy.42.refs_0_, f32[1024,512]{1,0:T(8,128)S(1)} %bitcast.78, bf16[2048,512]{1,0:T(8,128)(2,1)S(1)} %bitcast.79, ...), custom_call_target="tpu_custom_call" | custom-call | flops 6442450944 | bytes 20971520 | tf_op jit(solution)/shard_map/pallas_call | solution.py:175
  (127 shorter events, 41.5 us)
Async XLA Ops:
  7.2 57.5 %all-gather.9.cloned.1.call-start = ((), (), s32[]{:S(2)}) async-start(), calls=%async_computation.1 | async-start | bytes 1179648 | tf_op jit(solution)/shard_map/all_gather | solution.py:269
  8.5 3.4 %collective-permute-start.9 = (f32[64,512]{1,0:T(8,128)S(1)}, f32[64,512]{1,0:T(8,128)S(1)}, u32[]{:S(2)}, u32[]{:S(2)}) collective-permute-start(f32[64,512]{1,0:T(8,128)S(1)} %get-tuple-element.33), channel_id=1, source_target_pairs={{0,4}} | collective-permute-start | bytes 393224 | tf_op jit(solution)/shard_map/ppermute | solution.py:267
  9.2 3.4 %collective-permute-start.8 = (f32[64,512]{1,0:T(8,128)S(1)}, f32[64,512]{1,0:T(8,128)S(1)}, u32[]{:S(2)}, u32[]{:S(2)}) collective-permute-start(f32[64,512]{1,0:T(8,128)S(1)} %get-tuple-element.34), channel_id=1, source_target_pairs={{0,8}} | collective-permute-start | bytes 393224 | tf_op jit(solution)/shard_map/ppermute | solution.py:267
  9.9 3.4 %collective-permute-start.7 = (f32[64,512]{1,0:T(8,128)S(1)}, f32[64,512]{1,0:T(8,128)S(1)}, u32[]{:S(2)}, u32[]{:S(2)}) collective-permute-start(f32[64,512]{1,0:T(8,128)S(1)} %get-tuple-element.35), channel_id=1, source_target_pairs={{0,12}} | collective-permute-start | bytes 393224 | tf_op jit(solution)/shard_map/ppermute | solution.py:267
  10.6 2.8 collective-permute-start.6
  11.2 2.1 collective-permute-start.5
  11.9 1.4 collective-permute-start.4
  12.6 0.8 collective-permute-start.3
  15.1 121.2 %all-gather.11.cloned.1.call-start = ((), (), s32[]{:S(2)}) async-start(), calls=%async_computation.2 | async-start | bytes 1310720 | tf_op jit(solution)/shard_map/all_gather | solution.py:274
  17.4 68.0 %collective-permute-start.2 = (f32[256,512]{1,0:T(8,128)}, f32[256,512]{1,0:T(8,128)S(1)}, u32[]{:S(2)}, u32[]{:S(2)}) collective-permute-start(f32[256,512]{1,0:T(8,128)} %get-tuple-element.40), channel_id=1, source_target_pairs={{0,1},{4,5},{8,9},{12,13},{16,17},{20,21},{24,25},{28,29}} | collective-permute-start | bytes 1572872 | tf_op jit(solution)/shard_map/ppermute | solution.py:316
  18.1 67.3 %collective-permute-start.1 = (f32[256,512]{1,0:T(8,128)S(1)}, f32[256,512]{1,0:T(8,128)S(1)}, u32[]{:S(2)}, u32[]{:S(2)}) collective-permute-start(f32[256,512]{1,0:T(8,128)S(1)} %get-tuple-element.41), channel_id=1, source_target_pairs={{0,2},{4,6},{8,10},{12,14},{16,18},{20,22},{24,26},{28,30}} | collective-permute-start | bytes 1572872 | tf_op jit(solution)/shard_map/ppermute | solution.py:316
  66.6 3.1 collective-permute-start.12
  67.2 8.3 %collective-permute-start.11 = (f32[128,512]{1,0:T(8,128)S(1)}, f32[128,512]{1,0:T(8,128)S(1)}, u32[]{:S(2)}, u32[]{:S(2)}) collective-permute-start(f32[128,512]{1,0:T(8,128)S(1)} %get-tuple-element.50), channel_id=1, source_target_pairs={{0,2},{4,6},{8,10},{12,14},{16,18},{20,22},{24,26},{28,30}} | collective-permute-start | bytes 786440 | tf_op jit(solution)/shard_map/ppermute | solution.py:273
  68.5 7.0 %collective-permute-start.10 = (f32[128,512]{1,0:T(8,128)S(1)}, f32[128,512]{1,0:T(8,128)S(1)}, u32[]{:S(2)}, u32[]{:S(2)}) collective-permute-start(f32[128,512]{1,0:T(8,128)S(1)} %get-tuple-element.51), channel_id=1, source_target_pairs={{0,3},{4,7},{8,11},{12,15},{16,19},{20,23},{24,27},{28,31}} | collective-permute-start | bytes 786440 | tf_op jit(solution)/shard_map/ppermute | solution.py:273
  69.7 15.7 %collective-permute-start = (f32[256,512]{1,0:T(8,128)S(1)}, f32[256,512]{1,0:T(8,128)}, u32[]{:S(2)}, u32[]{:S(2)}) collective-permute-start(f32[256,512]{1,0:T(8,128)S(1)} %get-tuple-element.42), channel_id=1, source_target_pairs={{0,3},{4,7},{8,11},{12,15},{16,19},{20,23},{24,27},{28,31}} | collective-permute-start | bytes 1572872 | tf_op jit(solution)/shard_map/ppermute | solution.py:316
  77.3 143.0 %all-gather.7.cloned.1.call-start = ((), (), s32[]{:S(2)}) async-start(), calls=%async_computation | async-start | bytes 2621440 | tf_op jit(solution)/shard_map/all_gather | solution.py:318
  87.5 148.6 %all-gather.13.cloned.1.call-start = ((), (), s32[]{:S(2)}) async-start(), calls=%async_computation.3 | async-start | bytes 6045696 | tf_op jit(solution)/shard_map/all_gather | solution.py:323
  89.0 10.3 %copy-start.4 = (f32[256,512]{1,0:T(8,128)S(1)}, f32[256,512]{1,0:T(8,128)}, u32[]{:S(2)}) copy-start(f32[256,512]{1,0:T(8,128)} %select_select_fusion) | copy-start | bytes 1572868
  99.4 36.0 %collective-permute-start.13 = (f32[328,512]{1,0:T(8,128)S(1)}, f32[328,512]{1,0:T(8,128)S(1)}, u32[]{:S(2)}, u32[]{:S(2)}) collective-permute-start(f32[328,512]{1,0:T(8,128)S(1)} %select_maximum_fusion), channel_id=1, source_target_pairs={{0,0},{1,4},{2,8},{3,12},{4,16},{5,20},{6,24},{7,28},{8,1},{9,5},{... | collective-permute-start | bytes 2015240 | tf_op jit(solution)/shard_map/ppermute | solution.py:322
  139.2 86.8 %collective-permute-start.16 = (f32[8,128,128]{2,1,0:T(8,128)}, f32[8,128,128]{2,1,0:T(8,128)}, u32[]{:S(2)}, u32[]{:S(2)}) collective-permute-start(f32[8,128,128]{2,1,0:T(8,128)} %get-tuple-element.44), channel_id=1, source_target_pairs={{0,3},{1,0},{2,1},{3,2},{4,7},{5,4},{6,5},{7,6},{8,11},{9,8},{10,9... | collective-permute-start | bytes 1572872 | tf_op jit(solution)/shard_map/ppermute | solution.py:290
  153.1 72.8 %collective-permute-start.15 = (f32[8,128,128]{2,1,0:T(8,128)}, f32[8,128,128]{2,1,0:T(8,128)}, u32[]{:S(2)}, u32[]{:S(2)}) collective-permute-start(f32[8,128,128]{2,1,0:T(8,128)} %get-tuple-element.45), channel_id=1, source_target_pairs={{0,2},{1,3},{2,0},{3,1},{4,6},{5,7},{6,4},{7,5},{8,10},{9,11},{10,... | collective-permute-start | bytes 1572872 | tf_op jit(solution)/shard_map/ppermute | solution.py:290
  153.2 72.8 %collective-permute-start.14 = (f32[8,128,128]{2,1,0:T(8,128)}, f32[8,128,128]{2,1,0:T(8,128)}, u32[]{:S(2)}, u32[]{:S(2)}) collective-permute-start(f32[8,128,128]{2,1,0:T(8,128)} %get-tuple-element.46), channel_id=1, source_target_pairs={{0,1},{1,2},{2,3},{3,0},{4,5},{5,6},{6,7},{7,4},{8,9},{9,10},{10,1... | collective-permute-start | bytes 1572872 | tf_op jit(solution)/shard_map/ppermute | solution.py:290
  269.1 20.9 %copy-start.2 = (bf16[2048,512]{1,0:T(8,128)(2,1)S(1)}, bf16[2048,512]{1,0:T(8,128)(2,1)}, u32[]{:S(2)}) copy-start(bf16[2048,512]{1,0:T(8,128)(2,1)} %get-tuple-element.26.refs_2_.refs_5_) | copy-start | bytes 6291460
  290.0 10.5 %copy-start = (bf16[16,128,512]{2,1,0:T(8,128)(2,1)S(1)}, bf16[16,128,512]{2,1,0:T(8,128)(2,1)}, u32[]{:S(2)}) copy-start(bf16[16,128,512]{2,1,0:T(8,128)(2,1)} %gather_fusion.5) | copy-start | bytes 6291460
  (8 other events, 42.4 us)
Sparse Core Ops, SparseCore 0:
  15.2 49.4 all-gather.8
  77.4 17.7 all-gather.10
  97.3 35.0 all-gather.6
  136.4 99.3 all-gather.12

commit v15 on v14

--- a/solution.py
+++ b/solution.py
@@ -195,15 +195,23 @@
     lo_ref[...] = (acc - hi.astype(jnp.float32)).astype(jnp.bfloat16)
 
 
-def apply_inverse(x, f_hi, f_lo):
-    rows = x.shape[0]
-    tm = 256 if rows % 256 == 0 else MSLOT
+def apply_inverse(x, f_hi, f_lo, parts=None):
+    if parts is None:
+        rows = x.shape[0]
+        tm = 256 if rows % 256 == 0 else MSLOT
+        grid = rows // tm
+        x_spec = pl.BlockSpec((tm, PANEL), lambda i: (i, 0))
+    else:
+        tm, at = parts
+        grid = x.shape[0]
+        rows = grid * tm
+        x_spec = pl.BlockSpec((None, tm, PANEL), lambda i: (i, at, 0))
     spec = pl.BlockSpec((tm, PANEL), lambda i: (i, 0))
     return pl.pallas_call(
         solve_kernel,
-        grid=(rows // tm,),
+        grid=(grid,),
         in_specs=[
-            spec,
+            x_spec,
             pl.BlockSpec((PANEL, PANEL), lambda i: (0, 0)),
             pl.BlockSpec((PANEL, PANEL), lambda i: (0, 0)),
         ],
@@ -321,8 +329,6 @@
     perm = [(i * C + k, ((i % ratio) * C + k) * C + i // ratio) for i in range(R) for k in range(C)]
     b_slice = lax.ppermute(payload, AXES, perm)
     col_parts = lax.all_gather(b_slice, "row", axis=0, tiled=False)
-    m_col = col_parts[:, :rps].reshape(W, PANEL)
-    z_col = col_parts[:, rps:rps + zps].reshape(ratio * cap0 * MSLOT, PANEL)
 
     slot_c = []
     for j in range(ratio):
@@ -332,9 +338,9 @@
 
     f_hi, f_lo = split_bf16(finv)
     low_r, _, _ = apply_inverse(m_row, f_hi, f_lo)
-    _, lowc_hi, lowc_lo = apply_inverse(m_col, f_hi, f_lo)
+    _, lowc_hi, lowc_lo = apply_inverse(col_parts, f_hi, f_lo, (rps, 0))
     lowmi_r, _, _ = apply_inverse(z_rows, f_hi, f_lo)
-    _, lmc_hi, lmc_lo = apply_inverse(z_col, f_hi, f_lo)
+    _, lmc_hi, lmc_lo = apply_inverse(col_parts, f_hi, f_lo, (zps, rps // zps))
 
     ones = jnp.ones((H // MSLOT,), jnp.int32)
     none = jnp.zeros((1,), jnp.int32)

time: 322 us -> 321 us (level)
  Pallas kernels: 122 us -> 131 us
  local copies, waits for them, and re-layouts: 41.5 us -> 34.6 us
    slice x2 -> x0, local copies, waits for them, and re-layouts: 6.9 us -> none  [the longest x1 4.64 us: per_device(): m_col = col_parts[:, :rps].reshape(W, PANEL)]
    pallas_call x4, Pallas kernels: 22 us -> 26.5 us  [apply_inverse(): pl.pallas_call(solve_kernel, grid=(grid,), in_specs=[x_spec, pl.BlockSpec...]
    pallas_call x3, Pallas kernels: 40.4 us -> 44.3 us  [panel_update(): pl.pallas_call(functools.partial(update_kernel, kind, tm, width, len(base...]
where the time goes in v15:
time: 321 us; the launch traced here: 318 us
  Pallas kernels  131 us (41%)
  waiting for transfers between devices  76.7 us (24%)
  local copies, waits for them, and re-layouts  34.6 us (11%)
  starting transfers between devices  31.4 us (10%)
  other arithmetic  14.9 us (5%)
  between operations  14.3 us (4%)
  blocking collectives  7.96 us (2%)
  matrix products  7.19 us (2%)
    pallas_call x1, Pallas kernels, chol_inverse(): pl.pallas_call(chol_inv_kernel, out_shape=jax.ShapeDtypeStruct((n, n), jn...  59.8 us
    all_gather x1, waiting for transfers between devices, per_device(): kpp_col0 = lax.all_gather(kpp_part, 'row', axis=0, tiled=True)  45.2 us
    pallas_call x3, Pallas kernels, panel_update(): pl.pallas_call(functools.partial(update_kernel, kind, tm, width, len(base...  44.3 us
    ppermute x1, waiting for transfers between devices, per_device(): b_slice = lax.ppermute(payload, AXES, perm)  27 us
    pallas_call x4, Pallas kernels, apply_inverse(): pl.pallas_call(solve_kernel, grid=(grid,), in_specs=[x_spec, pl.BlockSpec...  26.5 us
    ppermute x3, starting transfers between devices, per_device(): lax.ppermute(out_k, 'col', [(i, (i + k) % C) for i in range(C)])  14.1 us
    all_gather x1, blocking collectives, per_device(): z_all = lax.all_gather(z_local, 'col', axis=0, tiled=False)  7.96 us
    dot_general x1, matrix products, per_device(): jnp.einsum('sim,sitp->stmp', eigvecs, coupling, preferred_element_type=jn...  7.19 us
  transfers between devices with their start and end apart: 21, of which 3 were waited for; matrix products, arithmetic and copies ran while one was open for 13% of the time, Pallas kernels for 22%

profile of v15, /device:TPU:6, one launch (start us, length us, event | category | flops | bytes accessed | tf_op | source)
XLA Modules:
  0.0 317.6 jit_solution(10201280961852667801)
XLA Ops:
  15.1 2.3 fusion.29
  19.5 45.2 %all-gather.9.cloned.1.call-done = f32[512,512]{1,0:T(8,128)} async-done(((f32[64,512]{1,0:T(8,128)}), f32[512,512]{1,0:T(8,128)}) %all-gather.9.cloned.1.call-update) | async-done | bytes 1048592 | tf_op jit(solution)/shard_map/all_gather | solution.py:277
  71.1 4.4 %collective-permute-done.11 = f32[128,512]{1,0:T(8,128)S(1)} collective-permute-done((f32[128,512]{1,0:T(8,128)S(1)}, f32[128,512]{1,0:T(8,128)S(1)}, u32[]{:S(2)}, u32[]{:S(2)}) %collective-permute-start.11) | collective-permute-done | bytes 262176 | tf_op jit(solution)/shard_map/ppermute | solution.py:281
  77.3 7.2 %fusion.3 = f32[8,2,128,128]{3,2,1,0:T(8,128)S(1)} fusion(bf16[8,2048,128]{2,1,0:T(8,128)(2,1)} %param.8, bf16[8,2048,2,128]{3,2,1,0:T(2,128)(2,1)} %param.9, f32[8,128]{1,0:T(8,128)S(1)} %fusion.16), kind=kOutput, calls=%fused_computation.14 | convolution fusion | flops 1074003968 | bytes 13635584 | tf_op jit(solution)/shard_map/sim,sitp->stmp/dot_general | solution.py:266
  85.4 2.0 select_select_fusion
  89.7 8.0 %all-gather = f32[8,128,128]{2,1,0:T(8,128)S(1)} all-gather(f32[2,128,128]{2,1,0:T(8,128)S(1)} %gather_fusion.1), channel_id=2, replica_groups=mesh['row'=8,'col'=4] {'col'}, dimensions={0}, use_global_device_ids=true | all-gather | bytes 655360 | tf_op jit(solution)/shard_map/all_gather | solution.py:316
  99.3 6.4 %collective-permute-start.13 = (f32[328,512]{1,0:T(8,128)S(1)}, f32[328,512]{1,0:T(8,128)S(1)}, u32[]{:S(2)}, u32[]{:S(2)}) collective-permute-start(f32[328,512]{1,0:T(8,128)S(1)} %select_maximum_fusion), channel_id=1, source_target_pairs={{0,0},{1,4},{2,8},{3,12},{4,16},{5,20},{6,24},{7,28},{8,1},{9,5},{... | collective-permute-start | bytes 2015240 | tf_op jit(solution)/shard_map/ppermute | solution.py:330
  106.2 2.0 gather_fusion.2
  108.3 27.0 %collective-permute-done.13 = f32[328,512]{1,0:T(8,128)S(1)} collective-permute-done((f32[328,512]{1,0:T(8,128)S(1)}, f32[328,512]{1,0:T(8,128)S(1)}, u32[]{:S(2)}, u32[]{:S(2)}) %collective-permute-start.13) | collective-permute-done | bytes 671776 | tf_op jit(solution)/shard_map/ppermute | solution.py:330
  136.2 2.9 constant_dynamic-slice_fusion
  139.2 14.0 %collective-permute-start.16 = (f32[8,128,128]{2,1,0:T(8,128)}, f32[8,128,128]{2,1,0:T(8,128)}, u32[]{:S(2)}, u32[]{:S(2)}) collective-permute-start(f32[8,128,128]{2,1,0:T(8,128)} %get-tuple-element.44), channel_id=1, source_target_pairs={{0,3},{1,0},{2,1},{3,2},{4,7},{5,4},{6,5},{7,6},{8,11},{9,8},{10,9... | collective-permute-start | bytes 1572872 | tf_op jit(solution)/shard_map/ppermute | solution.py:298
  153.3 59.8 %shard_map.85 = f32[512,512]{1,0:T(8,128)} custom-call(f32[512,512]{1,0:T(8,128)} %all-gather.11.cloned.1.call-done.a_ref), custom_call_target="tpu_custom_call" | custom-call | flops 107374182400 | bytes 2097152 | tf_op jit(solution)/shard_map/pallas_call | solution.py:93
  213.0 2.4 fusion.8
  215.5 2.9 shard_map.89
  220.3 5.7 %shard_map.86 = (f32[1024,512]{1,0:T(8,128)}, bf16[1024,512]{1,0:T(8,128)(2,1)}, bf16[1024,512]{1,0:T(8,128)(2,1)}) custom-call(f32[1024,512]{1,0:T(8,128)} %all-gather.7.cloned.1.call-done.x_ref, bf16[512,512]{1,0:T(8,128)(2,1)} %get-tuple-element.48.fhi_ref, bf16[512,512]{1,0:T(8,128)(2,1)} %get-tuple-element.47.flo_ref), custom_call_target="tpu_custom_call" | custom-call | flops 1610612736 | bytes 4194304 | tf_op jit(solution)/shard_map/pallas_call | solution.py:210
  226.0 3.0 pad_maximum_fusion
  229.0 3.6 %gather_fusion.3 = f32[4,8,128,128]{3,2,1,0:T(8,128)} fusion(f32[4,8,128,128]{3,2,1,0:T(8,128)} %pad_maximum_fusion, s32[1024]{0:T(1024)S(1)} %pad_clamp_fusion.2), kind=kCustom, calls=%fused_computation.3 | custom fusion | bytes 4194320 | tf_op jit(solution)/shard_map/gather | solution.py:300
  237.5 8.1 %shard_map.91 = (f32[512,512]{1,0:T(8,128)}, bf16[512,512]{1,0:T(8,128)(2,1)}, bf16[512,512]{1,0:T(8,128)(2,1)}) custom-call(f32[8,328,512]{2,1,0:T(8,128)} %bitcast.81, bf16[512,512]{1,0:T(8,128)(2,1)} %get-tuple-element.48.fhi_ref, bf16[512,512]{1,0:T(8,128)(2,1)} %get-tuple-element.47.flo_ref), custom_call_target="tpu_custom_call" | custom-call | flops 805306368 | bytes 2097152 | tf_op jit(solution)/shard_map/pallas_call | solution.py:210
  245.6 9.8 %shard_map.87 = (f32[2048,512]{1,0:T(8,128)}, bf16[2048,512]{1,0:T(8,128)(2,1)}, bf16[2048,512]{1,0:T(8,128)(2,1)}) custom-call(f32[8,328,512]{2,1,0:T(8,128)} %bitcast.82, bf16[512,512]{1,0:T(8,128)(2,1)} %get-tuple-element.48.fhi_ref, bf16[512,512]{1,0:T(8,128)(2,1)} %get-tuple-element.47.flo_ref), custom_call_target="tpu_custom_call" | custom-call | flops 3221225472 | bytes 8388608 | tf_op jit(solution)/shard_map/pallas_call | solution.py:210
  258.4 3.1 gather_fusion.5
  261.5 2.0 gather_fusion.6
  266.7 21.0 %shard_map.88 = f32[1024,2048]{1,0:T(8,128)} custom-call(s32[8]{0:T(128)S(1)} %broadcast_31_flags_ref.2.flags_ref, s32[4]{0:T(128)S(1)} %get-tuple-element.61.info_ref, s32[1]{0:T(128)} %constant.134.clone.1.slots_ref, f32[1024,2048]{1,0:T(8,128)} %refs_0_.1, f32[1024,512]{1,0:T(8,128)S(1)} %copy-done.3, bf16[2048,512]{1,0:T(8,128)(2,1)S(1)} %copy-done.1, ...), custom_call_target="tpu_custom_call" | custom-call | flops 6442450944 | bytes 20971520 | tf_op jit(solution)/shard_map/pallas_call | solution.py:175
  287.7 12.4 %shard_map.90 = f32[1024,2048]{1,0:T(8,128)} custom-call(s32[8]{0:T(128)S(1)} %get-tuple-element.58.flags_ref, s32[4]{0:T(128)S(1)} %get-tuple-element.61.info_ref, s32[32]{0:T(128)S(1)} %select_n.302.slots_ref, f32[9,128,512]{2,1,0:T(8,128)} %concatenate.48.refs_0_.refs_1_.refs_2_.refs_3_, f32[9,128,512]{2,1,0:T(8,128)} %concatenate.48.refs_0_.refs_1_.refs_2_.refs_3_, ...), custom_call_target="tpu_custom_call" | custom-call | flops 6442450944 | bytes 20971520 | tf_op jit(solution)/shard_map/pallas_call | solution.py:175
  300.1 11.0 %shard_map.92 = f32[1024,2048]{1,0:T(8,128)} custom-call(s32[8]{0:T(128)S(1)} %get-tuple-element.58.flags_ref, s32[4]{0:T(128)S(1)} %get-tuple-element.60.info_ref, s32[1]{0:T(128)} %constant.134.clone.1.slots_ref, f32[1024,1]{1,0:T(8,128)S(1)} %copy.42.refs_0_, f32[1024,512]{1,0:T(8,128)S(1)} %bitcast.76, bf16[2048,512]{1,0:T(8,128)(2,1)S(1)} %bitcast.77, ...), custom_call_target="tpu_custom_call" | custom-call | flops 6442450944 | bytes 20971520 | tf_op jit(solution)/shard_map/pallas_call | solution.py:175
  (125 shorter events, 37.4 us)
Async XLA Ops:
  7.2 57.5 %all-gather.9.cloned.1.call-start = ((), (), s32[]{:S(2)}) async-start(), calls=%async_computation.1 | async-start | bytes 1179648 | tf_op jit(solution)/shard_map/all_gather | solution.py:277
  8.5 3.4 %collective-permute-start.9 = (f32[64,512]{1,0:T(8,128)S(1)}, f32[64,512]{1,0:T(8,128)S(1)}, u32[]{:S(2)}, u32[]{:S(2)}) collective-permute-start(f32[64,512]{1,0:T(8,128)S(1)} %get-tuple-element.33), channel_id=1, source_target_pairs={{0,4}} | collective-permute-start | bytes 393224 | tf_op jit(solution)/shard_map/ppermute | solution.py:275
  9.2 3.4 %collective-permute-start.8 = (f32[64,512]{1,0:T(8,128)S(1)}, f32[64,512]{1,0:T(8,128)S(1)}, u32[]{:S(2)}, u32[]{:S(2)}) collective-permute-start(f32[64,512]{1,0:T(8,128)S(1)} %get-tuple-element.34), channel_id=1, source_target_pairs={{0,8}} | collective-permute-start | bytes 393224 | tf_op jit(solution)/shard_map/ppermute | solution.py:275
  9.9 3.4 %collective-permute-start.7 = (f32[64,512]{1,0:T(8,128)S(1)}, f32[64,512]{1,0:T(8,128)S(1)}, u32[]{:S(2)}, u32[]{:S(2)}) collective-permute-start(f32[64,512]{1,0:T(8,128)S(1)} %get-tuple-element.35), channel_id=1, source_target_pairs={{0,12}} | collective-permute-start | bytes 393224 | tf_op jit(solution)/shard_map/ppermute | solution.py:275
  10.6 2.8 collective-permute-start.6
  11.2 2.1 collective-permute-start.5
  11.9 1.4 collective-permute-start.4
  12.6 0.8 collective-permute-start.3
  15.1 121.2 %all-gather.11.cloned.1.call-start = ((), (), s32[]{:S(2)}) async-start(), calls=%async_computation.2 | async-start | bytes 1310720 | tf_op jit(solution)/shard_map/all_gather | solution.py:282
  17.4 68.0 %collective-permute-start.2 = (f32[256,512]{1,0:T(8,128)}, f32[256,512]{1,0:T(8,128)S(1)}, u32[]{:S(2)}, u32[]{:S(2)}) collective-permute-start(f32[256,512]{1,0:T(8,128)} %get-tuple-element.40), channel_id=1, source_target_pairs={{0,1},{4,5},{8,9},{12,13},{16,17},{20,21},{24,25},{28,29}} | collective-permute-start | bytes 1572872 | tf_op jit(solution)/shard_map/ppermute | solution.py:324
  18.1 67.3 %collective-permute-start.1 = (f32[256,512]{1,0:T(8,128)S(1)}, f32[256,512]{1,0:T(8,128)S(1)}, u32[]{:S(2)}, u32[]{:S(2)}) collective-permute-start(f32[256,512]{1,0:T(8,128)S(1)} %get-tuple-element.41), channel_id=1, source_target_pairs={{0,2},{4,6},{8,10},{12,14},{16,18},{20,22},{24,26},{28,30}} | collective-permute-start | bytes 1572872 | tf_op jit(solution)/shard_map/ppermute | solution.py:324
  66.6 3.1 collective-permute-start.12
  67.2 8.3 %collective-permute-start.11 = (f32[128,512]{1,0:T(8,128)S(1)}, f32[128,512]{1,0:T(8,128)S(1)}, u32[]{:S(2)}, u32[]{:S(2)}) collective-permute-start(f32[128,512]{1,0:T(8,128)S(1)} %get-tuple-element.50), channel_id=1, source_target_pairs={{0,2},{4,6},{8,10},{12,14},{16,18},{20,22},{24,26},{28,30}} | collective-permute-start | bytes 786440 | tf_op jit(solution)/shard_map/ppermute | solution.py:281
  68.5 7.0 %collective-permute-start.10 = (f32[128,512]{1,0:T(8,128)S(1)}, f32[128,512]{1,0:T(8,128)S(1)}, u32[]{:S(2)}, u32[]{:S(2)}) collective-permute-start(f32[128,512]{1,0:T(8,128)S(1)} %get-tuple-element.51), channel_id=1, source_target_pairs={{0,3},{4,7},{8,11},{12,15},{16,19},{20,23},{24,27},{28,31}} | collective-permute-start | bytes 786440 | tf_op jit(solution)/shard_map/ppermute | solution.py:281
  69.7 15.7 %collective-permute-start = (f32[256,512]{1,0:T(8,128)S(1)}, f32[256,512]{1,0:T(8,128)}, u32[]{:S(2)}, u32[]{:S(2)}) collective-permute-start(f32[256,512]{1,0:T(8,128)S(1)} %get-tuple-element.42), channel_id=1, source_target_pairs={{0,3},{4,7},{8,11},{12,15},{16,19},{20,23},{24,27},{28,31}} | collective-permute-start | bytes 1572872 | tf_op jit(solution)/shard_map/ppermute | solution.py:324
  77.3 143.0 %all-gather.7.cloned.1.call-start = ((), (), s32[]{:S(2)}) async-start(), calls=%async_computation | async-start | bytes 2621440 | tf_op jit(solution)/shard_map/all_gather | solution.py:326
  87.5 148.7 %all-gather.13.cloned.1.call-start = ((), (), s32[]{:S(2)}) async-start(), calls=%async_computation.3 | async-start | bytes 6045696 | tf_op jit(solution)/shard_map/all_gather | solution.py:331
  89.0 10.3 %copy-start.4 = (f32[256,512]{1,0:T(8,128)S(1)}, f32[256,512]{1,0:T(8,128)}, u32[]{:S(2)}) copy-start(f32[256,512]{1,0:T(8,128)} %select_select_fusion) | copy-start | bytes 1572868
  99.3 36.0 %collective-permute-start.13 = (f32[328,512]{1,0:T(8,128)S(1)}, f32[328,512]{1,0:T(8,128)S(1)}, u32[]{:S(2)}, u32[]{:S(2)}) collective-permute-start(f32[328,512]{1,0:T(8,128)S(1)} %select_maximum_fusion), channel_id=1, source_target_pairs={{0,0},{1,4},{2,8},{3,12},{4,16},{5,20},{6,24},{7,28},{8,1},{9,5},{... | collective-permute-start | bytes 2015240 | tf_op jit(solution)/shard_map/ppermute | solution.py:330
  139.2 86.9 %collective-permute-start.16 = (f32[8,128,128]{2,1,0:T(8,128)}, f32[8,128,128]{2,1,0:T(8,128)}, u32[]{:S(2)}, u32[]{:S(2)}) collective-permute-start(f32[8,128,128]{2,1,0:T(8,128)} %get-tuple-element.44), channel_id=1, source_target_pairs={{0,3},{1,0},{2,1},{3,2},{4,7},{5,4},{6,5},{7,6},{8,11},{9,8},{10,9... | collective-permute-start | bytes 1572872 | tf_op jit(solution)/shard_map/ppermute | solution.py:298
  153.1 72.9 %collective-permute-start.15 = (f32[8,128,128]{2,1,0:T(8,128)}, f32[8,128,128]{2,1,0:T(8,128)}, u32[]{:S(2)}, u32[]{:S(2)}) collective-permute-start(f32[8,128,128]{2,1,0:T(8,128)} %get-tuple-element.45), channel_id=1, source_target_pairs={{0,2},{1,3},{2,0},{3,1},{4,6},{5,7},{6,4},{7,5},{8,10},{9,11},{10,... | collective-permute-start | bytes 1572872 | tf_op jit(solution)/shard_map/ppermute | solution.py:298
  153.1 72.9 %collective-permute-start.14 = (f32[8,128,128]{2,1,0:T(8,128)}, f32[8,128,128]{2,1,0:T(8,128)}, u32[]{:S(2)}, u32[]{:S(2)}) collective-permute-start(f32[8,128,128]{2,1,0:T(8,128)} %get-tuple-element.46), channel_id=1, source_target_pairs={{0,1},{1,2},{2,3},{3,0},{4,5},{5,6},{6,7},{7,4},{8,9},{9,10},{10,1... | collective-permute-start | bytes 1572872 | tf_op jit(solution)/shard_map/ppermute | solution.py:298
  266.7 21.0 %copy-start.2 = (bf16[2048,512]{1,0:T(8,128)(2,1)S(1)}, bf16[2048,512]{1,0:T(8,128)(2,1)}, u32[]{:S(2)}) copy-start(bf16[2048,512]{1,0:T(8,128)(2,1)} %get-tuple-element.26.refs_2_.refs_5_) | copy-start | bytes 6291460
  287.7 12.4 %copy-start = (bf16[16,128,512]{2,1,0:T(8,128)(2,1)S(1)}, bf16[16,128,512]{2,1,0:T(8,128)(2,1)}, u32[]{:S(2)}) copy-start(bf16[16,128,512]{2,1,0:T(8,128)(2,1)} %gather_fusion.5) | copy-start | bytes 6291460
  (8 other events, 42.4 us)
Sparse Core Ops, SparseCore 0:
  15.2 49.4 all-gather.8
  77.4 17.7 all-gather.10
  97.3 34.9 all-gather.6
  136.3 99.3 all-gather.12

commit v16 on v15

--- a/solution.py
+++ b/solution.py
@@ -110,7 +110,10 @@
     base_refs = refs[:nbase]
     a_ref, bhi_ref, blo_ref, out_ref = refs[nbase:]
     i = pl.program_id(0)
-    active = flags_ref[i] != 0
+    per = tm // MSLOT
+    active = flags_ref[i * per] != 0
+    for q in range(1, per):
+        active = jnp.logical_or(active, flags_ref[i * per + q] != 0)
 
     def base_cols(g):
         cols = pl.ds(g * PANEL, PANEL)
@@ -147,7 +150,7 @@
 
 
 def panel_update(kind, base, a, b_hi, b_lo, flags, info, slots, rows, width):
-    tm = MSLOT
+    tm = MSLOT if kind == "gather" or rows % (2 * MSLOT) else 2 * MSLOT
     nseg = width // PANEL
     if kind == "gather":
         bases = [base] * nseg

time: 321 us -> 307 us (0.956)
  Pallas kernels: 131 us -> 117 us
    pallas_call x3, Pallas kernels: 44.3 us -> 30.5 us  [panel_update(): pl.pallas_call(functools.partial(update_kernel, kind, tm, width, len(base...]
  transfers between devices with their start and end apart: 21 -> 21, of which waited for: 3 -> 3; matrix products, arithmetic and copies ran while one was open for 13% -> 13% of each run, Pallas kernels for 22% -> 23%
where the time goes in v16:
time: 307 us; the launch traced here: 304 us
  Pallas kernels  117 us (38%)
  waiting for transfers between devices  76.7 us (25%)
  local copies, waits for them, and re-layouts  34.6 us (11%)
  starting transfers between devices  31.4 us (10%)
  other arithmetic  14.9 us (5%)
  between operations  14.3 us (5%)
  blocking collectives  7.96 us (3%)
  matrix products  7.19 us (2%)
    pallas_call x1, Pallas kernels, chol_inverse(): pl.pallas_call(chol_inv_kernel, out_shape=jax.ShapeDtypeStruct((n, n), jn...  59.8 us
    all_gather x1, waiting for transfers between devices, per_device(): kpp_col0 = lax.all_gather(kpp_part, 'row', axis=0, tiled=True)  45.2 us
    pallas_call x3, Pallas kernels, panel_update(): pl.pallas_call(functools.partial(update_kernel, kind, tm, width, len(base...  30.5 us
    ppermute x1, waiting for transfers between devices, per_device(): b_slice = lax.ppermute(payload, AXES, perm)  27 us
    pallas_call x4, Pallas kernels, apply_inverse(): pl.pallas_call(solve_kernel, grid=(grid,), in_specs=[x_spec, pl.BlockSpec...  26.5 us
    ppermute x3, starting transfers between devices, per_device(): lax.ppermute(out_k, 'col', [(i, (i + k) % C) for i in range(C)])  14.1 us
    all_gather x1, blocking collectives, per_device(): z_all = lax.all_gather(z_local, 'col', axis=0, tiled=False)  7.96 us
    dot_general x1, matrix products, per_device(): jnp.einsum('sim,sitp->stmp', eigvecs, coupling, preferred_element_type=jn...  7.19 us
  transfers between devices with their start and end apart: 21, of which 3 were waited for; matrix products, arithmetic and copies ran while one was open for 13% of the time, Pallas kernels for 23%

profile of v16, /device:TPU:6, one launch (start us, length us, event | category | flops | bytes accessed | tf_op | source)
XLA Modules:
  0.0 303.8 jit_solution(13613526807124594694)
XLA Ops:
  15.1 2.3 fusion.29
  19.5 45.2 %all-gather.9.cloned.1.call-done = f32[512,512]{1,0:T(8,128)} async-done(((f32[64,512]{1,0:T(8,128)}), f32[512,512]{1,0:T(8,128)}) %all-gather.9.cloned.1.call-update) | async-done | bytes 1048592 | tf_op jit(solution)/shard_map/all_gather | solution.py:280
  71.1 4.4 %collective-permute-done.11 = f32[128,512]{1,0:T(8,128)S(1)} collective-permute-done((f32[128,512]{1,0:T(8,128)S(1)}, f32[128,512]{1,0:T(8,128)S(1)}, u32[]{:S(2)}, u32[]{:S(2)}) %collective-permute-start.11) | collective-permute-done | bytes 262176 | tf_op jit(solution)/shard_map/ppermute | solution.py:284
  77.3 7.2 %fusion.3 = f32[8,2,128,128]{3,2,1,0:T(8,128)S(1)} fusion(bf16[8,2048,128]{2,1,0:T(8,128)(2,1)} %param.8, bf16[8,2048,2,128]{3,2,1,0:T(2,128)(2,1)} %param.9, f32[8,128]{1,0:T(8,128)S(1)} %fusion.16), kind=kOutput, calls=%fused_computation.14 | convolution fusion | flops 1074003968 | bytes 13635584 | tf_op jit(solution)/shard_map/sim,sitp->stmp/dot_general | solution.py:269
  85.4 2.0 select_select_fusion
  89.7 8.0 %all-gather = f32[8,128,128]{2,1,0:T(8,128)S(1)} all-gather(f32[2,128,128]{2,1,0:T(8,128)S(1)} %gather_fusion.1), channel_id=2, replica_groups=mesh['row'=8,'col'=4] {'col'}, dimensions={0}, use_global_device_ids=true | all-gather | bytes 655360 | tf_op jit(solution)/shard_map/all_gather | solution.py:319
  99.3 6.4 %collective-permute-start.13 = (f32[328,512]{1,0:T(8,128)S(1)}, f32[328,512]{1,0:T(8,128)S(1)}, u32[]{:S(2)}, u32[]{:S(2)}) collective-permute-start(f32[328,512]{1,0:T(8,128)S(1)} %select_maximum_fusion), channel_id=1, source_target_pairs={{0,0},{1,4},{2,8},{3,12},{4,16},{5,20},{6,24},{7,28},{8,1},{9,5},{... | collective-permute-start | bytes 2015240 | tf_op jit(solution)/shard_map/ppermute | solution.py:333
  106.2 2.0 gather_fusion.2
  108.3 27.0 %collective-permute-done.13 = f32[328,512]{1,0:T(8,128)S(1)} collective-permute-done((f32[328,512]{1,0:T(8,128)S(1)}, f32[328,512]{1,0:T(8,128)S(1)}, u32[]{:S(2)}, u32[]{:S(2)}) %collective-permute-start.13) | collective-permute-done | bytes 671776 | tf_op jit(solution)/shard_map/ppermute | solution.py:333
  136.2 2.9 constant_dynamic-slice_fusion
  139.2 14.0 %collective-permute-start.16 = (f32[8,128,128]{2,1,0:T(8,128)}, f32[8,128,128]{2,1,0:T(8,128)}, u32[]{:S(2)}, u32[]{:S(2)}) collective-permute-start(f32[8,128,128]{2,1,0:T(8,128)} %get-tuple-element.44), channel_id=1, source_target_pairs={{0,3},{1,0},{2,1},{3,2},{4,7},{5,4},{6,5},{7,6},{8,11},{9,8},{10,9... | collective-permute-start | bytes 1572872 | tf_op jit(solution)/shard_map/ppermute | solution.py:301
  153.3 59.8 %shard_map.85 = f32[512,512]{1,0:T(8,128)} custom-call(f32[512,512]{1,0:T(8,128)} %all-gather.11.cloned.1.call-done.a_ref), custom_call_target="tpu_custom_call" | custom-call | flops 107374182400 | bytes 2097152 | tf_op jit(solution)/shard_map/pallas_call | solution.py:93
  213.0 2.4 fusion.8
  215.5 2.9 shard_map.89
  220.3 5.7 %shard_map.86 = (f32[1024,512]{1,0:T(8,128)}, bf16[1024,512]{1,0:T(8,128)(2,1)}, bf16[1024,512]{1,0:T(8,128)(2,1)}) custom-call(f32[1024,512]{1,0:T(8,128)} %all-gather.7.cloned.1.call-done.x_ref, bf16[512,512]{1,0:T(8,128)(2,1)} %get-tuple-element.48.fhi_ref, bf16[512,512]{1,0:T(8,128)(2,1)} %get-tuple-element.47.flo_ref), custom_call_target="tpu_custom_call" | custom-call | flops 1610612736 | bytes 4194304 | tf_op jit(solution)/shard_map/pallas_call | solution.py:213
  226.0 3.0 pad_maximum_fusion
  229.0 3.6 %gather_fusion.3 = f32[4,8,128,128]{3,2,1,0:T(8,128)} fusion(f32[4,8,128,128]{3,2,1,0:T(8,128)} %pad_maximum_fusion, s32[1024]{0:T(1024)S(1)} %pad_clamp_fusion.2), kind=kCustom, calls=%fused_computation.3 | custom fusion | bytes 4194320 | tf_op jit(solution)/shard_map/gather | solution.py:303
  237.5 8.1 %shard_map.91 = (f32[512,512]{1,0:T(8,128)}, bf16[512,512]{1,0:T(8,128)(2,1)}, bf16[512,512]{1,0:T(8,128)(2,1)}) custom-call(f32[8,328,512]{2,1,0:T(8,128)} %bitcast.81, bf16[512,512]{1,0:T(8,128)(2,1)} %get-tuple-element.48.fhi_ref, bf16[512,512]{1,0:T(8,128)(2,1)} %get-tuple-element.47.flo_ref), custom_call_target="tpu_custom_call" | custom-call | flops 805306368 | bytes 2097152 | tf_op jit(solution)/shard_map/pallas_call | solution.py:213
  245.6 9.8 %shard_map.87 = (f32[2048,512]{1,0:T(8,128)}, bf16[2048,512]{1,0:T(8,128)(2,1)}, bf16[2048,512]{1,0:T(8,128)(2,1)}) custom-call(f32[8,328,512]{2,1,0:T(8,128)} %bitcast.82, bf16[512,512]{1,0:T(8,128)(2,1)} %get-tuple-element.48.fhi_ref, bf16[512,512]{1,0:T(8,128)(2,1)} %get-tuple-element.47.flo_ref), custom_call_target="tpu_custom_call" | custom-call | flops 3221225472 | bytes 8388608 | tf_op jit(solution)/shard_map/pallas_call | solution.py:213
  258.4 3.1 %gather_fusion.5 = bf16[16,128,512]{2,1,0:T(8,128)(2,1)} fusion(bf16[5,128,512]{2,1,0:T(8,128)(2,1)} %concatenate.50, s32[1024]{0:T(1024)S(1)} %pad_clamp_fusion), kind=kCustom, calls=%fused_computation.5 | custom fusion | bytes 4194368 | tf_op jit(solution)/shard_map/gather | solution.py:367
  261.5 2.0 gather_fusion.6
  266.7 12.3 %shard_map.88 = f32[1024,2048]{1,0:T(8,128)} custom-call(s32[8]{0:T(128)S(1)} %broadcast_31_flags_ref.2.flags_ref, s32[4]{0:T(128)S(1)} %get-tuple-element.61.info_ref, s32[1]{0:T(128)} %constant.134.clone.1.slots_ref, f32[1024,2048]{1,0:T(8,128)} %refs_0_.1, f32[1024,512]{1,0:T(8,128)S(1)} %copy-done.3, bf16[2048,512]{1,0:T(8,128)(2,1)S(1)} %copy-done.1, ...), custom_call_target="tpu_custom_call" | custom-call | flops 6442450944 | bytes 20971520 | tf_op jit(solution)/shard_map/pallas_call | solution.py:178
  279.0 10.7 %shard_map.90 = f32[1024,2048]{1,0:T(8,128)} custom-call(s32[8]{0:T(128)S(1)} %get-tuple-element.58.flags_ref, s32[4]{0:T(128)S(1)} %get-tuple-element.61.info_ref, s32[32]{0:T(128)S(1)} %select_n.302.slots_ref, f32[9,128,512]{2,1,0:T(8,128)} %concatenate.48.refs_0_.refs_1_.refs_2_.refs_3_, f32[9,128,512]{2,1,0:T(8,128)} %concatenate.48.refs_0_.refs_1_.refs_2_.refs_3_, ...), custom_call_target="tpu_custom_call" | custom-call | flops 6442450944 | bytes 20971520 | tf_op jit(solution)/shard_map/pallas_call | solution.py:178
  289.7 7.6 %shard_map.92 = f32[1024,2048]{1,0:T(8,128)} custom-call(s32[8]{0:T(128)S(1)} %get-tuple-element.58.flags_ref, s32[4]{0:T(128)S(1)} %get-tuple-element.60.info_ref, s32[1]{0:T(128)} %constant.134.clone.1.slots_ref, f32[1024,1]{1,0:T(8,128)S(1)} %copy.42.refs_0_, f32[1024,512]{1,0:T(8,128)S(1)} %bitcast.76, bf16[2048,512]{1,0:T(8,128)(2,1)S(1)} %bitcast.77, ...), custom_call_target="tpu_custom_call" | custom-call | flops 6442450944 | bytes 20971520 | tf_op jit(solution)/shard_map/pallas_call | solution.py:178
  (125 shorter events, 37.4 us)
Async XLA Ops:
  7.2 57.5 %all-gather.9.cloned.1.call-start = ((), (), s32[]{:S(2)}) async-start(), calls=%async_computation.1 | async-start | bytes 1179648 | tf_op jit(solution)/shard_map/all_gather | solution.py:280
  8.5 3.4 %collective-permute-start.9 = (f32[64,512]{1,0:T(8,128)S(1)}, f32[64,512]{1,0:T(8,128)S(1)}, u32[]{:S(2)}, u32[]{:S(2)}) collective-permute-start(f32[64,512]{1,0:T(8,128)S(1)} %get-tuple-element.33), channel_id=1, source_target_pairs={{0,4}} | collective-permute-start | bytes 393224 | tf_op jit(solution)/shard_map/ppermute | solution.py:278
  9.2 3.4 %collective-permute-start.8 = (f32[64,512]{1,0:T(8,128)S(1)}, f32[64,512]{1,0:T(8,128)S(1)}, u32[]{:S(2)}, u32[]{:S(2)}) collective-permute-start(f32[64,512]{1,0:T(8,128)S(1)} %get-tuple-element.34), channel_id=1, source_target_pairs={{0,8}} | collective-permute-start | bytes 393224 | tf_op jit(solution)/shard_map/ppermute | solution.py:278
  9.9 3.4 %collective-permute-start.7 = (f32[64,512]{1,0:T(8,128)S(1)}, f32[64,512]{1,0:T(8,128)S(1)}, u32[]{:S(2)}, u32[]{:S(2)}) collective-permute-start(f32[64,512]{1,0:T(8,128)S(1)} %get-tuple-element.35), channel_id=1, source_target_pairs={{0,12}} | collective-permute-start | bytes 393224 | tf_op jit(solution)/shard_map/ppermute | solution.py:278
  10.6 2.8 collective-permute-start.6
  11.2 2.1 collective-permute-start.5
  11.9 1.4 collective-permute-start.4
  12.6 0.8 collective-permute-start.3
  15.1 121.2 %all-gather.11.cloned.1.call-start = ((), (), s32[]{:S(2)}) async-start(), calls=%async_computation.2 | async-start | bytes 1310720 | tf_op jit(solution)/shard_map/all_gather | solution.py:285
  17.4 68.0 %collective-permute-start.2 = (f32[256,512]{1,0:T(8,128)}, f32[256,512]{1,0:T(8,128)S(1)}, u32[]{:S(2)}, u32[]{:S(2)}) collective-permute-start(f32[256,512]{1,0:T(8,128)} %get-tuple-element.40), channel_id=1, source_target_pairs={{0,1},{4,5},{8,9},{12,13},{16,17},{20,21},{24,25},{28,29}} | collective-permute-start | bytes 1572872 | tf_op jit(solution)/shard_map/ppermute | solution.py:327
  18.1 67.3 %collective-permute-start.1 = (f32[256,512]{1,0:T(8,128)S(1)}, f32[256,512]{1,0:T(8,128)S(1)}, u32[]{:S(2)}, u32[]{:S(2)}) collective-permute-start(f32[256,512]{1,0:T(8,128)S(1)} %get-tuple-element.41), channel_id=1, source_target_pairs={{0,2},{4,6},{8,10},{12,14},{16,18},{20,22},{24,26},{28,30}} | collective-permute-start | bytes 1572872 | tf_op jit(solution)/shard_map/ppermute | solution.py:327
  66.6 3.1 %collective-permute-start.12 = (f32[128,512]{1,0:T(8,128)}, f32[128,512]{1,0:T(8,128)S(1)}, u32[]{:S(2)}, u32[]{:S(2)}) collective-permute-start(f32[128,512]{1,0:T(8,128)} %get-tuple-element.49), channel_id=1, source_target_pairs={{0,1},{4,5},{8,9},{12,13},{16,17},{20,21},{24,25},{28,29}} | collective-permute-start | bytes 786440 | tf_op jit(solution)/shard_map/ppermute | solution.py:284
  67.2 8.3 %collective-permute-start.11 = (f32[128,512]{1,0:T(8,128)S(1)}, f32[128,512]{1,0:T(8,128)S(1)}, u32[]{:S(2)}, u32[]{:S(2)}) collective-permute-start(f32[128,512]{1,0:T(8,128)S(1)} %get-tuple-element.50), channel_id=1, source_target_pairs={{0,2},{4,6},{8,10},{12,14},{16,18},{20,22},{24,26},{28,30}} | collective-permute-start | bytes 786440 | tf_op jit(solution)/shard_map/ppermute | solution.py:284
  68.5 7.0 %collective-permute-start.10 = (f32[128,512]{1,0:T(8,128)S(1)}, f32[128,512]{1,0:T(8,128)S(1)}, u32[]{:S(2)}, u32[]{:S(2)}) collective-permute-start(f32[128,512]{1,0:T(8,128)S(1)} %get-tuple-element.51), channel_id=1, source_target_pairs={{0,3},{4,7},{8,11},{12,15},{16,19},{20,23},{24,27},{28,31}} | collective-permute-start | bytes 786440 | tf_op jit(solution)/shard_map/ppermute | solution.py:284
  69.7 15.7 %collective-permute-start = (f32[256,512]{1,0:T(8,128)S(1)}, f32[256,512]{1,0:T(8,128)}, u32[]{:S(2)}, u32[]{:S(2)}) collective-permute-start(f32[256,512]{1,0:T(8,128)S(1)} %get-tuple-element.42), channel_id=1, source_target_pairs={{0,3},{4,7},{8,11},{12,15},{16,19},{20,23},{24,27},{28,31}} | collective-permute-start | bytes 1572872 | tf_op jit(solution)/shard_map/ppermute | solution.py:327
  77.3 143.0 %all-gather.7.cloned.1.call-start = ((), (), s32[]{:S(2)}) async-start(), calls=%async_computation | async-start | bytes 2621440 | tf_op jit(solution)/shard_map/all_gather | solution.py:329
  87.5 148.7 %all-gather.13.cloned.1.call-start = ((), (), s32[]{:S(2)}) async-start(), calls=%async_computation.3 | async-start | bytes 6045696 | tf_op jit(solution)/shard_map/all_gather | solution.py:334
  89.0 10.3 %copy-start.4 = (f32[256,512]{1,0:T(8,128)S(1)}, f32[256,512]{1,0:T(8,128)}, u32[]{:S(2)}) copy-start(f32[256,512]{1,0:T(8,128)} %select_select_fusion) | copy-start | bytes 1572868
  99.3 36.0 %collective-permute-start.13 = (f32[328,512]{1,0:T(8,128)S(1)}, f32[328,512]{1,0:T(8,128)S(1)}, u32[]{:S(2)}, u32[]{:S(2)}) collective-permute-start(f32[328,512]{1,0:T(8,128)S(1)} %select_maximum_fusion), channel_id=1, source_target_pairs={{0,0},{1,4},{2,8},{3,12},{4,16},{5,20},{6,24},{7,28},{8,1},{9,5},{... | collective-permute-start | bytes 2015240 | tf_op jit(solution)/shard_map/ppermute | solution.py:333
  139.2 86.9 %collective-permute-start.16 = (f32[8,128,128]{2,1,0:T(8,128)}, f32[8,128,128]{2,1,0:T(8,128)}, u32[]{:S(2)}, u32[]{:S(2)}) collective-permute-start(f32[8,128,128]{2,1,0:T(8,128)} %get-tuple-element.44), channel_id=1, source_target_pairs={{0,3},{1,0},{2,1},{3,2},{4,7},{5,4},{6,5},{7,6},{8,11},{9,8},{10,9... | collective-permute-start | bytes 1572872 | tf_op jit(solution)/shard_map/ppermute | solution.py:301
  153.1 72.9 %collective-permute-start.15 = (f32[8,128,128]{2,1,0:T(8,128)}, f32[8,128,128]{2,1,0:T(8,128)}, u32[]{:S(2)}, u32[]{:S(2)}) collective-permute-start(f32[8,128,128]{2,1,0:T(8,128)} %get-tuple-element.45), channel_id=1, source_target_pairs={{0,2},{1,3},{2,0},{3,1},{4,6},{5,7},{6,4},{7,5},{8,10},{9,11},{10,... | collective-permute-start | bytes 1572872 | tf_op jit(solution)/shard_map/ppermute | solution.py:301
  153.1 72.9 %collective-permute-start.14 = (f32[8,128,128]{2,1,0:T(8,128)}, f32[8,128,128]{2,1,0:T(8,128)}, u32[]{:S(2)}, u32[]{:S(2)}) collective-permute-start(f32[8,128,128]{2,1,0:T(8,128)} %get-tuple-element.46), channel_id=1, source_target_pairs={{0,1},{1,2},{2,3},{3,0},{4,5},{5,6},{6,7},{7,4},{8,9},{9,10},{10,1... | collective-permute-start | bytes 1572872 | tf_op jit(solution)/shard_map/ppermute | solution.py:301
  266.7 12.3 %copy-start.2 = (bf16[2048,512]{1,0:T(8,128)(2,1)S(1)}, bf16[2048,512]{1,0:T(8,128)(2,1)}, u32[]{:S(2)}) copy-start(bf16[2048,512]{1,0:T(8,128)(2,1)} %get-tuple-element.26.refs_2_.refs_5_) | copy-start | bytes 6291460
  279.0 10.7 %copy-start = (bf16[16,128,512]{2,1,0:T(8,128)(2,1)S(1)}, bf16[16,128,512]{2,1,0:T(8,128)(2,1)}, u32[]{:S(2)}) copy-start(bf16[16,128,512]{2,1,0:T(8,128)(2,1)} %gather_fusion.5) | copy-start | bytes 6291460
  (8 other events, 42.4 us)
Sparse Core Ops, SparseCore 0:
  15.2 49.4 all-gather.8
  77.4 17.7 all-gather.10
  97.3 34.9 all-gather.6
  136.3 99.3 all-gather.12

commit v17 on v16

--- a/solution.py
+++ b/solution.py
@@ -150,7 +150,7 @@
 
 
 def panel_update(kind, base, a, b_hi, b_lo, flags, info, slots, rows, width):
-    tm = MSLOT if kind == "gather" or rows % (2 * MSLOT) else 2 * MSLOT
+    tm = MSLOT if kind == "gather" or rows % (4 * MSLOT) else 4 * MSLOT
     nseg = width // PANEL
     if kind == "gather":
         bases = [base] * nseg

time: 307 us -> 310 us (level)
  transfers between devices with their start and end apart: 21 -> 21, of which waited for: 3 -> 3; matrix products, arithmetic and copies ran while one was open for 13% -> 13% of each run, Pallas kernels for 23% -> 22%
where the time goes in v17:
time: 310 us; the launch traced here: 306 us
  Pallas kernels  118 us (38%)
  waiting for transfers between devices  76.7 us (25%)
  local copies, waits for them, and re-layouts  34.6 us (11%)
  starting transfers between devices  31.4 us (10%)
  other arithmetic  14.9 us (5%)
  between operations  14.3 us (5%)
  blocking collectives  7.96 us (3%)
  matrix products  7.19 us (2%)
    pallas_call x1, Pallas kernels, chol_inverse(): pl.pallas_call(chol_inv_kernel, out_shape=jax.ShapeDtypeStruct((n, n), jn...  59.8 us
    all_gather x1, waiting for transfers between devices, per_device(): kpp_col0 = lax.all_gather(kpp_part, 'row', axis=0, tiled=True)  45.2 us
    pallas_call x3, Pallas kernels, panel_update(): pl.pallas_call(functools.partial(update_kernel, kind, tm, width, len(base...  32.2 us
    ppermute x1, waiting for transfers between devices, per_device(): b_slice = lax.ppermute(payload, AXES, perm)  27 us
    pallas_call x4, Pallas kernels, apply_inverse(): pl.pallas_call(solve_kernel, grid=(grid,), in_specs=[x_spec, pl.BlockSpec...  26.5 us
    ppermute x3, starting transfers between devices, per_device(): lax.ppermute(out_k, 'col', [(i, (i + k) % C) for i in range(C)])  14.1 us
    all_gather x1, blocking collectives, per_device(): z_all = lax.all_gather(z_local, 'col', axis=0, tiled=False)  7.96 us
    dot_general x1, matrix products, per_device(): jnp.einsum('sim,sitp->stmp', eigvecs, coupling, preferred_element_type=jn...  7.19 us
  transfers between devices with their start and end apart: 21, of which 3 were waited for; matrix products, arithmetic and copies ran while one was open for 13% of the time, Pallas kernels for 22%

profile of v17, /device:TPU:6, one launch (start us, length us, event | category | flops | bytes accessed | tf_op | source)
XLA Modules:
  0.0 305.5 jit_solution(4968293972889986077)
XLA Ops:
  15.1 2.3 fusion.29
  19.5 45.2 %all-gather.9.cloned.1.call-done = f32[512,512]{1,0:T(8,128)} async-done(((f32[64,512]{1,0:T(8,128)}), f32[512,512]{1,0:T(8,128)}) %all-gather.9.cloned.1.call-update) | async-done | bytes 1048592 | tf_op jit(solution)/shard_map/all_gather | solution.py:280
  71.1 4.4 %collective-permute-done.11 = f32[128,512]{1,0:T(8,128)S(1)} collective-permute-done((f32[128,512]{1,0:T(8,128)S(1)}, f32[128,512]{1,0:T(8,128)S(1)}, u32[]{:S(2)}, u32[]{:S(2)}) %collective-permute-start.11) | collective-permute-done | bytes 262176 | tf_op jit(solution)/shard_map/ppermute | solution.py:284
  77.3 7.2 %fusion.3 = f32[8,2,128,128]{3,2,1,0:T(8,128)S(1)} fusion(bf16[8,2048,128]{2,1,0:T(8,128)(2,1)} %param.8, bf16[8,2048,2,128]{3,2,1,0:T(2,128)(2,1)} %param.9, f32[8,128]{1,0:T(8,128)S(1)} %fusion.16), kind=kOutput, calls=%fused_computation.14 | convolution fusion | flops 1074003968 | bytes 13635584 | tf_op jit(solution)/shard_map/sim,sitp->stmp/dot_general | solution.py:269
  85.4 2.0 select_select_fusion
  89.7 8.0 %all-gather = f32[8,128,128]{2,1,0:T(8,128)S(1)} all-gather(f32[2,128,128]{2,1,0:T(8,128)S(1)} %gather_fusion.1), channel_id=2, replica_groups=mesh['row'=8,'col'=4] {'col'}, dimensions={0}, use_global_device_ids=true | all-gather | bytes 655360 | tf_op jit(solution)/shard_map/all_gather | solution.py:319
  99.3 6.4 %collective-permute-start.13 = (f32[328,512]{1,0:T(8,128)S(1)}, f32[328,512]{1,0:T(8,128)S(1)}, u32[]{:S(2)}, u32[]{:S(2)}) collective-permute-start(f32[328,512]{1,0:T(8,128)S(1)} %select_maximum_fusion), channel_id=1, source_target_pairs={{0,0},{1,4},{2,8},{3,12},{4,16},{5,20},{6,24},{7,28},{8,1},{9,5},{... | collective-permute-start | bytes 2015240 | tf_op jit(solution)/shard_map/ppermute | solution.py:333
  106.2 2.0 gather_fusion.2
  108.3 27.0 %collective-permute-done.13 = f32[328,512]{1,0:T(8,128)S(1)} collective-permute-done((f32[328,512]{1,0:T(8,128)S(1)}, f32[328,512]{1,0:T(8,128)S(1)}, u32[]{:S(2)}, u32[]{:S(2)}) %collective-permute-start.13) | collective-permute-done | bytes 671776 | tf_op jit(solution)/shard_map/ppermute | solution.py:333
  136.2 2.9 constant_dynamic-slice_fusion
  139.2 14.0 %collective-permute-start.16 = (f32[8,128,128]{2,1,0:T(8,128)}, f32[8,128,128]{2,1,0:T(8,128)}, u32[]{:S(2)}, u32[]{:S(2)}) collective-permute-start(f32[8,128,128]{2,1,0:T(8,128)} %get-tuple-element.44), channel_id=1, source_target_pairs={{0,3},{1,0},{2,1},{3,2},{4,7},{5,4},{6,5},{7,6},{8,11},{9,8},{10,9... | collective-permute-start | bytes 1572872 | tf_op jit(solution)/shard_map/ppermute | solution.py:301
  153.3 59.8 %shard_map.85 = f32[512,512]{1,0:T(8,128)} custom-call(f32[512,512]{1,0:T(8,128)} %all-gather.11.cloned.1.call-done.a_ref), custom_call_target="tpu_custom_call" | custom-call | flops 107374182400 | bytes 2097152 | tf_op jit(solution)/shard_map/pallas_call | solution.py:93
  213.0 2.4 fusion.8
  215.5 2.9 shard_map.89
  220.3 5.7 %shard_map.86 = (f32[1024,512]{1,0:T(8,128)}, bf16[1024,512]{1,0:T(8,128)(2,1)}, bf16[1024,512]{1,0:T(8,128)(2,1)}) custom-call(f32[1024,512]{1,0:T(8,128)} %all-gather.7.cloned.1.call-done.x_ref, bf16[512,512]{1,0:T(8,128)(2,1)} %get-tuple-element.48.fhi_ref, bf16[512,512]{1,0:T(8,128)(2,1)} %get-tuple-element.47.flo_ref), custom_call_target="tpu_custom_call" | custom-call | flops 1610612736 | bytes 4194304 | tf_op jit(solution)/shard_map/pallas_call | solution.py:213
  226.0 3.0 pad_maximum_fusion
  229.0 3.6 %gather_fusion.3 = f32[4,8,128,128]{3,2,1,0:T(8,128)} fusion(f32[4,8,128,128]{3,2,1,0:T(8,128)} %pad_maximum_fusion, s32[1024]{0:T(1024)S(1)} %pad_clamp_fusion.2), kind=kCustom, calls=%fused_computation.3 | custom fusion | bytes 4194320 | tf_op jit(solution)/shard_map/gather | solution.py:303
  237.5 8.1 %shard_map.91 = (f32[512,512]{1,0:T(8,128)}, bf16[512,512]{1,0:T(8,128)(2,1)}, bf16[512,512]{1,0:T(8,128)(2,1)}) custom-call(f32[8,328,512]{2,1,0:T(8,128)} %bitcast.81, bf16[512,512]{1,0:T(8,128)(2,1)} %get-tuple-element.48.fhi_ref, bf16[512,512]{1,0:T(8,128)(2,1)} %get-tuple-element.47.flo_ref), custom_call_target="tpu_custom_call" | custom-call | flops 805306368 | bytes 2097152 | tf_op jit(solution)/shard_map/pallas_call | solution.py:213
  245.6 9.8 %shard_map.87 = (f32[2048,512]{1,0:T(8,128)}, bf16[2048,512]{1,0:T(8,128)(2,1)}, bf16[2048,512]{1,0:T(8,128)(2,1)}) custom-call(f32[8,328,512]{2,1,0:T(8,128)} %bitcast.82, bf16[512,512]{1,0:T(8,128)(2,1)} %get-tuple-element.48.fhi_ref, bf16[512,512]{1,0:T(8,128)(2,1)} %get-tuple-element.47.flo_ref), custom_call_target="tpu_custom_call" | custom-call | flops 3221225472 | bytes 8388608 | tf_op jit(solution)/shard_map/pallas_call | solution.py:213
  258.4 3.1 %gather_fusion.5 = bf16[16,128,512]{2,1,0:T(8,128)(2,1)} fusion(bf16[5,128,512]{2,1,0:T(8,128)(2,1)} %concatenate.50, s32[1024]{0:T(1024)S(1)} %pad_clamp_fusion), kind=kCustom, calls=%fused_computation.5 | custom fusion | bytes 4194368 | tf_op jit(solution)/shard_map/gather | solution.py:367
  261.5 2.0 gather_fusion.6
  266.7 12.5 %shard_map.88 = f32[1024,2048]{1,0:T(8,128)} custom-call(s32[8]{0:T(128)S(1)} %broadcast_31_flags_ref.2.flags_ref, s32[4]{0:T(128)S(1)} %get-tuple-element.61.info_ref, s32[1]{0:T(128)} %constant.134.clone.1.slots_ref, f32[1024,2048]{1,0:T(8,128)} %refs_0_.1, f32[1024,512]{1,0:T(8,128)S(1)} %copy-done.3, bf16[2048,512]{1,0:T(8,128)(2,1)S(1)} %copy-done.1, ...), custom_call_target="tpu_custom_call" | custom-call | flops 6442450944 | bytes 20971520 | tf_op jit(solution)/shard_map/pallas_call | solution.py:178
  279.2 10.5 %shard_map.90 = f32[1024,2048]{1,0:T(8,128)} custom-call(s32[8]{0:T(128)S(1)} %get-tuple-element.58.flags_ref, s32[4]{0:T(128)S(1)} %get-tuple-element.61.info_ref, s32[32]{0:T(128)S(1)} %select_n.302.slots_ref, f32[9,128,512]{2,1,0:T(8,128)} %concatenate.48.refs_0_.refs_1_.refs_2_.refs_3_, f32[9,128,512]{2,1,0:T(8,128)} %concatenate.48.refs_0_.refs_1_.refs_2_.refs_3_, ...), custom_call_target="tpu_custom_call" | custom-call | flops 6442450944 | bytes 20971520 | tf_op jit(solution)/shard_map/pallas_call | solution.py:178
  289.7 9.2 %shard_map.92 = f32[1024,2048]{1,0:T(8,128)} custom-call(s32[8]{0:T(128)S(1)} %get-tuple-element.58.flags_ref, s32[4]{0:T(128)S(1)} %get-tuple-element.60.info_ref, s32[1]{0:T(128)} %constant.134.clone.1.slots_ref, f32[1024,1]{1,0:T(8,128)S(1)} %copy.42.refs_0_, f32[1024,512]{1,0:T(8,128)S(1)} %bitcast.76, bf16[2048,512]{1,0:T(8,128)(2,1)S(1)} %bitcast.77, ...), custom_call_target="tpu_custom_call" | custom-call | flops 6442450944 | bytes 20971520 | tf_op jit(solution)/shard_map/pallas_call | solution.py:178
  (125 shorter events, 37.4 us)
Async XLA Ops:
  7.2 57.5 %all-gather.9.cloned.1.call-start = ((), (), s32[]{:S(2)}) async-start(), calls=%async_computation.1 | async-start | bytes 1179648 | tf_op jit(solution)/shard_map/all_gather | solution.py:280
  8.5 3.4 %collective-permute-start.9 = (f32[64,512]{1,0:T(8,128)S(1)}, f32[64,512]{1,0:T(8,128)S(1)}, u32[]{:S(2)}, u32[]{:S(2)}) collective-permute-start(f32[64,512]{1,0:T(8,128)S(1)} %get-tuple-element.33), channel_id=1, source_target_pairs={{0,4}} | collective-permute-start | bytes 393224 | tf_op jit(solution)/shard_map/ppermute | solution.py:278
  9.2 3.4 %collective-permute-start.8 = (f32[64,512]{1,0:T(8,128)S(1)}, f32[64,512]{1,0:T(8,128)S(1)}, u32[]{:S(2)}, u32[]{:S(2)}) collective-permute-start(f32[64,512]{1,0:T(8,128)S(1)} %get-tuple-element.34), channel_id=1, source_target_pairs={{0,8}} | collective-permute-start | bytes 393224 | tf_op jit(solution)/shard_map/ppermute | solution.py:278
  9.9 3.4 %collective-permute-start.7 = (f32[64,512]{1,0:T(8,128)S(1)}, f32[64,512]{1,0:T(8,128)S(1)}, u32[]{:S(2)}, u32[]{:S(2)}) collective-permute-start(f32[64,512]{1,0:T(8,128)S(1)} %get-tuple-element.35), channel_id=1, source_target_pairs={{0,12}} | collective-permute-start | bytes 393224 | tf_op jit(solution)/shard_map/ppermute | solution.py:278
  10.6 2.8 collective-permute-start.6
  11.2 2.1 collective-permute-start.5
  11.9 1.4 collective-permute-start.4
  12.6 0.8 collective-permute-start.3
  15.1 121.2 %all-gather.11.cloned.1.call-start = ((), (), s32[]{:S(2)}) async-start(), calls=%async_computation.2 | async-start | bytes 1310720 | tf_op jit(solution)/shard_map/all_gather | solution.py:285
  17.4 68.0 %collective-permute-start.2 = (f32[256,512]{1,0:T(8,128)}, f32[256,512]{1,0:T(8,128)S(1)}, u32[]{:S(2)}, u32[]{:S(2)}) collective-permute-start(f32[256,512]{1,0:T(8,128)} %get-tuple-element.40), channel_id=1, source_target_pairs={{0,1},{4,5},{8,9},{12,13},{16,17},{20,21},{24,25},{28,29}} | collective-permute-start | bytes 1572872 | tf_op jit(solution)/shard_map/ppermute | solution.py:327
  18.1 67.3 %collective-permute-start.1 = (f32[256,512]{1,0:T(8,128)S(1)}, f32[256,512]{1,0:T(8,128)S(1)}, u32[]{:S(2)}, u32[]{:S(2)}) collective-permute-start(f32[256,512]{1,0:T(8,128)S(1)} %get-tuple-element.41), channel_id=1, source_target_pairs={{0,2},{4,6},{8,10},{12,14},{16,18},{20,22},{24,26},{28,30}} | collective-permute-start | bytes 1572872 | tf_op jit(solution)/shard_map/ppermute | solution.py:327
  66.6 3.1 %collective-permute-start.12 = (f32[128,512]{1,0:T(8,128)}, f32[128,512]{1,0:T(8,128)S(1)}, u32[]{:S(2)}, u32[]{:S(2)}) collective-permute-start(f32[128,512]{1,0:T(8,128)} %get-tuple-element.49), channel_id=1, source_target_pairs={{0,1},{4,5},{8,9},{12,13},{16,17},{20,21},{24,25},{28,29}} | collective-permute-start | bytes 786440 | tf_op jit(solution)/shard_map/ppermute | solution.py:284
  67.2 8.3 %collective-permute-start.11 = (f32[128,512]{1,0:T(8,128)S(1)}, f32[128,512]{1,0:T(8,128)S(1)}, u32[]{:S(2)}, u32[]{:S(2)}) collective-permute-start(f32[128,512]{1,0:T(8,128)S(1)} %get-tuple-element.50), channel_id=1, source_target_pairs={{0,2},{4,6},{8,10},{12,14},{16,18},{20,22},{24,26},{28,30}} | collective-permute-start | bytes 786440 | tf_op jit(solution)/shard_map/ppermute | solution.py:284
  68.5 7.0 %collective-permute-start.10 = (f32[128,512]{1,0:T(8,128)S(1)}, f32[128,512]{1,0:T(8,128)S(1)}, u32[]{:S(2)}, u32[]{:S(2)}) collective-permute-start(f32[128,512]{1,0:T(8,128)S(1)} %get-tuple-element.51), channel_id=1, source_target_pairs={{0,3},{4,7},{8,11},{12,15},{16,19},{20,23},{24,27},{28,31}} | collective-permute-start | bytes 786440 | tf_op jit(solution)/shard_map/ppermute | solution.py:284
  69.7 15.7 %collective-permute-start = (f32[256,512]{1,0:T(8,128)S(1)}, f32[256,512]{1,0:T(8,128)}, u32[]{:S(2)}, u32[]{:S(2)}) collective-permute-start(f32[256,512]{1,0:T(8,128)S(1)} %get-tuple-element.42), channel_id=1, source_target_pairs={{0,3},{4,7},{8,11},{12,15},{16,19},{20,23},{24,27},{28,31}} | collective-permute-start | bytes 1572872 | tf_op jit(solution)/shard_map/ppermute | solution.py:327
  77.3 143.0 %all-gather.7.cloned.1.call-start = ((), (), s32[]{:S(2)}) async-start(), calls=%async_computation | async-start | bytes 2621440 | tf_op jit(solution)/shard_map/all_gather | solution.py:329
  87.5 148.7 %all-gather.13.cloned.1.call-start = ((), (), s32[]{:S(2)}) async-start(), calls=%async_computation.3 | async-start | bytes 6045696 | tf_op jit(solution)/shard_map/all_gather | solution.py:334
  89.0 10.3 %copy-start.4 = (f32[256,512]{1,0:T(8,128)S(1)}, f32[256,512]{1,0:T(8,128)}, u32[]{:S(2)}) copy-start(f32[256,512]{1,0:T(8,128)} %select_select_fusion) | copy-start | bytes 1572868
  99.3 36.0 %collective-permute-start.13 = (f32[328,512]{1,0:T(8,128)S(1)}, f32[328,512]{1,0:T(8,128)S(1)}, u32[]{:S(2)}, u32[]{:S(2)}) collective-permute-start(f32[328,512]{1,0:T(8,128)S(1)} %select_maximum_fusion), channel_id=1, source_target_pairs={{0,0},{1,4},{2,8},{3,12},{4,16},{5,20},{6,24},{7,28},{8,1},{9,5},{... | collective-permute-start | bytes 2015240 | tf_op jit(solution)/shard_map/ppermute | solution.py:333
  139.2 86.9 %collective-permute-start.16 = (f32[8,128,128]{2,1,0:T(8,128)}, f32[8,128,128]{2,1,0:T(8,128)}, u32[]{:S(2)}, u32[]{:S(2)}) collective-permute-start(f32[8,128,128]{2,1,0:T(8,128)} %get-tuple-element.44), channel_id=1, source_target_pairs={{0,3},{1,0},{2,1},{3,2},{4,7},{5,4},{6,5},{7,6},{8,11},{9,8},{10,9... | collective-permute-start | bytes 1572872 | tf_op jit(solution)/shard_map/ppermute | solution.py:301
  153.1 72.9 %collective-permute-start.15 = (f32[8,128,128]{2,1,0:T(8,128)}, f32[8,128,128]{2,1,0:T(8,128)}, u32[]{:S(2)}, u32[]{:S(2)}) collective-permute-start(f32[8,128,128]{2,1,0:T(8,128)} %get-tuple-element.45), channel_id=1, source_target_pairs={{0,2},{1,3},{2,0},{3,1},{4,6},{5,7},{6,4},{7,5},{8,10},{9,11},{10,... | collective-permute-start | bytes 1572872 | tf_op jit(solution)/shard_map/ppermute | solution.py:301
  153.1 72.9 %collective-permute-start.14 = (f32[8,128,128]{2,1,0:T(8,128)}, f32[8,128,128]{2,1,0:T(8,128)}, u32[]{:S(2)}, u32[]{:S(2)}) collective-permute-start(f32[8,128,128]{2,1,0:T(8,128)} %get-tuple-element.46), channel_id=1, source_target_pairs={{0,1},{1,2},{2,3},{3,0},{4,5},{5,6},{6,7},{7,4},{8,9},{9,10},{10,1... | collective-permute-start | bytes 1572872 | tf_op jit(solution)/shard_map/ppermute | solution.py:301
  266.7 12.5 %copy-start.2 = (bf16[2048,512]{1,0:T(8,128)(2,1)S(1)}, bf16[2048,512]{1,0:T(8,128)(2,1)}, u32[]{:S(2)}) copy-start(bf16[2048,512]{1,0:T(8,128)(2,1)} %get-tuple-element.26.refs_2_.refs_5_) | copy-start | bytes 6291460
  279.2 10.5 %copy-start = (bf16[16,128,512]{2,1,0:T(8,128)(2,1)S(1)}, bf16[16,128,512]{2,1,0:T(8,128)(2,1)}, u32[]{:S(2)}) copy-start(bf16[16,128,512]{2,1,0:T(8,128)(2,1)} %gather_fusion.5) | copy-start | bytes 6291460
  (8 other events, 42.4 us)
Sparse Core Ops, SparseCore 0:
  15.2 49.4 all-gather.8
  77.4 17.7 all-gather.10
  97.3 34.9 all-gather.6
  136.3 99.3 all-gather.12
